TPU v7x, 128 devices: a whole 4x4x4 slice. The times are simulated.
128 devices in a mesh: req: 32 (over x, z, core), tp: 4 (over y).
Axes of the slice: x: 4, y: 4, z: 4, core: 2. Of those that a mesh axis runs over, the one named last changes fastest.
Arguments:
- hidden: bfloat16 [8192, 2048], P('req', 'tp'), may hold values from -45 to 45
- routes: int32 [8192, 2], P('req'), may hold values from 0 to 7, all different within a row; in each aligned block of 256 rows (0 to 255, 256 to 511, ...) at most 128 rows name the same one
- route_weights: float32 [8192, 2], P('req'), may hold values from 0.2 to 1
- pre_gain: float32 [2048], replicated, may hold values from 0.1 to 1.9
- out_gain: float32 [2048], P('tp'), may hold values from 0.1 to 1.9
- gate_weight: bfloat16 [32, 2048, 5632], P('req', None, 'tp'), as said below
- up_weight: bfloat16 [32, 2048, 5632], P('req', None, 'tp'), as said below
- down_weight: bfloat16 [32, 5632, 2048], P('req', 'tp'), as said below
Outputs:
- residual_out: bfloat16 [8192, 2048], P('req', 'tp')
- normed_out: bfloat16 [8192, 2048], P('req', 'tp')
Inputs may be any that keep to these rules, and one draw needn't show every extreme that they name: `routes`: each row names 2 different experts; in the rows of one index of req no expert is named by more than 128 rows, a bound that some block reaches. `gate_weight`: index r holds expert r % 8. `up_weight`: index r holds expert r % 8. `down_weight`: index r holds expert r % 8.
All inputs are finite; a program needn't handle non-finite values.
Results may differ from a plain program's by a relative error of at most 0.007.
Values may be sent and summed in bfloat16 or wider, within the bound.
No kernel may reach another device: no remote copies, remote signals or barrier semaphores. Data moves between devices by JAX's collectives and lax.ppermute only.
A program may use at most 128 MiB of HBM per device.

v0:
```python
import jax
import jax.numpy as jnp
from jax import lax
from jax.sharding import PartitionSpec as P

E = 8
CAP = 128


epsilon = 1e-05


def shards(hidden, routes, route_weights, pre_gain, out_gain, gate_weight, up_weight, down_weight):
    row_count, col_part = hidden.shape
    tp_count = lax.axis_size("tp")
    req_count = lax.axis_size("req")
    full_width = col_part * tp_count
    copies = req_count // E
    slot_count = CAP // copies
    stream = hidden.astype(jnp.float32)
    whole_rows = lax.all_gather(hidden, "tp", axis=1, tiled=True).astype(jnp.float32)
    meansq = jnp.sum(whole_rows * whole_rows, axis=1) / full_width
    normed_in = (whole_rows * lax.rsqrt(meansq + epsilon)[:, None] * pre_gain[None, :]).astype(
        jnp.bfloat16
    )
    send_cols = normed_in.shape[1]
    chosen = routes.reshape(-1)
    onehot = (chosen[:, None] == jnp.arange(E, dtype=jnp.int32)[None, :]).astype(jnp.int32)
    slot_rank = jnp.sum((jnp.cumsum(onehot, axis=0) - 1) * onehot, axis=1)
    position = chosen * CAP + slot_rank
    entry_rows = jnp.arange(chosen.shape[0], dtype=jnp.int32) // routes.shape[1]
    slot_row = jnp.zeros((E * CAP,), jnp.int32).at[position].set(entry_rows)
    slot_live = jnp.zeros((E * CAP,), jnp.bool_).at[position].set(True)
    outgoing = jnp.where(slot_live[:, None], normed_in[slot_row], jnp.zeros((), jnp.bfloat16))
    outgoing = outgoing.reshape(E, slot_count, copies, send_cols).transpose(2, 0, 1, 3)
    outgoing = outgoing.reshape(req_count, slot_count, send_cols)
    pieces = lax.all_to_all(outgoing, "req", split_axis=0, concat_axis=0, tiled=True)
    sources, items, widths = pieces.shape
    flat_rows = pieces.reshape(sources * items, widths)
    gate_val = jnp.dot(flat_rows, gate_weight[0], preferred_element_type=jnp.float32)
    up_val = jnp.dot(flat_rows, up_weight[0], preferred_element_type=jnp.float32)
    activ = (jax.nn.silu(gate_val) * up_val).astype(jnp.bfloat16)
    partial_out = jnp.dot(activ, down_weight[0], preferred_element_type=jnp.float32)
    partial_out = lax.optimization_barrier(partial_out.astype(jnp.bfloat16)).astype(jnp.float32)
    summed = lax.psum_scatter(
        partial_out.reshape(sources, items, widths).astype(jnp.bfloat16),
        "tp",
        scatter_dimension=2,
        tiled=True,
    )
    returned = lax.all_to_all(summed, "req", split_axis=0, concat_axis=0, tiled=True)
    returned = returned.reshape(copies, E, slot_count, col_part).transpose(1, 2, 0, 3)
    returned = returned.reshape(E * CAP, col_part)
    picked = returned[position].reshape(row_count, routes.shape[1], col_part).astype(jnp.float32)
    mixed = jnp.sum(picked * route_weights[:, :, None], axis=1)
    total_stream = stream + mixed
    out_sums = lax.psum(jnp.sum(total_stream * total_stream, axis=1), "tp")
    normed_out = (
        total_stream * lax.rsqrt(out_sums / full_width + epsilon)[:, None] * out_gain[None, :]
    )
    return (total_stream.astype(jnp.bfloat16), normed_out.astype(jnp.bfloat16))


def solution(mesh):
    return jax.shard_map(
        shards,
        mesh=mesh,
        in_specs=(
            P("req", "tp"),
            P("req", None),
            P("req", None),
            P(),
            P("tp"),
            P("req", None, "tp"),
            P("req", None, "tp"),
            P("req", "tp", None),
        ),
        out_specs=(P("req", "tp"), P("req", "tp")),
        check_vma=False,
    )
```

profile of v0, /device:TPU:1, one launch (start us, length us, event | category | flops | bytes accessed | tf_op | source)
XLA Modules:
  0.0 240.4 jit_solution(10688515270769743538)
XLA Ops:
  7.2 0.7 all-gather.2.cloned.1.call-update
  7.9 0.8 copy.13
  9.1 1.1 reduce-window.6
  10.5 0.7 broadcast_multiply_fusion
  11.6 2.4 %scatter_custom_fusion.1 = s32[1024]{0:T(1024)S(1)} fusion(s32[512]{0:T(512)S(1)} %bitcast.42, s32[512]{0:T(512)S(1)} %add_select_fusion, s32[]{:T(128)} %constant.37.clone.1), kind=kCustom, calls=%fused_computation.41 | custom fusion | bytes 4100 | tf_op jit(solution)/shard_map/scatter | solution.py:32
  14.0 2.4 %scatter_custom_fusion = pred[1024]{0:T(1024)(128)(4,1)S(1)} fusion(s32[512]{0:T(512)S(1)} %bitcast.43, pred[512]{0:T(512)(128)(4,1)S(1)} %broadcast.99, pred[]{:T(512)} %constant.20.clone.1), kind=kCustom, calls=%fused_computation.44 | custom fusion | bytes 1025 | tf_op jit(solution)/shard_map/scatter | solution.py:33
  16.8 19.2 %all-gather.2.cloned.1.call-done = bf16[256,2048]{1,0:T(8,128)(2,1)} async-done(((bf16[256,512]{1,0:T(8,128)(2,1)}), bf16[256,2048]{1,0:T(8,128)(2,1)}) %all-gather.2.cloned.1.call-update) | async-done | bytes 1048592 | tf_op jit(solution)/shard_map/all_gather | solution.py:21
  36.0 1.5 fusion.16
  37.5 1.5 fusion.18
  39.0 6.0 %gather_fusion = bf16[1024,2048]{1,0:T(8,128)(2,1)} fusion(bf16[256,2048]{1,0:T(8,128)(2,1)S(1)} %fusion.18, s32[1024]{0:T(1024)S(1)} %fusion.22), kind=kCustom, calls=%fused_computation | custom fusion | bytes 8392704 | tf_op jit(solution)/shard_map/gather | solution.py:34
  45.1 7.2 %gather.9 = bf16[8,32,4,2048]{3,2,1,0:T(4,128)(2,1)} reshape(bf16[1024,2048]{1,0:T(8,128)(2,1)} %gather_fusion) | data formatting | bytes 8388608 | tf_op jit(solution)/shard_map/gather | solution.py:34
  52.3 8.5 %copy_select_fusion = bf16[8,32,4,2048]{3,1,0,2:T(8,128)(2,1)S(1)} fusion(bf16[8,32,4,2048]{3,2,1,0:T(4,128)(2,1)} %gather.9, pred[8,32,4]{1,0,2:T(8,128)(4,1)S(1)} %copy.15), kind=kLoop, calls=%fused_computation.11 | loop fusion | flops 2097152 | bytes 8389632 | tf_op jit(solution)/shard_map/jit(_where)/select_n | solution.py:34
  60.7 59.0 %all_to_all.10 = bf16[32,32,2048]{2,1,0:T(8,128)(2,1)S(1)} all-to-all(bf16[32,32,2048]{2,1,0:T(8,128)(2,1)S(1)} %bitcast.36), channel_id=1, replica_groups=mesh['req'=32,'tp'=4] {'req'}, dimensions={0} | all-to-all | bytes 8388608 | tf_op jit(solution)/shard_map/all_to_all | solution.py:37
  119.7 2.1 copy-done
  121.8 10.2 %fusion.4 = f32[1024,1408]{1,0:T(8,128)} fusion(bf16[1024,2048]{1,0:T(8,128)(2,1)S(1)} %bitcast.38, bf16[1,2048,1408]{2,1,0:T(8,128)(2,1)} %param.13), kind=kOutput, calls=%fused_computation.8 | convolution fusion | flops 5905580032 | bytes 15728640 | tf_op jit(solution)/shard_map/dot_general | solution.py:40
  132.0 20.6 %fusion.10 = bf16[1024,2048]{1,0:T(8,128)(2,1)} fusion(bf16[1,1408,2048]{2,1,0:T(8,128)(2,1)} %param.15, f32[1024,1408]{1,0:T(8,128)} %fusion.4, bf16[1024,2048]{1,0:T(8,128)(2,1)} %bitcast.39, bf16[1,2048,1408]{2,1,0:T(8,128)(2,1)} %param.14), kind=kOutput, calls=%fused_computation.12 | convolution fusion | flops 11821907968 | bytes 25690112 | tf_op jit(solution)/shard_map/dot_general | solution.py:43
  152.7 43.6 %reduce-scatter.2.cloned.1.call-done = bf16[32,32,512]{2,1,0:T(8,128)(2,1)} async-done(((bf16[32,32,2048]{2,1,0:T(8,128)(2,1)}), bf16[32,32,512]{2,1,0:T(8,128)(2,1)}) %reduce-scatter.2.cloned.1.call-update) | async-done | bytes 1048592 | tf_op jit(solution)/shard_map/reduce_scatter | solution.py:45
  196.3 7.6 %all-to-all-start.1 = ((bf16[32,32,512]{2,1,0:T(8,128)(2,1)}), bf16[32,32,512]{2,1,0:T(8,128)(2,1)S(1)}, u32[]{:S(2)}, u32[]{:S(2)}) async-start(bf16[32,32,512]{2,1,0:T(8,128)(2,1)} %reduce-scatter.2.cloned.1.call-done), calls=%async_computation.2 | async-start | bytes 2097152 | tf_op jit(solution)/shard_map/all_to_all | solution.py:51
  204.1 16.7 %all-to-all-done.1 = bf16[32,32,512]{2,1,0:T(8,128)(2,1)S(1)} async-done(((bf16[32,32,512]{2,1,0:T(8,128)(2,1)}), bf16[32,32,512]{2,1,0:T(8,128)(2,1)S(1)}, u32[]{:S(2)}, u32[]{:S(2)}) %all-to-all-start.1) | async-done | bytes 1048608 | tf_op jit(solution)/shard_map/all_to_all | solution.py:51
  220.9 0.8 copy.21
  222.0 2.0 gather_fusion.1
  224.6 1.3 multiply_reduce_fusion
  226.1 6.5 %psum.7 = f32[256]{0:T(256)S(1)} all-reduce(f32[256]{0:T(256)S(1)} %multiply_reduce_fusion.1), channel_id=1, replica_groups=mesh['req'=32,'tp'=4] {'tp'}, use_global_device_ids=true, to_apply=%region_9.10 | all-reduce | flops 256 | bytes 2048 | tf_op jit(solution)/shard_map/psum | solution.py:57
  232.7 0.8 multiply_convert_fusion.1
  (32 shorter events, 2.6 us)
Async XLA Ops:
  7.2 28.8 %all-gather.2.cloned.1.call-start = ((), (), s32[]{:S(2)}) async-start(), calls=%async_computation.3 | async-start | bytes 1310720 | tf_op jit(solution)/shard_map/all_gather | solution.py:21
  7.9 188.4 %reduce-scatter.2.cloned.1.call-start = ((), (), s32[]{:S(2)}) async-start(), calls=%async_computation.4 | async-start | bytes 5242880 | tf_op jit(solution)/shard_map/reduce_scatter | solution.py:45
  119.7 2.1 copy-start
  152.7 51.3 %copy-start.2 = (f32[256,2]{0,1:T(2,128)S(1)}, f32[256,2]{0,1:T(2,128)}, u32[]{:S(2)}) copy-start(f32[256,2]{0,1:T(2,128)} %param.10) | copy-start | bytes 6148
  196.3 24.5 %all-to-all-start.1 = ((bf16[32,32,512]{2,1,0:T(8,128)(2,1)}), bf16[32,32,512]{2,1,0:T(8,128)(2,1)S(1)}, u32[]{:S(2)}, u32[]{:S(2)}) async-start(bf16[32,32,512]{2,1,0:T(8,128)(2,1)} %reduce-scatter.2.cloned.1.call-done), calls=%async_computation.2 | async-start | bytes 2097152 | tf_op jit(solution)/shard_map/all_to_all | solution.py:51
  222.0 4.0 %copy-start.1 = (bf16[256,512]{1,0:T(8,128)(2,1)S(1)}, bf16[256,512]{1,0:T(8,128)(2,1)}, u32[]{:S(2)}) copy-start(bf16[256,512]{1,0:T(8,128)(2,1)} %param.8) | copy-start | bytes 786436
  222.0 10.7 %copy-start.3 = (f32[512]{0:T(512)S(1)}, f32[512]{0:T(512)}, u32[]{:S(2)}) copy-start(f32[512]{0:T(512)} %param.12) | copy-start | bytes 6148
Sparse Core Ops, SparseCore 0:
  9.7 26.2 all-gather.1
  152.8 43.4 reduce-scatter.1
where the time goes:
time: 242 us; the launch traced here: 240 us
  waiting for transfers between devices  80.3 us (33%)
  blocking collectives  65.5 us (27%)
  matrix products  30.9 us (13%)
  local copies, waits for them, and re-layouts  25.9 us (11%)
  other arithmetic  15.9 us (7%)
  between operations  14.2 us (6%)
  starting transfers between devices  7.68 us (3%)
    all_to_all x1, blocking collectives, shards(): lax.all_to_all(outgoing, 'req', split_axis=0, concat_axis=0, tiled=True)  59 us
    reduce_scatter x1, waiting for transfers between devices, shards(): lax.psum_scatter(partial_out.reshape(sources, items, widths).astype(jnp.b...  43.6 us
    dot_general x1, matrix products, shards(): jnp.dot(activ, down_weight[0], preferred_element_type=jnp.float32)  20.6 us
    all_gather x1, waiting for transfers between devices, shards(): lax.all_gather(hidden, 'tp', axis=1, tiled=True).astype(jnp.float32)  19.2 us
    all_to_all x1, waiting for transfers between devices, shards(): lax.all_to_all(summed, 'req', split_axis=0, concat_axis=0, tiled=True)  16.7 us
    gather x2, local copies, waits for them, and re-layouts, shards(): normed_in[slot_row]  13.2 us
    dot_general x1, matrix products, shards(): jnp.dot(flat_rows, gate_weight[0], preferred_element_type=jnp.float32)  10.2 us
    select_n x1, other arithmetic, shards(): jnp.where(slot_live[:, None], normed_in[slot_row], jnp.zeros((), jnp.bflo...  8.47 us
  transfers between devices with their start and end apart: 3, of which 3 were waited for; matrix products, arithmetic and copies ran while one was open for 4% of the time, Pallas kernels for 0%

commit v1 on v0

--- a/solution.py
+++ b/solution.py
@@ -24,15 +24,20 @@
         jnp.bfloat16
     )
     send_cols = normed_in.shape[1]
+    top = routes.shape[1]
     chosen = routes.reshape(-1)
     onehot = (chosen[:, None] == jnp.arange(E, dtype=jnp.int32)[None, :]).astype(jnp.int32)
     slot_rank = jnp.sum((jnp.cumsum(onehot, axis=0) - 1) * onehot, axis=1)
-    position = chosen * CAP + slot_rank
-    entry_rows = jnp.arange(chosen.shape[0], dtype=jnp.int32) // routes.shape[1]
-    slot_row = jnp.zeros((E * CAP,), jnp.int32).at[position].set(entry_rows)
-    slot_live = jnp.zeros((E * CAP,), jnp.bool_).at[position].set(True)
-    outgoing = jnp.where(slot_live[:, None], normed_in[slot_row], jnp.zeros((), jnp.bfloat16))
-    outgoing = outgoing.reshape(E, slot_count, copies, send_cols).transpose(2, 0, 1, 3)
+    dest = (slot_rank % copies) * E + chosen
+    out_idx = dest * slot_count + slot_rank // copies
+    out_pairs = out_idx.reshape(row_count, top)
+    slot_ids = jnp.arange(req_count * slot_count, dtype=jnp.int32)
+    dispatch = jnp.zeros((req_count * slot_count, row_count), jnp.bool_)
+    for k in range(top):
+        dispatch = dispatch | (slot_ids[:, None] == out_pairs[None, :, k])
+    outgoing = jnp.dot(
+        dispatch.astype(jnp.bfloat16), normed_in, preferred_element_type=jnp.float32
+    ).astype(jnp.bfloat16)
     outgoing = outgoing.reshape(req_count, slot_count, send_cols)
     pieces = lax.all_to_all(outgoing, "req", split_axis=0, concat_axis=0, tiled=True)
     sources, items, widths = pieces.shape
@@ -49,9 +54,8 @@
         tiled=True,
     )
     returned = lax.all_to_all(summed, "req", split_axis=0, concat_axis=0, tiled=True)
-    returned = returned.reshape(copies, E, slot_count, col_part).transpose(1, 2, 0, 3)
-    returned = returned.reshape(E * CAP, col_part)
-    picked = returned[position].reshape(row_count, routes.shape[1], col_part).astype(jnp.float32)
+    returned = returned.reshape(req_count * slot_count, col_part)
+    picked = returned[out_idx].reshape(row_count, top, col_part).astype(jnp.float32)
     mixed = jnp.sum(picked * route_weights[:, :, None], axis=1)
     total_stream = stream + mixed
     out_sums = lax.psum(jnp.sum(total_stream * total_stream, axis=1), "tp")

time: 242 us -> 218 us (0.901)
  local copies, waits for them, and re-layouts: 25.9 us -> 6.53 us
  other arithmetic: 15.9 us -> 6.04 us
  waiting for transfers between devices: 80.3 us -> 85.3 us
    gather x3 -> x1, local copies, waits for them, and re-layouts: 15.2 us -> 1.96 us  [shards(): returned[out_idx].reshape(row_count, top, col_part).astype(jnp.float32)]
    select_n x3 -> x1, other arithmetic: 8.48 us -> 0.03 us  [shards(): returned[out_idx].reshape(row_count, top, col_part).astype(jnp.float32)]
    all_gather x1, waiting for transfers between devices: 19.2 us -> 24.5 us  [shards(): lax.all_gather(hidden, 'tp', axis=1, tiled=True).astype(jnp.float32)]
    scatter x2 -> x0, local copies, waits for them, and re-layouts: 4.89 us -> none  [the longest x1 2.45 us: shards(): slot_live = jnp.zeros((E * CAP,), jnp.bool_).at[position].set(True)]
    dot_general x0 -> x1, matrix products: none -> 2.74 us  [shards(): jnp.dot(dispatch.astype(jnp.bfloat16), normed_in, preferred_element_type=...]
  transfers between devices with their start and end apart: 3 -> 3, of which waited for: 3 -> 3; matrix products, arithmetic and copies ran while one was open for 4% -> 2% of each run, Pallas kernels for 0% -> 0%
where the time goes in v1:
time: 218 us; the launch traced here: 217 us
  waiting for transfers between devices  85.3 us (39%)
  blocking collectives  65.5 us (30%)
  matrix products  31.8 us (15%)
  between operations  14.2 us (7%)
  starting transfers between devices  7.69 us (4%)
  local copies, waits for them, and re-layouts  6.53 us (3%)
  other arithmetic  6.04 us (3%)
    all_to_all x1, blocking collectives, shards(): lax.all_to_all(outgoing, 'req', split_axis=0, concat_axis=0, tiled=True)  59 us
    reduce_scatter x1, waiting for transfers between devices, shards(): lax.psum_scatter(partial_out.reshape(sources, items, widths).astype(jnp.b...  43.6 us
    all_gather x1, waiting for transfers between devices, shards(): lax.all_gather(hidden, 'tp', axis=1, tiled=True).astype(jnp.float32)  24.5 us
    dot_general x1, matrix products, shards(): jnp.dot(activ, down_weight[0], preferred_element_type=jnp.float32)  20.6 us
    all_to_all x1, waiting for transfers between devices, shards(): lax.all_to_all(summed, 'req', split_axis=0, concat_axis=0, tiled=True)  16.6 us
    dot_general x1, matrix products, shards(): jnp.dot(flat_rows, gate_weight[0], preferred_element_type=jnp.float32)  8.44 us
    all_to_all x1, starting transfers between devices, shards(): lax.all_to_all(summed, 'req', split_axis=0, concat_axis=0, tiled=True)  7.61 us
    psum x1, blocking collectives, shards(): out_sums = lax.psum(jnp.sum(total_stream * total_stream, axis=1), 'tp')  6.55 us
  transfers between devices with their start and end apart: 3, of which 3 were waited for; matrix products, arithmetic and copies ran while one was open for 2% of the time, Pallas kernels for 0%

profile of v1, /device:TPU:1, one launch (start us, length us, event | category | flops | bytes accessed | tf_op | source)
XLA Modules:
  0.0 217.2 jit_solution(11316550749932052494)
XLA Ops:
  7.2 0.7 all-gather.2.cloned.1.call-update
  7.9 0.8 copy.27
  8.8 0.1 eq.62
  8.9 0.1 eq.58
  9.1 1.1 reduce-window.6
  10.2 0.2 slice_reduce_fusion
  10.6 0.1 reduce_sum.41
  10.8 0.7 fusion.31
  11.5 24.5 %all-gather.2.cloned.1.call-done = bf16[256,2048]{1,0:T(8,128)(2,1)} async-done(((bf16[256,512]{1,0:T(8,128)(2,1)}), bf16[256,2048]{1,0:T(8,128)(2,1)}) %all-gather.2.cloned.1.call-update) | async-done | bytes 1048592 | tf_op jit(solution)/shard_map/all_gather | solution.py:21
  36.0 1.7 fusion.16
  37.7 2.7 %convolution_convert_fusion = bf16[1024,2048]{1,0:T(8,128)(2,1)S(1)} fusion(bf16[256,2048]{1,0:T(8,128)(2,1)} %all-gather.2.cloned.1.call-done, f32[2048]{0:T(1024)} %param.11, f32[256]{0:T(256)S(1)} %add_rsqrt_fusion.1, s32[256]{0:T(256)S(1)} %bitcast.40, s32[256]{0:T(256)S(1)} %bitcast.39), kind=kOutput, calls=%fused_computation.8 | convolution fusion | flops 1078722560 | bytes 5254144 | tf_op jit(solution)/shard_map/dot_general | solution.py:38
  40.4 59.0 %all_to_all.10 = bf16[32,32,2048]{2,1,0:T(8,128)(2,1)S(1)} all-to-all(bf16[32,32,2048]{2,1,0:T(8,128)(2,1)S(1)} %bitcast.33), channel_id=1, replica_groups=mesh['req'=32,'tp'=4] {'req'}, dimensions={0} | all-to-all | bytes 8388608 | tf_op jit(solution)/shard_map/all_to_all | solution.py:42
  99.4 2.1 copy-done
  101.5 8.4 %fusion.4 = f32[1024,1408]{1,0:T(8,128)} fusion(bf16[1024,2048]{1,0:T(8,128)(2,1)S(1)} %bitcast.36, bf16[1,2048,1408]{2,1,0:T(8,128)(2,1)S(1)} %bitcast.43), kind=kOutput, calls=%fused_computation.5 | convolution fusion | flops 5905580032 | bytes 15728640 | tf_op jit(solution)/shard_map/dot_general | solution.py:45
  109.9 20.6 %fusion.10 = bf16[1024,2048]{1,0:T(8,128)(2,1)} fusion(bf16[1,1408,2048]{2,1,0:T(8,128)(2,1)} %param.15, f32[1024,1408]{1,0:T(8,128)} %fusion.4, bf16[1024,2048]{1,0:T(8,128)(2,1)} %bitcast.37, bf16[1,2048,1408]{2,1,0:T(8,128)(2,1)} %param.14), kind=kOutput, calls=%fused_computation.9 | convolution fusion | flops 11821907968 | bytes 25690112 | tf_op jit(solution)/shard_map/dot_general | solution.py:48
  130.6 43.6 %reduce-scatter.2.cloned.1.call-done = bf16[32,32,512]{2,1,0:T(8,128)(2,1)} async-done(((bf16[32,32,2048]{2,1,0:T(8,128)(2,1)}), bf16[32,32,512]{2,1,0:T(8,128)(2,1)}) %reduce-scatter.2.cloned.1.call-update) | async-done | bytes 1048592 | tf_op jit(solution)/shard_map/reduce_scatter | solution.py:50
  174.2 7.6 %all-to-all-start.1 = ((bf16[32,32,512]{2,1,0:T(8,128)(2,1)}), bf16[32,32,512]{2,1,0:T(8,128)(2,1)S(1)}, u32[]{:S(2)}, u32[]{:S(2)}) async-start(bf16[32,32,512]{2,1,0:T(8,128)(2,1)} %reduce-scatter.2.cloned.1.call-done), calls=%async_computation.2 | async-start | bytes 2097152 | tf_op jit(solution)/shard_map/all_to_all | solution.py:56
  182.2 16.6 %all-to-all-done.1 = bf16[32,32,512]{2,1,0:T(8,128)(2,1)S(1)} async-done(((bf16[32,32,512]{2,1,0:T(8,128)(2,1)}), bf16[32,32,512]{2,1,0:T(8,128)(2,1)S(1)}, u32[]{:S(2)}, u32[]{:S(2)}) %all-to-all-start.1) | async-done | bytes 1048608 | tf_op jit(solution)/shard_map/all_to_all | solution.py:56
  198.8 2.0 gather_fusion
  200.7 0.7 reshape.154
  201.4 1.3 multiply_reduce_fusion
  202.7 0.2 multiply_reduce_fusion.1
  202.9 6.5 %psum.7 = f32[256]{0:T(256)S(1)} all-reduce(f32[256]{0:T(256)S(1)} %multiply_reduce_fusion.1), channel_id=1, replica_groups=mesh['req'=32,'tp'=4] {'tp'}, use_global_device_ids=true, to_apply=%region_7.8 | all-reduce | flops 256 | bytes 2048 | tf_op jit(solution)/shard_map/psum | solution.py:61
  209.4 0.9 multiply_convert_fusion.1
  (27 shorter events, 0.7 us)
Async XLA Ops:
  7.2 28.8 %all-gather.2.cloned.1.call-start = ((), (), s32[]{:S(2)}) async-start(), calls=%async_computation.3 | async-start | bytes 1310720 | tf_op jit(solution)/shard_map/all_gather | solution.py:21
  7.9 166.3 %reduce-scatter.2.cloned.1.call-start = ((), (), s32[]{:S(2)}) async-start(), calls=%async_computation.4 | async-start | bytes 5242880 | tf_op jit(solution)/shard_map/reduce_scatter | solution.py:50
  36.0 65.5 %slice-start = ((s8[5767168]{0:T(1024)(128)(4,1)}), s8[4194304]{0:T(1024)(128)(4,1)S(1)}, s32[]{:S(2)}) async-start(s8[5767168]{0:T(1024)(128)(4,1)} %bitcast.42), calls=%async_computation.5 | async-start | bytes 8388608
  37.7 63.8 %slice-start.1 = ((s8[5767168]{0:T(1024)(128)(4,1)}), s8[1572864]{0:T(1024)(128)(4,1)S(1)}, s32[]{:S(2)}) async-start(s8[5767168]{0:T(1024)(128)(4,1)} %bitcast.42), calls=%async_computation.6 | async-start | bytes 3145728
  99.4 2.1 copy-start
  130.6 51.4 %copy-start.2 = (f32[256,2]{0,1:T(2,128)S(1)}, f32[256,2]{0,1:T(2,128)}, u32[]{:S(2)}) copy-start(f32[256,2]{0,1:T(2,128)} %param.10) | copy-start | bytes 6148
  130.6 72.1 %copy-start.1 = (bf16[256,512]{1,0:T(8,128)(2,1)S(1)}, bf16[256,512]{1,0:T(8,128)(2,1)}, u32[]{:S(2)}) copy-start(bf16[256,512]{1,0:T(8,128)(2,1)} %param.8) | copy-start | bytes 786436
  130.6 78.8 %copy-start.3 = (f32[512]{0:T(512)S(1)}, f32[512]{0:T(512)}, u32[]{:S(2)}) copy-start(f32[512]{0:T(512)} %param.12) | copy-start | bytes 6148
  174.2 24.5 %all-to-all-start.1 = ((bf16[32,32,512]{2,1,0:T(8,128)(2,1)}), bf16[32,32,512]{2,1,0:T(8,128)(2,1)S(1)}, u32[]{:S(2)}, u32[]{:S(2)}) async-start(bf16[32,32,512]{2,1,0:T(8,128)(2,1)} %reduce-scatter.2.cloned.1.call-done), calls=%async_computation.2 | async-start | bytes 2097152 | tf_op jit(solution)/shard_map/all_to_all | solution.py:56
Sparse Core Ops, SparseCore 0:
  9.7 26.2 all-gather.1
  130.7 43.4 reduce-scatter.1

commit v2 on v1

v2 whole, which is shorter than its diff:
```python
import jax
import jax.numpy as jnp
from jax import lax
from jax.sharding import PartitionSpec as P

E = 8
CAP = 128
CHUNKS = 2


epsilon = 1e-05


def shards(hidden, routes, route_weights, pre_gain, out_gain, gate_weight, up_weight, down_weight):
    row_count, col_part = hidden.shape
    tp_count = lax.axis_size("tp")
    req_count = lax.axis_size("req")
    full_width = col_part * tp_count
    copies = req_count // E
    slot_count = CAP // copies
    chunk_items = slot_count // CHUNKS
    stream = hidden.astype(jnp.float32)
    whole_rows = lax.all_gather(hidden, "tp", axis=1, tiled=True).astype(jnp.float32)
    meansq = jnp.sum(whole_rows * whole_rows, axis=1) / full_width
    normed_in = (whole_rows * lax.rsqrt(meansq + epsilon)[:, None] * pre_gain[None, :]).astype(
        jnp.bfloat16
    )
    send_cols = normed_in.shape[1]
    top = routes.shape[1]
    chosen = routes.reshape(-1)
    onehot = (chosen[:, None] == jnp.arange(E, dtype=jnp.int32)[None, :]).astype(jnp.int32)
    slot_rank = jnp.sum((jnp.cumsum(onehot, axis=0) - 1) * onehot, axis=1)
    dest = (slot_rank % copies) * E + chosen
    item = slot_rank // copies
    chunk_of = item // chunk_items
    in_chunk = dest * chunk_items + item % chunk_items
    chunk_pairs = in_chunk.reshape(row_count, top)
    owner_pairs = chunk_of.reshape(row_count, top)
    slot_ids = jnp.arange(req_count * chunk_items, dtype=jnp.int32)
    returned = []
    for c in range(CHUNKS):
        dispatch = jnp.zeros((req_count * chunk_items, row_count), jnp.bool_)
        for k in range(top):
            hit = (slot_ids[:, None] == chunk_pairs[None, :, k]) & (owner_pairs[None, :, k] == c)
            dispatch = dispatch | hit
        outgoing = jnp.dot(
            dispatch.astype(jnp.bfloat16), normed_in, preferred_element_type=jnp.float32
        ).astype(jnp.bfloat16)
        outgoing = outgoing.reshape(req_count, chunk_items, send_cols)
        pieces = lax.all_to_all(outgoing, "req", split_axis=0, concat_axis=0, tiled=True)
        sources, items, widths = pieces.shape
        flat_rows = pieces.reshape(sources * items, widths)
        gate_val = jnp.dot(flat_rows, gate_weight[0], preferred_element_type=jnp.float32)
        up_val = jnp.dot(flat_rows, up_weight[0], preferred_element_type=jnp.float32)
        activ = (jax.nn.silu(gate_val) * up_val).astype(jnp.bfloat16)
        partial_out = jnp.dot(activ, down_weight[0], preferred_element_type=jnp.float32)
        partial_out = lax.optimization_barrier(partial_out.astype(jnp.bfloat16)).astype(jnp.float32)
        summed = lax.psum_scatter(
            partial_out.reshape(sources, items, widths).astype(jnp.bfloat16),
            "tp",
            scatter_dimension=2,
            tiled=True,
        )
        back = lax.all_to_all(summed, "req", split_axis=0, concat_axis=0, tiled=True)
        returned.append(back.reshape(req_count * chunk_items, col_part))
    returned = jnp.concatenate(returned, axis=0)
    out_idx = chunk_of * (req_count * chunk_items) + in_chunk
    picked = returned[out_idx].reshape(row_count, top, col_part).astype(jnp.float32)
    mixed = jnp.sum(picked * route_weights[:, :, None], axis=1)
    total_stream = stream + mixed
    out_sums = lax.psum(jnp.sum(total_stream * total_stream, axis=1), "tp")
    normed_out = (
        total_stream * lax.rsqrt(out_sums / full_width + epsilon)[:, None] * out_gain[None, :]
    )
    return (total_stream.astype(jnp.bfloat16), normed_out.astype(jnp.bfloat16))


def solution(mesh):
    return jax.shard_map(
        shards,
        mesh=mesh,
        in_specs=(
            P("req", "tp"),
            P("req", None),
            P("req", None),
            P(),
            P("tp"),
            P("req", None, "tp"),
            P("req", None, "tp"),
            P("req", "tp", None),
        ),
        out_specs=(P("req", "tp"), P("req", "tp")),
        check_vma=False,
    )
```

time: 218 us -> 207 us (0.950)
  blocking collectives: 65.5 us -> 6.55 us
  starting transfers between devices: 7.69 us -> 28.7 us
  matrix products: 31.8 us -> 48.9 us
  waiting for transfers between devices: 85.3 us -> 95.6 us
    all_to_all x1 -> x0, blocking collectives: 59 us -> none  [shards(): lax.all_to_all(outgoing, 'req', split_axis=0, concat_axis=0, tiled=True)]
    all_to_all x0 -> x2, waiting for transfers between devices: none -> 32 us  [shards(): lax.all_to_all(outgoing, 'req', split_axis=0, concat_axis=0, tiled=True)]
    reduce_scatter x1 -> x2, waiting for transfers between devices: 43.6 us -> 27.1 us  [shards(): lax.psum_scatter(partial_out.reshape(sources, items, widths).astype(jnp.b...]
    all_to_all x0 -> x2, starting transfers between devices: none -> 13.2 us  [shards(): lax.all_to_all(outgoing, 'req', split_axis=0, concat_axis=0, tiled=True)]
    all_to_all x1 -> x2, starting transfers between devices: 7.61 us -> 15.2 us  [shards(): lax.all_to_all(summed, 'req', split_axis=0, concat_axis=0, tiled=True)]
    dot_general x1 -> x2, matrix products: 8.44 us -> 15.9 us  [shards(): jnp.dot(flat_rows, gate_weight[0], preferred_element_type=jnp.float32)]
    dot_general x1 -> x2, matrix products: 20.6 us -> 27.2 us  [shards(): jnp.dot(activ, down_weight[0], preferred_element_type=jnp.float32)]
    all_to_all x1 -> x2, waiting for transfers between devices: 16.6 us -> 11.3 us  [shards(): lax.all_to_all(summed, 'req', split_axis=0, concat_axis=0, tiled=True)]
  transfers between devices with their start and end apart: 3 -> 7, of which waited for: 3 -> 6; matrix products, arithmetic and copies ran while one was open for 2% -> 24% of each run, Pallas kernels for 0% -> 0%
where the time goes in v2:
time: 207 us; the launch traced here: 206 us
  waiting for transfers between devices  95.6 us (46%)
  matrix products  48.9 us (24%)
  starting transfers between devices  28.7 us (14%)
  between operations  13.9 us (7%)
  blocking collectives  6.55 us (3%)
  other arithmetic  5.99 us (3%)
  local copies, waits for them, and re-layouts  5.86 us (3%)
    all_to_all x2, waiting for transfers between devices, shards(): lax.all_to_all(outgoing, 'req', split_axis=0, concat_axis=0, tiled=True)  32 us
    dot_general x2, matrix products, shards(): jnp.dot(activ, down_weight[0], preferred_element_type=jnp.float32)  27.2 us
    reduce_scatter x2, waiting for transfers between devices, shards(): lax.psum_scatter(partial_out.reshape(sources, items, widths).astype(jnp.b...  27.1 us
    all_gather x1, waiting for transfers between devices, shards(): lax.all_gather(hidden, 'tp', axis=1, tiled=True).astype(jnp.float32)  24.5 us
    dot_general x2, matrix products, shards(): jnp.dot(flat_rows, gate_weight[0], preferred_element_type=jnp.float32)  15.9 us
    all_to_all x2, starting transfers between devices, shards(): lax.all_to_all(summed, 'req', split_axis=0, concat_axis=0, tiled=True)  15.2 us
    all_to_all x2, starting transfers between devices, shards(): lax.all_to_all(outgoing, 'req', split_axis=0, concat_axis=0, tiled=True)  13.2 us
    all_to_all x2, waiting for transfers between devices, shards(): lax.all_to_all(summed, 'req', split_axis=0, concat_axis=0, tiled=True)  11.3 us
  transfers between devices with their start and end apart: 7, of which 6 were waited for; matrix products, arithmetic and copies ran while one was open for 24% of the time, Pallas kernels for 0%

profile of v2, /device:TPU:1, one launch (start us, length us, event | category | flops | bytes accessed | tf_op | source)
XLA Modules:
  0.0 205.5 jit_solution(5052789571543952319)
XLA Ops:
  7.9 0.8 copy.27
  9.0 1.1 reduce-window.6
  11.5 24.5 %all-gather.2.cloned.1.call-done = bf16[256,2048]{1,0:T(8,128)(2,1)} async-done(((bf16[256,512]{1,0:T(8,128)(2,1)}), bf16[256,2048]{1,0:T(8,128)(2,1)}) %all-gather.2.cloned.1.call-update) | async-done | bytes 1048592 | tf_op jit(solution)/shard_map/all_gather | solution.py:23
  36.0 1.5 fusion.30
  37.5 3.5 %convolution_convert_fusion.1 = bf16[512,2048]{1,0:T(8,128)(2,1)} fusion(bf16[256,2048]{1,0:T(8,128)(2,1)} %all-gather.2.cloned.1.call-done, f32[2048]{0:T(1024)} %param.11, f32[256]{0:T(256)S(1)} %add_rsqrt_fusion.1, s32[256]{0:T(256)S(1)} %bitcast.66, s32[256]{0:T(256)S(1)} %bitcast.64, pred[256]{0:T(512)(128)(4,1)S(1)} %get-tuple-element.5, ...), kind=kOutput, calls=%fused_computation.16 | convolution fusion | flops 540672000 | bytes 3157504 | tf_op jit(solution)/shard_map/dot_general | solution.py:46
  41.0 8.7 %all-to-all-start = ((bf16[32,16,2048]{2,1,0:T(8,128)(2,1)}), bf16[32,16,2048]{2,1,0:T(8,128)(2,1)S(1)}, u32[]{:S(2)}, u32[]{:S(2)}) async-start(bf16[32,16,2048]{2,1,0:T(8,128)(2,1)} %bitcast.59), calls=%async_computation | async-start | bytes 4194304 | tf_op jit(solution)/shard_map/all_to_all | solution.py:50
  49.7 2.3 %convolution_convert_fusion = bf16[512,2048]{1,0:T(8,128)(2,1)} fusion(bf16[256,2048]{1,0:T(8,128)(2,1)S(1)} %copy-done.2, f32[2048]{0:T(1024)S(1)} %copy-done.5, f32[256]{0:T(256)S(1)} %add_rsqrt_fusion.1, s32[256]{0:T(256)S(1)} %bitcast.67, s32[256]{0:T(256)S(1)} %bitcast.65, pred[256]{0:T(512)(128)(4,1)S(1)} %get-tuple-element.4, ...), kind=kOutput, calls=%fused_computation.15 | convolution fusion | flops 540672000 | bytes 3157504 | tf_op jit(solution)/shard_map/dot_general | solution.py:46
  52.0 26.0 %all-to-all-done = bf16[32,16,2048]{2,1,0:T(8,128)(2,1)S(1)} async-done(((bf16[32,16,2048]{2,1,0:T(8,128)(2,1)}), bf16[32,16,2048]{2,1,0:T(8,128)(2,1)S(1)}, u32[]{:S(2)}, u32[]{:S(2)}) %all-to-all-start) | async-done | bytes 2097184 | tf_op jit(solution)/shard_map/all_to_all | solution.py:50
  78.0 1.4 copy-done.1
  79.4 4.5 %all-to-all-start.2 = ((bf16[32,16,2048]{2,1,0:T(8,128)(2,1)}), bf16[32,16,2048]{2,1,0:T(8,128)(2,1)S(1)}, u32[]{:S(2)}, u32[]{:S(2)}) async-start(bf16[32,16,2048]{2,1,0:T(8,128)(2,1)} %bitcast.11), calls=%async_computation.3 | async-start | bytes 4194304 | tf_op jit(solution)/shard_map/all_to_all | solution.py:50
  84.0 8.3 %fusion.10 = f32[512,1408]{1,0:T(8,128)} fusion(bf16[512,2048]{1,0:T(8,128)(2,1)} %bitcast.56, bf16[1,2048,1408]{2,1,0:T(8,128)(2,1)} %param.13), kind=kOutput, calls=%fused_computation.11 | convolution fusion | flops 2952790016 | bytes 10747904 | tf_op jit(solution)/shard_map/dot_general | solution.py:53
  92.3 13.8 %fusion.24 = bf16[512,2048]{1,0:T(8,128)(2,1)} fusion(bf16[1,1408,2048]{2,1,0:T(8,128)(2,1)} %param.15, bf16[512,2048]{1,0:T(8,128)(2,1)} %bitcast.57, bf16[1,2048,1408]{2,1,0:T(8,128)(2,1)} %param.14, f32[512,1408]{1,0:T(8,128)} %fusion.10), kind=kOutput, calls=%fused_computation.19 | convolution fusion | flops 5910953984 | bytes 18612224 | tf_op jit(solution)/shard_map/dot_general | solution.py:56
  106.3 6.0 %all-to-all-done.2 = bf16[32,16,2048]{2,1,0:T(8,128)(2,1)S(1)} async-done(((bf16[32,16,2048]{2,1,0:T(8,128)(2,1)}), bf16[32,16,2048]{2,1,0:T(8,128)(2,1)S(1)}, u32[]{:S(2)}, u32[]{:S(2)}) %all-to-all-start.2) | async-done | bytes 2097184 | tf_op jit(solution)/shard_map/all_to_all | solution.py:50
  112.3 7.6 %fusion.8 = f32[512,1408]{1,0:T(8,128)} fusion(bf16[512,2048]{1,0:T(8,128)(2,1)S(1)} %bitcast.54, bf16[1,2048,1408]{2,1,0:T(8,128)(2,1)} %param.13), kind=kOutput, calls=%fused_computation.9 | convolution fusion | flops 2952790016 | bytes 10747904 | tf_op jit(solution)/shard_map/dot_general | solution.py:53
  119.9 13.4 %fusion.27 = bf16[512,2048]{1,0:T(8,128)(2,1)} fusion(bf16[1,1408,2048]{2,1,0:T(8,128)(2,1)} %param.15, bf16[512,2048]{1,0:T(8,128)(2,1)S(1)} %bitcast.55, bf16[1,2048,1408]{2,1,0:T(8,128)(2,1)} %param.14, f32[512,1408]{1,0:T(8,128)} %fusion.8), kind=kOutput, calls=%fused_computation.20 | convolution fusion | flops 5910953984 | bytes 18612224 | tf_op jit(solution)/shard_map/dot_general | solution.py:56
  133.4 2.8 %reduce-scatter.3.cloned.1.call-done = bf16[32,16,512]{2,1,0:T(8,128)(2,1)} async-done(((bf16[32,16,2048]{2,1,0:T(8,128)(2,1)}), bf16[32,16,512]{2,1,0:T(8,128)(2,1)}) %reduce-scatter.3.cloned.1.call-update) | async-done | bytes 524304 | tf_op jit(solution)/shard_map/reduce_scatter | solution.py:58
  136.1 7.6 %all-to-all-start.1 = ((bf16[32,16,512]{2,1,0:T(8,128)(2,1)}), bf16[32,16,512]{2,1,0:T(8,128)(2,1)S(1)}, u32[]{:S(2)}, u32[]{:S(2)}) async-start(bf16[32,16,512]{2,1,0:T(8,128)(2,1)} %reduce-scatter.3.cloned.1.call-done), calls=%async_computation.2 | async-start | bytes 1048576 | tf_op jit(solution)/shard_map/all_to_all | solution.py:64
  143.8 24.4 %reduce-scatter.5.cloned.1.call-done = bf16[32,16,512]{2,1,0:T(8,128)(2,1)} async-done(((bf16[32,16,2048]{2,1,0:T(8,128)(2,1)}), bf16[32,16,512]{2,1,0:T(8,128)(2,1)}) %reduce-scatter.5.cloned.1.call-update) | async-done | bytes 524304 | tf_op jit(solution)/shard_map/reduce_scatter | solution.py:58
  168.1 7.6 %all-to-all-start.3 = ((bf16[32,16,512]{2,1,0:T(8,128)(2,1)}), bf16[32,16,512]{2,1,0:T(8,128)(2,1)S(1)}, u32[]{:S(2)}, u32[]{:S(2)}) async-start(bf16[32,16,512]{2,1,0:T(8,128)(2,1)} %reduce-scatter.5.cloned.1.call-done), calls=%async_computation.5 | async-start | bytes 1048576 | tf_op jit(solution)/shard_map/all_to_all | solution.py:64
  176.1 11.3 %all-to-all-done.3 = bf16[32,16,512]{2,1,0:T(8,128)(2,1)S(1)} async-done(((bf16[32,16,512]{2,1,0:T(8,128)(2,1)}), bf16[32,16,512]{2,1,0:T(8,128)(2,1)S(1)}, u32[]{:S(2)}, u32[]{:S(2)}) %all-to-all-start.3) | async-done | bytes 524320 | tf_op jit(solution)/shard_map/all_to_all | solution.py:64
  187.4 2.0 gather_fusion
  190.1 1.3 multiply_reduce_fusion
  191.6 6.6 %psum.7 = f32[256]{0:T(256)S(1)} all-reduce(f32[256]{0:T(256)S(1)} %multiply_reduce_fusion.1), channel_id=1, replica_groups=mesh['req'=32,'tp'=4] {'tp'}, use_global_device_ids=true, to_apply=%region_8.9 | all-reduce | flops 256 | bytes 2048 | tf_op jit(solution)/shard_map/psum | solution.py:71
  198.1 0.8 multiply_convert_fusion
  (40 shorter events, 3.9 us)
Async XLA Ops:
  7.2 28.8 %all-gather.2.cloned.1.call-start = ((), (), s32[]{:S(2)}) async-start(), calls=%async_computation.6 | async-start | bytes 1310720 | tf_op jit(solution)/shard_map/all_gather | solution.py:23
  41.0 8.7 %copy-start.2 = (bf16[256,2048]{1,0:T(8,128)(2,1)S(1)}, bf16[256,2048]{1,0:T(8,128)(2,1)}, u32[]{:S(2)}) copy-start(bf16[256,2048]{1,0:T(8,128)(2,1)} %all-gather.2.cloned.1.call-done) | copy-start | bytes 3145732
  41.0 8.7 %copy-start.5 = (f32[2048]{0:T(1024)S(1)}, f32[2048]{0:T(1024)}, u32[]{:S(2)}) copy-start(f32[2048]{0:T(1024)} %param.11) | copy-start | bytes 24580
  41.0 37.0 %all-to-all-start = ((bf16[32,16,2048]{2,1,0:T(8,128)(2,1)}), bf16[32,16,2048]{2,1,0:T(8,128)(2,1)S(1)}, u32[]{:S(2)}, u32[]{:S(2)}) async-start(bf16[32,16,2048]{2,1,0:T(8,128)(2,1)} %bitcast.59), calls=%async_computation | async-start | bytes 4194304 | tf_op jit(solution)/shard_map/all_to_all | solution.py:50
  78.0 1.4 copy-start.1
  79.4 32.9 %all-to-all-start.2 = ((bf16[32,16,2048]{2,1,0:T(8,128)(2,1)}), bf16[32,16,2048]{2,1,0:T(8,128)(2,1)S(1)}, u32[]{:S(2)}, u32[]{:S(2)}) async-start(bf16[32,16,2048]{2,1,0:T(8,128)(2,1)} %bitcast.11), calls=%async_computation.3 | async-start | bytes 4194304 | tf_op jit(solution)/shard_map/all_to_all | solution.py:50
  83.9 52.2 %reduce-scatter.3.cloned.1.call-start = ((), (), s32[]{:S(2)}) async-start(), calls=%async_computation.7 | async-start | bytes 2621440 | tf_op jit(solution)/shard_map/reduce_scatter | solution.py:58
  106.1 62.0 %reduce-scatter.5.cloned.1.call-start = ((), (), s32[]{:S(2)}) async-start(), calls=%async_computation.8 | async-start | bytes 2621440 | tf_op jit(solution)/shard_map/reduce_scatter | solution.py:58
  133.3 42.5 %copy-start.3 = (f32[256,2]{0,1:T(2,128)S(1)}, f32[256,2]{0,1:T(2,128)}, u32[]{:S(2)}) copy-start(f32[256,2]{0,1:T(2,128)} %param.10) | copy-start | bytes 6148
  136.1 32.0 %all-to-all-start.1 = ((bf16[32,16,512]{2,1,0:T(8,128)(2,1)}), bf16[32,16,512]{2,1,0:T(8,128)(2,1)S(1)}, u32[]{:S(2)}, u32[]{:S(2)}) async-start(bf16[32,16,512]{2,1,0:T(8,128)(2,1)} %reduce-scatter.3.cloned.1.call-done), calls=%async_computation.2 | async-start | bytes 1048576 | tf_op jit(solution)/shard_map/all_to_all | solution.py:64
  168.1 19.2 %all-to-all-start.3 = ((bf16[32,16,512]{2,1,0:T(8,128)(2,1)}), bf16[32,16,512]{2,1,0:T(8,128)(2,1)S(1)}, u32[]{:S(2)}, u32[]{:S(2)}) async-start(bf16[32,16,512]{2,1,0:T(8,128)(2,1)} %reduce-scatter.5.cloned.1.call-done), calls=%async_computation.5 | async-start | bytes 1048576 | tf_op jit(solution)/shard_map/all_to_all | solution.py:64
  187.4 4.0 %copy-start = (bf16[256,512]{1,0:T(8,128)(2,1)S(1)}, bf16[256,512]{1,0:T(8,128)(2,1)}, u32[]{:S(2)}) copy-start(bf16[256,512]{1,0:T(8,128)(2,1)} %param.8) | copy-start | bytes 786436
  189.4 8.7 %copy-start.4 = (f32[512]{0:T(512)S(1)}, f32[512]{0:T(512)}, u32[]{:S(2)}) copy-start(f32[512]{0:T(512)} %param.12) | copy-start | bytes 6148
Sparse Core Ops, SparseCore 0:
  9.7 26.2 all-gather.1
  106.2 29.8 reduce-scatter.2
  138.7 29.3 reduce-scatter.4

commit v3 on v2

--- a/solution.py
+++ b/solution.py
@@ -11,6 +11,45 @@
 epsilon = 1e-05
 
 
+def shift_tp(value, step, tp_count):
+    return lax.ppermute(value, "tp", [(j, (j + step) % tp_count) for j in range(tp_count)])
+
+
+def by_source(value, tp_count):
+    me = lax.axis_index("tp")
+    parts = [value] + [shift_tp(value, s, tp_count) for s in range(1, tp_count)]
+    stacked = jnp.stack(parts)
+    return jnp.take(stacked, (me - jnp.arange(tp_count)) % tp_count, axis=0)
+
+
+def gather_tp(value, tp_count):
+    rows, cols = value.shape
+    ordered = by_source(value, tp_count)
+    return ordered.transpose(1, 0, 2).reshape(rows, tp_count * cols)
+
+
+def sum_tp(value, tp_count):
+    ordered = by_source(value, tp_count)
+    total = ordered[0]
+    for s in range(1, tp_count):
+        total = total + ordered[s]
+    return total
+
+
+def scatter_sum_tp(value, tp_count):
+    me = lax.axis_index("tp")
+    width = value.shape[1] // tp_count
+    terms = []
+    for s in range(tp_count):
+        block = lax.dynamic_slice_in_dim(value, ((me + s) % tp_count) * width, width, axis=1)
+        terms.append(block if s == 0 else shift_tp(block, s, tp_count))
+    ordered = jnp.take(jnp.stack(terms), (me - jnp.arange(tp_count)) % tp_count, axis=0)
+    total = ordered[0].astype(jnp.float32)
+    for s in range(1, tp_count):
+        total = total + ordered[s].astype(jnp.float32)
+    return total.astype(value.dtype)
+
+
 def shards(hidden, routes, route_weights, pre_gain, out_gain, gate_weight, up_weight, down_weight):
     row_count, col_part = hidden.shape
     tp_count = lax.axis_size("tp")
@@ -20,7 +59,7 @@
     slot_count = CAP // copies
     chunk_items = slot_count // CHUNKS
     stream = hidden.astype(jnp.float32)
-    whole_rows = lax.all_gather(hidden, "tp", axis=1, tiled=True).astype(jnp.float32)
+    whole_rows = gather_tp(hidden, tp_count).astype(jnp.float32)
     meansq = jnp.sum(whole_rows * whole_rows, axis=1) / full_width
     normed_in = (whole_rows * lax.rsqrt(meansq + epsilon)[:, None] * pre_gain[None, :]).astype(
         jnp.bfloat16
@@ -55,12 +94,8 @@
         activ = (jax.nn.silu(gate_val) * up_val).astype(jnp.bfloat16)
         partial_out = jnp.dot(activ, down_weight[0], preferred_element_type=jnp.float32)
         partial_out = lax.optimization_barrier(partial_out.astype(jnp.bfloat16)).astype(jnp.float32)
-        summed = lax.psum_scatter(
-            partial_out.reshape(sources, items, widths).astype(jnp.bfloat16),
-            "tp",
-            scatter_dimension=2,
-            tiled=True,
-        )
+        summed = scatter_sum_tp(partial_out.astype(jnp.bfloat16), tp_count)
+        summed = summed.reshape(sources, items, col_part)
         back = lax.all_to_all(summed, "req", split_axis=0, concat_axis=0, tiled=True)
         returned.append(back.reshape(req_count * chunk_items, col_part))
     returned = jnp.concatenate(returned, axis=0)
@@ -68,7 +103,7 @@
     picked = returned[out_idx].reshape(row_count, top, col_part).astype(jnp.float32)
     mixed = jnp.sum(picked * route_weights[:, :, None], axis=1)
     total_stream = stream + mixed
-    out_sums = lax.psum(jnp.sum(total_stream * total_stream, axis=1), "tp")
+    out_sums = sum_tp(jnp.sum(total_stream * total_stream, axis=1), tp_count)
     normed_out = (
         total_stream * lax.rsqrt(out_sums / full_width + epsilon)[:, None] * out_gain[None, :]
     )

time: 207 us -> 199 us (0.961)
  waiting for transfers between devices: 95.6 us -> 75.5 us
  starting transfers between devices: 28.7 us -> 44.8 us
  between operations: 13.9 us -> 0.99 us
  other arithmetic: 5.99 us -> 16.1 us
  local copies, waits for them, and re-layouts: 5.86 us -> 15.5 us
  blocking collectives: 6.55 us -> 0 us
  matrix products: 48.9 us -> 45.8 us
    ppermute x0 -> x12, waiting for transfers between devices: none -> 27.3 us  [shift_tp(): lax.ppermute(value, 'tp', [(j, (j + step) % tp_count) for j in range(tp_c...]
    reduce_scatter x2 -> x0, waiting for transfers between devices: 27.1 us -> none  [shards(): lax.psum_scatter(partial_out.reshape(sources, items, widths).astype(jnp.b...]
    all_gather x1 -> x0, waiting for transfers between devices: 24.5 us -> none  [shards(): lax.all_gather(hidden, 'tp', axis=1, tiled=True).astype(jnp.float32)]
    ppermute x0 -> x12, starting transfers between devices: none -> 18 us  [shift_tp(): lax.ppermute(value, 'tp', [(j, (j + step) % tp_count) for j in range(tp_c...]
    all_to_all x2, waiting for transfers between devices: 11.3 us -> 21.5 us  [shards(): lax.all_to_all(summed, 'req', split_axis=0, concat_axis=0, tiled=True)]
    psum x1 -> x0, blocking collectives: 6.55 us -> none  [shards(): out_sums = lax.psum(jnp.sum(total_stream * total_stream, axis=1), 'tp')]
    another operation x2 -> x8, other arithmetic: 1.18 us -> 7.66 us
    all_to_all x2, waiting for transfers between devices: 32 us -> 26.6 us  [shards(): lax.all_to_all(outgoing, 'req', split_axis=0, concat_axis=0, tiled=True)]
  transfers between devices with their start and end apart: 7 -> 16, of which waited for: 6 -> 12; matrix products, arithmetic and copies ran while one was open for 24% -> 28% of each run, Pallas kernels for 0% -> 0%
where the time goes in v3:
time: 199 us
  waiting for transfers between devices  75.5 us (38%)
  matrix products  45.8 us (23%)
  starting transfers between devices  44.8 us (23%)
  other arithmetic  16.1 us (8%)
  local copies, waits for them, and re-layouts  15.5 us (8%)
    ppermute x12, waiting for transfers between devices, shift_tp(): lax.ppermute(value, 'tp', [(j, (j + step) % tp_count) for j in range(tp_c...  27.3 us
    all_to_all x2, waiting for transfers between devices, shards(): lax.all_to_all(outgoing, 'req', split_axis=0, concat_axis=0, tiled=True)  26.6 us
    dot_general x2, matrix products, shards(): jnp.dot(activ, down_weight[0], preferred_element_type=jnp.float32)  25.7 us
    all_to_all x2, waiting for transfers between devices, shards(): lax.all_to_all(summed, 'req', split_axis=0, concat_axis=0, tiled=True)  21.5 us
    ppermute x12, starting transfers between devices, shift_tp(): lax.ppermute(value, 'tp', [(j, (j + step) % tp_count) for j in range(tp_c...  18 us
    dot_general x2, matrix products, shards(): jnp.dot(flat_rows, gate_weight[0], preferred_element_type=jnp.float32)  15.9 us
    all_to_all x2, starting transfers between devices, shards(): lax.all_to_all(outgoing, 'req', split_axis=0, concat_axis=0, tiled=True)  14.7 us
    all_to_all x2, starting transfers between devices, shards(): lax.all_to_all(summed, 'req', split_axis=0, concat_axis=0, tiled=True)  12.1 us
  transfers between devices with their start and end apart: 16, of which 12 were waited for; matrix products, arithmetic and copies ran while one was open for 28% of the time, Pallas kernels for 0%

profile of v3, /device:TPU:1, one launch (start us, length us, event | category | flops | bytes accessed | tf_op | source)
XLA Modules:
  0.0 198.7 jit_solution(14429677282418381992)
XLA Ops:
  0.6 2.2 %collective-permute-start = (bf16[256,512]{1,0:T(8,128)(2,1)}, bf16[256,512]{1,0:T(8,128)(2,1)S(1)}, u32[]{:S(2)}, u32[]{:S(2)}) collective-permute-start(bf16[256,512]{1,0:T(8,128)(2,1)} %param.10), channel_id=1, source_target_pairs={{0,1},{1,2},{2,3},{3,0},{4,5},{5,6},{6,7},{7,4},{8,9},{9,10},{10,1... | collective-permute-start | bytes 786440 | tf_op jit(solution)/shard_map/ppermute | solution.py:15
  2.8 2.6 %collective-permute-start.1 = (bf16[256,512]{1,0:T(8,128)(2,1)}, bf16[256,512]{1,0:T(8,128)(2,1)S(1)}, u32[]{:S(2)}, u32[]{:S(2)}) collective-permute-start(bf16[256,512]{1,0:T(8,128)(2,1)} %param.10), channel_id=1, source_target_pairs={{0,2},{1,3},{2,0},{3,1},{4,6},{5,7},{6,4},{7,5},{8,10},{9,11},{10,... | collective-permute-start | bytes 786440 | tf_op jit(solution)/shard_map/ppermute | solution.py:15
  10.4 6.6 %collective-permute-done.1 = bf16[256,512]{1,0:T(8,128)(2,1)S(1)} collective-permute-done((bf16[256,512]{1,0:T(8,128)(2,1)}, bf16[256,512]{1,0:T(8,128)(2,1)S(1)}, u32[]{:S(2)}, u32[]{:S(2)}) %collective-permute-start.1) | collective-permute-done | bytes 262176 | tf_op jit(solution)/shard_map/ppermute | solution.py:15
  23.0 2.1 %convolution_convert_fusion = bf16[512,2048]{1,0:T(8,128)(2,1)} fusion(bf16[256,2048]{0,1:T(8,128)(2,1)S(1)} %fusion.32, s32[256]{0:T(256)S(1)} %bitcast.95, s32[256]{0:T(256)S(1)} %bitcast.93, pred[256]{0:T(512)(128)(4,1)S(1)} %get-tuple-element.5, pred[256]{0:T(512)(128)(4,1)S(1)} %get-tuple-element.4), kind=kOutput, calls=%fused_computation.19 | convolution fusion | flops 538574848 | bytes 3148288 | tf_op jit(solution)/shard_map/dot_general | solution.py:85
  25.1 9.5 %all-to-all-start.2 = ((bf16[32,16,2048]{2,1,0:T(8,128)(2,1)}), bf16[32,16,2048]{2,1,0:T(8,128)(2,1)S(1)}, u32[]{:S(2)}, u32[]{:S(2)}) async-start(bf16[32,16,2048]{2,1,0:T(8,128)(2,1)} %bitcast.22), calls=%async_computation.2 | async-start | bytes 4194304 | tf_op jit(solution)/shard_map/all_to_all | solution.py:89
  34.6 2.1 %convolution_convert_fusion.1 = bf16[512,2048]{1,0:T(8,128)(2,1)} fusion(bf16[256,2048]{0,1:T(8,128)(2,1)S(1)} %fusion.32, s32[256]{0:T(256)S(1)} %bitcast.96, s32[256]{0:T(256)S(1)} %bitcast.94, pred[256]{0:T(512)(128)(4,1)S(1)} %get-tuple-element.6, pred[256]{0:T(512)(128)(4,1)S(1)} %get-tuple-element.3), kind=kOutput, calls=%fused_computation.20 | convolution fusion | flops 538574848 | bytes 3148288 | tf_op jit(solution)/shard_map/dot_general | solution.py:85
  36.8 26.1 %all-to-all-done.2 = bf16[32,16,2048]{2,1,0:T(8,128)(2,1)S(1)} async-done(((bf16[32,16,2048]{2,1,0:T(8,128)(2,1)}), bf16[32,16,2048]{2,1,0:T(8,128)(2,1)S(1)}, u32[]{:S(2)}, u32[]{:S(2)}) %all-to-all-start.2) | async-done | bytes 2097184 | tf_op jit(solution)/shard_map/all_to_all | solution.py:89
  62.9 5.2 %all-to-all-start = ((bf16[32,16,2048]{2,1,0:T(8,128)(2,1)}), bf16[32,16,2048]{2,1,0:T(8,128)(2,1)}, u32[]{:S(2)}, u32[]{:S(2)}) async-start(bf16[32,16,2048]{2,1,0:T(8,128)(2,1)} %bitcast.11), calls=%async_computation | async-start | bytes 4194304 | tf_op jit(solution)/shard_map/all_to_all | solution.py:89
  68.1 7.6 %fusion.8 = f32[512,1408]{1,0:T(8,128)} fusion(bf16[512,2048]{1,0:T(8,128)(2,1)S(1)} %bitcast.85, bf16[1,2048,1408]{2,1,0:T(8,128)(2,1)} %param.15), kind=kOutput, calls=%fused_computation.13 | convolution fusion | flops 2952790016 | bytes 10747904 | tf_op jit(solution)/shard_map/dot_general | solution.py:92
  75.7 13.3 %fusion.27 = bf16[512,2048]{1,0:T(8,128)(2,1)} fusion(bf16[1,1408,2048]{2,1,0:T(8,128)(2,1)} %param.17, bf16[512,2048]{1,0:T(8,128)(2,1)S(1)} %bitcast.86, bf16[1,2048,1408]{2,1,0:T(8,128)(2,1)} %param.16, f32[512,1408]{1,0:T(8,128)} %fusion.8), kind=kOutput, calls=%fused_computation.24 | convolution fusion | flops 5910953984 | bytes 18612224 | tf_op jit(solution)/shard_map/dot_general | solution.py:95
  89.0 2.7 %dynamic-slice_bitcast_fusion = (bf16[1,512,512]{2,1,0:T(8,128)(2,1)S(1)}, bf16[512,512]{1,0:T(8,128)(2,1)}, bf16[512,512]{1,0:T(8,128)(2,1)}, bf16[512,512]{1,0:T(8,128)(2,1)}) fusion(bf16[512,2048]{1,0:T(8,128)(2,1)} %fusion.27, s32[]{:T(128)S(6)} %select_n.179, s32[]{:T(128)S(6)} %select_n.185, s32[]{:T(128)S(6)} %select_n.183, s32[]{:T(128)S(6)} %select_n.181), kind=kLoop, calls=%fused_computation.43 | loop fusion | bytes 4194320 | tf_op jit(solution)/shard_map/stack | solution.py:46
  92.6 2.1 %collective-permute-start.7 = (bf16[512,512]{1,0:T(8,128)(2,1)}, bf16[512,512]{1,0:T(8,128)(2,1)}, u32[]{:S(2)}, u32[]{:S(2)}) collective-permute-start(bf16[512,512]{1,0:T(8,128)(2,1)} %get-tuple-element.15), channel_id=1, source_target_pairs={{0,2},{1,3},{2,0},{3,1},{4,6},{5,7},{6,4},{7,5},{8,10},{9,11},{10,... | collective-permute-start | bytes 1572872 | tf_op jit(solution)/shard_map/ppermute | solution.py:15
  96.5 8.2 %fusion.10 = f32[512,1408]{1,0:T(8,128)} fusion(bf16[512,2048]{1,0:T(8,128)(2,1)} %bitcast.12, bf16[1,2048,1408]{2,1,0:T(8,128)(2,1)} %param.15), kind=kOutput, calls=%fused_computation.15 | convolution fusion | flops 2952790016 | bytes 10747904 | tf_op jit(solution)/shard_map/dot_general | solution.py:92
  104.8 12.5 %fusion.24 = bf16[512,2048]{1,0:T(8,128)(2,1)S(1)} fusion(bf16[1,1408,2048]{2,1,0:T(8,128)(2,1)} %param.17, bf16[512,2048]{1,0:T(8,128)(2,1)} %bitcast.12, bf16[1,2048,1408]{2,1,0:T(8,128)(2,1)} %param.16, f32[512,1408]{1,0:T(8,128)} %fusion.10), kind=kOutput, calls=%fused_computation.23 | convolution fusion | flops 5910953984 | bytes 18612224 | tf_op jit(solution)/shard_map/dot_general | solution.py:95
  119.4 2.1 %collective-permute-start.4 = (bf16[512,512]{1,0:T(8,128)(2,1)}, bf16[512,512]{1,0:T(8,128)(2,1)}, u32[]{:S(2)}, u32[]{:S(2)}) collective-permute-start(bf16[512,512]{1,0:T(8,128)(2,1)} %get-tuple-element.11), channel_id=1, source_target_pairs={{0,2},{1,3},{2,0},{3,1},{4,6},{5,7},{6,4},{7,5},{8,10},{9,11},{10,... | collective-permute-start | bytes 1572872 | tf_op jit(solution)/shard_map/ppermute | solution.py:15
  126.5 6.0 %collective-permute-done.3 = bf16[512,512]{1,0:T(8,128)(2,1)} collective-permute-done((bf16[512,512]{1,0:T(8,128)(2,1)}, bf16[512,512]{1,0:T(8,128)(2,1)}, u32[]{:S(2)}, u32[]{:S(2)}) %collective-permute-start.3) | collective-permute-done | bytes 524320 | tf_op jit(solution)/shard_map/ppermute | solution.py:15
  132.6 11.6 %collective-permute-done.4 = bf16[512,512]{1,0:T(8,128)(2,1)} collective-permute-done((bf16[512,512]{1,0:T(8,128)(2,1)}, bf16[512,512]{1,0:T(8,128)(2,1)}, u32[]{:S(2)}, u32[]{:S(2)}) %collective-permute-start.4) | collective-permute-done | bytes 524320 | tf_op jit(solution)/shard_map/ppermute | solution.py:15
  146.2 2.0 %gather_fusion.3 = bf16[4,512,512]{2,1,0:T(8,128)(2,1)} fusion(bf16[4,512,512]{2,1,0:T(8,128)(2,1)S(1)} %pad_maximum_fusion, s32[1024]{0:T(1024)S(1)} %pad_clamp_fusion.1), kind=kCustom, calls=%fused_computation.clone | custom fusion | bytes 4194320 | tf_op jit(solution)/shard_map/jit(_take)/gather | solution.py:46
  148.3 2.7 %broadcast_select_fusion.1 = (bf16[4,512,512]{2,1,0:T(8,128)(2,1)S(1)}, bf16[4,512,512]{2,1,0:T(8,128)(2,1)S(1)}) fusion(bf16[4,512,512]{2,1,0:T(8,128)(2,1)} %gather_fusion.3, pred[4]{0:T(512)(128)(4,1)S(1)} %compare_and_fusion, bf16[4,512,512]{2,1,0:T(8,128)(2,1)} %gather_fusion.4), kind=kLoop, calls=%fused_computation.34 | loop fusion | flops 2097152 | bytes 8388612 | tf_op jit(solution)/shard_map/jit(_take)/select_n | solution.py:46
  152.0 8.2 %all-to-all-start.1 = ((bf16[32,16,512]{2,1,0:T(8,128)(2,1)}), bf16[32,16,512]{2,1,0:T(8,128)(2,1)S(1)}, u32[]{:S(2)}, u32[]{:S(2)}) async-start(bf16[32,16,512]{2,1,0:T(8,128)(2,1)} %bitcast.20), calls=%async_computation.1 | async-start | bytes 1048576 | tf_op jit(solution)/shard_map/all_to_all | solution.py:99
  161.4 10.6 %all-to-all-done.1 = bf16[32,16,512]{2,1,0:T(8,128)(2,1)S(1)} async-done(((bf16[32,16,512]{2,1,0:T(8,128)(2,1)}), bf16[32,16,512]{2,1,0:T(8,128)(2,1)S(1)}, u32[]{:S(2)}, u32[]{:S(2)}) %all-to-all-start.1) | async-done | bytes 524320 | tf_op jit(solution)/shard_map/all_to_all | solution.py:99
  171.9 3.9 %all-to-all-start.3 = ((bf16[32,16,512]{2,1,0:T(8,128)(2,1)}), bf16[32,16,512]{2,1,0:T(8,128)(2,1)S(1)}, u32[]{:S(2)}, u32[]{:S(2)}) async-start(bf16[32,16,512]{2,1,0:T(8,128)(2,1)} %bitcast.28), calls=%async_computation.3 | async-start | bytes 1048576 | tf_op jit(solution)/shard_map/all_to_all | solution.py:99
  176.2 11.0 %all-to-all-done.3 = bf16[32,16,512]{2,1,0:T(8,128)(2,1)S(1)} async-done(((bf16[32,16,512]{2,1,0:T(8,128)(2,1)}), bf16[32,16,512]{2,1,0:T(8,128)(2,1)S(1)}, u32[]{:S(2)}, u32[]{:S(2)}) %all-to-all-start.3) | async-done | bytes 524320 | tf_op jit(solution)/shard_map/all_to_all | solution.py:99
  191.5 3.3 %collective-permute-start.10 = (f32[256]{0:T(256)S(1)}, f32[256]{0:T(256)S(1)}, u32[]{:S(2)}, u32[]{:S(2)}) collective-permute-start(f32[256]{0:T(256)S(1)} %multiply_reduce_fusion.1), channel_id=1, source_target_pairs={{0,2},{1,3},{2,0},{3,1},{4,6},{5,7},{6,4},{7,5},{8,10},{9,11},{10,... | collective-permute-start | bytes 3080 | tf_op jit(solution)/shard_map/ppermute | solution.py:15
  (72 shorter events, 33.4 us)
Async XLA Ops:
  0.6 9.7 %collective-permute-start = (bf16[256,512]{1,0:T(8,128)(2,1)}, bf16[256,512]{1,0:T(8,128)(2,1)S(1)}, u32[]{:S(2)}, u32[]{:S(2)}) collective-permute-start(bf16[256,512]{1,0:T(8,128)(2,1)} %param.10), channel_id=1, source_target_pairs={{0,1},{1,2},{2,3},{3,0},{4,5},{5,6},{6,7},{7,4},{8,9},{9,10},{10,1... | collective-permute-start | bytes 786440 | tf_op jit(solution)/shard_map/ppermute | solution.py:15
  2.8 14.2 %collective-permute-start.1 = (bf16[256,512]{1,0:T(8,128)(2,1)}, bf16[256,512]{1,0:T(8,128)(2,1)S(1)}, u32[]{:S(2)}, u32[]{:S(2)}) collective-permute-start(bf16[256,512]{1,0:T(8,128)(2,1)} %param.10), channel_id=1, source_target_pairs={{0,2},{1,3},{2,0},{3,1},{4,6},{5,7},{6,4},{7,5},{8,10},{9,11},{10,... | collective-permute-start | bytes 786440 | tf_op jit(solution)/shard_map/ppermute | solution.py:15
  5.4 11.5 %collective-permute-start.2 = (bf16[256,512]{1,0:T(8,128)(2,1)}, bf16[256,512]{1,0:T(8,128)(2,1)S(1)}, u32[]{:S(2)}, u32[]{:S(2)}) collective-permute-start(bf16[256,512]{1,0:T(8,128)(2,1)} %param.10), channel_id=1, source_target_pairs={{0,3},{1,0},{2,1},{3,2},{4,7},{5,4},{6,5},{7,6},{8,11},{9,8},{10,9... | collective-permute-start | bytes 786440 | tf_op jit(solution)/shard_map/ppermute | solution.py:15
  20.7 2.0 copy-start.1
  25.1 37.8 %all-to-all-start.2 = ((bf16[32,16,2048]{2,1,0:T(8,128)(2,1)}), bf16[32,16,2048]{2,1,0:T(8,128)(2,1)S(1)}, u32[]{:S(2)}, u32[]{:S(2)}) async-start(bf16[32,16,2048]{2,1,0:T(8,128)(2,1)} %bitcast.22), calls=%async_computation.2 | async-start | bytes 4194304 | tf_op jit(solution)/shard_map/all_to_all | solution.py:89
  62.9 33.6 %all-to-all-start = ((bf16[32,16,2048]{2,1,0:T(8,128)(2,1)}), bf16[32,16,2048]{2,1,0:T(8,128)(2,1)}, u32[]{:S(2)}, u32[]{:S(2)}) async-start(bf16[32,16,2048]{2,1,0:T(8,128)(2,1)} %bitcast.11), calls=%async_computation | async-start | bytes 4194304 | tf_op jit(solution)/shard_map/all_to_all | solution.py:89
  91.7 29.8 %collective-permute-start.6 = (bf16[512,512]{1,0:T(8,128)(2,1)}, bf16[512,512]{1,0:T(8,128)(2,1)}, u32[]{:S(2)}, u32[]{:S(2)}) collective-permute-start(bf16[512,512]{1,0:T(8,128)(2,1)} %get-tuple-element.16), channel_id=1, source_target_pairs={{0,1},{1,2},{2,3},{3,0},{4,5},{5,6},{6,7},{7,4},{8,9},{9,10},{10,1... | collective-permute-start | bytes 1572872 | tf_op jit(solution)/shard_map/ppermute | solution.py:15
  92.6 30.2 %collective-permute-start.7 = (bf16[512,512]{1,0:T(8,128)(2,1)}, bf16[512,512]{1,0:T(8,128)(2,1)}, u32[]{:S(2)}, u32[]{:S(2)}) collective-permute-start(bf16[512,512]{1,0:T(8,128)(2,1)} %get-tuple-element.15), channel_id=1, source_target_pairs={{0,2},{1,3},{2,0},{3,1},{4,6},{5,7},{6,4},{7,5},{8,10},{9,11},{10,... | collective-permute-start | bytes 1572872 | tf_op jit(solution)/shard_map/ppermute | solution.py:15
  94.8 28.1 %collective-permute-start.8 = (bf16[512,512]{1,0:T(8,128)(2,1)}, bf16[512,512]{1,0:T(8,128)(2,1)}, u32[]{:S(2)}, u32[]{:S(2)}) collective-permute-start(bf16[512,512]{1,0:T(8,128)(2,1)} %get-tuple-element.14), channel_id=1, source_target_pairs={{0,3},{1,0},{2,1},{3,2},{4,7},{5,4},{6,5},{7,6},{8,11},{9,8},{10,9... | collective-permute-start | bytes 1572872 | tf_op jit(solution)/shard_map/ppermute | solution.py:15
  118.5 14.1 %collective-permute-start.3 = (bf16[512,512]{1,0:T(8,128)(2,1)}, bf16[512,512]{1,0:T(8,128)(2,1)}, u32[]{:S(2)}, u32[]{:S(2)}) collective-permute-start(bf16[512,512]{1,0:T(8,128)(2,1)} %get-tuple-element.12), channel_id=1, source_target_pairs={{0,1},{1,2},{2,3},{3,0},{4,5},{5,6},{6,7},{7,4},{8,9},{9,10},{10,1... | collective-permute-start | bytes 1572872 | tf_op jit(solution)/shard_map/ppermute | solution.py:15
  119.4 24.8 %collective-permute-start.4 = (bf16[512,512]{1,0:T(8,128)(2,1)}, bf16[512,512]{1,0:T(8,128)(2,1)}, u32[]{:S(2)}, u32[]{:S(2)}) collective-permute-start(bf16[512,512]{1,0:T(8,128)(2,1)} %get-tuple-element.11), channel_id=1, source_target_pairs={{0,2},{1,3},{2,0},{3,1},{4,6},{5,7},{6,4},{7,5},{8,10},{9,11},{10,... | collective-permute-start | bytes 1572872 | tf_op jit(solution)/shard_map/ppermute | solution.py:15
  121.5 23.1 %collective-permute-start.5 = (bf16[512,512]{1,0:T(8,128)(2,1)}, bf16[512,512]{1,0:T(8,128)(2,1)}, u32[]{:S(2)}, u32[]{:S(2)}) collective-permute-start(bf16[512,512]{1,0:T(8,128)(2,1)} %get-tuple-element.10), channel_id=1, source_target_pairs={{0,3},{1,0},{2,1},{3,2},{4,7},{5,4},{6,5},{7,6},{8,11},{9,8},{10,9... | collective-permute-start | bytes 1572872 | tf_op jit(solution)/shard_map/ppermute | solution.py:15
  152.0 19.9 %all-to-all-start.1 = ((bf16[32,16,512]{2,1,0:T(8,128)(2,1)}), bf16[32,16,512]{2,1,0:T(8,128)(2,1)S(1)}, u32[]{:S(2)}, u32[]{:S(2)}) async-start(bf16[32,16,512]{2,1,0:T(8,128)(2,1)} %bitcast.20), calls=%async_computation.1 | async-start | bytes 1048576 | tf_op jit(solution)/shard_map/all_to_all | solution.py:99
  160.3 15.7 %copy-start.2 = (f32[256,2]{0,1:T(2,128)S(1)}, f32[256,2]{0,1:T(2,128)}, u32[]{:S(2)}) copy-start(f32[256,2]{0,1:T(2,128)} %param.12) | copy-start | bytes 6148
  171.9 15.3 %all-to-all-start.3 = ((bf16[32,16,512]{2,1,0:T(8,128)(2,1)}), bf16[32,16,512]{2,1,0:T(8,128)(2,1)S(1)}, u32[]{:S(2)}, u32[]{:S(2)}) async-start(bf16[32,16,512]{2,1,0:T(8,128)(2,1)} %bitcast.28), calls=%async_computation.3 | async-start | bytes 1048576 | tf_op jit(solution)/shard_map/all_to_all | solution.py:99
  189.2 2.0 %copy-start = (bf16[256,512]{1,0:T(8,128)(2,1)S(1)}, bf16[256,512]{1,0:T(8,128)(2,1)}, u32[]{:S(2)}) copy-start(bf16[256,512]{1,0:T(8,128)(2,1)} %param.10) | copy-start | bytes 786436
  189.2 8.6 %copy-start.3 = (f32[512]{0:T(512)S(1)}, f32[512]{0:T(512)}, u32[]{:S(2)}) copy-start(f32[512]{0:T(512)} %param.14) | copy-start | bytes 6148
  191.4 3.7 %collective-permute-start.9 = (f32[256]{0:T(256)S(1)}, f32[256]{0:T(256)S(1)}, u32[]{:S(2)}, u32[]{:S(2)}) collective-permute-start(f32[256]{0:T(256)S(1)} %multiply_reduce_fusion.1), channel_id=1, source_target_pairs={{0,1},{1,2},{2,3},{3,0},{4,5},{5,6},{6,7},{7,4},{8,9},{9,10},{10,1... | collective-permute-start | bytes 3080 | tf_op jit(solution)/shard_map/ppermute | solution.py:15
  191.5 4.2 %collective-permute-start.10 = (f32[256]{0:T(256)S(1)}, f32[256]{0:T(256)S(1)}, u32[]{:S(2)}, u32[]{:S(2)}) collective-permute-start(f32[256]{0:T(256)S(1)} %multiply_reduce_fusion.1), channel_id=1, source_target_pairs={{0,2},{1,3},{2,0},{3,1},{4,6},{5,7},{6,4},{7,5},{8,10},{9,11},{10,... | collective-permute-start | bytes 3080 | tf_op jit(solution)/shard_map/ppermute | solution.py:15
  194.8 2.4 %collective-permute-start.11 = (f32[256]{0:T(256)S(1)}, f32[256]{0:T(256)S(1)}, u32[]{:S(2)}, u32[]{:S(2)}) collective-permute-start(f32[256]{0:T(256)S(1)} %multiply_reduce_fusion.1), channel_id=1, source_target_pairs={{0,3},{1,0},{2,1},{3,2},{4,7},{5,4},{6,5},{7,6},{8,11},{9,8},{10,9... | collective-permute-start | bytes 3080 | tf_op jit(solution)/shard_map/ppermute | solution.py:15

commit v4 on v3

--- a/solution.py
+++ b/solution.py
@@ -23,9 +23,13 @@
 
 
 def gather_tp(value, tp_count):
+    me = lax.axis_index("tp")
     rows, cols = value.shape
-    ordered = by_source(value, tp_count)
-    return ordered.transpose(1, 0, 2).reshape(rows, tp_count * cols)
+    whole = jnp.zeros((rows, tp_count * cols), value.dtype)
+    for s in range(tp_count):
+        part = value if s == 0 else shift_tp(value, s, tp_count)
+        whole = lax.dynamic_update_slice_in_dim(whole, part, ((me - s) % tp_count) * cols, axis=1)
+    return whole
 
 
 def sum_tp(value, tp_count):
@@ -43,10 +47,9 @@
     for s in range(tp_count):
         block = lax.dynamic_slice_in_dim(value, ((me + s) % tp_count) * width, width, axis=1)
         terms.append(block if s == 0 else shift_tp(block, s, tp_count))
-    ordered = jnp.take(jnp.stack(terms), (me - jnp.arange(tp_count)) % tp_count, axis=0)
-    total = ordered[0].astype(jnp.float32)
+    total = terms[0].astype(jnp.float32)
     for s in range(1, tp_count):
-        total = total + ordered[s].astype(jnp.float32)
+        total = total + terms[s].astype(jnp.float32)
     return total.astype(value.dtype)
 
 

time: 199 us -> 173 us (0.87)
  waiting for transfers between devices: 75.5 us -> 58.1 us
  other arithmetic: 16.1 us -> 9.99 us
  local copies, waits for them, and re-layouts: 15.5 us -> 9.85 us
  starting transfers between devices: 44.8 us -> 47.4 us
    all_to_all x2, waiting for transfers between devices: 21.5 us -> 11.5 us  [shards(): lax.all_to_all(summed, 'req', split_axis=0, concat_axis=0, tiled=True)]
    ppermute x12, waiting for transfers between devices: 27.3 us -> 19.9 us  [shift_tp(): lax.ppermute(value, 'tp', [(j, (j + step) % tp_count) for j in range(tp_c...]
    another operation x6 -> x2, other arithmetic: 6.57 us -> 1.18 us
    gather x2 -> x0, local copies, waits for them, and re-layouts: 4.03 us -> none  [scatter_sum_tp(): jnp.take(jnp.stack(terms), (me - jnp.arange(tp_count)) % tp_count, axis=0)]
    another operation x3 -> x1, local copies, waits for them, and re-layouts: 3.95 us -> 0.01 us  [the longest x2 3.94 us: scatter_sum_tp(): jnp.stack(terms)]
    dynamic_slice x0 -> x2, local copies, waits for them, and re-layouts: none -> 3.66 us  [scatter_sum_tp(): lax.dynamic_slice_in_dim(value, (me + s) % tp_count * width, width, axis=1)]
    convert_element_type x2, other arithmetic: 1.9 us -> 5.09 us  [scatter_sum_tp(): return total.astype(value.dtype)]
    all_to_all x2, starting transfers between devices: 12.1 us -> 15 us  [shards(): lax.all_to_all(summed, 'req', split_axis=0, concat_axis=0, tiled=True)]
  transfers between devices with their start and end apart: 16 -> 16, of which waited for: 12 -> 9; matrix products, arithmetic and copies ran while one was open for 28% -> 33% of each run, Pallas kernels for 0% -> 0%
where the time goes in v4:
time: 173 us
  waiting for transfers between devices  58.1 us (34%)
  starting transfers between devices  47.4 us (27%)
  matrix products  46.3 us (27%)
  other arithmetic  9.99 us (6%)
  local copies, waits for them, and re-layouts  9.85 us (6%)
    all_to_all x2, waiting for transfers between devices, shards(): lax.all_to_all(outgoing, 'req', split_axis=0, concat_axis=0, tiled=True)  26.7 us
    dot_general x2, matrix products, shards(): jnp.dot(activ, down_weight[0], preferred_element_type=jnp.float32)  25.7 us
    ppermute x12, waiting for transfers between devices, shift_tp(): lax.ppermute(value, 'tp', [(j, (j + step) % tp_count) for j in range(tp_c...  19.9 us
    ppermute x12, starting transfers between devices, shift_tp(): lax.ppermute(value, 'tp', [(j, (j + step) % tp_count) for j in range(tp_c...  17.8 us
    dot_general x2, matrix products, shards(): jnp.dot(flat_rows, gate_weight[0], preferred_element_type=jnp.float32)  16 us
    all_to_all x2, starting transfers between devices, shards(): lax.all_to_all(summed, 'req', split_axis=0, concat_axis=0, tiled=True)  15 us
    all_to_all x2, starting transfers between devices, shards(): lax.all_to_all(outgoing, 'req', split_axis=0, concat_axis=0, tiled=True)  14.7 us
    all_to_all x2, waiting for transfers between devices, shards(): lax.all_to_all(summed, 'req', split_axis=0, concat_axis=0, tiled=True)  11.5 us
  transfers between devices with their start and end apart: 16, of which 9 were waited for; matrix products, arithmetic and copies ran while one was open for 33% of the time, Pallas kernels for 0%

profile of v4, /device:TPU:1, one launch (start us, length us, event | category | flops | bytes accessed | tf_op | source)
XLA Modules:
  0.0 172.7 jit_solution(1848926880250121172)
XLA Ops:
  0.6 2.2 %collective-permute-start = (bf16[256,512]{1,0:T(8,128)(2,1)}, bf16[256,512]{1,0:T(8,128)(2,1)S(1)}, u32[]{:S(2)}, u32[]{:S(2)}) collective-permute-start(bf16[256,512]{1,0:T(8,128)(2,1)} %param.8), channel_id=1, source_target_pairs={{0,1},{1,2},{2,3},{3,0},{4,5},{5,6},{6,7},{7,4},{8,9},{9,10},{10,1... | collective-permute-start | bytes 786440 | tf_op jit(solution)/shard_map/ppermute | solution.py:15
  2.8 2.6 %collective-permute-start.1 = (bf16[256,512]{1,0:T(8,128)(2,1)}, bf16[256,512]{1,0:T(8,128)(2,1)S(1)}, u32[]{:S(2)}, u32[]{:S(2)}) collective-permute-start(bf16[256,512]{1,0:T(8,128)(2,1)} %param.8), channel_id=1, source_target_pairs={{0,2},{1,3},{2,0},{3,1},{4,6},{5,7},{6,4},{7,5},{8,10},{9,11},{10,... | collective-permute-start | bytes 786440 | tf_op jit(solution)/shard_map/ppermute | solution.py:15
  11.4 5.6 %collective-permute-done.1 = bf16[256,512]{1,0:T(8,128)(2,1)S(1)} collective-permute-done((bf16[256,512]{1,0:T(8,128)(2,1)}, bf16[256,512]{1,0:T(8,128)(2,1)S(1)}, u32[]{:S(2)}, u32[]{:S(2)}) %collective-permute-start.1) | collective-permute-done | bytes 262176 | tf_op jit(solution)/shard_map/ppermute | solution.py:15
  17.4 2.3 %convolution_convert_fusion.1 = bf16[512,2048]{1,0:T(8,128)(2,1)} fusion(bf16[256,2048]{1,0:T(8,128)(2,1)S(1)} %constant_dynamic-update-slice_fusion, f32[2048]{0:T(1024)S(1)} %copy-done.3, f32[256]{0:T(256)S(1)} %add_rsqrt_fusion.1, s32[256]{0:T(256)S(1)} %bitcast.72, s32[256]{0:T(256)S(1)} %bitcast.70, pred[256]{0:T(512)(128)(4,1)S(1)} %get-tuple-element.5, ...), kind=kOutput, calls=%fused_computation.17 | convolution fusion | flops 540672000 | bytes 3157504 | tf_op jit(solution)/shard_map/dot_general | solution.py:88
  19.6 9.5 %all-to-all-start = ((bf16[32,16,2048]{2,1,0:T(8,128)(2,1)}), bf16[32,16,2048]{2,1,0:T(8,128)(2,1)S(1)}, u32[]{:S(2)}, u32[]{:S(2)}) async-start(bf16[32,16,2048]{2,1,0:T(8,128)(2,1)} %bitcast.62), calls=%async_computation | async-start | bytes 4194304 | tf_op jit(solution)/shard_map/all_to_all | solution.py:92
  29.2 2.3 %convolution_convert_fusion = bf16[512,2048]{1,0:T(8,128)(2,1)} fusion(bf16[256,2048]{1,0:T(8,128)(2,1)S(1)} %constant_dynamic-update-slice_fusion, f32[2048]{0:T(1024)S(1)} %copy-done.3, f32[256]{0:T(256)S(1)} %add_rsqrt_fusion.1, s32[256]{0:T(256)S(1)} %bitcast.73, s32[256]{0:T(256)S(1)} %bitcast.71, pred[256]{0:T(512)(128)(4,1)S(1)} %get-tuple-element.4, ...), kind=kOutput, calls=%fused_computation.16 | convolution fusion | flops 540672000 | bytes 3157504 | tf_op jit(solution)/shard_map/dot_general | solution.py:88
  31.5 25.9 %all-to-all-done = bf16[32,16,2048]{2,1,0:T(8,128)(2,1)S(1)} async-done(((bf16[32,16,2048]{2,1,0:T(8,128)(2,1)}), bf16[32,16,2048]{2,1,0:T(8,128)(2,1)S(1)}, u32[]{:S(2)}, u32[]{:S(2)}) %all-to-all-start) | async-done | bytes 2097184 | tf_op jit(solution)/shard_map/all_to_all | solution.py:92
  57.4 5.2 %all-to-all-start.2 = ((bf16[32,16,2048]{2,1,0:T(8,128)(2,1)}), bf16[32,16,2048]{2,1,0:T(8,128)(2,1)}, u32[]{:S(2)}, u32[]{:S(2)}) async-start(bf16[32,16,2048]{2,1,0:T(8,128)(2,1)} %bitcast.63), calls=%async_computation.2 | async-start | bytes 4194304 | tf_op jit(solution)/shard_map/all_to_all | solution.py:92
  62.6 7.6 %fusion.10 = f32[512,1408]{1,0:T(8,128)} fusion(bf16[512,2048]{1,0:T(8,128)(2,1)S(1)} %bitcast.60, bf16[1,2048,1408]{2,1,0:T(8,128)(2,1)} %param.13), kind=kOutput, calls=%fused_computation.12 | convolution fusion | flops 2952790016 | bytes 10747904 | tf_op jit(solution)/shard_map/dot_general | solution.py:95
  70.3 13.2 %fusion.24 = bf16[512,2048]{1,0:T(8,128)(2,1)} fusion(bf16[1,1408,2048]{2,1,0:T(8,128)(2,1)} %param.15, bf16[512,2048]{1,0:T(8,128)(2,1)S(1)} %bitcast.61, bf16[1,2048,1408]{2,1,0:T(8,128)(2,1)} %param.14, f32[512,1408]{1,0:T(8,128)} %fusion.10), kind=kOutput, calls=%fused_computation.20 | convolution fusion | flops 5910953984 | bytes 18612224 | tf_op jit(solution)/shard_map/dot_general | solution.py:98
  83.5 2.5 %constant_dynamic-slice_fusion.5 = (bf16[512,512]{1,0:T(8,128)(2,1)}, bf16[512,512]{1,0:T(8,128)(2,1)S(1)}, bf16[512,512]{1,0:T(8,128)(2,1)}) fusion(bf16[512,2048]{1,0:T(8,128)(2,1)} %fusion.24, s32[]{:T(128)S(6)} %select_n.186, s32[]{:T(128)S(6)} %select_n.190, s32[]{:T(128)S(6)} %select_n.188), kind=kLoop, calls=%fused_computation.90 | loop fusion | bytes 3145740 | tf_op jit(solution)/shard_map/dynamic_slice | solution.py:48
  86.9 2.1 %collective-permute-start.4 = (bf16[512,512]{1,0:T(8,128)(2,1)}, bf16[512,512]{1,0:T(8,128)(2,1)}, u32[]{:S(2)}, u32[]{:S(2)}) collective-permute-start(bf16[512,512]{1,0:T(8,128)(2,1)} %get-tuple-element.10), channel_id=1, source_target_pairs={{0,2},{1,3},{2,0},{3,1},{4,6},{5,7},{6,4},{7,5},{8,10},{9,11},{10,... | collective-permute-start | bytes 1572872 | tf_op jit(solution)/shard_map/ppermute | solution.py:15
  91.1 8.3 %fusion.8 = f32[512,1408]{1,0:T(8,128)} fusion(bf16[512,2048]{1,0:T(8,128)(2,1)} %bitcast.12, bf16[1,2048,1408]{2,1,0:T(8,128)(2,1)} %param.13), kind=kOutput, calls=%fused_computation.10 | convolution fusion | flops 2952790016 | bytes 10747904 | tf_op jit(solution)/shard_map/dot_general | solution.py:95
  99.4 12.5 %fusion.27 = bf16[512,2048]{1,0:T(8,128)(2,1)S(1)} fusion(bf16[1,1408,2048]{2,1,0:T(8,128)(2,1)} %param.15, bf16[512,2048]{1,0:T(8,128)(2,1)} %bitcast.12, bf16[1,2048,1408]{2,1,0:T(8,128)(2,1)} %param.14, f32[512,1408]{1,0:T(8,128)} %fusion.8), kind=kOutput, calls=%fused_computation.21 | convolution fusion | flops 5910953984 | bytes 18612224 | tf_op jit(solution)/shard_map/dot_general | solution.py:98
  114.0 2.1 %collective-permute-start.7 = (bf16[512,512]{1,0:T(8,128)(2,1)}, bf16[512,512]{1,0:T(8,128)(2,1)}, u32[]{:S(2)}, u32[]{:S(2)}) collective-permute-start(bf16[512,512]{1,0:T(8,128)(2,1)} %get-tuple-element.13), channel_id=1, source_target_pairs={{0,2},{1,3},{2,0},{3,1},{4,6},{5,7},{6,4},{7,5},{8,10},{9,11},{10,... | collective-permute-start | bytes 1572872 | tf_op jit(solution)/shard_map/ppermute | solution.py:15
  117.4 2.6 %add_convert_fusion.1 = bf16[512,512]{1,0:T(8,128)(2,1)} fusion(bf16[512,512]{1,0:T(8,128)(2,1)} %collective-permute-done.5, bf16[512,512]{1,0:T(8,128)(2,1)} %collective-permute-done.4, bf16[512,512]{1,0:T(8,128)(2,1)} %collective-permute-done.3, bf16[512,2048]{1,0:T(8,128)(2,1)} %fusion.24, s32[]{:T(128)S(6)} %select_n.178), kind=kLoop, calls=%fused_computation.30 | loop fusion | flops 2097152 | bytes 2621444 | tf_op jit(solution)/shard_map/convert_element_type | solution.py:53
  120.0 6.9 %all-to-all-start.1 = ((bf16[32,16,512]{2,1,0:T(8,128)(2,1)}), bf16[32,16,512]{2,1,0:T(8,128)(2,1)S(1)}, u32[]{:S(2)}, u32[]{:S(2)}) async-start(bf16[32,16,512]{2,1,0:T(8,128)(2,1)} %bitcast.9), calls=%async_computation.1 | async-start | bytes 1048576 | tf_op jit(solution)/shard_map/all_to_all | solution.py:102
  127.2 11.5 %collective-permute-done.7 = bf16[512,512]{1,0:T(8,128)(2,1)} collective-permute-done((bf16[512,512]{1,0:T(8,128)(2,1)}, bf16[512,512]{1,0:T(8,128)(2,1)}, u32[]{:S(2)}, u32[]{:S(2)}) %collective-permute-start.7) | collective-permute-done | bytes 524320 | tf_op jit(solution)/shard_map/ppermute | solution.py:15
  139.1 2.5 %add_convert_fusion = bf16[512,512]{1,0:T(8,128)(2,1)} fusion(bf16[512,512]{1,0:T(8,128)(2,1)} %collective-permute-done.8, bf16[512,512]{1,0:T(8,128)(2,1)} %collective-permute-done.7, bf16[512,512]{1,0:T(8,128)(2,1)} %collective-permute-done.6, bf16[512,2048]{1,0:T(8,128)(2,1)S(1)} %fusion.27, s32[]{:T(128)S(6)} %select_n.178), kind=kLoop, calls=%fused_computation.29 | loop fusion | flops 2097152 | bytes 2621444 | tf_op jit(solution)/shard_map/convert_element_type | solution.py:53
  141.6 8.1 %all-to-all-start.3 = ((bf16[32,16,512]{2,1,0:T(8,128)(2,1)}), bf16[32,16,512]{2,1,0:T(8,128)(2,1)S(1)}, u32[]{:S(2)}, u32[]{:S(2)}) async-start(bf16[32,16,512]{2,1,0:T(8,128)(2,1)} %bitcast.13), calls=%async_computation.3 | async-start | bytes 1048576 | tf_op jit(solution)/shard_map/all_to_all | solution.py:102
  149.8 11.5 %all-to-all-done.3 = bf16[32,16,512]{2,1,0:T(8,128)(2,1)S(1)} async-done(((bf16[32,16,512]{2,1,0:T(8,128)(2,1)}), bf16[32,16,512]{2,1,0:T(8,128)(2,1)S(1)}, u32[]{:S(2)}, u32[]{:S(2)}) %all-to-all-start.3) | async-done | bytes 524320 | tf_op jit(solution)/shard_map/all_to_all | solution.py:102
  161.4 2.0 %gather_fusion = bf16[512,512]{1,0:T(8,128)(2,1)S(1)} fusion(bf16[1024,512]{1,0:T(8,128)(2,1)S(1)} %pad_maximum_fusion, s32[1024]{0:T(1024)S(1)} %pad_clamp_fusion.1), kind=kCustom, calls=%fused_computation | custom fusion | bytes 1050624 | tf_op jit(solution)/shard_map/gather | solution.py:106
  165.7 3.1 %collective-permute-start.10 = (f32[256]{0:T(256)S(1)}, f32[256]{0:T(256)S(1)}, u32[]{:S(2)}, u32[]{:S(2)}) collective-permute-start(f32[256]{0:T(256)S(1)} %multiply_reduce_fusion.1), channel_id=1, source_target_pairs={{0,2},{1,3},{2,0},{3,1},{4,6},{5,7},{6,4},{7,5},{8,10},{9,11},{10,... | collective-permute-start | bytes 3080 | tf_op jit(solution)/shard_map/ppermute | solution.py:15
  169.7 1.5 collective-permute-done.11
  (65 shorter events, 18.0 us)
Async XLA Ops:
  0.6 16.7 %copy-start.3 = (f32[2048]{0:T(1024)S(1)}, f32[2048]{0:T(1024)}, u32[]{:S(2)}) copy-start(f32[2048]{0:T(1024)} %param.11) | copy-start | bytes 24580
  0.6 10.7 %collective-permute-start = (bf16[256,512]{1,0:T(8,128)(2,1)}, bf16[256,512]{1,0:T(8,128)(2,1)S(1)}, u32[]{:S(2)}, u32[]{:S(2)}) collective-permute-start(bf16[256,512]{1,0:T(8,128)(2,1)} %param.8), channel_id=1, source_target_pairs={{0,1},{1,2},{2,3},{3,0},{4,5},{5,6},{6,7},{7,4},{8,9},{9,10},{10,1... | collective-permute-start | bytes 786440 | tf_op jit(solution)/shard_map/ppermute | solution.py:15
  2.8 14.2 %collective-permute-start.1 = (bf16[256,512]{1,0:T(8,128)(2,1)}, bf16[256,512]{1,0:T(8,128)(2,1)S(1)}, u32[]{:S(2)}, u32[]{:S(2)}) collective-permute-start(bf16[256,512]{1,0:T(8,128)(2,1)} %param.8), channel_id=1, source_target_pairs={{0,2},{1,3},{2,0},{3,1},{4,6},{5,7},{6,4},{7,5},{8,10},{9,11},{10,... | collective-permute-start | bytes 786440 | tf_op jit(solution)/shard_map/ppermute | solution.py:15
  5.5 11.6 %collective-permute-start.2 = (bf16[256,512]{1,0:T(8,128)(2,1)}, bf16[256,512]{1,0:T(8,128)(2,1)S(1)}, u32[]{:S(2)}, u32[]{:S(2)}) collective-permute-start(bf16[256,512]{1,0:T(8,128)(2,1)} %param.8), channel_id=1, source_target_pairs={{0,3},{1,0},{2,1},{3,2},{4,7},{5,4},{6,5},{7,6},{8,11},{9,8},{10,9... | collective-permute-start | bytes 786440 | tf_op jit(solution)/shard_map/ppermute | solution.py:15
  19.6 37.8 %all-to-all-start = ((bf16[32,16,2048]{2,1,0:T(8,128)(2,1)}), bf16[32,16,2048]{2,1,0:T(8,128)(2,1)S(1)}, u32[]{:S(2)}, u32[]{:S(2)}) async-start(bf16[32,16,2048]{2,1,0:T(8,128)(2,1)} %bitcast.62), calls=%async_computation | async-start | bytes 4194304 | tf_op jit(solution)/shard_map/all_to_all | solution.py:92
  57.4 33.6 %all-to-all-start.2 = ((bf16[32,16,2048]{2,1,0:T(8,128)(2,1)}), bf16[32,16,2048]{2,1,0:T(8,128)(2,1)}, u32[]{:S(2)}, u32[]{:S(2)}) async-start(bf16[32,16,2048]{2,1,0:T(8,128)(2,1)} %bitcast.63), calls=%async_computation.2 | async-start | bytes 4194304 | tf_op jit(solution)/shard_map/all_to_all | solution.py:92
  86.0 30.1 %collective-permute-start.3 = (bf16[512,512]{1,0:T(8,128)(2,1)}, bf16[512,512]{1,0:T(8,128)(2,1)}, u32[]{:S(2)}, u32[]{:S(2)}) collective-permute-start(bf16[512,512]{1,0:T(8,128)(2,1)} %get-tuple-element.8), channel_id=1, source_target_pairs={{0,1},{1,2},{2,3},{3,0},{4,5},{5,6},{6,7},{7,4},{8,9},{9,10},{10,1... | collective-permute-start | bytes 1572872 | tf_op jit(solution)/shard_map/ppermute | solution.py:15
  86.9 30.5 %collective-permute-start.4 = (bf16[512,512]{1,0:T(8,128)(2,1)}, bf16[512,512]{1,0:T(8,128)(2,1)}, u32[]{:S(2)}, u32[]{:S(2)}) collective-permute-start(bf16[512,512]{1,0:T(8,128)(2,1)} %get-tuple-element.10), channel_id=1, source_target_pairs={{0,2},{1,3},{2,0},{3,1},{4,6},{5,7},{6,4},{7,5},{8,10},{9,11},{10,... | collective-permute-start | bytes 1572872 | tf_op jit(solution)/shard_map/ppermute | solution.py:15
  89.0 28.3 %collective-permute-start.5 = (bf16[512,512]{1,0:T(8,128)(2,1)S(1)}, bf16[512,512]{1,0:T(8,128)(2,1)}, u32[]{:S(2)}, u32[]{:S(2)}) collective-permute-start(bf16[512,512]{1,0:T(8,128)(2,1)S(1)} %get-tuple-element.9), channel_id=1, source_target_pairs={{0,3},{1,0},{2,1},{3,2},{4,7},{5,4},{6,5},{7,6},{8,11},{9,8},{10,9... | collective-permute-start | bytes 1572872 | tf_op jit(solution)/shard_map/ppermute | solution.py:15
  111.9 15.2 %copy-start.1 = (f32[256,2]{0,1:T(2,128)S(1)}, f32[256,2]{0,1:T(2,128)}, u32[]{:S(2)}) copy-start(f32[256,2]{0,1:T(2,128)} %param.10) | copy-start | bytes 6148
  113.1 14.2 %collective-permute-start.6 = (bf16[512,512]{1,0:T(8,128)(2,1)}, bf16[512,512]{1,0:T(8,128)(2,1)}, u32[]{:S(2)}, u32[]{:S(2)}) collective-permute-start(bf16[512,512]{1,0:T(8,128)(2,1)} %get-tuple-element.11), channel_id=1, source_target_pairs={{0,1},{1,2},{2,3},{3,0},{4,5},{5,6},{6,7},{7,4},{8,9},{9,10},{10,1... | collective-permute-start | bytes 1572872 | tf_op jit(solution)/shard_map/ppermute | solution.py:15
  114.0 24.8 %collective-permute-start.7 = (bf16[512,512]{1,0:T(8,128)(2,1)}, bf16[512,512]{1,0:T(8,128)(2,1)}, u32[]{:S(2)}, u32[]{:S(2)}) collective-permute-start(bf16[512,512]{1,0:T(8,128)(2,1)} %get-tuple-element.13), channel_id=1, source_target_pairs={{0,2},{1,3},{2,0},{3,1},{4,6},{5,7},{6,4},{7,5},{8,10},{9,11},{10,... | collective-permute-start | bytes 1572872 | tf_op jit(solution)/shard_map/ppermute | solution.py:15
  116.1 23.0 %collective-permute-start.8 = (bf16[512,512]{1,0:T(8,128)(2,1)S(1)}, bf16[512,512]{1,0:T(8,128)(2,1)}, u32[]{:S(2)}, u32[]{:S(2)}) collective-permute-start(bf16[512,512]{1,0:T(8,128)(2,1)S(1)} %get-tuple-element.12), channel_id=1, source_target_pairs={{0,3},{1,0},{2,1},{3,2},{4,7},{5,4},{6,5},{7,6},{8,11},{9,8},{10,9... | collective-permute-start | bytes 1572872 | tf_op jit(solution)/shard_map/ppermute | solution.py:15
  120.0 21.6 %all-to-all-start.1 = ((bf16[32,16,512]{2,1,0:T(8,128)(2,1)}), bf16[32,16,512]{2,1,0:T(8,128)(2,1)S(1)}, u32[]{:S(2)}, u32[]{:S(2)}) async-start(bf16[32,16,512]{2,1,0:T(8,128)(2,1)} %bitcast.9), calls=%async_computation.1 | async-start | bytes 1048576 | tf_op jit(solution)/shard_map/all_to_all | solution.py:102
  141.6 19.7 %all-to-all-start.3 = ((bf16[32,16,512]{2,1,0:T(8,128)(2,1)}), bf16[32,16,512]{2,1,0:T(8,128)(2,1)S(1)}, u32[]{:S(2)}, u32[]{:S(2)}) async-start(bf16[32,16,512]{2,1,0:T(8,128)(2,1)} %bitcast.13), calls=%async_computation.3 | async-start | bytes 1048576 | tf_op jit(solution)/shard_map/all_to_all | solution.py:102
  161.4 4.0 %copy-start = (bf16[256,512]{1,0:T(8,128)(2,1)S(1)}, bf16[256,512]{1,0:T(8,128)(2,1)}, u32[]{:S(2)}) copy-start(bf16[256,512]{1,0:T(8,128)(2,1)} %param.8) | copy-start | bytes 786436
  163.4 8.5 %copy-start.2 = (f32[512]{0:T(512)S(1)}, f32[512]{0:T(512)}, u32[]{:S(2)}) copy-start(f32[512]{0:T(512)} %param.12) | copy-start | bytes 6148
  165.5 3.7 %collective-permute-start.9 = (f32[256]{0:T(256)S(1)}, f32[256]{0:T(256)S(1)}, u32[]{:S(2)}, u32[]{:S(2)}) collective-permute-start(f32[256]{0:T(256)S(1)} %multiply_reduce_fusion.1), channel_id=1, source_target_pairs={{0,1},{1,2},{2,3},{3,0},{4,5},{5,6},{6,7},{7,4},{8,9},{9,10},{10,1... | collective-permute-start | bytes 3080 | tf_op jit(solution)/shard_map/ppermute | solution.py:15
  165.7 4.0 %collective-permute-start.10 = (f32[256]{0:T(256)S(1)}, f32[256]{0:T(256)S(1)}, u32[]{:S(2)}, u32[]{:S(2)}) collective-permute-start(f32[256]{0:T(256)S(1)} %multiply_reduce_fusion.1), channel_id=1, source_target_pairs={{0,2},{1,3},{2,0},{3,1},{4,6},{5,7},{6,4},{7,5},{8,10},{9,11},{10,... | collective-permute-start | bytes 3080 | tf_op jit(solution)/shard_map/ppermute | solution.py:15
  168.8 2.4 %collective-permute-start.11 = (f32[256]{0:T(256)S(1)}, f32[256]{0:T(256)S(1)}, u32[]{:S(2)}, u32[]{:S(2)}) collective-permute-start(f32[256]{0:T(256)S(1)} %multiply_reduce_fusion.1), channel_id=1, source_target_pairs={{0,3},{1,0},{2,1},{3,2},{4,7},{5,4},{6,5},{7,6},{8,11},{9,8},{10,9... | collective-permute-start | bytes 3080 | tf_op jit(solution)/shard_map/ppermute | solution.py:15

commit v5 on v4

--- a/solution.py
+++ b/solution.py
@@ -5,7 +5,7 @@
 
 E = 8
 CAP = 128
-CHUNKS = 2
+CHUNKS = 4
 
 
 epsilon = 1e-05

time: 173 us -> 205 us (1.18)
  starting transfers between devices: 47.4 us -> 74.4 us
  matrix products: 46.3 us -> 62.6 us
  waiting for transfers between devices: 58.1 us -> 41.8 us
  other arithmetic: 9.99 us -> 14.2 us
    all_to_all x2 -> x4, starting transfers between devices: 14.7 us -> 28.4 us  [shards(): lax.all_to_all(outgoing, 'req', split_axis=0, concat_axis=0, tiled=True)]
    ppermute x12 -> x18, waiting for transfers between devices: 19.9 us -> 8.77 us  [shift_tp(): lax.ppermute(value, 'tp', [(j, (j + step) % tp_count) for j in range(tp_c...]
    all_to_all x2 -> x4, waiting for transfers between devices: 26.7 us -> 15.8 us  [shards(): lax.all_to_all(outgoing, 'req', split_axis=0, concat_axis=0, tiled=True)]
    reshape x0 -> x4, other arithmetic: none -> 7.74 us  [shards(): summed = summed.reshape(sources, items, col_part)]
    dot_general x2 -> x4, matrix products: 25.7 us -> 33.4 us  [shards(): jnp.dot(activ, down_weight[0], preferred_element_type=jnp.float32)]
    dot_general x2 -> x4, matrix products: 16 us -> 22.9 us  [shards(): jnp.dot(flat_rows, gate_weight[0], preferred_element_type=jnp.float32)]
    all_to_all x2 -> x4, starting transfers between devices: 15 us -> 21.7 us  [shards(): lax.all_to_all(summed, 'req', split_axis=0, concat_axis=0, tiled=True)]
    ppermute x12 -> x18, starting transfers between devices: 17.8 us -> 24.3 us  [shift_tp(): lax.ppermute(value, 'tp', [(j, (j + step) % tp_count) for j in range(tp_c...]
  transfers between devices with their start and end apart: 16 -> 26, of which waited for: 9 -> 10; matrix products, arithmetic and copies ran while one was open for 33% -> 38% of each run, Pallas kernels for 0% -> 0%
where the time goes in v5:
time: 205 us; the launch traced here: 203 us
  starting transfers between devices  74.4 us (36%)
  matrix products  62.6 us (31%)
  waiting for transfers between devices  41.8 us (20%)
  other arithmetic  14.2 us (7%)
  local copies, waits for them, and re-layouts  9.2 us (4%)
    dot_general x4, matrix products, shards(): jnp.dot(activ, down_weight[0], preferred_element_type=jnp.float32)  33.4 us
    all_to_all x4, starting transfers between devices, shards(): lax.all_to_all(outgoing, 'req', split_axis=0, concat_axis=0, tiled=True)  28.4 us
    ppermute x18, starting transfers between devices, shift_tp(): lax.ppermute(value, 'tp', [(j, (j + step) % tp_count) for j in range(tp_c...  24.3 us
    dot_general x4, matrix products, shards(): jnp.dot(flat_rows, gate_weight[0], preferred_element_type=jnp.float32)  22.9 us
    all_to_all x4, starting transfers between devices, shards(): lax.all_to_all(summed, 'req', split_axis=0, concat_axis=0, tiled=True)  21.7 us
    all_to_all x4, waiting for transfers between devices, shards(): lax.all_to_all(summed, 'req', split_axis=0, concat_axis=0, tiled=True)  17.2 us
    all_to_all x4, waiting for transfers between devices, shards(): lax.all_to_all(outgoing, 'req', split_axis=0, concat_axis=0, tiled=True)  15.8 us
    ppermute x18, waiting for transfers between devices, shift_tp(): lax.ppermute(value, 'tp', [(j, (j + step) % tp_count) for j in range(tp_c...  8.77 us
  transfers between devices with their start and end apart: 26, of which 10 were waited for; matrix products, arithmetic and copies ran while one was open for 38% of the time, Pallas kernels for 0%

profile of v5, /device:TPU:1, one launch (start us, length us, event | category | flops | bytes accessed | tf_op | source)
XLA Modules:
  0.0 203.3 jit_solution(9141514731732655574)
XLA Ops:
  2.8 2.6 %collective-permute-start.1 = (bf16[256,512]{1,0:T(8,128)(2,1)}, bf16[256,512]{1,0:T(8,128)(2,1)S(1)}, u32[]{:S(2)}, u32[]{:S(2)}) collective-permute-start(bf16[256,512]{1,0:T(8,128)(2,1)} %param.8), channel_id=1, source_target_pairs={{0,2},{1,3},{2,0},{3,1},{4,6},{5,7},{6,4},{7,5},{8,10},{9,11},{10,... | collective-permute-start | bytes 786440 | tf_op jit(solution)/shard_map/ppermute | solution.py:15
  11.4 5.6 %collective-permute-done.1 = bf16[256,512]{1,0:T(8,128)(2,1)S(1)} collective-permute-done((bf16[256,512]{1,0:T(8,128)(2,1)}, bf16[256,512]{1,0:T(8,128)(2,1)S(1)}, u32[]{:S(2)}, u32[]{:S(2)}) %collective-permute-start.1) | collective-permute-done | bytes 262176 | tf_op jit(solution)/shard_map/ppermute | solution.py:15
  19.0 9.5 %all-to-all-start = ((bf16[32,8,2048]{2,1,0:T(8,128)(2,1)}), bf16[32,8,2048]{2,1,0:T(8,128)(2,1)S(1)}, u32[]{:S(2)}, u32[]{:S(2)}) async-start(bf16[32,8,2048]{2,1,0:T(8,128)(2,1)} %fusion.60), calls=%async_computation | async-start | bytes 2097152 | tf_op jit(solution)/shard_map/all_to_all | solution.py:92
  33.4 12.0 %all-to-all-done = bf16[32,8,2048]{2,1,0:T(8,128)(2,1)S(1)} async-done(((bf16[32,8,2048]{2,1,0:T(8,128)(2,1)}), bf16[32,8,2048]{2,1,0:T(8,128)(2,1)S(1)}, u32[]{:S(2)}, u32[]{:S(2)}) %all-to-all-start) | async-done | bytes 1048608 | tf_op jit(solution)/shard_map/all_to_all | solution.py:92
  45.4 4.0 %all-to-all-start.2 = ((bf16[32,8,2048]{2,1,0:T(8,128)(2,1)}), bf16[32,8,2048]{2,1,0:T(8,128)(2,1)S(1)}, u32[]{:S(2)}, u32[]{:S(2)}) async-start(bf16[32,8,2048]{2,1,0:T(8,128)(2,1)} %fusion.61), calls=%async_computation.2 | async-start | bytes 2097152 | tf_op jit(solution)/shard_map/all_to_all | solution.py:92
  49.3 5.5 %fusion.22 = f32[256,1408]{1,0:T(8,128)} fusion(bf16[1,2048,1408]{2,1,0:T(8,128)(2,1)} %param.13, bf16[32,8,2048]{2,1,0:T(8,128)(2,1)S(1)} %all-to-all-done), kind=kOutput, calls=%fused_computation.24 | convolution fusion | flops 1476395008 | bytes 8257536 | tf_op jit(solution)/shard_map/dot_general | solution.py:95
  54.9 8.2 %fusion.48 = bf16[256,2048]{1,0:T(8,128)(2,1)S(1)} fusion(bf16[1,1408,2048]{2,1,0:T(8,128)(2,1)} %param.15, bf16[1,2048,1408]{2,1,0:T(8,128)(2,1)} %param.14, f32[256,1408]{1,0:T(8,128)} %fusion.22, bf16[32,8,2048]{2,1,0:T(8,128)(2,1)S(1)} %all-to-all-done), kind=kOutput, calls=%fused_computation.40 | convolution fusion | flops 2955476992 | bytes 15073280 | tf_op jit(solution)/shard_map/dot_general | solution.py:98
  68.3 8.3 %all-to-all-start.4 = ((bf16[32,8,2048]{2,1,0:T(8,128)(2,1)}), bf16[32,8,2048]{2,1,0:T(8,128)(2,1)}, u32[]{:S(2)}, u32[]{:S(2)}) async-start(bf16[32,8,2048]{2,1,0:T(8,128)(2,1)} %fusion.62), calls=%async_computation.4 | async-start | bytes 2097152 | tf_op jit(solution)/shard_map/all_to_all | solution.py:92
  76.6 5.5 %fusion.20 = f32[256,1408]{1,0:T(8,128)} fusion(bf16[1,2048,1408]{2,1,0:T(8,128)(2,1)} %param.13, bf16[32,8,2048]{2,1,0:T(8,128)(2,1)S(1)} %all-to-all-done.2), kind=kOutput, calls=%fused_computation.22 | convolution fusion | flops 1476395008 | bytes 8257536 | tf_op jit(solution)/shard_map/dot_general | solution.py:95
  82.2 8.2 %fusion.51 = bf16[256,2048]{1,0:T(8,128)(2,1)S(1)} fusion(bf16[1,1408,2048]{2,1,0:T(8,128)(2,1)} %param.15, bf16[1,2048,1408]{2,1,0:T(8,128)(2,1)} %param.14, f32[256,1408]{1,0:T(8,128)} %fusion.20, bf16[32,8,2048]{2,1,0:T(8,128)(2,1)S(1)} %all-to-all-done.2), kind=kOutput, calls=%fused_computation.41 | convolution fusion | flops 2955476992 | bytes 15073280 | tf_op jit(solution)/shard_map/dot_general | solution.py:98
  93.6 6.7 %all-to-all-start.6 = ((bf16[32,8,2048]{2,1,0:T(8,128)(2,1)}), bf16[32,8,2048]{2,1,0:T(8,128)(2,1)}, u32[]{:S(2)}, u32[]{:S(2)}) async-start(bf16[32,8,2048]{2,1,0:T(8,128)(2,1)} %fusion.63), calls=%async_computation.6 | async-start | bytes 2097152 | tf_op jit(solution)/shard_map/all_to_all | solution.py:92
  100.3 5.9 %fusion.18 = f32[256,1408]{1,0:T(8,128)} fusion(bf16[1,2048,1408]{2,1,0:T(8,128)(2,1)} %param.13, bf16[32,8,2048]{2,1,0:T(8,128)(2,1)} %all-to-all-done.4), kind=kOutput, calls=%fused_computation.20 | convolution fusion | flops 1476395008 | bytes 8257536 | tf_op jit(solution)/shard_map/dot_general | solution.py:95
  106.2 8.5 %fusion.54 = bf16[256,2048]{1,0:T(8,128)(2,1)S(1)} fusion(bf16[1,1408,2048]{2,1,0:T(8,128)(2,1)} %param.15, bf16[1,2048,1408]{2,1,0:T(8,128)(2,1)} %param.14, f32[256,1408]{1,0:T(8,128)} %fusion.18, bf16[32,8,2048]{2,1,0:T(8,128)(2,1)} %all-to-all-done.4), kind=kOutput, calls=%fused_computation.42 | convolution fusion | flops 2955476992 | bytes 15073280 | tf_op jit(solution)/shard_map/dot_general | solution.py:98
  114.7 2.6 %all-to-all-done.6 = bf16[32,8,2048]{2,1,0:T(8,128)(2,1)} async-done(((bf16[32,8,2048]{2,1,0:T(8,128)(2,1)}), bf16[32,8,2048]{2,1,0:T(8,128)(2,1)}, u32[]{:S(2)}, u32[]{:S(2)}) %all-to-all-start.6) | async-done | bytes 1048608 | tf_op jit(solution)/shard_map/all_to_all | solution.py:92
  117.3 5.9 %fusion.16 = f32[256,1408]{1,0:T(8,128)} fusion(bf16[1,2048,1408]{2,1,0:T(8,128)(2,1)} %param.13, bf16[32,8,2048]{2,1,0:T(8,128)(2,1)} %all-to-all-done.6), kind=kOutput, calls=%fused_computation.18 | convolution fusion | flops 1476395008 | bytes 8257536 | tf_op jit(solution)/shard_map/dot_general | solution.py:95
  130.8 5.5 %all-to-all-start.1 = ((bf16[32,8,512]{2,1,0:T(8,128)(2,1)}), bf16[32,8,512]{2,1,0:T(8,128)(2,1)}, u32[]{:S(2)}, u32[]{:S(2)}) async-start(bf16[32,8,512]{2,1,0:T(8,128)(2,1)} %fusion.95), calls=%async_computation.1 | async-start | bytes 524288 | tf_op jit(solution)/shard_map/all_to_all | solution.py:102
  136.2 8.5 %fusion.57 = bf16[256,2048]{1,0:T(8,128)(2,1)S(1)} fusion(bf16[1,1408,2048]{2,1,0:T(8,128)(2,1)} %param.15, bf16[1,2048,1408]{2,1,0:T(8,128)(2,1)} %param.14, f32[256,1408]{1,0:T(8,128)} %fusion.16, bf16[32,8,2048]{2,1,0:T(8,128)(2,1)} %all-to-all-done.6), kind=kOutput, calls=%fused_computation.43 | convolution fusion | flops 2955476992 | bytes 15073280 | tf_op jit(solution)/shard_map/dot_general | solution.py:98
  147.8 7.7 %all-to-all-start.3 = ((bf16[32,8,512]{2,1,0:T(8,128)(2,1)}), bf16[32,8,512]{2,1,0:T(8,128)(2,1)S(1)}, u32[]{:S(2)}, u32[]{:S(2)}) async-start(bf16[32,8,512]{2,1,0:T(8,128)(2,1)} %fusion.96), calls=%async_computation.3 | async-start | bytes 524288 | tf_op jit(solution)/shard_map/all_to_all | solution.py:102
  156.4 2.8 %collective-permute-start.13 = (bf16[256,512]{1,0:T(8,128)(2,1)}, bf16[256,512]{1,0:T(8,128)(2,1)}, u32[]{:S(2)}, u32[]{:S(2)}) collective-permute-start(bf16[256,512]{1,0:T(8,128)(2,1)} %get-tuple-element.23), channel_id=1, source_target_pairs={{0,2},{1,3},{2,0},{3,1},{4,6},{5,7},{6,4},{7,5},{8,10},{9,11},{10,... | collective-permute-start | bytes 786440 | tf_op jit(solution)/shard_map/ppermute | solution.py:15
  161.2 3.3 %all-to-all-done.3 = bf16[32,8,512]{2,1,0:T(8,128)(2,1)S(1)} async-done(((bf16[32,8,512]{2,1,0:T(8,128)(2,1)}), bf16[32,8,512]{2,1,0:T(8,128)(2,1)S(1)}, u32[]{:S(2)}, u32[]{:S(2)}) %all-to-all-start.3) | async-done | bytes 262176 | tf_op jit(solution)/shard_map/all_to_all | solution.py:102
  164.5 4.9 %all-to-all-start.5 = ((bf16[32,8,512]{2,1,0:T(8,128)(2,1)}), bf16[32,8,512]{2,1,0:T(8,128)(2,1)S(1)}, u32[]{:S(2)}, u32[]{:S(2)}) async-start(bf16[32,8,512]{2,1,0:T(8,128)(2,1)} %fusion.97), calls=%async_computation.5 | async-start | bytes 524288 | tf_op jit(solution)/shard_map/all_to_all | solution.py:102
  173.4 5.0 %all-to-all-done.5 = bf16[32,8,512]{2,1,0:T(8,128)(2,1)S(1)} async-done(((bf16[32,8,512]{2,1,0:T(8,128)(2,1)}), bf16[32,8,512]{2,1,0:T(8,128)(2,1)S(1)}, u32[]{:S(2)}, u32[]{:S(2)}) %all-to-all-start.5) | async-done | bytes 262176 | tf_op jit(solution)/shard_map/all_to_all | solution.py:102
  178.4 3.7 %all-to-all-start.7 = ((bf16[32,8,512]{2,1,0:T(8,128)(2,1)}), bf16[32,8,512]{2,1,0:T(8,128)(2,1)S(1)}, u32[]{:S(2)}, u32[]{:S(2)}) async-start(bf16[32,8,512]{2,1,0:T(8,128)(2,1)} %fusion.98), calls=%async_computation.7 | async-start | bytes 524288 | tf_op jit(solution)/shard_map/all_to_all | solution.py:102
  182.3 8.9 %all-to-all-done.7 = bf16[32,8,512]{2,1,0:T(8,128)(2,1)S(1)} async-done(((bf16[32,8,512]{2,1,0:T(8,128)(2,1)}), bf16[32,8,512]{2,1,0:T(8,128)(2,1)S(1)}, u32[]{:S(2)}, u32[]{:S(2)}) %all-to-all-start.7) | async-done | bytes 262176 | tf_op jit(solution)/shard_map/all_to_all | solution.py:102
  (97 shorter events, 53.0 us)
Async XLA Ops:
  0.6 10.7 %collective-permute-start = (bf16[256,512]{1,0:T(8,128)(2,1)}, bf16[256,512]{1,0:T(8,128)(2,1)S(1)}, u32[]{:S(2)}, u32[]{:S(2)}) collective-permute-start(bf16[256,512]{1,0:T(8,128)(2,1)} %param.8), channel_id=1, source_target_pairs={{0,1},{1,2},{2,3},{3,0},{4,5},{5,6},{6,7},{7,4},{8,9},{9,10},{10,1... | collective-permute-start | bytes 786440 | tf_op jit(solution)/shard_map/ppermute | solution.py:15
  2.8 14.2 %collective-permute-start.1 = (bf16[256,512]{1,0:T(8,128)(2,1)}, bf16[256,512]{1,0:T(8,128)(2,1)S(1)}, u32[]{:S(2)}, u32[]{:S(2)}) collective-permute-start(bf16[256,512]{1,0:T(8,128)(2,1)} %param.8), channel_id=1, source_target_pairs={{0,2},{1,3},{2,0},{3,1},{4,6},{5,7},{6,4},{7,5},{8,10},{9,11},{10,... | collective-permute-start | bytes 786440 | tf_op jit(solution)/shard_map/ppermute | solution.py:15
  5.5 11.6 %collective-permute-start.2 = (bf16[256,512]{1,0:T(8,128)(2,1)}, bf16[256,512]{1,0:T(8,128)(2,1)S(1)}, u32[]{:S(2)}, u32[]{:S(2)}) collective-permute-start(bf16[256,512]{1,0:T(8,128)(2,1)} %param.8), channel_id=1, source_target_pairs={{0,3},{1,0},{2,1},{3,2},{4,7},{5,4},{6,5},{7,6},{8,11},{9,8},{10,9... | collective-permute-start | bytes 786440 | tf_op jit(solution)/shard_map/ppermute | solution.py:15
  19.0 26.4 %all-to-all-start = ((bf16[32,8,2048]{2,1,0:T(8,128)(2,1)}), bf16[32,8,2048]{2,1,0:T(8,128)(2,1)S(1)}, u32[]{:S(2)}, u32[]{:S(2)}) async-start(bf16[32,8,2048]{2,1,0:T(8,128)(2,1)} %fusion.60), calls=%async_computation | async-start | bytes 2097152 | tf_op jit(solution)/shard_map/all_to_all | solution.py:92
  45.4 23.0 %all-to-all-start.2 = ((bf16[32,8,2048]{2,1,0:T(8,128)(2,1)}), bf16[32,8,2048]{2,1,0:T(8,128)(2,1)S(1)}, u32[]{:S(2)}, u32[]{:S(2)}) async-start(bf16[32,8,2048]{2,1,0:T(8,128)(2,1)} %fusion.61), calls=%async_computation.2 | async-start | bytes 2097152 | tf_op jit(solution)/shard_map/all_to_all | solution.py:92
  64.0 60.1 %collective-permute-start.3 = (bf16[256,512]{1,0:T(8,128)(2,1)}, bf16[256,512]{1,0:T(8,128)(2,1)}, u32[]{:S(2)}, u32[]{:S(2)}) collective-permute-start(bf16[256,512]{1,0:T(8,128)(2,1)} %get-tuple-element.12), channel_id=1, source_target_pairs={{0,1},{1,2},{2,3},{3,0},{4,5},{5,6},{6,7},{7,4},{8,9},{9,10},{10,1... | collective-permute-start | bytes 786440 | tf_op jit(solution)/shard_map/ppermute | solution.py:15
  64.9 61.0 %collective-permute-start.4 = (bf16[256,512]{1,0:T(8,128)(2,1)}, bf16[256,512]{1,0:T(8,128)(2,1)}, u32[]{:S(2)}, u32[]{:S(2)}) collective-permute-start(bf16[256,512]{1,0:T(8,128)(2,1)} %get-tuple-element.14), channel_id=1, source_target_pairs={{0,2},{1,3},{2,0},{3,1},{4,6},{5,7},{6,4},{7,5},{8,10},{9,11},{10,... | collective-permute-start | bytes 786440 | tf_op jit(solution)/shard_map/ppermute | solution.py:15
  67.0 61.1 %collective-permute-start.5 = (bf16[256,512]{1,0:T(8,128)(2,1)}, bf16[256,512]{1,0:T(8,128)(2,1)}, u32[]{:S(2)}, u32[]{:S(2)}) collective-permute-start(bf16[256,512]{1,0:T(8,128)(2,1)} %get-tuple-element.13), channel_id=1, source_target_pairs={{0,3},{1,0},{2,1},{3,2},{4,7},{5,4},{6,5},{7,6},{8,11},{9,8},{10,9... | collective-permute-start | bytes 786440 | tf_op jit(solution)/shard_map/ppermute | solution.py:15
  68.3 25.2 %all-to-all-start.4 = ((bf16[32,8,2048]{2,1,0:T(8,128)(2,1)}), bf16[32,8,2048]{2,1,0:T(8,128)(2,1)}, u32[]{:S(2)}, u32[]{:S(2)}) async-start(bf16[32,8,2048]{2,1,0:T(8,128)(2,1)} %fusion.62), calls=%async_computation.4 | async-start | bytes 2097152 | tf_op jit(solution)/shard_map/all_to_all | solution.py:92
  91.3 53.5 %collective-permute-start.6 = (bf16[256,512]{1,0:T(8,128)(2,1)}, bf16[256,512]{1,0:T(8,128)(2,1)}, u32[]{:S(2)}, u32[]{:S(2)}) collective-permute-start(bf16[256,512]{1,0:T(8,128)(2,1)} %get-tuple-element.15), channel_id=1, source_target_pairs={{0,1},{1,2},{2,3},{3,0},{4,5},{5,6},{6,7},{7,4},{8,9},{9,10},{10,1... | collective-permute-start | bytes 786440 | tf_op jit(solution)/shard_map/ppermute | solution.py:15
  91.4 54.4 %collective-permute-start.7 = (bf16[256,512]{1,0:T(8,128)(2,1)}, bf16[256,512]{1,0:T(8,128)(2,1)}, u32[]{:S(2)}, u32[]{:S(2)}) collective-permute-start(bf16[256,512]{1,0:T(8,128)(2,1)} %get-tuple-element.17), channel_id=1, source_target_pairs={{0,2},{1,3},{2,0},{3,1},{4,6},{5,7},{6,4},{7,5},{8,10},{9,11},{10,... | collective-permute-start | bytes 786440 | tf_op jit(solution)/shard_map/ppermute | solution.py:15
  93.6 23.7 %all-to-all-start.6 = ((bf16[32,8,2048]{2,1,0:T(8,128)(2,1)}), bf16[32,8,2048]{2,1,0:T(8,128)(2,1)}, u32[]{:S(2)}, u32[]{:S(2)}) async-start(bf16[32,8,2048]{2,1,0:T(8,128)(2,1)} %fusion.63), calls=%async_computation.6 | async-start | bytes 2097152 | tf_op jit(solution)/shard_map/all_to_all | solution.py:92
  124.1 21.8 %collective-permute-start.8 = (bf16[256,512]{1,0:T(8,128)(2,1)}, bf16[256,512]{1,0:T(8,128)(2,1)}, u32[]{:S(2)}, u32[]{:S(2)}) collective-permute-start(bf16[256,512]{1,0:T(8,128)(2,1)} %get-tuple-element.16), channel_id=1, source_target_pairs={{0,3},{1,0},{2,1},{3,2},{4,7},{5,4},{6,5},{7,6},{8,11},{9,8},{10,9... | collective-permute-start | bytes 786440 | tf_op jit(solution)/shard_map/ppermute | solution.py:15
  125.9 33.3 %collective-permute-start.10 = (bf16[256,512]{1,0:T(8,128)(2,1)}, bf16[256,512]{1,0:T(8,128)(2,1)}, u32[]{:S(2)}, u32[]{:S(2)}) collective-permute-start(bf16[256,512]{1,0:T(8,128)(2,1)} %get-tuple-element.20), channel_id=1, source_target_pairs={{0,2},{1,3},{2,0},{3,1},{4,6},{5,7},{6,4},{7,5},{8,10},{9,11},{10,... | collective-permute-start | bytes 786440 | tf_op jit(solution)/shard_map/ppermute | solution.py:15
  128.1 31.1 %collective-permute-start.11 = (bf16[256,512]{1,0:T(8,128)(2,1)}, bf16[256,512]{1,0:T(8,128)(2,1)}, u32[]{:S(2)}, u32[]{:S(2)}) collective-permute-start(bf16[256,512]{1,0:T(8,128)(2,1)} %get-tuple-element.19), channel_id=1, source_target_pairs={{0,3},{1,0},{2,1},{3,2},{4,7},{5,4},{6,5},{7,6},{8,11},{9,8},{10,9... | collective-permute-start | bytes 786440 | tf_op jit(solution)/shard_map/ppermute | solution.py:15
  130.8 17.1 %all-to-all-start.1 = ((bf16[32,8,512]{2,1,0:T(8,128)(2,1)}), bf16[32,8,512]{2,1,0:T(8,128)(2,1)}, u32[]{:S(2)}, u32[]{:S(2)}) async-start(bf16[32,8,512]{2,1,0:T(8,128)(2,1)} %fusion.95), calls=%async_computation.1 | async-start | bytes 524288 | tf_op jit(solution)/shard_map/all_to_all | solution.py:102
  144.7 14.5 %collective-permute-start.9 = (bf16[256,512]{1,0:T(8,128)(2,1)}, bf16[256,512]{1,0:T(8,128)(2,1)}, u32[]{:S(2)}, u32[]{:S(2)}) collective-permute-start(bf16[256,512]{1,0:T(8,128)(2,1)} %get-tuple-element.18), channel_id=1, source_target_pairs={{0,1},{1,2},{2,3},{3,0},{4,5},{5,6},{6,7},{7,4},{8,9},{9,10},{10,1... | collective-permute-start | bytes 786440 | tf_op jit(solution)/shard_map/ppermute | solution.py:15
  147.8 16.7 %all-to-all-start.3 = ((bf16[32,8,512]{2,1,0:T(8,128)(2,1)}), bf16[32,8,512]{2,1,0:T(8,128)(2,1)S(1)}, u32[]{:S(2)}, u32[]{:S(2)}) async-start(bf16[32,8,512]{2,1,0:T(8,128)(2,1)} %fusion.96), calls=%async_computation.3 | async-start | bytes 524288 | tf_op jit(solution)/shard_map/all_to_all | solution.py:102
  156.4 13.0 %collective-permute-start.12 = (bf16[256,512]{1,0:T(8,128)(2,1)}, bf16[256,512]{1,0:T(8,128)(2,1)S(1)}, u32[]{:S(2)}, u32[]{:S(2)}) collective-permute-start(bf16[256,512]{1,0:T(8,128)(2,1)} %get-tuple-element.21), channel_id=1, source_target_pairs={{0,1},{1,2},{2,3},{3,0},{4,5},{5,6},{6,7},{7,4},{8,9},{9,10},{10,1... | collective-permute-start | bytes 786440 | tf_op jit(solution)/shard_map/ppermute | solution.py:15
  156.4 14.9 %collective-permute-start.13 = (bf16[256,512]{1,0:T(8,128)(2,1)}, bf16[256,512]{1,0:T(8,128)(2,1)}, u32[]{:S(2)}, u32[]{:S(2)}) collective-permute-start(bf16[256,512]{1,0:T(8,128)(2,1)} %get-tuple-element.23), channel_id=1, source_target_pairs={{0,2},{1,3},{2,0},{3,1},{4,6},{5,7},{6,4},{7,5},{8,10},{9,11},{10,... | collective-permute-start | bytes 786440 | tf_op jit(solution)/shard_map/ppermute | solution.py:15
  159.2 12.3 %collective-permute-start.14 = (bf16[256,512]{1,0:T(8,128)(2,1)S(1)}, bf16[256,512]{1,0:T(8,128)(2,1)}, u32[]{:S(2)}, u32[]{:S(2)}) collective-permute-start(bf16[256,512]{1,0:T(8,128)(2,1)S(1)} %get-tuple-element.22), channel_id=1, source_target_pairs={{0,3},{1,0},{2,1},{3,2},{4,7},{5,4},{6,5},{7,6},{8,11},{9,8},{10,9... | collective-permute-start | bytes 786440 | tf_op jit(solution)/shard_map/ppermute | solution.py:15
  164.5 13.9 %all-to-all-start.5 = ((bf16[32,8,512]{2,1,0:T(8,128)(2,1)}), bf16[32,8,512]{2,1,0:T(8,128)(2,1)S(1)}, u32[]{:S(2)}, u32[]{:S(2)}) async-start(bf16[32,8,512]{2,1,0:T(8,128)(2,1)} %fusion.97), calls=%async_computation.5 | async-start | bytes 524288 | tf_op jit(solution)/shard_map/all_to_all | solution.py:102
  178.4 12.8 %all-to-all-start.7 = ((bf16[32,8,512]{2,1,0:T(8,128)(2,1)}), bf16[32,8,512]{2,1,0:T(8,128)(2,1)S(1)}, u32[]{:S(2)}, u32[]{:S(2)}) async-start(bf16[32,8,512]{2,1,0:T(8,128)(2,1)} %fusion.98), calls=%async_computation.7 | async-start | bytes 524288 | tf_op jit(solution)/shard_map/all_to_all | solution.py:102
  196.3 4.4 %collective-permute-start.15 = (f32[256]{0:T(256)S(1)}, f32[256]{0:T(256)S(1)}, u32[]{:S(2)}, u32[]{:S(2)}) collective-permute-start(f32[256]{0:T(256)S(1)} %multiply_reduce_fusion.1), channel_id=1, source_target_pairs={{0,1},{1,2},{2,3},{3,0},{4,5},{5,6},{6,7},{7,4},{8,9},{9,10},{10,1... | collective-permute-start | bytes 3080 | tf_op jit(solution)/shard_map/ppermute | solution.py:15
  (6 other events, 57.5 us)

commit v6 on v4

--- a/solution.py
+++ b/solution.py
@@ -40,17 +40,18 @@
     return total
 
 
-def scatter_sum_tp(value, tp_count):
+def down_scatter_sum_tp(activ, w_down, tp_count):
     me = lax.axis_index("tp")
-    width = value.shape[1] // tp_count
+    width = w_down.shape[1] // tp_count
     terms = []
-    for s in range(tp_count):
-        block = lax.dynamic_slice_in_dim(value, ((me + s) % tp_count) * width, width, axis=1)
+    for s in list(range(1, tp_count)) + [0]:
+        w_block = lax.dynamic_slice_in_dim(w_down, ((me + s) % tp_count) * width, width, axis=1)
+        block = jnp.dot(activ, w_block, preferred_element_type=jnp.float32).astype(jnp.bfloat16)
         terms.append(block if s == 0 else shift_tp(block, s, tp_count))
     total = terms[0].astype(jnp.float32)
-    for s in range(1, tp_count):
-        total = total + terms[s].astype(jnp.float32)
-    return total.astype(value.dtype)
+    for term in terms[1:]:
+        total = total + term.astype(jnp.float32)
+    return total.astype(jnp.bfloat16)
 
 
 def shards(hidden, routes, route_weights, pre_gain, out_gain, gate_weight, up_weight, down_weight):
@@ -95,9 +96,7 @@
         gate_val = jnp.dot(flat_rows, gate_weight[0], preferred_element_type=jnp.float32)
         up_val = jnp.dot(flat_rows, up_weight[0], preferred_element_type=jnp.float32)
         activ = (jax.nn.silu(gate_val) * up_val).astype(jnp.bfloat16)
-        partial_out = jnp.dot(activ, down_weight[0], preferred_element_type=jnp.float32)
-        partial_out = lax.optimization_barrier(partial_out.astype(jnp.bfloat16)).astype(jnp.float32)
-        summed = scatter_sum_tp(partial_out.astype(jnp.bfloat16), tp_count)
+        summed = down_scatter_sum_tp(activ, down_weight[0], tp_count)
         summed = summed.reshape(sources, items, col_part)
         back = lax.all_to_all(summed, "req", split_axis=0, concat_axis=0, tiled=True)
         returned.append(back.reshape(req_count * chunk_items, col_part))

time: 173 us -> 168 us (0.971)
  waiting for transfers between devices: 58.1 us -> 65.9 us
  other arithmetic: 9.99 us -> 4.89 us
  local copies, waits for them, and re-layouts: 9.85 us -> 6.23 us
  starting transfers between devices: 47.4 us -> 44 us
    all_to_all x2, waiting for transfers between devices: 26.7 us -> 32.4 us  [shards(): lax.all_to_all(outgoing, 'req', split_axis=0, concat_axis=0, tiled=True)]
    convert_element_type x2 -> x0, other arithmetic: 5.09 us -> none  [scatter_sum_tp(): return total.astype(value.dtype)]
    all_to_all x2, starting transfers between devices: 15 us -> 10.3 us  [shards(): lax.all_to_all(summed, 'req', split_axis=0, concat_axis=0, tiled=True)]
    dynamic_slice x2 -> x0, local copies, waits for them, and re-layouts: 3.66 us -> none  [scatter_sum_tp(): lax.dynamic_slice_in_dim(value, (me + s) % tp_count * width, width, axis=1)]
    dot_general x2, matrix products: 16 us -> 12.5 us  [shards(): jnp.dot(flat_rows, gate_weight[0], preferred_element_type=jnp.float32)]
    dot_general x2 -> x10, matrix products: 25.7 us -> 27.9 us  [the longest x8 16.3 us: down_scatter_sum_tp(): jnp.dot(activ, w_block, preferred_element_type=jnp.float32)]
    ppermute x12, waiting for transfers between devices: 19.9 us -> 21.9 us  [shift_tp(): lax.ppermute(value, 'tp', [(j, (j + step) % tp_count) for j in range(tp_c...]
  transfers between devices with their start and end apart: 16 -> 16, of which waited for: 9 -> 8; matrix products, arithmetic and copies ran while one was open for 33% -> 29% of each run, Pallas kernels for 0% -> 0%
where the time goes in v6:
time: 168 us; the launch traced here: 167 us
  waiting for transfers between devices  65.9 us (39%)
  matrix products  44.9 us (27%)
  starting transfers between devices  44 us (26%)
  local copies, waits for them, and re-layouts  6.23 us (4%)
  other arithmetic  4.89 us (3%)
    all_to_all x2, waiting for transfers between devices, shards(): lax.all_to_all(outgoing, 'req', split_axis=0, concat_axis=0, tiled=True)  32.4 us
    ppermute x12, waiting for transfers between devices, shift_tp(): lax.ppermute(value, 'tp', [(j, (j + step) % tp_count) for j in range(tp_c...  21.9 us
    ppermute x12, starting transfers between devices, shift_tp(): lax.ppermute(value, 'tp', [(j, (j + step) % tp_count) for j in range(tp_c...  18.9 us
    dot_general x8, matrix products, down_scatter_sum_tp(): jnp.dot(activ, w_block, preferred_element_type=jnp.float32)  16.3 us
    all_to_all x2, starting transfers between devices, shards(): lax.all_to_all(outgoing, 'req', split_axis=0, concat_axis=0, tiled=True)  14.7 us
    dot_general x2, matrix products, shards(): jnp.dot(flat_rows, gate_weight[0], preferred_element_type=jnp.float32)  12.5 us
    all_to_all x2, waiting for transfers between devices, shards(): lax.all_to_all(summed, 'req', split_axis=0, concat_axis=0, tiled=True)  11.6 us
    dot_general x2, matrix products, shards(): jnp.dot(flat_rows, up_weight[0], preferred_element_type=jnp.float32)  11.6 us
  transfers between devices with their start and end apart: 16, of which 8 were waited for; matrix products, arithmetic and copies ran while one was open for 29% of the time, Pallas kernels for 0%

profile of v6, /device:TPU:1, one launch (start us, length us, event | category | flops | bytes accessed | tf_op | source)
XLA Modules:
  0.0 167.1 jit_solution(1455101768592337589)
XLA Ops:
  0.6 2.2 %collective-permute-start = (bf16[256,512]{1,0:T(8,128)(2,1)}, bf16[256,512]{1,0:T(8,128)(2,1)S(1)}, u32[]{:S(2)}, u32[]{:S(2)}) collective-permute-start(bf16[256,512]{1,0:T(8,128)(2,1)} %param.8), channel_id=1, source_target_pairs={{0,1},{1,2},{2,3},{3,0},{4,5},{5,6},{6,7},{7,4},{8,9},{9,10},{10,1... | collective-permute-start | bytes 786440 | tf_op jit(solution)/shard_map/ppermute | solution.py:15
  2.8 2.6 %collective-permute-start.1 = (bf16[256,512]{1,0:T(8,128)(2,1)}, bf16[256,512]{1,0:T(8,128)(2,1)S(1)}, u32[]{:S(2)}, u32[]{:S(2)}) collective-permute-start(bf16[256,512]{1,0:T(8,128)(2,1)} %param.8), channel_id=1, source_target_pairs={{0,2},{1,3},{2,0},{3,1},{4,6},{5,7},{6,4},{7,5},{8,10},{9,11},{10,... | collective-permute-start | bytes 786440 | tf_op jit(solution)/shard_map/ppermute | solution.py:15
  11.4 5.6 %collective-permute-done.1 = bf16[256,512]{1,0:T(8,128)(2,1)S(1)} collective-permute-done((bf16[256,512]{1,0:T(8,128)(2,1)}, bf16[256,512]{1,0:T(8,128)(2,1)S(1)}, u32[]{:S(2)}, u32[]{:S(2)}) %collective-permute-start.1) | collective-permute-done | bytes 262176 | tf_op jit(solution)/shard_map/ppermute | solution.py:15
  17.4 2.2 %convolution_convert_fusion.1 = bf16[512,2048]{1,0:T(8,128)(2,1)} fusion(bf16[256,2048]{1,0:T(8,128)(2,1)S(1)} %constant_dynamic-update-slice_fusion, f32[2048]{0:T(1024)S(1)} %copy-done.3, f32[256]{0:T(256)S(1)} %add_rsqrt_fusion.1, s32[256]{0:T(256)S(1)} %bitcast.111, s32[256]{0:T(256)S(1)} %bitcast.109, pred[256]{0:T(512)(128)(4,1)S(1)} %get-tuple-element.5, ...), kind=kOutput, calls=%fused_computation.13 | convolution fusion | flops 540672000 | bytes 3157504 | tf_op jit(solution)/shard_map/dot_general | solution.py:89
  19.6 9.5 %all-to-all-start = ((bf16[32,16,2048]{2,1,0:T(8,128)(2,1)}), bf16[32,16,2048]{2,1,0:T(8,128)(2,1)S(1)}, u32[]{:S(2)}, u32[]{:S(2)}) async-start(bf16[32,16,2048]{2,1,0:T(8,128)(2,1)} %bitcast.101), calls=%async_computation | async-start | bytes 4194304 | tf_op jit(solution)/shard_map/all_to_all | solution.py:93
  29.1 2.2 %convolution_convert_fusion = bf16[512,2048]{1,0:T(8,128)(2,1)} fusion(bf16[256,2048]{1,0:T(8,128)(2,1)S(1)} %constant_dynamic-update-slice_fusion, f32[2048]{0:T(1024)S(1)} %copy-done.3, f32[256]{0:T(256)S(1)} %add_rsqrt_fusion.1, s32[256]{0:T(256)S(1)} %bitcast.112, s32[256]{0:T(256)S(1)} %bitcast.110, pred[256]{0:T(512)(128)(4,1)S(1)} %get-tuple-element.4, ...), kind=kOutput, calls=%fused_computation.12 | convolution fusion | flops 540672000 | bytes 3157504 | tf_op jit(solution)/shard_map/dot_general | solution.py:89
  31.4 26.0 %all-to-all-done = bf16[32,16,2048]{2,1,0:T(8,128)(2,1)S(1)} async-done(((bf16[32,16,2048]{2,1,0:T(8,128)(2,1)}), bf16[32,16,2048]{2,1,0:T(8,128)(2,1)S(1)}, u32[]{:S(2)}, u32[]{:S(2)}) %all-to-all-start) | async-done | bytes 2097184 | tf_op jit(solution)/shard_map/all_to_all | solution.py:93
  57.4 5.2 %all-to-all-start.2 = ((bf16[32,16,2048]{2,1,0:T(8,128)(2,1)}), bf16[32,16,2048]{2,1,0:T(8,128)(2,1)}, u32[]{:S(2)}, u32[]{:S(2)}) async-start(bf16[32,16,2048]{2,1,0:T(8,128)(2,1)} %bitcast.102), calls=%async_computation.2 | async-start | bytes 4194304 | tf_op jit(solution)/shard_map/all_to_all | solution.py:93
  62.6 6.0 %fusion.6 = f32[512,1408]{1,0:T(8,128)S(1)} fusion(bf16[512,2048]{1,0:T(8,128)(2,1)S(1)} %bitcast.99, bf16[1,2048,1408]{2,1,0:T(8,128)(2,1)} %param.13), kind=kOutput, calls=%fused_computation.8 | convolution fusion | flops 2952790016 | bytes 10747904 | tf_op jit(solution)/shard_map/dot_general | solution.py:96
  68.6 6.3 %fusion.17 = bf16[512,1408]{1,0:T(8,128)(2,1)S(1)} fusion(bf16[512,2048]{1,0:T(8,128)(2,1)S(1)} %bitcast.100, bf16[1,2048,1408]{2,1,0:T(8,128)(2,1)} %param.14, f32[512,1408]{1,0:T(8,128)S(1)} %fusion.6), kind=kOutput, calls=%fused_computation.15 | convolution fusion | flops 2957115392 | bytes 12189696 | tf_op jit(solution)/shard_map/dot_general | solution.py:97
  79.4 2.1 %collective-permute-start.4 = (bf16[512,512]{1,0:T(8,128)(2,1)}, bf16[512,512]{1,0:T(8,128)(2,1)S(1)}, u32[]{:S(2)}, u32[]{:S(2)}) collective-permute-start(bf16[512,512]{1,0:T(8,128)(2,1)} %fusion.45), channel_id=1, source_target_pairs={{0,2},{1,3},{2,0},{3,1},{4,6},{5,7},{6,4},{7,5},{8,10},{9,11},{10,... | collective-permute-start | bytes 1572872 | tf_op jit(solution)/shard_map/ppermute | solution.py:15
  84.7 6.4 %all-to-all-done.2 = bf16[32,16,2048]{2,1,0:T(8,128)(2,1)} async-done(((bf16[32,16,2048]{2,1,0:T(8,128)(2,1)}), bf16[32,16,2048]{2,1,0:T(8,128)(2,1)}, u32[]{:S(2)}, u32[]{:S(2)}) %all-to-all-start.2) | async-done | bytes 2097184 | tf_op jit(solution)/shard_map/all_to_all | solution.py:93
  91.0 6.6 %fusion.4 = f32[512,1408]{1,0:T(8,128)S(1)} fusion(bf16[512,2048]{1,0:T(8,128)(2,1)} %bitcast.15, bf16[1,2048,1408]{2,1,0:T(8,128)(2,1)} %param.13), kind=kOutput, calls=%fused_computation.6 | convolution fusion | flops 2952790016 | bytes 10747904 | tf_op jit(solution)/shard_map/dot_general | solution.py:96
  97.6 5.3 %fusion.14 = bf16[512,1408]{1,0:T(8,128)(2,1)S(1)} fusion(bf16[512,2048]{1,0:T(8,128)(2,1)} %bitcast.15, bf16[1,2048,1408]{2,1,0:T(8,128)(2,1)S(1)} %bitcast.117, f32[512,1408]{1,0:T(8,128)S(1)} %fusion.4), kind=kOutput, calls=%fused_computation.14 | convolution fusion | flops 2957115392 | bytes 12189696 | tf_op jit(solution)/shard_map/dot_general | solution.py:97
  109.2 2.1 %collective-permute-start.7 = (bf16[512,512]{1,0:T(8,128)(2,1)}, bf16[512,512]{1,0:T(8,128)(2,1)S(1)}, u32[]{:S(2)}, u32[]{:S(2)}) collective-permute-start(bf16[512,512]{1,0:T(8,128)(2,1)} %fusion.48), channel_id=1, source_target_pairs={{0,2},{1,3},{2,0},{3,1},{4,6},{5,7},{6,4},{7,5},{8,10},{9,11},{10,... | collective-permute-start | bytes 1572872 | tf_op jit(solution)/shard_map/ppermute | solution.py:15
  112.7 1.8 %add_convert_fusion.1 = bf16[512,512]{1,0:T(8,128)(2,1)} fusion(bf16[512,512]{1,0:T(8,128)(2,1)S(1)} %collective-permute-done.5, bf16[512,512]{1,0:T(8,128)(2,1)S(1)} %collective-permute-done.4, bf16[512,512]{1,0:T(8,128)(2,1)S(1)} %collective-permute-done.3, bf16[512,1408]{1,0:T(8,128)(2,1)S(1)} %copy-done.6, bf16[1,1408,2048]{2,1,0:T(8,128)(2,1)S(1)} %bitcast.121, ...), kind=kOutput, calls=%fused_computation.58 | convolution fusion | flops 740556800 | bytes 4980740 | tf_op jit(solution)/shard_map/dot_general | solution.py:49
  114.5 5.2 %all-to-all-start.1 = ((bf16[32,16,512]{2,1,0:T(8,128)(2,1)}), bf16[32,16,512]{2,1,0:T(8,128)(2,1)S(1)}, u32[]{:S(2)}, u32[]{:S(2)}) async-start(bf16[32,16,512]{2,1,0:T(8,128)(2,1)} %bitcast.12), calls=%async_computation.1 | async-start | bytes 1048576 | tf_op jit(solution)/shard_map/all_to_all | solution.py:101
  120.1 10.3 %collective-permute-done.7 = bf16[512,512]{1,0:T(8,128)(2,1)S(1)} collective-permute-done((bf16[512,512]{1,0:T(8,128)(2,1)}, bf16[512,512]{1,0:T(8,128)(2,1)S(1)}, u32[]{:S(2)}, u32[]{:S(2)}) %collective-permute-start.7) | collective-permute-done | bytes 524320 | tf_op jit(solution)/shard_map/ppermute | solution.py:15
  130.3 4.2 %collective-permute-done.8 = bf16[512,512]{1,0:T(8,128)(2,1)} collective-permute-done((bf16[512,512]{1,0:T(8,128)(2,1)}, bf16[512,512]{1,0:T(8,128)(2,1)}, u32[]{:S(2)}, u32[]{:S(2)}) %collective-permute-start.8) | collective-permute-done | bytes 524320 | tf_op jit(solution)/shard_map/ppermute | solution.py:15
  134.5 3.7 %add_convert_fusion = bf16[512,512]{1,0:T(8,128)(2,1)} fusion(bf16[512,512]{1,0:T(8,128)(2,1)} %collective-permute-done.8, bf16[512,512]{1,0:T(8,128)(2,1)S(1)} %collective-permute-done.7, bf16[512,512]{1,0:T(8,128)(2,1)S(1)} %collective-permute-done.6, bf16[512,1408]{1,0:T(8,128)(2,1)} %copy-done.4, bf16[1,1408,2048]{2,1,0:T(8,128)(2,1)} %param.15, ...), kind=kOutput, calls=%fused_computation.57 | convolution fusion | flops 740556800 | bytes 4980740 | tf_op jit(solution)/shard_map/dot_general | solution.py:49
  138.2 5.1 %all-to-all-start.3 = ((bf16[32,16,512]{2,1,0:T(8,128)(2,1)}), bf16[32,16,512]{2,1,0:T(8,128)(2,1)S(1)}, u32[]{:S(2)}, u32[]{:S(2)}) async-start(bf16[32,16,512]{2,1,0:T(8,128)(2,1)} %bitcast.16), calls=%async_computation.3 | async-start | bytes 1048576 | tf_op jit(solution)/shard_map/all_to_all | solution.py:101
  143.4 11.6 %all-to-all-done.3 = bf16[32,16,512]{2,1,0:T(8,128)(2,1)S(1)} async-done(((bf16[32,16,512]{2,1,0:T(8,128)(2,1)}), bf16[32,16,512]{2,1,0:T(8,128)(2,1)S(1)}, u32[]{:S(2)}, u32[]{:S(2)}) %all-to-all-start.3) | async-done | bytes 524320 | tf_op jit(solution)/shard_map/all_to_all | solution.py:101
  155.1 2.0 %gather_fusion = bf16[512,512]{1,0:T(8,128)(2,1)S(1)} fusion(bf16[1024,512]{1,0:T(8,128)(2,1)S(1)} %pad_maximum_fusion, s32[1024]{0:T(1024)S(1)} %pad_clamp_fusion.1), kind=kCustom, calls=%fused_computation | custom fusion | bytes 1050624 | tf_op jit(solution)/shard_map/gather | solution.py:105
  160.8 2.1 %collective-permute-start.10 = (f32[256]{0:T(256)S(1)}, f32[256]{0:T(256)S(1)}, u32[]{:S(2)}, u32[]{:S(2)}) collective-permute-start(f32[256]{0:T(256)S(1)} %multiply_reduce_fusion.1), channel_id=1, source_target_pairs={{0,2},{1,3},{2,0},{3,1},{4,6},{5,7},{6,4},{7,5},{8,10},{9,11},{10,... | collective-permute-start | bytes 3080 | tf_op jit(solution)/shard_map/ppermute | solution.py:15
  (90 shorter events, 29.5 us)
Async XLA Ops:
  0.6 10.7 %collective-permute-start = (bf16[256,512]{1,0:T(8,128)(2,1)}, bf16[256,512]{1,0:T(8,128)(2,1)S(1)}, u32[]{:S(2)}, u32[]{:S(2)}) collective-permute-start(bf16[256,512]{1,0:T(8,128)(2,1)} %param.8), channel_id=1, source_target_pairs={{0,1},{1,2},{2,3},{3,0},{4,5},{5,6},{6,7},{7,4},{8,9},{9,10},{10,1... | collective-permute-start | bytes 786440 | tf_op jit(solution)/shard_map/ppermute | solution.py:15
  2.8 14.2 %collective-permute-start.1 = (bf16[256,512]{1,0:T(8,128)(2,1)}, bf16[256,512]{1,0:T(8,128)(2,1)S(1)}, u32[]{:S(2)}, u32[]{:S(2)}) collective-permute-start(bf16[256,512]{1,0:T(8,128)(2,1)} %param.8), channel_id=1, source_target_pairs={{0,2},{1,3},{2,0},{3,1},{4,6},{5,7},{6,4},{7,5},{8,10},{9,11},{10,... | collective-permute-start | bytes 786440 | tf_op jit(solution)/shard_map/ppermute | solution.py:15
  5.4 11.6 %collective-permute-start.2 = (bf16[256,512]{1,0:T(8,128)(2,1)}, bf16[256,512]{1,0:T(8,128)(2,1)S(1)}, u32[]{:S(2)}, u32[]{:S(2)}) collective-permute-start(bf16[256,512]{1,0:T(8,128)(2,1)} %param.8), channel_id=1, source_target_pairs={{0,3},{1,0},{2,1},{3,2},{4,7},{5,4},{6,5},{7,6},{8,11},{9,8},{10,9... | collective-permute-start | bytes 786440 | tf_op jit(solution)/shard_map/ppermute | solution.py:15
  10.1 7.2 %copy-start.3 = (f32[2048]{0:T(1024)S(1)}, f32[2048]{0:T(1024)}, u32[]{:S(2)}) copy-start(f32[2048]{0:T(1024)} %param.11) | copy-start | bytes 24580
  19.6 37.8 %all-to-all-start = ((bf16[32,16,2048]{2,1,0:T(8,128)(2,1)}), bf16[32,16,2048]{2,1,0:T(8,128)(2,1)S(1)}, u32[]{:S(2)}, u32[]{:S(2)}) async-start(bf16[32,16,2048]{2,1,0:T(8,128)(2,1)} %bitcast.101), calls=%async_computation | async-start | bytes 4194304 | tf_op jit(solution)/shard_map/all_to_all | solution.py:93
  57.4 33.7 %all-to-all-start.2 = ((bf16[32,16,2048]{2,1,0:T(8,128)(2,1)}), bf16[32,16,2048]{2,1,0:T(8,128)(2,1)}, u32[]{:S(2)}, u32[]{:S(2)}) async-start(bf16[32,16,2048]{2,1,0:T(8,128)(2,1)} %bitcast.102), calls=%async_computation.2 | async-start | bytes 4194304 | tf_op jit(solution)/shard_map/all_to_all | solution.py:93
  62.6 12.3 %slice-start.2 = ((s8[5767168]{0:T(1024)(128)(4,1)}), s8[4194304]{0:T(1024)(128)(4,1)S(1)}, s32[]{:S(2)}) async-start(s8[5767168]{0:T(1024)(128)(4,1)} %bitcast.118), calls=%async_computation.6 | async-start | bytes 8388608
  74.9 6.6 %copy-start.5 = (bf16[512,1408]{1,0:T(8,128)(2,1)}, bf16[512,1408]{1,0:T(8,128)(2,1)S(1)}, u32[]{:S(2)}) copy-start(bf16[512,1408]{1,0:T(8,128)(2,1)S(1)} %fusion.17) | copy-start | bytes 4325380
  76.8 34.6 %collective-permute-start.3 = (bf16[512,512]{1,0:T(8,128)(2,1)}, bf16[512,512]{1,0:T(8,128)(2,1)S(1)}, u32[]{:S(2)}, u32[]{:S(2)}) collective-permute-start(bf16[512,512]{1,0:T(8,128)(2,1)} %fusion.39), channel_id=1, source_target_pairs={{0,1},{1,2},{2,3},{3,0},{4,5},{5,6},{6,7},{7,4},{8,9},{9,10},{10,1... | collective-permute-start | bytes 1572872 | tf_op jit(solution)/shard_map/ppermute | solution.py:15
  79.4 33.2 %collective-permute-start.4 = (bf16[512,512]{1,0:T(8,128)(2,1)}, bf16[512,512]{1,0:T(8,128)(2,1)S(1)}, u32[]{:S(2)}, u32[]{:S(2)}) collective-permute-start(bf16[512,512]{1,0:T(8,128)(2,1)} %fusion.45), channel_id=1, source_target_pairs={{0,2},{1,3},{2,0},{3,1},{4,6},{5,7},{6,4},{7,5},{8,10},{9,11},{10,... | collective-permute-start | bytes 1572872 | tf_op jit(solution)/shard_map/ppermute | solution.py:15
  81.5 16.1 %slice-start = ((s8[5767168]{0:T(1024)(128)(4,1)}), s8[1572864]{0:T(1024)(128)(4,1)S(1)}, s32[]{:S(2)}) async-start(s8[5767168]{0:T(1024)(128)(4,1)} %bitcast.116), calls=%async_computation.4 | async-start | bytes 3145728
  83.3 29.3 %collective-permute-start.5 = (bf16[512,512]{1,0:T(8,128)(2,1)}, bf16[512,512]{1,0:T(8,128)(2,1)S(1)}, u32[]{:S(2)}, u32[]{:S(2)}) collective-permute-start(bf16[512,512]{1,0:T(8,128)(2,1)} %fusion.51), channel_id=1, source_target_pairs={{0,3},{1,0},{2,1},{3,2},{4,7},{5,4},{6,5},{7,6},{8,11},{9,8},{10,9... | collective-permute-start | bytes 1572872 | tf_op jit(solution)/shard_map/ppermute | solution.py:15
  91.0 6.6 %slice-start.1 = ((s8[5767168]{0:T(1024)(128)(4,1)}), s8[4194304]{0:T(1024)(128)(4,1)S(1)}, s32[]{:S(2)}) async-start(s8[5767168]{0:T(1024)(128)(4,1)} %bitcast.116), calls=%async_computation.5 | async-start | bytes 8388608
  91.0 11.9 %slice-start.4 = ((s8[5767168]{0:T(1024)(128)(4,1)}), s8[4194304]{0:T(1024)(128)(4,1)S(1)}, s32[]{:S(2)}) async-start(s8[5767168]{0:T(1024)(128)(4,1)} %bitcast.120), calls=%async_computation.8 | async-start | bytes 8388608
  104.8 15.3 %collective-permute-start.6 = (bf16[512,512]{1,0:T(8,128)(2,1)}, bf16[512,512]{1,0:T(8,128)(2,1)S(1)}, u32[]{:S(2)}, u32[]{:S(2)}) collective-permute-start(bf16[512,512]{1,0:T(8,128)(2,1)} %fusion.42), channel_id=1, source_target_pairs={{0,1},{1,2},{2,3},{3,0},{4,5},{5,6},{6,7},{7,4},{8,9},{9,10},{10,1... | collective-permute-start | bytes 1572872 | tf_op jit(solution)/shard_map/ppermute | solution.py:15
  109.2 10.7 %copy-start.1 = (f32[256,2]{0,1:T(2,128)S(1)}, f32[256,2]{0,1:T(2,128)}, u32[]{:S(2)}) copy-start(f32[256,2]{0,1:T(2,128)} %param.10) | copy-start | bytes 6148
  109.2 21.1 %collective-permute-start.7 = (bf16[512,512]{1,0:T(8,128)(2,1)}, bf16[512,512]{1,0:T(8,128)(2,1)S(1)}, u32[]{:S(2)}, u32[]{:S(2)}) collective-permute-start(bf16[512,512]{1,0:T(8,128)(2,1)} %fusion.48), channel_id=1, source_target_pairs={{0,2},{1,3},{2,0},{3,1},{4,6},{5,7},{6,4},{7,5},{8,10},{9,11},{10,... | collective-permute-start | bytes 1572872 | tf_op jit(solution)/shard_map/ppermute | solution.py:15
  111.3 23.2 %collective-permute-start.8 = (bf16[512,512]{1,0:T(8,128)(2,1)}, bf16[512,512]{1,0:T(8,128)(2,1)}, u32[]{:S(2)}, u32[]{:S(2)}) collective-permute-start(bf16[512,512]{1,0:T(8,128)(2,1)} %fusion.54), channel_id=1, source_target_pairs={{0,3},{1,0},{2,1},{3,2},{4,7},{5,4},{6,5},{7,6},{8,11},{9,8},{10,9... | collective-permute-start | bytes 1572872 | tf_op jit(solution)/shard_map/ppermute | solution.py:15
  114.5 23.7 %all-to-all-start.1 = ((bf16[32,16,512]{2,1,0:T(8,128)(2,1)}), bf16[32,16,512]{2,1,0:T(8,128)(2,1)S(1)}, u32[]{:S(2)}, u32[]{:S(2)}) async-start(bf16[32,16,512]{2,1,0:T(8,128)(2,1)} %bitcast.12), calls=%async_computation.1 | async-start | bytes 1048576 | tf_op jit(solution)/shard_map/all_to_all | solution.py:101
  138.2 16.8 %all-to-all-start.3 = ((bf16[32,16,512]{2,1,0:T(8,128)(2,1)}), bf16[32,16,512]{2,1,0:T(8,128)(2,1)S(1)}, u32[]{:S(2)}, u32[]{:S(2)}) async-start(bf16[32,16,512]{2,1,0:T(8,128)(2,1)} %bitcast.16), calls=%async_computation.3 | async-start | bytes 1048576 | tf_op jit(solution)/shard_map/all_to_all | solution.py:101
  157.1 9.1 %copy-start.2 = (f32[512]{0:T(512)S(1)}, f32[512]{0:T(512)}, u32[]{:S(2)}) copy-start(f32[512]{0:T(512)} %param.12) | copy-start | bytes 6148
  159.3 4.4 %collective-permute-start.9 = (f32[256]{0:T(256)S(1)}, f32[256]{0:T(256)S(1)}, u32[]{:S(2)}, u32[]{:S(2)}) collective-permute-start(f32[256]{0:T(256)S(1)} %multiply_reduce_fusion.1), channel_id=1, source_target_pairs={{0,1},{1,2},{2,3},{3,0},{4,5},{5,6},{6,7},{7,4},{8,9},{9,10},{10,1... | collective-permute-start | bytes 3080 | tf_op jit(solution)/shard_map/ppermute | solution.py:15
  160.8 3.9 %collective-permute-start.10 = (f32[256]{0:T(256)S(1)}, f32[256]{0:T(256)S(1)}, u32[]{:S(2)}, u32[]{:S(2)}) collective-permute-start(f32[256]{0:T(256)S(1)} %multiply_reduce_fusion.1), channel_id=1, source_target_pairs={{0,2},{1,3},{2,0},{3,1},{4,6},{5,7},{6,4},{7,5},{8,10},{9,11},{10,... | collective-permute-start | bytes 3080 | tf_op jit(solution)/shard_map/ppermute | solution.py:15
  162.9 2.6 %collective-permute-start.11 = (f32[256]{0:T(256)S(1)}, f32[256]{0:T(256)S(1)}, u32[]{:S(2)}, u32[]{:S(2)}) collective-permute-start(f32[256]{0:T(256)S(1)} %multiply_reduce_fusion.1), channel_id=1, source_target_pairs={{0,3},{1,0},{2,1},{3,2},{4,7},{5,4},{6,5},{7,6},{8,11},{9,8},{10,9... | collective-permute-start | bytes 3080 | tf_op jit(solution)/shard_map/ppermute | solution.py:15
  (5 other events, 23.4 us)

commit v7 on v6

--- a/solution.py
+++ b/solution.py
@@ -64,11 +64,11 @@
     chunk_items = slot_count // CHUNKS
     stream = hidden.astype(jnp.float32)
     whole_rows = gather_tp(hidden, tp_count).astype(jnp.float32)
-    meansq = jnp.sum(whole_rows * whole_rows, axis=1) / full_width
-    normed_in = (whole_rows * lax.rsqrt(meansq + epsilon)[:, None] * pre_gain[None, :]).astype(
-        jnp.bfloat16
-    )
-    send_cols = normed_in.shape[1]
+    meansq = sum_tp(jnp.sum(stream * stream, axis=1), tp_count) / full_width
+    row_scale = lax.rsqrt(meansq + epsilon)[:, None]
+    normed_in = (whole_rows * row_scale * pre_gain[None, :]).astype(jnp.bfloat16)
+    own_gain = lax.dynamic_slice_in_dim(pre_gain, lax.axis_index("tp") * col_part, col_part)
+    normed_own = (stream * row_scale * own_gain[None, :]).astype(jnp.bfloat16)
     top = routes.shape[1]
     chosen = routes.reshape(-1)
     onehot = (chosen[:, None] == jnp.arange(E, dtype=jnp.int32)[None, :]).astype(jnp.int32)
@@ -86,13 +86,17 @@
         for k in range(top):
             hit = (slot_ids[:, None] == chunk_pairs[None, :, k]) & (owner_pairs[None, :, k] == c)
             dispatch = dispatch | hit
+        relay = c == 0
+        source = normed_own if relay else normed_in
         outgoing = jnp.dot(
-            dispatch.astype(jnp.bfloat16), normed_in, preferred_element_type=jnp.float32
+            dispatch.astype(jnp.bfloat16), source, preferred_element_type=jnp.float32
         ).astype(jnp.bfloat16)
-        outgoing = outgoing.reshape(req_count, chunk_items, send_cols)
+        outgoing = outgoing.reshape(req_count, chunk_items, source.shape[1])
         pieces = lax.all_to_all(outgoing, "req", split_axis=0, concat_axis=0, tiled=True)
         sources, items, widths = pieces.shape
         flat_rows = pieces.reshape(sources * items, widths)
+        if relay:
+            flat_rows = gather_tp(flat_rows, tp_count)
         gate_val = jnp.dot(flat_rows, gate_weight[0], preferred_element_type=jnp.float32)
         up_val = jnp.dot(flat_rows, up_weight[0], preferred_element_type=jnp.float32)
         activ = (jax.nn.silu(gate_val) * up_val).astype(jnp.bfloat16)

time: 168 us -> 165 us (0.982)
  waiting for transfers between devices: 65.9 us -> 45 us
  starting transfers between devices: 44 us -> 60.3 us
  local copies, waits for them, and re-layouts: 6.23 us -> 9.2 us
  matrix products: 44.9 us -> 42.4 us
    all_to_all x2, waiting for transfers between devices: 32.4 us -> 0.01 us  [shards(): lax.all_to_all(outgoing, 'req', split_axis=0, concat_axis=0, tiled=True)]
    ppermute x12 -> x18, waiting for transfers between devices: 21.9 us -> 33.7 us  [shift_tp(): lax.ppermute(value, 'tp', [(j, (j + step) % tp_count) for j in range(tp_c...]
    all_to_all x2, starting transfers between devices: 10.3 us -> 18.5 us  [shards(): lax.all_to_all(summed, 'req', split_axis=0, concat_axis=0, tiled=True)]
    ppermute x12 -> x18, starting transfers between devices: 18.9 us -> 24.1 us  [shift_tp(): lax.ppermute(value, 'tp', [(j, (j + step) % tp_count) for j in range(tp_c...]
    all_to_all x2, starting transfers between devices: 14.7 us -> 17.6 us  [shards(): lax.all_to_all(outgoing, 'req', split_axis=0, concat_axis=0, tiled=True)]
    dot_general x2, matrix products: 11.6 us -> 9.66 us  [shards(): jnp.dot(flat_rows, up_weight[0], preferred_element_type=jnp.float32)]
  transfers between devices with their start and end apart: 16 -> 22, of which waited for: 8 -> 8; matrix products, arithmetic and copies ran while one was open for 29% -> 29% of each run, Pallas kernels for 0% -> 0%
where the time goes in v7:
time: 165 us; the launch traced here: 164 us
  starting transfers between devices  60.3 us (37%)
  waiting for transfers between devices  45 us (27%)
  matrix products  42.4 us (26%)
  local copies, waits for them, and re-layouts  9.2 us (6%)
  other arithmetic  5.84 us (4%)
    ppermute x18, waiting for transfers between devices, shift_tp(): lax.ppermute(value, 'tp', [(j, (j + step) % tp_count) for j in range(tp_c...  33.7 us
    ppermute x18, starting transfers between devices, shift_tp(): lax.ppermute(value, 'tp', [(j, (j + step) % tp_count) for j in range(tp_c...  24.1 us
    all_to_all x2, starting transfers between devices, shards(): lax.all_to_all(summed, 'req', split_axis=0, concat_axis=0, tiled=True)  18.5 us
    all_to_all x2, starting transfers between devices, shards(): lax.all_to_all(outgoing, 'req', split_axis=0, concat_axis=0, tiled=True)  17.6 us
    dot_general x8, matrix products, down_scatter_sum_tp(): jnp.dot(activ, w_block, preferred_element_type=jnp.float32)  16.6 us
    dot_general x2, matrix products, shards(): jnp.dot(flat_rows, gate_weight[0], preferred_element_type=jnp.float32)  11.8 us
    all_to_all x2, waiting for transfers between devices, shards(): lax.all_to_all(summed, 'req', split_axis=0, concat_axis=0, tiled=True)  11.3 us
    dot_general x2, matrix products, shards(): jnp.dot(flat_rows, up_weight[0], preferred_element_type=jnp.float32)  9.66 us
  transfers between devices with their start and end apart: 22, of which 8 were waited for; matrix products, arithmetic and copies ran while one was open for 29% of the time, Pallas kernels for 0%

profile of v7, /device:TPU:1, one launch (start us, length us, event | category | flops | bytes accessed | tf_op | source)
XLA Modules:
  0.0 164.0 jit_solution(4937317662400799702)
XLA Ops:
  1.8 2.2 %collective-permute-start = (f32[256]{0:T(256)S(1)}, f32[256]{0:T(256)S(1)}, u32[]{:S(2)}, u32[]{:S(2)}) collective-permute-start(f32[256]{0:T(256)S(1)} %fusion.70), channel_id=1, source_target_pairs={{0,1},{1,2},{2,3},{3,0},{4,5},{5,6},{6,7},{7,4},{8,9},{9,10},{10,1... | collective-permute-start | bytes 3080 | tf_op jit(solution)/shard_map/ppermute | solution.py:15
  4.0 2.6 %collective-permute-start.1 = (f32[256]{0:T(256)S(1)}, f32[256]{0:T(256)S(1)}, u32[]{:S(2)}, u32[]{:S(2)}) collective-permute-start(f32[256]{0:T(256)S(1)} %fusion.70), channel_id=1, source_target_pairs={{0,2},{1,3},{2,0},{3,1},{4,6},{5,7},{6,4},{7,5},{8,10},{9,11},{10,... | collective-permute-start | bytes 3080 | tf_op jit(solution)/shard_map/ppermute | solution.py:15
  12.8 2.2 %convolution_convert_fusion.1 = bf16[512,512]{1,0:T(8,128)(2,1)} fusion(bf16[256,512]{1,0:T(8,128)(2,1)} %param.10, f32[512]{0:T(512)S(1)} %dynamic_slice.27, f32[256]{0:T(256)S(1)} %bitcast.113, s32[256]{0:T(256)S(1)} %bitcast.117, s32[256]{0:T(256)S(1)} %bitcast.115, pred[256]{0:T(512)(128)(4,1)S(1)} %get-tuple-element.6, ...), kind=kOutput, calls=%fused_computation.40 | convolution fusion | flops 135659520 | bytes 792064 | tf_op jit(solution)/shard_map/dot_general | solution.py:91
  15.0 9.6 %all-to-all-start = ((bf16[32,16,512]{2,1,0:T(8,128)(2,1)}), bf16[32,16,512]{2,1,0:T(8,128)(2,1)S(1)}, u32[]{:S(2)}, u32[]{:S(2)}) async-start(bf16[32,16,512]{2,1,0:T(8,128)(2,1)} %bitcast.9), calls=%async_computation | async-start | bytes 1048576 | tf_op jit(solution)/shard_map/all_to_all | solution.py:95
  27.8 11.4 %collective-permute-done.9 = bf16[256,512]{1,0:T(8,128)(2,1)S(1)} collective-permute-done((bf16[256,512]{1,0:T(8,128)(2,1)S(1)}, bf16[256,512]{1,0:T(8,128)(2,1)S(1)}, u32[]{:S(2)}, u32[]{:S(2)}) %collective-permute-start.9) | collective-permute-done | bytes 262176 | tf_op jit(solution)/shard_map/ppermute | solution.py:15
  40.7 2.3 %collective-permute-start.5 = (bf16[512,512]{1,0:T(8,128)(2,1)S(1)}, bf16[512,512]{1,0:T(8,128)(2,1)S(1)}, u32[]{:S(2)}, u32[]{:S(2)}) collective-permute-start(bf16[512,512]{1,0:T(8,128)(2,1)S(1)} %bitcast.104), channel_id=1, source_target_pairs={{0,3},{1,0},{2,1},{3,2},{4,7},{5,4},{6,5},{7,6},{8,11},{9,8},{10,9... | collective-permute-start | bytes 1572872 | tf_op jit(solution)/shard_map/ppermute | solution.py:15
  43.0 2.2 %convolution_convert_fusion = bf16[512,2048]{1,0:T(8,128)(2,1)} fusion(bf16[256,2048]{1,0:T(8,128)(2,1)S(1)} %constant_dynamic-update-slice_fusion, f32[2048]{0:T(1024)S(1)} %copy-done.3, f32[256]{0:T(256)S(1)} %bitcast.114, s32[256]{0:T(256)S(1)} %bitcast.118, s32[256]{0:T(256)S(1)} %bitcast.116, pred[256]{0:T(512)(128)(4,1)S(1)} %get-tuple-element.5, ...), kind=kOutput, calls=%fused_computation.12 | convolution fusion | flops 540672000 | bytes 3157504 | tf_op jit(solution)/shard_map/dot_general | solution.py:91
  45.2 8.1 %all-to-all-start.2 = ((bf16[32,16,2048]{2,1,0:T(8,128)(2,1)}), bf16[32,16,2048]{2,1,0:T(8,128)(2,1)S(1)}, u32[]{:S(2)}, u32[]{:S(2)}) async-start(bf16[32,16,2048]{2,1,0:T(8,128)(2,1)} %bitcast.19), calls=%async_computation.2 | async-start | bytes 4194304 | tf_op jit(solution)/shard_map/all_to_all | solution.py:95
  53.6 10.6 %collective-permute-done.3 = bf16[512,512]{1,0:T(8,128)(2,1)} collective-permute-done((bf16[512,512]{1,0:T(8,128)(2,1)S(1)}, bf16[512,512]{1,0:T(8,128)(2,1)}, u32[]{:S(2)}, u32[]{:S(2)}) %collective-permute-start.3) | collective-permute-done | bytes 524320 | tf_op jit(solution)/shard_map/ppermute | solution.py:15
  66.6 5.9 %fusion.6 = f32[512,1408]{1,0:T(8,128)S(1)} fusion(bf16[512,2048]{1,0:T(8,128)(2,1)S(1)} %constant_dynamic-update-slice_fusion.4, bf16[1,2048,1408]{2,1,0:T(8,128)(2,1)} %param.15), kind=kOutput, calls=%fused_computation.9 | convolution fusion | flops 2952790016 | bytes 10747904 | tf_op jit(solution)/shard_map/dot_general | solution.py:100
  72.5 3.5 %multiply_convert_fusion = bf16[512,1408]{1,0:T(8,128)(2,1)S(1)} fusion(f32[512,1408]{1,0:T(8,128)S(1)} %fusion.6, bf16[512,2048]{1,0:T(8,128)(2,1)S(1)} %constant_dynamic-update-slice_fusion.4, bf16[1,2048,1408]{2,1,0:T(8,128)(2,1)S(1)} %bitcast.126), kind=kOutput, calls=%fused_computation.14 | convolution fusion | flops 2957115392 | bytes 12189696 | tf_op jit(solution)/shard_map/dot_general | solution.py:101
  80.2 3.2 %collective-permute-start.7 = (bf16[512,512]{1,0:T(8,128)(2,1)}, bf16[512,512]{1,0:T(8,128)(2,1)S(1)}, u32[]{:S(2)}, u32[]{:S(2)}) collective-permute-start(bf16[512,512]{1,0:T(8,128)(2,1)} %fusion.36), channel_id=1, source_target_pairs={{0,2},{1,3},{2,0},{3,1},{4,6},{5,7},{6,4},{7,5},{8,10},{9,11},{10,... | collective-permute-start | bytes 1572872 | tf_op jit(solution)/shard_map/ppermute | solution.py:15
  83.4 1.8 %fusion.42 = bf16[512,512]{1,0:T(8,128)(2,1)} fusion(bf16[512,1408]{1,0:T(8,128)(2,1)S(1)} %multiply_convert_fusion, bf16[1,1408,2048]{2,1,0:T(8,128)(2,1)S(1)} %bitcast.128, s32[]{:T(128)S(6)} %select_n.185), kind=kOutput, calls=%fused_computation.36 | convolution fusion | flops 738459648 | bytes 3407876 | tf_op jit(solution)/shard_map/dot_general | solution.py:49
  85.3 5.9 %fusion.4 = f32[512,1408]{1,0:T(8,128)S(1)} fusion(bf16[512,2048]{1,0:T(8,128)(2,1)S(1)} %bitcast.100, bf16[1,2048,1408]{2,1,0:T(8,128)(2,1)} %param.15), kind=kOutput, calls=%fused_computation.7 | convolution fusion | flops 2952790016 | bytes 10747904 | tf_op jit(solution)/shard_map/dot_general | solution.py:100
  91.2 6.2 %fusion.11 = bf16[512,1408]{1,0:T(8,128)(2,1)S(1)} fusion(bf16[512,2048]{1,0:T(8,128)(2,1)S(1)} %bitcast.101, bf16[1,2048,1408]{2,1,0:T(8,128)(2,1)} %param.16, f32[512,1408]{1,0:T(8,128)S(1)} %fusion.4), kind=kOutput, calls=%fused_computation.13 | convolution fusion | flops 2957115392 | bytes 12189696 | tf_op jit(solution)/shard_map/dot_general | solution.py:101
  103.5 2.4 %collective-permute-start.14 = (bf16[512,512]{1,0:T(8,128)(2,1)}, bf16[512,512]{1,0:T(8,128)(2,1)}, u32[]{:S(2)}, u32[]{:S(2)}) collective-permute-start(bf16[512,512]{1,0:T(8,128)(2,1)} %fusion.45), channel_id=1, source_target_pairs={{0,3},{1,0},{2,1},{3,2},{4,7},{5,4},{6,5},{7,6},{8,11},{9,8},{10,9... | collective-permute-start | bytes 1572872 | tf_op jit(solution)/shard_map/ppermute | solution.py:15
  106.0 2.9 %add_convert_fusion.1 = bf16[512,512]{1,0:T(8,128)(2,1)} fusion(bf16[512,512]{1,0:T(8,128)(2,1)} %collective-permute-done.8, bf16[512,512]{1,0:T(8,128)(2,1)S(1)} %collective-permute-done.7, bf16[512,512]{1,0:T(8,128)(2,1)S(1)} %collective-permute-done.6, bf16[512,1408]{1,0:T(8,128)(2,1)S(1)} %copy-done.5, bf16[1,1408,2048]{2,1,0:T(8,128)(2,1)S(1)} %bitcast.130, ...), kind=kOutput, calls=%fused_computation.56 | convolution fusion | flops 740556800 | bytes 4980740 | tf_op jit(solution)/shard_map/dot_general | solution.py:49
  108.9 9.9 %all-to-all-start.1 = ((bf16[32,16,512]{2,1,0:T(8,128)(2,1)}), bf16[32,16,512]{2,1,0:T(8,128)(2,1)S(1)}, u32[]{:S(2)}, u32[]{:S(2)}) async-start(bf16[32,16,512]{2,1,0:T(8,128)(2,1)} %bitcast.17), calls=%async_computation.1 | async-start | bytes 1048576 | tf_op jit(solution)/shard_map/all_to_all | solution.py:105
  118.8 8.4 %collective-permute-done.13 = bf16[512,512]{1,0:T(8,128)(2,1)S(1)} collective-permute-done((bf16[512,512]{1,0:T(8,128)(2,1)}, bf16[512,512]{1,0:T(8,128)(2,1)S(1)}, u32[]{:S(2)}, u32[]{:S(2)}) %collective-permute-start.13) | collective-permute-done | bytes 524320 | tf_op jit(solution)/shard_map/ppermute | solution.py:15
  128.3 3.7 %add_convert_fusion = bf16[512,512]{1,0:T(8,128)(2,1)} fusion(bf16[512,512]{1,0:T(8,128)(2,1)} %collective-permute-done.14, bf16[512,512]{1,0:T(8,128)(2,1)S(1)} %collective-permute-done.13, bf16[512,512]{1,0:T(8,128)(2,1)S(1)} %collective-permute-done.12, bf16[512,1408]{1,0:T(8,128)(2,1)} %copy-done.6, bf16[1,1408,2048]{2,1,0:T(8,128)(2,1)} %param.17, ...), kind=kOutput, calls=%fused_computation.53 | convolution fusion | flops 740556800 | bytes 4980740 | tf_op jit(solution)/shard_map/dot_general | solution.py:49
  132.0 8.6 %all-to-all-start.3 = ((bf16[32,16,512]{2,1,0:T(8,128)(2,1)}), bf16[32,16,512]{2,1,0:T(8,128)(2,1)S(1)}, u32[]{:S(2)}, u32[]{:S(2)}) async-start(bf16[32,16,512]{2,1,0:T(8,128)(2,1)} %bitcast.21), calls=%async_computation.3 | async-start | bytes 1048576 | tf_op jit(solution)/shard_map/all_to_all | solution.py:105
  141.0 11.3 %all-to-all-done.3 = bf16[32,16,512]{2,1,0:T(8,128)(2,1)S(1)} async-done(((bf16[32,16,512]{2,1,0:T(8,128)(2,1)}), bf16[32,16,512]{2,1,0:T(8,128)(2,1)S(1)}, u32[]{:S(2)}, u32[]{:S(2)}) %all-to-all-start.3) | async-done | bytes 524320 | tf_op jit(solution)/shard_map/all_to_all | solution.py:105
  152.3 2.0 %gather_fusion = bf16[512,512]{1,0:T(8,128)(2,1)S(1)} fusion(bf16[1024,512]{1,0:T(8,128)(2,1)S(1)} %pad_maximum_fusion, s32[1024]{0:T(1024)S(1)} %pad_clamp_fusion), kind=kCustom, calls=%fused_computation.2 | custom fusion | bytes 1050624 | tf_op jit(solution)/shard_map/gather | solution.py:109
  157.6 2.4 %collective-permute-start.16 = (f32[256]{0:T(256)S(1)}, f32[256]{0:T(256)S(1)}, u32[]{:S(2)}, u32[]{:S(2)}) collective-permute-start(f32[256]{0:T(256)S(1)} %multiply_reduce_fusion.1), channel_id=1, source_target_pairs={{0,2},{1,3},{2,0},{3,1},{4,6},{5,7},{6,4},{7,5},{8,10},{9,11},{10,... | collective-permute-start | bytes 3080 | tf_op jit(solution)/shard_map/ppermute | solution.py:15
  (111 shorter events, 33.6 us)
Async XLA Ops:
  0.6 23.9 %copy-start = (bf16[256,512]{1,0:T(8,128)(2,1)S(1)}, bf16[256,512]{1,0:T(8,128)(2,1)}, u32[]{:S(2)}) copy-start(bf16[256,512]{1,0:T(8,128)(2,1)} %param.10) | copy-start | bytes 786436
  1.8 10.3 %collective-permute-start = (f32[256]{0:T(256)S(1)}, f32[256]{0:T(256)S(1)}, u32[]{:S(2)}, u32[]{:S(2)}) collective-permute-start(f32[256]{0:T(256)S(1)} %fusion.70), channel_id=1, source_target_pairs={{0,1},{1,2},{2,3},{3,0},{4,5},{5,6},{6,7},{7,4},{8,9},{9,10},{10,1... | collective-permute-start | bytes 3080 | tf_op jit(solution)/shard_map/ppermute | solution.py:15
  4.0 8.1 %collective-permute-start.1 = (f32[256]{0:T(256)S(1)}, f32[256]{0:T(256)S(1)}, u32[]{:S(2)}, u32[]{:S(2)}) collective-permute-start(f32[256]{0:T(256)S(1)} %fusion.70), channel_id=1, source_target_pairs={{0,2},{1,3},{2,0},{3,1},{4,6},{5,7},{6,4},{7,5},{8,10},{9,11},{10,... | collective-permute-start | bytes 3080 | tf_op jit(solution)/shard_map/ppermute | solution.py:15
  6.6 5.5 %collective-permute-start.2 = (f32[256]{0:T(256)S(1)}, f32[256]{0:T(256)S(1)}, u32[]{:S(2)}, u32[]{:S(2)}) collective-permute-start(f32[256]{0:T(256)S(1)} %fusion.70), channel_id=1, source_target_pairs={{0,3},{1,0},{2,1},{3,2},{4,7},{5,4},{6,5},{7,6},{8,11},{9,8},{10,9... | collective-permute-start | bytes 3080 | tf_op jit(solution)/shard_map/ppermute | solution.py:15
  15.0 28.0 %copy-start.3 = (f32[2048]{0:T(1024)S(1)}, f32[2048]{0:T(1024)}, u32[]{:S(2)}) copy-start(f32[2048]{0:T(1024)} %param.13) | copy-start | bytes 24580
  15.0 24.2 %all-to-all-start = ((bf16[32,16,512]{2,1,0:T(8,128)(2,1)}), bf16[32,16,512]{2,1,0:T(8,128)(2,1)S(1)}, u32[]{:S(2)}, u32[]{:S(2)}) async-start(bf16[32,16,512]{2,1,0:T(8,128)(2,1)} %bitcast.9), calls=%async_computation | async-start | bytes 1048576 | tf_op jit(solution)/shard_map/all_to_all | solution.py:95
  24.5 14.6 %collective-permute-start.9 = (bf16[256,512]{1,0:T(8,128)(2,1)S(1)}, bf16[256,512]{1,0:T(8,128)(2,1)S(1)}, u32[]{:S(2)}, u32[]{:S(2)}) collective-permute-start(bf16[256,512]{1,0:T(8,128)(2,1)S(1)} %copy-done), channel_id=1, source_target_pairs={{0,1},{1,2},{2,3},{3,0},{4,5},{5,6},{6,7},{7,4},{8,9},{9,10},{10,1... | collective-permute-start | bytes 786440 | tf_op jit(solution)/shard_map/ppermute | solution.py:15
  25.0 14.1 %collective-permute-start.10 = (bf16[256,512]{1,0:T(8,128)(2,1)S(1)}, bf16[256,512]{1,0:T(8,128)(2,1)S(1)}, u32[]{:S(2)}, u32[]{:S(2)}) collective-permute-start(bf16[256,512]{1,0:T(8,128)(2,1)S(1)} %copy-done), channel_id=1, source_target_pairs={{0,2},{1,3},{2,0},{3,1},{4,6},{5,7},{6,4},{7,5},{8,10},{9,11},{10,... | collective-permute-start | bytes 786440 | tf_op jit(solution)/shard_map/ppermute | solution.py:15
  25.8 13.6 %collective-permute-start.11 = (bf16[256,512]{1,0:T(8,128)(2,1)S(1)}, bf16[256,512]{1,0:T(8,128)(2,1)S(1)}, u32[]{:S(2)}, u32[]{:S(2)}) collective-permute-start(bf16[256,512]{1,0:T(8,128)(2,1)S(1)} %copy-done), channel_id=1, source_target_pairs={{0,3},{1,0},{2,1},{3,2},{4,7},{5,4},{6,5},{7,6},{8,11},{9,8},{10,9... | collective-permute-start | bytes 786440 | tf_op jit(solution)/shard_map/ppermute | solution.py:15
  39.2 25.0 %collective-permute-start.3 = (bf16[512,512]{1,0:T(8,128)(2,1)S(1)}, bf16[512,512]{1,0:T(8,128)(2,1)}, u32[]{:S(2)}, u32[]{:S(2)}) collective-permute-start(bf16[512,512]{1,0:T(8,128)(2,1)S(1)} %bitcast.102), channel_id=1, source_target_pairs={{0,1},{1,2},{2,3},{3,0},{4,5},{5,6},{6,7},{7,4},{8,9},{9,10},{10,1... | collective-permute-start | bytes 1572872 | tf_op jit(solution)/shard_map/ppermute | solution.py:15
  39.5 25.8 %collective-permute-start.4 = (bf16[512,512]{1,0:T(8,128)(2,1)S(1)}, bf16[512,512]{1,0:T(8,128)(2,1)}, u32[]{:S(2)}, u32[]{:S(2)}) collective-permute-start(bf16[512,512]{1,0:T(8,128)(2,1)S(1)} %bitcast.103), channel_id=1, source_target_pairs={{0,2},{1,3},{2,0},{3,1},{4,6},{5,7},{6,4},{7,5},{8,10},{9,11},{10,... | collective-permute-start | bytes 1572872 | tf_op jit(solution)/shard_map/ppermute | solution.py:15
  40.7 25.8 %collective-permute-start.5 = (bf16[512,512]{1,0:T(8,128)(2,1)S(1)}, bf16[512,512]{1,0:T(8,128)(2,1)S(1)}, u32[]{:S(2)}, u32[]{:S(2)}) collective-permute-start(bf16[512,512]{1,0:T(8,128)(2,1)S(1)} %bitcast.104), channel_id=1, source_target_pairs={{0,3},{1,0},{2,1},{3,2},{4,7},{5,4},{6,5},{7,6},{8,11},{9,8},{10,9... | collective-permute-start | bytes 1572872 | tf_op jit(solution)/shard_map/ppermute | solution.py:15
  45.2 40.1 %all-to-all-start.2 = ((bf16[32,16,2048]{2,1,0:T(8,128)(2,1)}), bf16[32,16,2048]{2,1,0:T(8,128)(2,1)S(1)}, u32[]{:S(2)}, u32[]{:S(2)}) async-start(bf16[32,16,2048]{2,1,0:T(8,128)(2,1)} %bitcast.19), calls=%async_computation.2 | async-start | bytes 4194304 | tf_op jit(solution)/shard_map/all_to_all | solution.py:95
  77.8 25.8 %collective-permute-start.6 = (bf16[512,512]{1,0:T(8,128)(2,1)}, bf16[512,512]{1,0:T(8,128)(2,1)S(1)}, u32[]{:S(2)}, u32[]{:S(2)}) collective-permute-start(bf16[512,512]{1,0:T(8,128)(2,1)} %fusion.30), channel_id=1, source_target_pairs={{0,1},{1,2},{2,3},{3,0},{4,5},{5,6},{6,7},{7,4},{8,9},{9,10},{10,1... | collective-permute-start | bytes 1572872 | tf_op jit(solution)/shard_map/ppermute | solution.py:15
  80.2 25.7 %collective-permute-start.7 = (bf16[512,512]{1,0:T(8,128)(2,1)}, bf16[512,512]{1,0:T(8,128)(2,1)S(1)}, u32[]{:S(2)}, u32[]{:S(2)}) collective-permute-start(bf16[512,512]{1,0:T(8,128)(2,1)} %fusion.36), channel_id=1, source_target_pairs={{0,2},{1,3},{2,0},{3,1},{4,6},{5,7},{6,4},{7,5},{8,10},{9,11},{10,... | collective-permute-start | bytes 1572872 | tf_op jit(solution)/shard_map/ppermute | solution.py:15
  85.3 20.7 %collective-permute-start.8 = (bf16[512,512]{1,0:T(8,128)(2,1)}, bf16[512,512]{1,0:T(8,128)(2,1)}, u32[]{:S(2)}, u32[]{:S(2)}) collective-permute-start(bf16[512,512]{1,0:T(8,128)(2,1)} %fusion.42), channel_id=1, source_target_pairs={{0,3},{1,0},{2,1},{3,2},{4,7},{5,4},{6,5},{7,6},{8,11},{9,8},{10,9... | collective-permute-start | bytes 1572872 | tf_op jit(solution)/shard_map/ppermute | solution.py:15
  98.4 20.3 %collective-permute-start.12 = (bf16[512,512]{1,0:T(8,128)(2,1)S(1)}, bf16[512,512]{1,0:T(8,128)(2,1)S(1)}, u32[]{:S(2)}, u32[]{:S(2)}) collective-permute-start(bf16[512,512]{1,0:T(8,128)(2,1)S(1)} %fusion.33), channel_id=1, source_target_pairs={{0,1},{1,2},{2,3},{3,0},{4,5},{5,6},{6,7},{7,4},{8,9},{9,10},{10,1... | collective-permute-start | bytes 1572872 | tf_op jit(solution)/shard_map/ppermute | solution.py:15
  103.5 23.6 %collective-permute-start.13 = (bf16[512,512]{1,0:T(8,128)(2,1)}, bf16[512,512]{1,0:T(8,128)(2,1)S(1)}, u32[]{:S(2)}, u32[]{:S(2)}) collective-permute-start(bf16[512,512]{1,0:T(8,128)(2,1)} %fusion.39), channel_id=1, source_target_pairs={{0,2},{1,3},{2,0},{3,1},{4,6},{5,7},{6,4},{7,5},{8,10},{9,11},{10,... | collective-permute-start | bytes 1572872 | tf_op jit(solution)/shard_map/ppermute | solution.py:15
  103.5 24.7 %collective-permute-start.14 = (bf16[512,512]{1,0:T(8,128)(2,1)}, bf16[512,512]{1,0:T(8,128)(2,1)}, u32[]{:S(2)}, u32[]{:S(2)}) collective-permute-start(bf16[512,512]{1,0:T(8,128)(2,1)} %fusion.45), channel_id=1, source_target_pairs={{0,3},{1,0},{2,1},{3,2},{4,7},{5,4},{6,5},{7,6},{8,11},{9,8},{10,9... | collective-permute-start | bytes 1572872 | tf_op jit(solution)/shard_map/ppermute | solution.py:15
  108.9 23.1 %all-to-all-start.1 = ((bf16[32,16,512]{2,1,0:T(8,128)(2,1)}), bf16[32,16,512]{2,1,0:T(8,128)(2,1)S(1)}, u32[]{:S(2)}, u32[]{:S(2)}) async-start(bf16[32,16,512]{2,1,0:T(8,128)(2,1)} %bitcast.17), calls=%async_computation.1 | async-start | bytes 1048576 | tf_op jit(solution)/shard_map/all_to_all | solution.py:105
  132.0 20.2 %all-to-all-start.3 = ((bf16[32,16,512]{2,1,0:T(8,128)(2,1)}), bf16[32,16,512]{2,1,0:T(8,128)(2,1)S(1)}, u32[]{:S(2)}, u32[]{:S(2)}) async-start(bf16[32,16,512]{2,1,0:T(8,128)(2,1)} %bitcast.21), calls=%async_computation.3 | async-start | bytes 1048576 | tf_op jit(solution)/shard_map/all_to_all | solution.py:105
  156.4 3.9 %collective-permute-start.15 = (f32[256]{0:T(256)S(1)}, f32[256]{0:T(256)S(1)}, u32[]{:S(2)}, u32[]{:S(2)}) collective-permute-start(f32[256]{0:T(256)S(1)} %multiply_reduce_fusion.1), channel_id=1, source_target_pairs={{0,1},{1,2},{2,3},{3,0},{4,5},{5,6},{6,7},{7,4},{8,9},{9,10},{10,1... | collective-permute-start | bytes 3080 | tf_op jit(solution)/shard_map/ppermute | solution.py:15
  157.6 3.9 %collective-permute-start.16 = (f32[256]{0:T(256)S(1)}, f32[256]{0:T(256)S(1)}, u32[]{:S(2)}, u32[]{:S(2)}) collective-permute-start(f32[256]{0:T(256)S(1)} %multiply_reduce_fusion.1), channel_id=1, source_target_pairs={{0,2},{1,3},{2,0},{3,1},{4,6},{5,7},{6,4},{7,5},{8,10},{9,11},{10,... | collective-permute-start | bytes 3080 | tf_op jit(solution)/shard_map/ppermute | solution.py:15
  160.0 2.4 %collective-permute-start.17 = (f32[256]{0:T(256)S(1)}, f32[256]{0:T(256)S(1)}, u32[]{:S(2)}, u32[]{:S(2)}) collective-permute-start(f32[256]{0:T(256)S(1)} %multiply_reduce_fusion.1), channel_id=1, source_target_pairs={{0,3},{1,0},{2,1},{3,2},{4,7},{5,4},{6,5},{7,6},{8,11},{9,8},{10,9... | collective-permute-start | bytes 3080 | tf_op jit(solution)/shard_map/ppermute | solution.py:15
  (11 other events, 90.0 us)

commit v8 on v7

--- a/solution.py
+++ b/solution.py
@@ -9,6 +9,11 @@
 
 
 epsilon = 1e-05
+
+
+def rms_norm(values, gain):
+    meansq = jnp.mean(values * values, axis=1, keepdims=True)
+    return values * lax.rsqrt(meansq + epsilon) * gain[None, :]
 
 
 def shift_tp(value, step, tp_count):
@@ -64,11 +69,7 @@
     chunk_items = slot_count // CHUNKS
     stream = hidden.astype(jnp.float32)
     whole_rows = gather_tp(hidden, tp_count).astype(jnp.float32)
-    meansq = sum_tp(jnp.sum(stream * stream, axis=1), tp_count) / full_width
-    row_scale = lax.rsqrt(meansq + epsilon)[:, None]
-    normed_in = (whole_rows * row_scale * pre_gain[None, :]).astype(jnp.bfloat16)
-    own_gain = lax.dynamic_slice_in_dim(pre_gain, lax.axis_index("tp") * col_part, col_part)
-    normed_own = (stream * row_scale * own_gain[None, :]).astype(jnp.bfloat16)
+    normed_in = rms_norm(whole_rows, pre_gain).astype(jnp.bfloat16)
     top = routes.shape[1]
     chosen = routes.reshape(-1)
     onehot = (chosen[:, None] == jnp.arange(E, dtype=jnp.int32)[None, :]).astype(jnp.int32)
@@ -87,7 +88,7 @@
             hit = (slot_ids[:, None] == chunk_pairs[None, :, k]) & (owner_pairs[None, :, k] == c)
             dispatch = dispatch | hit
         relay = c == 0
-        source = normed_own if relay else normed_in
+        source = hidden if relay else normed_in
         outgoing = jnp.dot(
             dispatch.astype(jnp.bfloat16), source, preferred_element_type=jnp.float32
         ).astype(jnp.bfloat16)
@@ -96,7 +97,8 @@
         sources, items, widths = pieces.shape
         flat_rows = pieces.reshape(sources * items, widths)
         if relay:
-            flat_rows = gather_tp(flat_rows, tp_count)
+            raw_rows = gather_tp(flat_rows, tp_count).astype(jnp.float32)
+            flat_rows = rms_norm(raw_rows, pre_gain).astype(jnp.bfloat16)
         gate_val = jnp.dot(flat_rows, gate_weight[0], preferred_element_type=jnp.float32)
         up_val = jnp.dot(flat_rows, up_weight[0], preferred_element_type=jnp.float32)
         activ = (jax.nn.silu(gate_val) * up_val).astype(jnp.bfloat16)
@@ -104,11 +106,12 @@
         summed = summed.reshape(sources, items, col_part)
         back = lax.all_to_all(summed, "req", split_axis=0, concat_axis=0, tiled=True)
         returned.append(back.reshape(req_count * chunk_items, col_part))
-    returned = jnp.concatenate(returned, axis=0)
-    out_idx = chunk_of * (req_count * chunk_items) + in_chunk
-    picked = returned[out_idx].reshape(row_count, top, col_part).astype(jnp.float32)
-    mixed = jnp.sum(picked * route_weights[:, :, None], axis=1)
-    total_stream = stream + mixed
+    total_stream = stream
+    for c in range(CHUNKS):
+        picked = returned[c][in_chunk].reshape(row_count, top, col_part).astype(jnp.float32)
+        mine = (owner_pairs == c)[:, :, None]
+        terms = jnp.where(mine, picked * route_weights[:, :, None], 0.0)
+        total_stream = total_stream + jnp.sum(terms, axis=1)
     out_sums = sum_tp(jnp.sum(total_stream * total_stream, axis=1), tp_count)
     normed_out = (
         total_stream * lax.rsqrt(out_sums / full_width + epsilon)[:, None] * out_gain[None, :]

time: 165 us -> 160 us (0.970)
  starting transfers between devices: 60.3 us -> 52.2 us
  local copies, waits for them, and re-layouts: 9.2 us -> 10.9 us
    ppermute x18 -> x15, waiting for transfers between devices: 33.7 us -> 22.1 us  [shift_tp(): lax.ppermute(value, 'tp', [(j, (j + step) % tp_count) for j in range(tp_c...]
    all_to_all x2, waiting for transfers between devices: 0.01 us -> 10.7 us  [shards(): lax.all_to_all(outgoing, 'req', split_axis=0, concat_axis=0, tiled=True)]
    all_to_all x2, starting transfers between devices: 17.6 us -> 13.6 us  [shards(): lax.all_to_all(outgoing, 'req', split_axis=0, concat_axis=0, tiled=True)]
    ppermute x18 -> x15, starting transfers between devices: 24.1 us -> 20.9 us  [shift_tp(): lax.ppermute(value, 'tp', [(j, (j + step) % tp_count) for j in range(tp_c...]
    gather x1 -> x2, local copies, waits for them, and re-layouts: 1.97 us -> 3.94 us  [shards(): returned[c][in_chunk].reshape(row_count, top, col_part).astype(jnp.float32)]
    reduce_sum x2 -> x3, other arithmetic: 2.47 us -> 4.02 us  [the longest x1 3.25 us: shards(): total_stream = total_stream + jnp.sum(terms, axis=1)]
  transfers between devices with their start and end apart: 22 -> 19, of which waited for: 8 -> 8; matrix products, arithmetic and copies ran while one was open for 29% -> 33% of each run, Pallas kernels for 0% -> 0%
where the time goes in v8:
time: 160 us
  starting transfers between devices  52.2 us (33%)
  waiting for transfers between devices  45.4 us (28%)
  matrix products  42.7 us (27%)
  local copies, waits for them, and re-layouts  10.9 us (7%)
  other arithmetic  7.24 us (5%)
    ppermute x15, waiting for transfers between devices, shift_tp(): lax.ppermute(value, 'tp', [(j, (j + step) % tp_count) for j in range(tp_c...  22.1 us
    ppermute x15, starting transfers between devices, shift_tp(): lax.ppermute(value, 'tp', [(j, (j + step) % tp_count) for j in range(tp_c...  20.9 us
    all_to_all x2, starting transfers between devices, shards(): lax.all_to_all(summed, 'req', split_axis=0, concat_axis=0, tiled=True)  17.6 us
    dot_general x8, matrix products, down_scatter_sum_tp(): jnp.dot(activ, w_block, preferred_element_type=jnp.float32)  16.7 us
    all_to_all x2, starting transfers between devices, shards(): lax.all_to_all(outgoing, 'req', split_axis=0, concat_axis=0, tiled=True)  13.6 us
    all_to_all x2, waiting for transfers between devices, shards(): lax.all_to_all(summed, 'req', split_axis=0, concat_axis=0, tiled=True)  12.7 us
    dot_general x2, matrix products, shards(): jnp.dot(flat_rows, gate_weight[0], preferred_element_type=jnp.float32)  12 us
    all_to_all x2, waiting for transfers between devices, shards(): lax.all_to_all(outgoing, 'req', split_axis=0, concat_axis=0, tiled=True)  10.7 us
  transfers between devices with their start and end apart: 19, of which 8 were waited for; matrix products, arithmetic and copies ran while one was open for 33% of the time, Pallas kernels for 0%

profile of v8, /device:TPU:1, one launch (start us, length us, event | category | flops | bytes accessed | tf_op | source)
XLA Modules:
  0.0 159.7 jit_solution(11008073875310909808)
XLA Ops:
  0.6 2.2 %collective-permute-start.6 = (bf16[256,512]{1,0:T(8,128)(2,1)}, bf16[256,512]{1,0:T(8,128)(2,1)S(1)}, u32[]{:S(2)}, u32[]{:S(2)}) collective-permute-start(bf16[256,512]{1,0:T(8,128)(2,1)} %param.8), channel_id=1, source_target_pairs={{0,1},{1,2},{2,3},{3,0},{4,5},{5,6},{6,7},{7,4},{8,9},{9,10},{10,1... | collective-permute-start | bytes 786440 | tf_op jit(solution)/shard_map/ppermute | solution.py:20
  2.8 2.6 %collective-permute-start.7 = (bf16[256,512]{1,0:T(8,128)(2,1)}, bf16[256,512]{1,0:T(8,128)(2,1)S(1)}, u32[]{:S(2)}, u32[]{:S(2)}) collective-permute-start(bf16[256,512]{1,0:T(8,128)(2,1)} %param.8), channel_id=1, source_target_pairs={{0,2},{1,3},{2,0},{3,1},{4,6},{5,7},{6,4},{7,5},{8,10},{9,11},{10,... | collective-permute-start | bytes 786440 | tf_op jit(solution)/shard_map/ppermute | solution.py:20
  10.1 2.1 %convolution_convert_fusion.1 = bf16[512,512]{1,0:T(8,128)(2,1)} fusion(bf16[256,512]{1,0:T(8,128)(2,1)} %param.8, s32[256]{0:T(256)S(1)} %bitcast.110, s32[256]{0:T(256)S(1)} %bitcast.108, pred[256]{0:T(512)(128)(4,1)S(1)} %get-tuple-element.7, pred[256]{0:T(512)(128)(4,1)S(1)} %get-tuple-element.4), kind=kOutput, calls=%fused_computation.49 | convolution fusion | flops 135135232 | bytes 788992 | tf_op jit(solution)/shard_map/dot_general | solution.py:92
  12.2 9.4 %all-to-all-start = ((bf16[32,16,512]{2,1,0:T(8,128)(2,1)}), bf16[32,16,512]{2,1,0:T(8,128)(2,1)S(1)}, u32[]{:S(2)}, u32[]{:S(2)}) async-start(bf16[32,16,512]{2,1,0:T(8,128)(2,1)} %bitcast.4), calls=%async_computation | async-start | bytes 1048576 | tf_op jit(solution)/shard_map/all_to_all | solution.py:96
  22.6 10.7 %all-to-all-done = bf16[32,16,512]{2,1,0:T(8,128)(2,1)S(1)} async-done(((bf16[32,16,512]{2,1,0:T(8,128)(2,1)}), bf16[32,16,512]{2,1,0:T(8,128)(2,1)S(1)}, u32[]{:S(2)}, u32[]{:S(2)}) %all-to-all-start) | async-done | bytes 524320 | tf_op jit(solution)/shard_map/all_to_all | solution.py:96
  36.2 2.2 %convolution_convert_fusion = bf16[512,2048]{1,0:T(8,128)(2,1)} fusion(bf16[256,2048]{1,0:T(8,128)(2,1)S(1)} %constant_dynamic-update-slice_fusion, f32[2048]{0:T(1024)S(1)} %copy-done.3, f32[256]{0:T(256)S(1)} %add_rsqrt_fusion.2, s32[256]{0:T(256)S(1)} %bitcast.111, s32[256]{0:T(256)S(1)} %bitcast.109, pred[256]{0:T(512)(128)(4,1)S(1)} %get-tuple-element.6, ...), kind=kOutput, calls=%fused_computation.17 | convolution fusion | flops 540672000 | bytes 3157504 | tf_op jit(solution)/shard_map/dot_general | solution.py:92
  38.4 4.2 %all-to-all-start.2 = ((bf16[32,16,2048]{2,1,0:T(8,128)(2,1)}), bf16[32,16,2048]{2,1,0:T(8,128)(2,1)S(1)}, u32[]{:S(2)}, u32[]{:S(2)}) async-start(bf16[32,16,2048]{2,1,0:T(8,128)(2,1)} %bitcast.16), calls=%async_computation.2 | async-start | bytes 4194304 | tf_op jit(solution)/shard_map/all_to_all | solution.py:96
  42.9 16.6 %collective-permute-done = bf16[512,512]{1,0:T(8,128)(2,1)} collective-permute-done((bf16[512,512]{1,0:T(8,128)(2,1)S(1)}, bf16[512,512]{1,0:T(8,128)(2,1)}, u32[]{:S(2)}, u32[]{:S(2)}) %collective-permute-start) | collective-permute-done | bytes 524320 | tf_op jit(solution)/shard_map/ppermute | solution.py:20
  62.4 6.1 %fusion.6 = f32[512,1408]{1,0:T(8,128)S(1)} fusion(bf16[1,2048,1408]{2,1,0:T(8,128)(2,1)} %param.13, bf16[512,2048]{1,0:T(8,128)(2,1)S(1)} %constant_dynamic-update-slice_fusion.4, f32[2048]{0:T(1024)S(1)} %copy-done.3, f32[512]{0:T(512)S(1)} %add_rsqrt_fusion), kind=kOutput, calls=%fused_computation.9 | convolution fusion | flops 2956984320 | bytes 10758144 | tf_op jit(solution)/shard_map/dot_general | solution.py:102
  68.5 3.5 %multiply_convert_fusion = bf16[512,1408]{1,0:T(8,128)(2,1)S(1)} fusion(f32[512,1408]{1,0:T(8,128)S(1)} %fusion.6, bf16[1,2048,1408]{2,1,0:T(8,128)(2,1)S(1)} %bitcast.116, bf16[512,2048]{1,0:T(8,128)(2,1)S(1)} %constant_dynamic-update-slice_fusion.4, f32[2048]{0:T(1024)S(1)} %copy-done.3, f32[512]{0:T(512)S(1)} %add_rsqrt_fusion), kind=kOutput, calls=%fused_computation.19 | convolution fusion | flops 2961309696 | bytes 12199936 | tf_op jit(solution)/shard_map/dot_general | solution.py:103
  80.2 5.9 %fusion.4 = f32[512,1408]{1,0:T(8,128)S(1)} fusion(bf16[512,2048]{1,0:T(8,128)(2,1)S(1)} %bitcast.98, bf16[1,2048,1408]{2,1,0:T(8,128)(2,1)} %param.13), kind=kOutput, calls=%fused_computation.7 | convolution fusion | flops 2952790016 | bytes 10747904 | tf_op jit(solution)/shard_map/dot_general | solution.py:102
  86.0 6.2 %fusion.14 = bf16[512,1408]{1,0:T(8,128)(2,1)S(1)} fusion(bf16[512,2048]{1,0:T(8,128)(2,1)S(1)} %bitcast.99, bf16[1,2048,1408]{2,1,0:T(8,128)(2,1)} %param.14, f32[512,1408]{1,0:T(8,128)S(1)} %fusion.4), kind=kOutput, calls=%fused_computation.18 | convolution fusion | flops 2957115392 | bytes 12189696 | tf_op jit(solution)/shard_map/dot_general | solution.py:103
  93.3 2.4 %collective-permute-start.10 = (bf16[512,512]{1,0:T(8,128)(2,1)S(1)}, bf16[512,512]{1,0:T(8,128)(2,1)S(1)}, u32[]{:S(2)}, u32[]{:S(2)}) collective-permute-start(bf16[512,512]{1,0:T(8,128)(2,1)S(1)} %fusion.45), channel_id=1, source_target_pairs={{0,2},{1,3},{2,0},{3,1},{4,6},{5,7},{6,4},{7,5},{8,10},{9,11},{10,... | collective-permute-start | bytes 1572872 | tf_op jit(solution)/shard_map/ppermute | solution.py:20
  99.4 2.7 %collective-permute-start.11 = (bf16[512,512]{1,0:T(8,128)(2,1)}, bf16[512,512]{1,0:T(8,128)(2,1)}, u32[]{:S(2)}, u32[]{:S(2)}) collective-permute-start(bf16[512,512]{1,0:T(8,128)(2,1)} %fusion.51), channel_id=1, source_target_pairs={{0,3},{1,0},{2,1},{3,2},{4,7},{5,4},{6,5},{7,6},{8,11},{9,8},{10,9... | collective-permute-start | bytes 1572872 | tf_op jit(solution)/shard_map/ppermute | solution.py:20
  102.7 3.0 %add_convert_fusion.1 = bf16[512,512]{1,0:T(8,128)(2,1)} fusion(bf16[512,512]{1,0:T(8,128)(2,1)} %collective-permute-done.5, bf16[512,512]{1,0:T(8,128)(2,1)} %collective-permute-done.4, bf16[512,512]{1,0:T(8,128)(2,1)S(1)} %collective-permute-done.3, bf16[512,1408]{1,0:T(8,128)(2,1)S(1)} %copy-done.6, bf16[1,1408,2048]{2,1,0:T(8,128)(2,1)S(1)} %bitcast.120, ...), kind=kOutput, calls=%fused_computation.65 | convolution fusion | flops 740556800 | bytes 4980740 | tf_op jit(solution)/shard_map/dot_general | solution.py:54
  105.7 13.7 %all-to-all-start.1 = ((bf16[32,16,512]{2,1,0:T(8,128)(2,1)}), bf16[32,16,512]{2,1,0:T(8,128)(2,1)S(1)}, u32[]{:S(2)}, u32[]{:S(2)}) async-start(bf16[32,16,512]{2,1,0:T(8,128)(2,1)} %bitcast.12), calls=%async_computation.1 | async-start | bytes 1048576 | tf_op jit(solution)/shard_map/all_to_all | solution.py:107
  120.0 2.2 %collective-permute-done.9 = bf16[512,512]{1,0:T(8,128)(2,1)S(1)} collective-permute-done((bf16[512,512]{1,0:T(8,128)(2,1)}, bf16[512,512]{1,0:T(8,128)(2,1)S(1)}, u32[]{:S(2)}, u32[]{:S(2)}) %collective-permute-start.9) | collective-permute-done | bytes 524320 | tf_op jit(solution)/shard_map/ppermute | solution.py:20
  123.4 3.7 %add_convert_fusion = bf16[512,512]{1,0:T(8,128)(2,1)} fusion(bf16[512,512]{1,0:T(8,128)(2,1)} %collective-permute-done.11, bf16[512,512]{1,0:T(8,128)(2,1)S(1)} %collective-permute-done.10, bf16[512,512]{1,0:T(8,128)(2,1)S(1)} %collective-permute-done.9, bf16[512,1408]{1,0:T(8,128)(2,1)} %copy-done.4, bf16[1,1408,2048]{2,1,0:T(8,128)(2,1)} %param.15, ...), kind=kOutput, calls=%fused_computation.61 | convolution fusion | flops 740556800 | bytes 4980740 | tf_op jit(solution)/shard_map/dot_general | solution.py:54
  127.1 4.1 %all-to-all-done.1 = bf16[32,16,512]{2,1,0:T(8,128)(2,1)S(1)} async-done(((bf16[32,16,512]{2,1,0:T(8,128)(2,1)}), bf16[32,16,512]{2,1,0:T(8,128)(2,1)S(1)}, u32[]{:S(2)}, u32[]{:S(2)}) %all-to-all-start.1) | async-done | bytes 524320 | tf_op jit(solution)/shard_map/all_to_all | solution.py:107
  131.2 3.9 %all-to-all-start.3 = ((bf16[32,16,512]{2,1,0:T(8,128)(2,1)}), bf16[32,16,512]{2,1,0:T(8,128)(2,1)S(1)}, u32[]{:S(2)}, u32[]{:S(2)}) async-start(bf16[32,16,512]{2,1,0:T(8,128)(2,1)} %bitcast.18), calls=%async_computation.3 | async-start | bytes 1048576 | tf_op jit(solution)/shard_map/all_to_all | solution.py:107
  135.2 2.0 %gather_fusion = bf16[512,512]{1,0:T(8,128)(2,1)S(1)} fusion(bf16[512,512]{1,0:T(8,128)(2,1)S(1)} %bitcast.96, s32[1024]{0:T(1024)S(1)} %pad_clamp_fusion.1), kind=kCustom, calls=%fused_computation | custom fusion | bytes 1050624 | tf_op jit(solution)/shard_map/gather | solution.py:111
  137.8 8.6 %all-to-all-done.3 = bf16[32,16,512]{2,1,0:T(8,128)(2,1)S(1)} async-done(((bf16[32,16,512]{2,1,0:T(8,128)(2,1)}), bf16[32,16,512]{2,1,0:T(8,128)(2,1)S(1)}, u32[]{:S(2)}, u32[]{:S(2)}) %all-to-all-start.3) | async-done | bytes 524320 | tf_op jit(solution)/shard_map/all_to_all | solution.py:107
  149.1 3.2 %select_reduce_fusion.1 = (f32[256,512]{1,0:T(8,128)S(1)}, f32[256,512]{1,0:T(8,128)S(1)}) fusion(f32[256,2,512]{2,1,0:T(2,128)S(1)} %reshape.395, pred[256,2]{1,0:T(8,128)(4,1)S(1)} %copy.35, f32[256,2]{1,0:T(8,128)S(1)} %copy.37, f32[256,2,512]{2,1,0:T(2,128)S(1)} %reshape.396, pred[256,2]{1,0:T(8,128)(4,1)S(1)} %copy.38), kind=kLoop, calls=%fused_computation.64 | loop fusion | flops 1310720 | bytes 3148800 | tf_op jit(solution)/shard_map/reduce_sum | solution.py:114
  154.6 2.2 %collective-permute-start.14 = (f32[256]{0:T(256)S(1)}, f32[256]{0:T(256)S(1)}, u32[]{:S(2)}, u32[]{:S(2)}) collective-permute-start(f32[256]{0:T(256)S(1)} %get-tuple-element.8), channel_id=1, source_target_pairs={{0,3},{1,0},{2,1},{3,2},{4,7},{5,4},{6,5},{7,6},{8,11},{9,8},{10,9... | collective-permute-start | bytes 3080 | tf_op jit(solution)/shard_map/ppermute | solution.py:20
  (107 shorter events, 34.8 us)
Async XLA Ops:
  0.6 21.2 %copy-start = (bf16[256,512]{1,0:T(8,128)(2,1)S(1)}, bf16[256,512]{1,0:T(8,128)(2,1)}, u32[]{:S(2)}) copy-start(bf16[256,512]{1,0:T(8,128)(2,1)} %param.8) | copy-start | bytes 786436
  0.6 21.5 %collective-permute-start.6 = (bf16[256,512]{1,0:T(8,128)(2,1)}, bf16[256,512]{1,0:T(8,128)(2,1)S(1)}, u32[]{:S(2)}, u32[]{:S(2)}) collective-permute-start(bf16[256,512]{1,0:T(8,128)(2,1)} %param.8), channel_id=1, source_target_pairs={{0,1},{1,2},{2,3},{3,0},{4,5},{5,6},{6,7},{7,4},{8,9},{9,10},{10,1... | collective-permute-start | bytes 786440 | tf_op jit(solution)/shard_map/ppermute | solution.py:20
  2.8 19.4 %collective-permute-start.7 = (bf16[256,512]{1,0:T(8,128)(2,1)}, bf16[256,512]{1,0:T(8,128)(2,1)S(1)}, u32[]{:S(2)}, u32[]{:S(2)}) collective-permute-start(bf16[256,512]{1,0:T(8,128)(2,1)} %param.8), channel_id=1, source_target_pairs={{0,2},{1,3},{2,0},{3,1},{4,6},{5,7},{6,4},{7,5},{8,10},{9,11},{10,... | collective-permute-start | bytes 786440 | tf_op jit(solution)/shard_map/ppermute | solution.py:20
  5.5 16.8 %collective-permute-start.8 = (bf16[256,512]{1,0:T(8,128)(2,1)}, bf16[256,512]{1,0:T(8,128)(2,1)S(1)}, u32[]{:S(2)}, u32[]{:S(2)}) collective-permute-start(bf16[256,512]{1,0:T(8,128)(2,1)} %param.8), channel_id=1, source_target_pairs={{0,3},{1,0},{2,1},{3,2},{4,7},{5,4},{6,5},{7,6},{8,11},{9,8},{10,9... | collective-permute-start | bytes 786440 | tf_op jit(solution)/shard_map/ppermute | solution.py:20
  12.2 21.1 %all-to-all-start = ((bf16[32,16,512]{2,1,0:T(8,128)(2,1)}), bf16[32,16,512]{2,1,0:T(8,128)(2,1)S(1)}, u32[]{:S(2)}, u32[]{:S(2)}) async-start(bf16[32,16,512]{2,1,0:T(8,128)(2,1)} %bitcast.4), calls=%async_computation | async-start | bytes 1048576 | tf_op jit(solution)/shard_map/all_to_all | solution.py:96
  21.7 14.5 %copy-start.3 = (f32[2048]{0:T(1024)S(1)}, f32[2048]{0:T(1024)}, u32[]{:S(2)}) copy-start(f32[2048]{0:T(1024)} %param.11) | copy-start | bytes 24580
  33.3 26.2 %collective-permute-start = (bf16[512,512]{1,0:T(8,128)(2,1)S(1)}, bf16[512,512]{1,0:T(8,128)(2,1)}, u32[]{:S(2)}, u32[]{:S(2)}) collective-permute-start(bf16[512,512]{1,0:T(8,128)(2,1)S(1)} %bitcast.100), channel_id=1, source_target_pairs={{0,1},{1,2},{2,3},{3,0},{4,5},{5,6},{6,7},{7,4},{8,9},{9,10},{10,1... | collective-permute-start | bytes 1572872 | tf_op jit(solution)/shard_map/ppermute | solution.py:20
  33.7 26.9 %collective-permute-start.1 = (bf16[512,512]{1,0:T(8,128)(2,1)S(1)}, bf16[512,512]{1,0:T(8,128)(2,1)}, u32[]{:S(2)}, u32[]{:S(2)}) collective-permute-start(bf16[512,512]{1,0:T(8,128)(2,1)S(1)} %bitcast.101), channel_id=1, source_target_pairs={{0,2},{1,3},{2,0},{3,1},{4,6},{5,7},{6,4},{7,5},{8,10},{9,11},{10,... | collective-permute-start | bytes 1572872 | tf_op jit(solution)/shard_map/ppermute | solution.py:20
  34.2 27.5 %collective-permute-start.2 = (bf16[512,512]{1,0:T(8,128)(2,1)S(1)}, bf16[512,512]{1,0:T(8,128)(2,1)S(1)}, u32[]{:S(2)}, u32[]{:S(2)}) collective-permute-start(bf16[512,512]{1,0:T(8,128)(2,1)S(1)} %bitcast.102), channel_id=1, source_target_pairs={{0,3},{1,0},{2,1},{3,2},{4,7},{5,4},{6,5},{7,6},{8,11},{9,8},{10,9... | collective-permute-start | bytes 1572872 | tf_op jit(solution)/shard_map/ppermute | solution.py:20
  38.4 41.7 %all-to-all-start.2 = ((bf16[32,16,2048]{2,1,0:T(8,128)(2,1)}), bf16[32,16,2048]{2,1,0:T(8,128)(2,1)S(1)}, u32[]{:S(2)}, u32[]{:S(2)}) async-start(bf16[32,16,2048]{2,1,0:T(8,128)(2,1)} %bitcast.16), calls=%async_computation.2 | async-start | bytes 4194304 | tf_op jit(solution)/shard_map/all_to_all | solution.py:96
  73.9 25.5 %collective-permute-start.3 = (bf16[512,512]{1,0:T(8,128)(2,1)}, bf16[512,512]{1,0:T(8,128)(2,1)S(1)}, u32[]{:S(2)}, u32[]{:S(2)}) collective-permute-start(bf16[512,512]{1,0:T(8,128)(2,1)} %fusion.36), channel_id=1, source_target_pairs={{0,1},{1,2},{2,3},{3,0},{4,5},{5,6},{6,7},{7,4},{8,9},{9,10},{10,1... | collective-permute-start | bytes 1572872 | tf_op jit(solution)/shard_map/ppermute | solution.py:20
  75.7 26.4 %collective-permute-start.4 = (bf16[512,512]{1,0:T(8,128)(2,1)}, bf16[512,512]{1,0:T(8,128)(2,1)}, u32[]{:S(2)}, u32[]{:S(2)}) collective-permute-start(bf16[512,512]{1,0:T(8,128)(2,1)} %fusion.42), channel_id=1, source_target_pairs={{0,2},{1,3},{2,0},{3,1},{4,6},{5,7},{6,4},{7,5},{8,10},{9,11},{10,... | collective-permute-start | bytes 1572872 | tf_op jit(solution)/shard_map/ppermute | solution.py:20
  79.2 23.4 %collective-permute-start.5 = (bf16[512,512]{1,0:T(8,128)(2,1)}, bf16[512,512]{1,0:T(8,128)(2,1)}, u32[]{:S(2)}, u32[]{:S(2)}) collective-permute-start(bf16[512,512]{1,0:T(8,128)(2,1)} %fusion.48), channel_id=1, source_target_pairs={{0,3},{1,0},{2,1},{3,2},{4,7},{5,4},{6,5},{7,6},{8,11},{9,8},{10,9... | collective-permute-start | bytes 1572872 | tf_op jit(solution)/shard_map/ppermute | solution.py:20
  80.2 12.1 %slice-start.4 = ((s8[5767168]{0:T(1024)(128)(4,1)}), s8[4194304]{0:T(1024)(128)(4,1)S(1)}, s32[]{:S(2)}) async-start(s8[5767168]{0:T(1024)(128)(4,1)} %bitcast.119), calls=%async_computation.8 | async-start | bytes 8388608
  93.3 26.7 %collective-permute-start.10 = (bf16[512,512]{1,0:T(8,128)(2,1)S(1)}, bf16[512,512]{1,0:T(8,128)(2,1)S(1)}, u32[]{:S(2)}, u32[]{:S(2)}) collective-permute-start(bf16[512,512]{1,0:T(8,128)(2,1)S(1)} %fusion.45), channel_id=1, source_target_pairs={{0,2},{1,3},{2,0},{3,1},{4,6},{5,7},{6,4},{7,5},{8,10},{9,11},{10,... | collective-permute-start | bytes 1572872 | tf_op jit(solution)/shard_map/ppermute | solution.py:20
  97.5 24.7 %collective-permute-start.9 = (bf16[512,512]{1,0:T(8,128)(2,1)}, bf16[512,512]{1,0:T(8,128)(2,1)S(1)}, u32[]{:S(2)}, u32[]{:S(2)}) collective-permute-start(bf16[512,512]{1,0:T(8,128)(2,1)} %fusion.39), channel_id=1, source_target_pairs={{0,1},{1,2},{2,3},{3,0},{4,5},{5,6},{6,7},{7,4},{8,9},{9,10},{10,1... | collective-permute-start | bytes 1572872 | tf_op jit(solution)/shard_map/ppermute | solution.py:20
  99.4 20.5 %copy-start.1 = (f32[256,2]{0,1:T(2,128)S(1)}, f32[256,2]{0,1:T(2,128)}, u32[]{:S(2)}) copy-start(f32[256,2]{0,1:T(2,128)} %param.10) | copy-start | bytes 6148
  99.4 24.1 %collective-permute-start.11 = (bf16[512,512]{1,0:T(8,128)(2,1)}, bf16[512,512]{1,0:T(8,128)(2,1)}, u32[]{:S(2)}, u32[]{:S(2)}) collective-permute-start(bf16[512,512]{1,0:T(8,128)(2,1)} %fusion.51), channel_id=1, source_target_pairs={{0,3},{1,0},{2,1},{3,2},{4,7},{5,4},{6,5},{7,6},{8,11},{9,8},{10,9... | collective-permute-start | bytes 1572872 | tf_op jit(solution)/shard_map/ppermute | solution.py:20
  105.7 25.5 %all-to-all-start.1 = ((bf16[32,16,512]{2,1,0:T(8,128)(2,1)}), bf16[32,16,512]{2,1,0:T(8,128)(2,1)S(1)}, u32[]{:S(2)}, u32[]{:S(2)}) async-start(bf16[32,16,512]{2,1,0:T(8,128)(2,1)} %bitcast.12), calls=%async_computation.1 | async-start | bytes 1048576 | tf_op jit(solution)/shard_map/all_to_all | solution.py:107
  131.2 15.2 %all-to-all-start.3 = ((bf16[32,16,512]{2,1,0:T(8,128)(2,1)}), bf16[32,16,512]{2,1,0:T(8,128)(2,1)S(1)}, u32[]{:S(2)}, u32[]{:S(2)}) async-start(bf16[32,16,512]{2,1,0:T(8,128)(2,1)} %bitcast.18), calls=%async_computation.3 | async-start | bytes 1048576 | tf_op jit(solution)/shard_map/all_to_all | solution.py:107
  149.0 9.8 %copy-start.2 = (f32[512]{0:T(512)S(1)}, f32[512]{0:T(512)}, u32[]{:S(2)}) copy-start(f32[512]{0:T(512)} %param.12) | copy-start | bytes 6148
  152.5 4.3 %collective-permute-start.12 = (f32[256]{0:T(256)S(1)}, f32[256]{0:T(256)S(1)}, u32[]{:S(2)}, u32[]{:S(2)}) collective-permute-start(f32[256]{0:T(256)S(1)} %get-tuple-element.8), channel_id=1, source_target_pairs={{0,1},{1,2},{2,3},{3,0},{4,5},{5,6},{6,7},{7,4},{8,9},{9,10},{10,1... | collective-permute-start | bytes 3080 | tf_op jit(solution)/shard_map/ppermute | solution.py:20
  154.3 3.9 %collective-permute-start.13 = (f32[256]{0:T(256)S(1)}, f32[256]{0:T(256)S(1)}, u32[]{:S(2)}, u32[]{:S(2)}) collective-permute-start(f32[256]{0:T(256)S(1)} %get-tuple-element.8), channel_id=1, source_target_pairs={{0,2},{1,3},{2,0},{3,1},{4,6},{5,7},{6,4},{7,5},{8,10},{9,11},{10,... | collective-permute-start | bytes 3080 | tf_op jit(solution)/shard_map/ppermute | solution.py:20
  154.6 3.7 %collective-permute-start.14 = (f32[256]{0:T(256)S(1)}, f32[256]{0:T(256)S(1)}, u32[]{:S(2)}, u32[]{:S(2)}) collective-permute-start(f32[256]{0:T(256)S(1)} %get-tuple-element.8), channel_id=1, source_target_pairs={{0,3},{1,0},{2,1},{3,2},{4,7},{5,4},{6,5},{7,6},{8,11},{9,8},{10,9... | collective-permute-start | bytes 3080 | tf_op jit(solution)/shard_map/ppermute | solution.py:20
  (8 other events, 49.8 us)

commit v9 on v8

--- a/solution.py
+++ b/solution.py
@@ -27,12 +27,25 @@
     return jnp.take(stacked, (me - jnp.arange(tp_count)) % tp_count, axis=0)
 
 
+def exchange_tp(blocks, tp_count):
+    if tp_count != 4:
+        return [None] + [shift_tp(blocks[s], s, tp_count) for s in range(1, tp_count)]
+    half = blocks[2].shape[0] // 2
+    rows = blocks[1].shape[0]
+    up = shift_tp(jnp.concatenate([blocks[1], blocks[2][:half]], axis=0), 1, tp_count)
+    down = shift_tp(jnp.concatenate([blocks[3], blocks[2][half:]], axis=0), 3, tp_count)
+    far_up = shift_tp(up[rows:], 1, tp_count)
+    far_down = shift_tp(down[rows:], 3, tp_count)
+    return [None, up[:rows], jnp.concatenate([far_up, far_down], axis=0), down[:rows]]
+
+
 def gather_tp(value, tp_count):
     me = lax.axis_index("tp")
     rows, cols = value.shape
+    came = exchange_tp([None] + [value] * (tp_count - 1), tp_count)
     whole = jnp.zeros((rows, tp_count * cols), value.dtype)
     for s in range(tp_count):
-        part = value if s == 0 else shift_tp(value, s, tp_count)
+        part = value if s == 0 else came[s]
         whole = lax.dynamic_update_slice_in_dim(whole, part, ((me - s) % tp_count) * cols, axis=1)
     return whole
 
@@ -48,13 +61,13 @@
 def down_scatter_sum_tp(activ, w_down, tp_count):
     me = lax.axis_index("tp")
     width = w_down.shape[1] // tp_count
-    terms = []
-    for s in list(range(1, tp_count)) + [0]:
+    blocks = {}
+    for s in list(range(tp_count - 1, 0, -1)) + [0]:
         w_block = lax.dynamic_slice_in_dim(w_down, ((me + s) % tp_count) * width, width, axis=1)
-        block = jnp.dot(activ, w_block, preferred_element_type=jnp.float32).astype(jnp.bfloat16)
-        terms.append(block if s == 0 else shift_tp(block, s, tp_count))
-    total = terms[0].astype(jnp.float32)
-    for term in terms[1:]:
+        blocks[s] = jnp.dot(activ, w_block, preferred_element_type=jnp.float32).astype(jnp.bfloat16)
+    came = exchange_tp([blocks[s] for s in range(tp_count)], tp_count)
+    total = blocks[0].astype(jnp.float32)
+    for term in came[1:]:
         total = total + term.astype(jnp.float32)
     return total.astype(jnp.bfloat16)
 

time: 160 us -> 189 us (1.18)
  waiting for transfers between devices: 45.4 us -> 60.9 us
  local copies, waits for them, and re-layouts: 10.9 us -> 20.7 us
  other arithmetic: 7.24 us -> 13 us
    ppermute x15 -> x19, waiting for transfers between devices: 22.1 us -> 29.8 us  [shift_tp(): lax.ppermute(value, 'tp', [(j, (j + step) % tp_count) for j in range(tp_c...]
    all_to_all x2, starting transfers between devices: 17.6 us -> 10.6 us  [shards(): lax.all_to_all(summed, 'req', split_axis=0, concat_axis=0, tiled=True)]
    all_to_all x2, waiting for transfers between devices: 10.7 us -> 16.5 us  [shards(): lax.all_to_all(outgoing, 'req', split_axis=0, concat_axis=0, tiled=True)]
    slice x1 -> x13, local copies, waits for them, and re-layouts: 0.21 us -> 5.64 us  [the longest x4 2.62 us: exchange_tp(): far_down = shift_tp(down[rows:], 3, tp_count)]
    ppermute x15 -> x19, starting transfers between devices: 20.9 us -> 25.3 us  [shift_tp(): lax.ppermute(value, 'tp', [(j, (j + step) % tp_count) for j in range(tp_c...]
    dot_general x8, matrix products: 16.7 us -> 13.8 us  [down_scatter_sum_tp(): jnp.dot(activ, w_block, preferred_element_type=jnp.float32)]
    concatenate x0 -> x6, other arithmetic: none -> 2.23 us  [the longest x4 1.22 us: exchange_tp(): jnp.concatenate([blocks[3], blocks[2][half:]], axis=0)]
    all_to_all x2, waiting for transfers between devices: 12.7 us -> 14.6 us  [shards(): lax.all_to_all(summed, 'req', split_axis=0, concat_axis=0, tiled=True)]
  transfers between devices with their start and end apart: 19 -> 23, of which waited for: 8 -> 10; matrix products, arithmetic and copies ran while one was open for 33% -> 34% of each run, Pallas kernels for 0% -> 0%
where the time goes in v9:
time: 189 us; the launch traced here: 188 us
  waiting for transfers between devices  60.9 us (32%)
  starting transfers between devices  50.5 us (27%)
  matrix products  41.5 us (22%)
  local copies, waits for them, and re-layouts  20.7 us (11%)
  other arithmetic  13 us (7%)
    ppermute x19, waiting for transfers between devices, shift_tp(): lax.ppermute(value, 'tp', [(j, (j + step) % tp_count) for j in range(tp_c...  29.8 us
    ppermute x19, starting transfers between devices, shift_tp(): lax.ppermute(value, 'tp', [(j, (j + step) % tp_count) for j in range(tp_c...  25.3 us
    all_to_all x2, waiting for transfers between devices, shards(): lax.all_to_all(outgoing, 'req', split_axis=0, concat_axis=0, tiled=True)  16.5 us
    all_to_all x2, waiting for transfers between devices, shards(): lax.all_to_all(summed, 'req', split_axis=0, concat_axis=0, tiled=True)  14.6 us
    all_to_all x2, starting transfers between devices, shards(): lax.all_to_all(outgoing, 'req', split_axis=0, concat_axis=0, tiled=True)  14.6 us
    dot_general x8, matrix products, down_scatter_sum_tp(): jnp.dot(activ, w_block, preferred_element_type=jnp.float32)  13.8 us
    dot_general x2, matrix products, shards(): jnp.dot(flat_rows, gate_weight[0], preferred_element_type=jnp.float32)  12.6 us
    all_to_all x2, starting transfers between devices, shards(): lax.all_to_all(summed, 'req', split_axis=0, concat_axis=0, tiled=True)  10.6 us
  transfers between devices with their start and end apart: 23, of which 10 were waited for; matrix products, arithmetic and copies ran while one was open for 34% of the time, Pallas kernels for 0%

profile of v9, /device:TPU:1, one launch (start us, length us, event | category | flops | bytes accessed | tf_op | source)
XLA Modules:
  0.0 188.0 jit_solution(3550673081236689486)
XLA Ops:
  11.1 9.0 %all-to-all-start = ((bf16[32,16,512]{2,1,0:T(8,128)(2,1)}), bf16[32,16,512]{2,1,0:T(8,128)(2,1)S(1)}, u32[]{:S(2)}, u32[]{:S(2)}) async-start(bf16[32,16,512]{2,1,0:T(8,128)(2,1)} %bitcast.4), calls=%async_computation | async-start | bytes 1048576 | tf_op jit(solution)/shard_map/all_to_all | solution.py:109
  25.8 6.0 %all-to-all-done = bf16[32,16,512]{2,1,0:T(8,128)(2,1)S(1)} async-done(((bf16[32,16,512]{2,1,0:T(8,128)(2,1)}), bf16[32,16,512]{2,1,0:T(8,128)(2,1)S(1)}, u32[]{:S(2)}, u32[]{:S(2)}) %all-to-all-start) | async-done | bytes 524320 | tf_op jit(solution)/shard_map/all_to_all | solution.py:109
  39.0 13.5 %collective-permute-done = bf16[768,512]{1,0:T(8,128)(2,1)S(1)} collective-permute-done((bf16[768,512]{1,0:T(8,128)(2,1)S(1)}, bf16[768,512]{1,0:T(8,128)(2,1)S(1)}, u32[]{:S(2)}, u32[]{:S(2)}) %collective-permute-start) | collective-permute-done | bytes 786464 | tf_op jit(solution)/shard_map/ppermute | solution.py:20
  53.7 2.6 %collective-permute-start.3 = (bf16[256,512]{1,0:T(8,128)(2,1)S(1)}, bf16[256,512]{1,0:T(8,128)(2,1)S(1)}, u32[]{:S(2)}, u32[]{:S(2)}) collective-permute-start(bf16[256,512]{1,0:T(8,128)(2,1)S(1)} %slice.163), channel_id=1, source_target_pairs={{0,3},{1,0},{2,1},{3,2},{4,7},{5,4},{6,5},{7,6},{8,11},{9,8},{10,9... | collective-permute-start | bytes 786440 | tf_op jit(solution)/shard_map/ppermute | solution.py:20
  56.3 3.5 %convolution_convert_fusion = bf16[512,2048]{1,0:T(8,128)(2,1)} fusion(bf16[256,2048]{1,0:T(8,128)(2,1)} %slice_dynamic-update-slice_fusion.2, f32[2048]{0:T(1024)S(1)} %copy-done.11, f32[256]{0:T(256)S(1)} %add_rsqrt_fusion.2, s32[256]{0:T(256)S(1)} %bitcast.112, s32[256]{0:T(256)S(1)} %bitcast.110, pred[256]{0:T(512)(128)(4,1)S(1)} %copy-done.10, ...), kind=kOutput, calls=%fused_computation.17 | convolution fusion | flops 540672000 | bytes 3157504 | tf_op jit(solution)/shard_map/dot_general | solution.py:105
  59.7 5.6 %all-to-all-start.2 = ((bf16[32,16,2048]{2,1,0:T(8,128)(2,1)}), bf16[32,16,2048]{2,1,0:T(8,128)(2,1)}, u32[]{:S(2)}, u32[]{:S(2)}) async-start(bf16[32,16,2048]{2,1,0:T(8,128)(2,1)} %bitcast.102), calls=%async_computation.2 | async-start | bytes 4194304 | tf_op jit(solution)/shard_map/all_to_all | solution.py:109
  67.3 6.1 %fusion.6 = f32[512,1408]{1,0:T(8,128)S(1)} fusion(bf16[1,2048,1408]{2,1,0:T(8,128)(2,1)} %param.13, bf16[512,2048]{1,0:T(8,128)(2,1)S(1)} %slice_dynamic-update-slice_fusion, f32[2048]{0:T(1024)S(1)} %copy-done.12, f32[512]{0:T(512)S(1)} %add_rsqrt_fusion), kind=kOutput, calls=%fused_computation.9 | convolution fusion | flops 2956984320 | bytes 10758144 | tf_op jit(solution)/shard_map/dot_general | solution.py:115
  73.4 3.6 %multiply_convert_fusion = bf16[512,1408]{1,0:T(8,128)(2,1)S(1)} fusion(f32[512,1408]{1,0:T(8,128)S(1)} %fusion.6, bf16[1,2048,1408]{2,1,0:T(8,128)(2,1)S(1)} %bitcast.117, bf16[512,2048]{1,0:T(8,128)(2,1)S(1)} %slice_dynamic-update-slice_fusion, f32[2048]{0:T(1024)S(1)} %copy-done.12, f32[512]{0:T(512)S(1)} %add_rsqrt_fusion), kind=kOutput, calls=%fused_computation.19 | convolution fusion | flops 2961309696 | bytes 12199936 | tf_op jit(solution)/shard_map/dot_general | solution.py:116
  80.3 3.0 %collective-permute-start.6 = (bf16[768,512]{1,0:T(8,128)(2,1)S(1)}, bf16[768,512]{1,0:T(8,128)(2,1)}, u32[]{:S(2)}, u32[]{:S(2)}) collective-permute-start(bf16[768,512]{1,0:T(8,128)(2,1)S(1)} %pad_maximum_fusion.3), channel_id=1, source_target_pairs={{0,3},{1,0},{2,1},{3,2},{4,7},{5,4},{6,5},{7,6},{8,11},{9,8},{10,9... | collective-permute-start | bytes 2359304 | tf_op jit(solution)/shard_map/ppermute | solution.py:20
  83.2 10.5 %all-to-all-done.2 = bf16[32,16,2048]{2,1,0:T(8,128)(2,1)} async-done(((bf16[32,16,2048]{2,1,0:T(8,128)(2,1)}), bf16[32,16,2048]{2,1,0:T(8,128)(2,1)}, u32[]{:S(2)}, u32[]{:S(2)}) %all-to-all-start.2) | async-done | bytes 2097184 | tf_op jit(solution)/shard_map/all_to_all | solution.py:109
  93.7 6.5 %fusion.4 = f32[512,1408]{1,0:T(8,128)S(1)} fusion(bf16[512,2048]{1,0:T(8,128)(2,1)} %bitcast.19, bf16[1,2048,1408]{2,1,0:T(8,128)(2,1)} %param.13), kind=kOutput, calls=%fused_computation.7 | convolution fusion | flops 2952790016 | bytes 10747904 | tf_op jit(solution)/shard_map/dot_general | solution.py:115
  100.3 6.8 %fusion.14 = bf16[512,1408]{1,0:T(8,128)(2,1)S(1)} fusion(bf16[512,2048]{1,0:T(8,128)(2,1)} %bitcast.19, bf16[1,2048,1408]{2,1,0:T(8,128)(2,1)} %param.14, f32[512,1408]{1,0:T(8,128)S(1)} %fusion.4), kind=kOutput, calls=%fused_computation.18 | convolution fusion | flops 2957115392 | bytes 12189696 | tf_op jit(solution)/shard_map/dot_general | solution.py:116
  111.2 2.7 %collective-permute-start.14 = (bf16[768,512]{1,0:T(8,128)(2,1)S(1)}, bf16[768,512]{1,0:T(8,128)(2,1)}, u32[]{:S(2)}, u32[]{:S(2)}) collective-permute-start(bf16[768,512]{1,0:T(8,128)(2,1)S(1)} %pad_maximum_fusion.5), channel_id=1, source_target_pairs={{0,3},{1,0},{2,1},{3,2},{4,7},{5,4},{6,5},{7,6},{8,11},{9,8},{10,9... | collective-permute-start | bytes 2359304 | tf_op jit(solution)/shard_map/ppermute | solution.py:20
  115.1 2.7 %collective-permute-start.7 = (bf16[256,512]{1,0:T(8,128)(2,1)S(1)}, bf16[256,512]{1,0:T(8,128)(2,1)}, u32[]{:S(2)}, u32[]{:S(2)}) collective-permute-start(bf16[256,512]{1,0:T(8,128)(2,1)S(1)} %slice.169), channel_id=1, source_target_pairs={{0,3},{1,0},{2,1},{3,2},{4,7},{5,4},{6,5},{7,6},{8,11},{9,8},{10,9... | collective-permute-start | bytes 786440 | tf_op jit(solution)/shard_map/ppermute | solution.py:20
  117.9 13.0 %collective-permute-done.12 = bf16[768,512]{1,0:T(8,128)(2,1)} collective-permute-done((bf16[768,512]{1,0:T(8,128)(2,1)}, bf16[768,512]{1,0:T(8,128)(2,1)}, u32[]{:S(2)}, u32[]{:S(2)}) %collective-permute-start.12) | collective-permute-done | bytes 786464 | tf_op jit(solution)/shard_map/ppermute | solution.py:20
  132.9 2.7 %collective-permute-start.15 = (bf16[256,512]{1,0:T(8,128)(2,1)S(1)}, bf16[256,512]{1,0:T(8,128)(2,1)S(1)}, u32[]{:S(2)}, u32[]{:S(2)}) collective-permute-start(bf16[256,512]{1,0:T(8,128)(2,1)S(1)} %slice.179), channel_id=1, source_target_pairs={{0,3},{1,0},{2,1},{3,2},{4,7},{5,4},{6,5},{7,6},{8,11},{9,8},{10,9... | collective-permute-start | bytes 786440 | tf_op jit(solution)/shard_map/ppermute | solution.py:20
  136.5 3.9 %add_convert_fusion.1 = bf16[512,512]{1,0:T(8,128)(2,1)} fusion(bf16[768,512]{1,0:T(8,128)(2,1)} %collective-permute-done.6, bf16[768,512]{1,0:T(8,128)(2,1)S(1)} %collective-permute-done.4, bf16[256,512]{1,0:T(8,128)(2,1)} %collective-permute-done.7, bf16[256,512]{1,0:T(8,128)(2,1)} %collective-permute-done.5, bf16[512,1408]{1,0:T(8,128)(2,1)} %copy-done.13, ...), kind=kOutput, calls=%fused_computation.65 | convolution fusion | flops 741343232 | bytes 4980740 | tf_op jit(solution)/shard_map/dot_general | solution.py:67
  140.4 6.7 %all-to-all-start.1 = ((bf16[32,16,512]{2,1,0:T(8,128)(2,1)}), bf16[32,16,512]{2,1,0:T(8,128)(2,1)S(1)}, u32[]{:S(2)}, u32[]{:S(2)}) async-start(bf16[32,16,512]{2,1,0:T(8,128)(2,1)} %bitcast.14), calls=%async_computation.1 | async-start | bytes 1048576 | tf_op jit(solution)/shard_map/all_to_all | solution.py:120
  148.8 4.0 %add_convert_fusion = bf16[512,512]{1,0:T(8,128)(2,1)} fusion(bf16[768,512]{1,0:T(8,128)(2,1)} %collective-permute-done.14, bf16[768,512]{1,0:T(8,128)(2,1)} %collective-permute-done.12, bf16[256,512]{1,0:T(8,128)(2,1)S(1)} %collective-permute-done.15, bf16[256,512]{1,0:T(8,128)(2,1)S(1)} %collective-permute-done.13, bf16[512,1408]{1,0:T(8,128)(2,1)} %copy-done.14, ...), kind=kOutput, calls=%fused_computation.61 | convolution fusion | flops 741343232 | bytes 4980740 | tf_op jit(solution)/shard_map/dot_general | solution.py:67
  152.8 6.1 %all-to-all-done.1 = bf16[32,16,512]{2,1,0:T(8,128)(2,1)S(1)} async-done(((bf16[32,16,512]{2,1,0:T(8,128)(2,1)}), bf16[32,16,512]{2,1,0:T(8,128)(2,1)S(1)}, u32[]{:S(2)}, u32[]{:S(2)}) %all-to-all-start.1) | async-done | bytes 524320 | tf_op jit(solution)/shard_map/all_to_all | solution.py:120
  158.9 3.9 %all-to-all-start.3 = ((bf16[32,16,512]{2,1,0:T(8,128)(2,1)}), bf16[32,16,512]{2,1,0:T(8,128)(2,1)S(1)}, u32[]{:S(2)}, u32[]{:S(2)}) async-start(bf16[32,16,512]{2,1,0:T(8,128)(2,1)} %bitcast.20), calls=%async_computation.3 | async-start | bytes 1048576 | tf_op jit(solution)/shard_map/all_to_all | solution.py:120
  165.5 8.5 %all-to-all-done.3 = bf16[32,16,512]{2,1,0:T(8,128)(2,1)S(1)} async-done(((bf16[32,16,512]{2,1,0:T(8,128)(2,1)}), bf16[32,16,512]{2,1,0:T(8,128)(2,1)S(1)}, u32[]{:S(2)}, u32[]{:S(2)}) %all-to-all-start.3) | async-done | bytes 524320 | tf_op jit(solution)/shard_map/all_to_all | solution.py:120
  176.7 4.0 %select_reduce_fusion.1 = (f32[256,512]{1,0:T(8,128)S(1)}, f32[256,512]{1,0:T(8,128)S(1)}) fusion(f32[256,2,512]{2,1,0:T(2,128)S(1)} %reshape.397, pred[256,2]{1,0:T(8,128)(4,1)} %copy.35, f32[256,2]{1,0:T(8,128)S(1)} %copy.37, f32[256,2,512]{2,1,0:T(2,128)S(1)} %reshape.398, pred[256,2]{1,0:T(8,128)(4,1)} %copy.38), kind=kLoop, calls=%fused_computation.64 | loop fusion | flops 1310720 | bytes 3148800 | tf_op jit(solution)/shard_map/reduce_sum | solution.py:127
  181.0 3.1 %collective-permute-start.17 = (f32[256]{0:T(256)S(1)}, f32[256]{0:T(256)S(1)}, u32[]{:S(2)}, u32[]{:S(2)}) collective-permute-start(f32[256]{0:T(256)S(1)} %get-tuple-element.8), channel_id=1, source_target_pairs={{0,2},{1,3},{2,0},{3,1},{4,6},{5,7},{6,4},{7,5},{8,10},{9,11},{10,... | collective-permute-start | bytes 3080 | tf_op jit(solution)/shard_map/ppermute | solution.py:20
  (149 shorter events, 48.5 us)
Async XLA Ops:
  2.7 21.6 %collective-permute-start.8 = (bf16[384,512]{1,0:T(8,128)(2,1)S(1)}, bf16[384,512]{1,0:T(8,128)(2,1)S(1)}, u32[]{:S(2)}, u32[]{:S(2)}) collective-permute-start(bf16[384,512]{1,0:T(8,128)(2,1)S(1)} %get-tuple-element.24), channel_id=1, source_target_pairs={{0,1},{1,2},{2,3},{3,0},{4,5},{5,6},{6,7},{7,4},{8,9},{9,10},{10,1... | collective-permute-start | bytes 1179656 | tf_op jit(solution)/shard_map/ppermute | solution.py:20
  4.9 17.2 %collective-permute-start.10 = (bf16[384,512]{1,0:T(8,128)(2,1)S(1)}, bf16[384,512]{1,0:T(8,128)(2,1)S(1)}, u32[]{:S(2)}, u32[]{:S(2)}) collective-permute-start(bf16[384,512]{1,0:T(8,128)(2,1)S(1)} %get-tuple-element.23), channel_id=1, source_target_pairs={{0,3},{1,0},{2,1},{3,2},{4,7},{5,4},{6,5},{7,6},{8,11},{9,8},{10,9... | collective-permute-start | bytes 1179656 | tf_op jit(solution)/shard_map/ppermute | solution.py:20
  11.1 20.6 %all-to-all-start = ((bf16[32,16,512]{2,1,0:T(8,128)(2,1)}), bf16[32,16,512]{2,1,0:T(8,128)(2,1)S(1)}, u32[]{:S(2)}, u32[]{:S(2)}) async-start(bf16[32,16,512]{2,1,0:T(8,128)(2,1)} %bitcast.4), calls=%async_computation | async-start | bytes 1048576 | tf_op jit(solution)/shard_map/all_to_all | solution.py:109
  22.8 12.3 %collective-permute-start.11 = (bf16[128,512]{1,0:T(8,128)(2,1)}, bf16[128,512]{1,0:T(8,128)(2,1)S(1)}, u32[]{:S(2)}, u32[]{:S(2)}) collective-permute-start(bf16[128,512]{1,0:T(8,128)(2,1)} %slice.173), channel_id=1, source_target_pairs={{0,3},{1,0},{2,1},{3,2},{4,7},{5,4},{6,5},{7,6},{8,11},{9,8},{10,9... | collective-permute-start | bytes 393224 | tf_op jit(solution)/shard_map/ppermute | solution.py:20
  25.0 10.1 %collective-permute-start.9 = (bf16[128,512]{1,0:T(8,128)(2,1)}, bf16[128,512]{1,0:T(8,128)(2,1)}, u32[]{:S(2)}, u32[]{:S(2)}) collective-permute-start(bf16[128,512]{1,0:T(8,128)(2,1)} %slice.172), channel_id=1, source_target_pairs={{0,1},{1,2},{2,3},{3,0},{4,5},{5,6},{6,7},{7,4},{8,9},{9,10},{10,1... | collective-permute-start | bytes 393224 | tf_op jit(solution)/shard_map/ppermute | solution.py:20
  31.9 20.6 %collective-permute-start = (bf16[768,512]{1,0:T(8,128)(2,1)S(1)}, bf16[768,512]{1,0:T(8,128)(2,1)S(1)}, u32[]{:S(2)}, u32[]{:S(2)}) collective-permute-start(bf16[768,512]{1,0:T(8,128)(2,1)S(1)} %get-tuple-element.20), channel_id=1, source_target_pairs={{0,1},{1,2},{2,3},{3,0},{4,5},{5,6},{6,7},{7,4},{8,9},{9,10},{10,1... | collective-permute-start | bytes 2359304 | tf_op jit(solution)/shard_map/ppermute | solution.py:20
  32.1 20.5 %collective-permute-start.2 = (bf16[768,512]{1,0:T(8,128)(2,1)S(1)}, bf16[768,512]{1,0:T(8,128)(2,1)S(1)}, u32[]{:S(2)}, u32[]{:S(2)}) collective-permute-start(bf16[768,512]{1,0:T(8,128)(2,1)S(1)} %get-tuple-element.19), channel_id=1, source_target_pairs={{0,3},{1,0},{2,1},{3,2},{4,7},{5,4},{6,5},{7,6},{8,11},{9,8},{10,9... | collective-permute-start | bytes 2359304 | tf_op jit(solution)/shard_map/ppermute | solution.py:20
  34.9 21.4 %copy-start.8 = (s32[256,1]{0,1:T(1,128)S(1)}, s32[256,1]{0,1:T(1,128)}, u32[]{:S(2)}) copy-start(s32[256,1]{0,1:T(1,128)} %copy-done.7) | copy-start | bytes 3076
  52.5 14.0 %collective-permute-start.1 = (bf16[256,512]{1,0:T(8,128)(2,1)S(1)}, bf16[256,512]{1,0:T(8,128)(2,1)S(1)}, u32[]{:S(2)}, u32[]{:S(2)}) collective-permute-start(bf16[256,512]{1,0:T(8,128)(2,1)S(1)} %slice.161), channel_id=1, source_target_pairs={{0,1},{1,2},{2,3},{3,0},{4,5},{5,6},{6,7},{7,4},{8,9},{9,10},{10,1... | collective-permute-start | bytes 786440 | tf_op jit(solution)/shard_map/ppermute | solution.py:20
  53.7 12.9 %collective-permute-start.3 = (bf16[256,512]{1,0:T(8,128)(2,1)S(1)}, bf16[256,512]{1,0:T(8,128)(2,1)S(1)}, u32[]{:S(2)}, u32[]{:S(2)}) collective-permute-start(bf16[256,512]{1,0:T(8,128)(2,1)S(1)} %slice.163), channel_id=1, source_target_pairs={{0,3},{1,0},{2,1},{3,2},{4,7},{5,4},{6,5},{7,6},{8,11},{9,8},{10,9... | collective-permute-start | bytes 786440 | tf_op jit(solution)/shard_map/ppermute | solution.py:20
  59.7 34.0 %all-to-all-start.2 = ((bf16[32,16,2048]{2,1,0:T(8,128)(2,1)}), bf16[32,16,2048]{2,1,0:T(8,128)(2,1)}, u32[]{:S(2)}, u32[]{:S(2)}) async-start(bf16[32,16,2048]{2,1,0:T(8,128)(2,1)} %bitcast.102), calls=%async_computation.2 | async-start | bytes 4194304 | tf_op jit(solution)/shard_map/all_to_all | solution.py:109
  79.1 34.9 %collective-permute-start.4 = (bf16[768,512]{1,0:T(8,128)(2,1)S(1)}, bf16[768,512]{1,0:T(8,128)(2,1)S(1)}, u32[]{:S(2)}, u32[]{:S(2)}) collective-permute-start(bf16[768,512]{1,0:T(8,128)(2,1)S(1)} %pad_maximum_fusion.2), channel_id=1, source_target_pairs={{0,1},{1,2},{2,3},{3,0},{4,5},{5,6},{6,7},{7,4},{8,9},{9,10},{10,1... | collective-permute-start | bytes 2359304 | tf_op jit(solution)/shard_map/ppermute | solution.py:20
  80.3 33.8 %collective-permute-start.6 = (bf16[768,512]{1,0:T(8,128)(2,1)S(1)}, bf16[768,512]{1,0:T(8,128)(2,1)}, u32[]{:S(2)}, u32[]{:S(2)}) collective-permute-start(bf16[768,512]{1,0:T(8,128)(2,1)S(1)} %pad_maximum_fusion.3), channel_id=1, source_target_pairs={{0,3},{1,0},{2,1},{3,2},{4,7},{5,4},{6,5},{7,6},{8,11},{9,8},{10,9... | collective-permute-start | bytes 2359304 | tf_op jit(solution)/shard_map/ppermute | solution.py:20
  111.2 19.7 %collective-permute-start.12 = (bf16[768,512]{1,0:T(8,128)(2,1)}, bf16[768,512]{1,0:T(8,128)(2,1)}, u32[]{:S(2)}, u32[]{:S(2)}) collective-permute-start(bf16[768,512]{1,0:T(8,128)(2,1)} %pad_maximum_fusion.4), channel_id=1, source_target_pairs={{0,1},{1,2},{2,3},{3,0},{4,5},{5,6},{6,7},{7,4},{8,9},{9,10},{10,1... | collective-permute-start | bytes 2359304 | tf_op jit(solution)/shard_map/ppermute | solution.py:20
  111.2 20.7 %collective-permute-start.14 = (bf16[768,512]{1,0:T(8,128)(2,1)S(1)}, bf16[768,512]{1,0:T(8,128)(2,1)}, u32[]{:S(2)}, u32[]{:S(2)}) collective-permute-start(bf16[768,512]{1,0:T(8,128)(2,1)S(1)} %pad_maximum_fusion.5), channel_id=1, source_target_pairs={{0,3},{1,0},{2,1},{3,2},{4,7},{5,4},{6,5},{7,6},{8,11},{9,8},{10,9... | collective-permute-start | bytes 2359304 | tf_op jit(solution)/shard_map/ppermute | solution.py:20
  114.0 22.5 %collective-permute-start.5 = (bf16[256,512]{1,0:T(8,128)(2,1)S(1)}, bf16[256,512]{1,0:T(8,128)(2,1)}, u32[]{:S(2)}, u32[]{:S(2)}) collective-permute-start(bf16[256,512]{1,0:T(8,128)(2,1)S(1)} %slice.167), channel_id=1, source_target_pairs={{0,1},{1,2},{2,3},{3,0},{4,5},{5,6},{6,7},{7,4},{8,9},{9,10},{10,1... | collective-permute-start | bytes 786440 | tf_op jit(solution)/shard_map/ppermute | solution.py:20
  115.1 21.4 %collective-permute-start.7 = (bf16[256,512]{1,0:T(8,128)(2,1)S(1)}, bf16[256,512]{1,0:T(8,128)(2,1)}, u32[]{:S(2)}, u32[]{:S(2)}) collective-permute-start(bf16[256,512]{1,0:T(8,128)(2,1)S(1)} %slice.169), channel_id=1, source_target_pairs={{0,3},{1,0},{2,1},{3,2},{4,7},{5,4},{6,5},{7,6},{8,11},{9,8},{10,9... | collective-permute-start | bytes 786440 | tf_op jit(solution)/shard_map/ppermute | solution.py:20
  131.9 17.0 %collective-permute-start.13 = (bf16[256,512]{1,0:T(8,128)(2,1)S(1)}, bf16[256,512]{1,0:T(8,128)(2,1)S(1)}, u32[]{:S(2)}, u32[]{:S(2)}) collective-permute-start(bf16[256,512]{1,0:T(8,128)(2,1)S(1)} %slice.177), channel_id=1, source_target_pairs={{0,1},{1,2},{2,3},{3,0},{4,5},{5,6},{6,7},{7,4},{8,9},{9,10},{10,1... | collective-permute-start | bytes 786440 | tf_op jit(solution)/shard_map/ppermute | solution.py:20
  132.9 15.9 %collective-permute-start.15 = (bf16[256,512]{1,0:T(8,128)(2,1)S(1)}, bf16[256,512]{1,0:T(8,128)(2,1)S(1)}, u32[]{:S(2)}, u32[]{:S(2)}) collective-permute-start(bf16[256,512]{1,0:T(8,128)(2,1)S(1)} %slice.179), channel_id=1, source_target_pairs={{0,3},{1,0},{2,1},{3,2},{4,7},{5,4},{6,5},{7,6},{8,11},{9,8},{10,9... | collective-permute-start | bytes 786440 | tf_op jit(solution)/shard_map/ppermute | solution.py:20
  140.4 18.4 %all-to-all-start.1 = ((bf16[32,16,512]{2,1,0:T(8,128)(2,1)}), bf16[32,16,512]{2,1,0:T(8,128)(2,1)S(1)}, u32[]{:S(2)}, u32[]{:S(2)}) async-start(bf16[32,16,512]{2,1,0:T(8,128)(2,1)} %bitcast.14), calls=%async_computation.1 | async-start | bytes 1048576 | tf_op jit(solution)/shard_map/all_to_all | solution.py:120
  158.9 15.2 %all-to-all-start.3 = ((bf16[32,16,512]{2,1,0:T(8,128)(2,1)}), bf16[32,16,512]{2,1,0:T(8,128)(2,1)S(1)}, u32[]{:S(2)}, u32[]{:S(2)}) async-start(bf16[32,16,512]{2,1,0:T(8,128)(2,1)} %bitcast.20), calls=%async_computation.3 | async-start | bytes 1048576 | tf_op jit(solution)/shard_map/all_to_all | solution.py:120
  180.9 3.7 %collective-permute-start.16 = (f32[256]{0:T(256)S(1)}, f32[256]{0:T(256)S(1)}, u32[]{:S(2)}, u32[]{:S(2)}) collective-permute-start(f32[256]{0:T(256)S(1)} %get-tuple-element.8), channel_id=1, source_target_pairs={{0,1},{1,2},{2,3},{3,0},{4,5},{5,6},{6,7},{7,4},{8,9},{9,10},{10,1... | collective-permute-start | bytes 3080 | tf_op jit(solution)/shard_map/ppermute | solution.py:20
  181.0 4.1 %collective-permute-start.17 = (f32[256]{0:T(256)S(1)}, f32[256]{0:T(256)S(1)}, u32[]{:S(2)}, u32[]{:S(2)}) collective-permute-start(f32[256]{0:T(256)S(1)} %get-tuple-element.8), channel_id=1, source_target_pairs={{0,2},{1,3},{2,0},{3,1},{4,6},{5,7},{6,4},{7,5},{8,10},{9,11},{10,... | collective-permute-start | bytes 3080 | tf_op jit(solution)/shard_map/ppermute | solution.py:20
  184.1 2.4 %collective-permute-start.18 = (f32[256]{0:T(256)S(1)}, f32[256]{0:T(256)S(1)}, u32[]{:S(2)}, u32[]{:S(2)}) collective-permute-start(f32[256]{0:T(256)S(1)} %get-tuple-element.8), channel_id=1, source_target_pairs={{0,3},{1,0},{2,1},{3,2},{4,7},{5,4},{6,5},{7,6},{8,11},{9,8},{10,9... | collective-permute-start | bytes 3080 | tf_op jit(solution)/shard_map/ppermute | solution.py:20
  (20 other events, 175.8 us)

commit v10 on v8

--- a/solution.py
+++ b/solution.py
@@ -6,6 +6,7 @@
 E = 8
 CAP = 128
 CHUNKS = 2
+RELAY_CHUNKS = ()
 
 
 epsilon = 1e-05
@@ -87,7 +88,7 @@
         for k in range(top):
             hit = (slot_ids[:, None] == chunk_pairs[None, :, k]) & (owner_pairs[None, :, k] == c)
             dispatch = dispatch | hit
-        relay = c == 0
+        relay = c in RELAY_CHUNKS
         source = hidden if relay else normed_in
         outgoing = jnp.dot(
             dispatch.astype(jnp.bfloat16), source, preferred_element_type=jnp.float32

time: 160 us -> 168 us (1.050)
  waiting for transfers between devices: 45.4 us -> 60.3 us
  starting transfers between devices: 52.2 us -> 43.9 us
  matrix products: 42.7 us -> 45.6 us
  local copies, waits for them, and re-layouts: 10.9 us -> 9.2 us
    all_to_all x2, waiting for transfers between devices: 10.7 us -> 32.4 us  [shards(): lax.all_to_all(outgoing, 'req', split_axis=0, concat_axis=0, tiled=True)]
    all_to_all x2, starting transfers between devices: 17.6 us -> 10.3 us  [shards(): lax.all_to_all(summed, 'req', split_axis=0, concat_axis=0, tiled=True)]
    all_to_all x2, waiting for transfers between devices: 12.7 us -> 9.01 us  [shards(): lax.all_to_all(summed, 'req', split_axis=0, concat_axis=0, tiled=True)]
    ppermute x15 -> x12, waiting for transfers between devices: 22.1 us -> 18.9 us  [shift_tp(): lax.ppermute(value, 'tp', [(j, (j + step) % tp_count) for j in range(tp_c...]
    ppermute x15 -> x12, starting transfers between devices: 20.9 us -> 18.9 us  [shift_tp(): lax.ppermute(value, 'tp', [(j, (j + step) % tp_count) for j in range(tp_c...]
  transfers between devices with their start and end apart: 19 -> 16, of which waited for: 8 -> 8; matrix products, arithmetic and copies ran while one was open for 33% -> 31% of each run, Pallas kernels for 0% -> 0%
where the time goes in v10:
time: 168 us; the launch traced here: 167 us
  waiting for transfers between devices  60.3 us (36%)
  matrix products  45.6 us (27%)
  starting transfers between devices  43.9 us (26%)
  local copies, waits for them, and re-layouts  9.2 us (5%)
  other arithmetic  6.75 us (4%)
    all_to_all x2, waiting for transfers between devices, shards(): lax.all_to_all(outgoing, 'req', split_axis=0, concat_axis=0, tiled=True)  32.4 us
    ppermute x12, starting transfers between devices, shift_tp(): lax.ppermute(value, 'tp', [(j, (j + step) % tp_count) for j in range(tp_c...  18.9 us
    ppermute x12, waiting for transfers between devices, shift_tp(): lax.ppermute(value, 'tp', [(j, (j + step) % tp_count) for j in range(tp_c...  18.9 us
    dot_general x8, matrix products, down_scatter_sum_tp(): jnp.dot(activ, w_block, preferred_element_type=jnp.float32)  17.3 us
    all_to_all x2, starting transfers between devices, shards(): lax.all_to_all(outgoing, 'req', split_axis=0, concat_axis=0, tiled=True)  14.7 us
    dot_general x2, matrix products, shards(): jnp.dot(flat_rows, gate_weight[0], preferred_element_type=jnp.float32)  12.4 us
    dot_general x2, matrix products, shards(): jnp.dot(flat_rows, up_weight[0], preferred_element_type=jnp.float32)  11.4 us
    all_to_all x2, starting transfers between devices, shards(): lax.all_to_all(summed, 'req', split_axis=0, concat_axis=0, tiled=True)  10.3 us
  transfers between devices with their start and end apart: 16, of which 8 were waited for; matrix products, arithmetic and copies ran while one was open for 31% of the time, Pallas kernels for 0%

profile of v10, /device:TPU:1, one launch (start us, length us, event | category | flops | bytes accessed | tf_op | source)
XLA Modules:
  0.0 167.0 jit_solution(9018383568404103739)
XLA Ops:
  0.6 2.2 %collective-permute-start = (bf16[256,512]{1,0:T(8,128)(2,1)}, bf16[256,512]{1,0:T(8,128)(2,1)S(1)}, u32[]{:S(2)}, u32[]{:S(2)}) collective-permute-start(bf16[256,512]{1,0:T(8,128)(2,1)} %param.8), channel_id=1, source_target_pairs={{0,1},{1,2},{2,3},{3,0},{4,5},{5,6},{6,7},{7,4},{8,9},{9,10},{10,1... | collective-permute-start | bytes 786440 | tf_op jit(solution)/shard_map/ppermute | solution.py:21
  2.8 2.6 %collective-permute-start.1 = (bf16[256,512]{1,0:T(8,128)(2,1)}, bf16[256,512]{1,0:T(8,128)(2,1)S(1)}, u32[]{:S(2)}, u32[]{:S(2)}) collective-permute-start(bf16[256,512]{1,0:T(8,128)(2,1)} %param.8), channel_id=1, source_target_pairs={{0,2},{1,3},{2,0},{3,1},{4,6},{5,7},{6,4},{7,5},{8,10},{9,11},{10,... | collective-permute-start | bytes 786440 | tf_op jit(solution)/shard_map/ppermute | solution.py:21
  11.4 5.6 %collective-permute-done.1 = bf16[256,512]{1,0:T(8,128)(2,1)S(1)} collective-permute-done((bf16[256,512]{1,0:T(8,128)(2,1)}, bf16[256,512]{1,0:T(8,128)(2,1)S(1)}, u32[]{:S(2)}, u32[]{:S(2)}) %collective-permute-start.1) | collective-permute-done | bytes 262176 | tf_op jit(solution)/shard_map/ppermute | solution.py:21
  17.4 2.2 %convolution_convert_fusion = bf16[512,2048]{1,0:T(8,128)(2,1)} fusion(bf16[256,2048]{1,0:T(8,128)(2,1)S(1)} %constant_dynamic-update-slice_fusion, f32[2048]{0:T(1024)S(1)} %copy-done.3, f32[256]{0:T(256)S(1)} %add_rsqrt_fusion.1, s32[256]{0:T(256)S(1)} %bitcast.111, s32[256]{0:T(256)S(1)} %bitcast.109, pred[256]{0:T(512)(128)(4,1)S(1)} %get-tuple-element.6, ...), kind=kOutput, calls=%fused_computation.13 | convolution fusion | flops 540672000 | bytes 3157504 | tf_op jit(solution)/shard_map/dot_general | solution.py:93
  19.6 9.5 %all-to-all-start.2 = ((bf16[32,16,2048]{2,1,0:T(8,128)(2,1)}), bf16[32,16,2048]{2,1,0:T(8,128)(2,1)S(1)}, u32[]{:S(2)}, u32[]{:S(2)}) async-start(bf16[32,16,2048]{2,1,0:T(8,128)(2,1)} %bitcast.103), calls=%async_computation.2 | async-start | bytes 4194304 | tf_op jit(solution)/shard_map/all_to_all | solution.py:97
  29.3 2.2 %convolution_convert_fusion.1 = bf16[512,2048]{1,0:T(8,128)(2,1)} fusion(bf16[256,2048]{1,0:T(8,128)(2,1)S(1)} %constant_dynamic-update-slice_fusion, f32[2048]{0:T(1024)S(1)} %copy-done.3, f32[256]{0:T(256)S(1)} %add_rsqrt_fusion.1, s32[256]{0:T(256)S(1)} %bitcast.112, s32[256]{0:T(256)S(1)} %bitcast.110, pred[256]{0:T(512)(128)(4,1)S(1)} %get-tuple-element.7, ...), kind=kOutput, calls=%fused_computation.14 | convolution fusion | flops 540672000 | bytes 3157504 | tf_op jit(solution)/shard_map/dot_general | solution.py:93
  31.5 25.9 %all-to-all-done.2 = bf16[32,16,2048]{2,1,0:T(8,128)(2,1)S(1)} async-done(((bf16[32,16,2048]{2,1,0:T(8,128)(2,1)}), bf16[32,16,2048]{2,1,0:T(8,128)(2,1)S(1)}, u32[]{:S(2)}, u32[]{:S(2)}) %all-to-all-start.2) | async-done | bytes 2097184 | tf_op jit(solution)/shard_map/all_to_all | solution.py:97
  57.4 5.2 %all-to-all-start = ((bf16[32,16,2048]{2,1,0:T(8,128)(2,1)}), bf16[32,16,2048]{2,1,0:T(8,128)(2,1)}, u32[]{:S(2)}, u32[]{:S(2)}) async-start(bf16[32,16,2048]{2,1,0:T(8,128)(2,1)} %bitcast.104), calls=%async_computation | async-start | bytes 4194304 | tf_op jit(solution)/shard_map/all_to_all | solution.py:97
  62.6 5.9 %fusion.4 = f32[512,1408]{1,0:T(8,128)S(1)} fusion(bf16[512,2048]{1,0:T(8,128)(2,1)S(1)} %bitcast.101, bf16[1,2048,1408]{2,1,0:T(8,128)(2,1)} %param.13), kind=kOutput, calls=%fused_computation.7 | convolution fusion | flops 2952790016 | bytes 10747904 | tf_op jit(solution)/shard_map/dot_general | solution.py:103
  68.5 6.2 %fusion.14 = bf16[512,1408]{1,0:T(8,128)(2,1)S(1)} fusion(bf16[512,2048]{1,0:T(8,128)(2,1)S(1)} %bitcast.102, bf16[1,2048,1408]{2,1,0:T(8,128)(2,1)} %param.14, f32[512,1408]{1,0:T(8,128)S(1)} %fusion.4), kind=kOutput, calls=%fused_computation.15 | convolution fusion | flops 2957115392 | bytes 12189696 | tf_op jit(solution)/shard_map/dot_general | solution.py:104
  79.2 2.1 %collective-permute-start.7 = (bf16[512,512]{1,0:T(8,128)(2,1)}, bf16[512,512]{1,0:T(8,128)(2,1)S(1)}, u32[]{:S(2)}, u32[]{:S(2)}) collective-permute-start(bf16[512,512]{1,0:T(8,128)(2,1)} %fusion.48), channel_id=1, source_target_pairs={{0,2},{1,3},{2,0},{3,1},{4,6},{5,7},{6,4},{7,5},{8,10},{9,11},{10,... | collective-permute-start | bytes 1572872 | tf_op jit(solution)/shard_map/ppermute | solution.py:21
  84.4 6.6 %all-to-all-done = bf16[32,16,2048]{2,1,0:T(8,128)(2,1)} async-done(((bf16[32,16,2048]{2,1,0:T(8,128)(2,1)}), bf16[32,16,2048]{2,1,0:T(8,128)(2,1)}, u32[]{:S(2)}, u32[]{:S(2)}) %all-to-all-start) | async-done | bytes 2097184 | tf_op jit(solution)/shard_map/all_to_all | solution.py:97
  91.0 6.5 %fusion.6 = f32[512,1408]{1,0:T(8,128)S(1)} fusion(bf16[512,2048]{1,0:T(8,128)(2,1)} %bitcast.5, bf16[1,2048,1408]{2,1,0:T(8,128)(2,1)} %param.13), kind=kOutput, calls=%fused_computation.9 | convolution fusion | flops 2952790016 | bytes 10747904 | tf_op jit(solution)/shard_map/dot_general | solution.py:103
  97.6 5.2 %fusion.17 = bf16[512,1408]{1,0:T(8,128)(2,1)S(1)} fusion(bf16[512,2048]{1,0:T(8,128)(2,1)} %bitcast.5, bf16[1,2048,1408]{2,1,0:T(8,128)(2,1)S(1)} %bitcast.117, f32[512,1408]{1,0:T(8,128)S(1)} %fusion.6), kind=kOutput, calls=%fused_computation.16 | convolution fusion | flops 2957115392 | bytes 12189696 | tf_op jit(solution)/shard_map/dot_general | solution.py:104
  107.3 2.1 %collective-permute-start.4 = (bf16[512,512]{1,0:T(8,128)(2,1)}, bf16[512,512]{1,0:T(8,128)(2,1)S(1)}, u32[]{:S(2)}, u32[]{:S(2)}) collective-permute-start(bf16[512,512]{1,0:T(8,128)(2,1)} %fusion.45), channel_id=1, source_target_pairs={{0,2},{1,3},{2,0},{3,1},{4,6},{5,7},{6,4},{7,5},{8,10},{9,11},{10,... | collective-permute-start | bytes 1572872 | tf_op jit(solution)/shard_map/ppermute | solution.py:21
  112.5 2.9 %add_convert_fusion = bf16[512,512]{1,0:T(8,128)(2,1)} fusion(bf16[512,512]{1,0:T(8,128)(2,1)} %collective-permute-done.8, bf16[512,512]{1,0:T(8,128)(2,1)S(1)} %collective-permute-done.7, bf16[512,512]{1,0:T(8,128)(2,1)S(1)} %collective-permute-done.6, bf16[512,1408]{1,0:T(8,128)(2,1)S(1)} %copy-done.6, bf16[1,1408,2048]{2,1,0:T(8,128)(2,1)S(1)} %bitcast.121, ...), kind=kOutput, calls=%fused_computation.57 | convolution fusion | flops 740556800 | bytes 4980740 | tf_op jit(solution)/shard_map/dot_general | solution.py:55
  115.4 5.2 %all-to-all-start.3 = ((bf16[32,16,512]{2,1,0:T(8,128)(2,1)}), bf16[32,16,512]{2,1,0:T(8,128)(2,1)S(1)}, u32[]{:S(2)}, u32[]{:S(2)}) async-start(bf16[32,16,512]{2,1,0:T(8,128)(2,1)} %bitcast.18), calls=%async_computation.3 | async-start | bytes 1048576 | tf_op jit(solution)/shard_map/all_to_all | solution.py:108
  121.2 9.0 %collective-permute-done.4 = bf16[512,512]{1,0:T(8,128)(2,1)S(1)} collective-permute-done((bf16[512,512]{1,0:T(8,128)(2,1)}, bf16[512,512]{1,0:T(8,128)(2,1)S(1)}, u32[]{:S(2)}, u32[]{:S(2)}) %collective-permute-start.4) | collective-permute-done | bytes 524320 | tf_op jit(solution)/shard_map/ppermute | solution.py:21
  130.1 2.4 %collective-permute-done.5 = bf16[512,512]{1,0:T(8,128)(2,1)} collective-permute-done((bf16[512,512]{1,0:T(8,128)(2,1)}, bf16[512,512]{1,0:T(8,128)(2,1)}, u32[]{:S(2)}, u32[]{:S(2)}) %collective-permute-start.5) | collective-permute-done | bytes 524320 | tf_op jit(solution)/shard_map/ppermute | solution.py:21
  132.6 3.7 %add_convert_fusion.1 = bf16[512,512]{1,0:T(8,128)(2,1)} fusion(bf16[512,512]{1,0:T(8,128)(2,1)} %collective-permute-done.5, bf16[512,512]{1,0:T(8,128)(2,1)S(1)} %collective-permute-done.4, bf16[512,512]{1,0:T(8,128)(2,1)S(1)} %collective-permute-done.3, bf16[512,1408]{1,0:T(8,128)(2,1)} %copy-done.4, bf16[1,1408,2048]{2,1,0:T(8,128)(2,1)} %param.15, ...), kind=kOutput, calls=%fused_computation.59 | convolution fusion | flops 740556800 | bytes 4980740 | tf_op jit(solution)/shard_map/dot_general | solution.py:55
  136.3 5.1 %all-to-all-start.1 = ((bf16[32,16,512]{2,1,0:T(8,128)(2,1)}), bf16[32,16,512]{2,1,0:T(8,128)(2,1)S(1)}, u32[]{:S(2)}, u32[]{:S(2)}) async-start(bf16[32,16,512]{2,1,0:T(8,128)(2,1)} %bitcast.12), calls=%async_computation.1 | async-start | bytes 1048576 | tf_op jit(solution)/shard_map/all_to_all | solution.py:108
  141.5 2.0 %gather_fusion.1 = bf16[512,512]{1,0:T(8,128)(2,1)S(1)} fusion(bf16[512,512]{1,0:T(8,128)(2,1)S(1)} %bitcast.99, s32[1024]{0:T(1024)S(1)} %pad_clamp_fusion.1), kind=kCustom, calls=%fused_computation.1 | custom fusion | bytes 1050624 | tf_op jit(solution)/shard_map/gather | solution.py:112
  144.1 9.0 %all-to-all-done.1 = bf16[32,16,512]{2,1,0:T(8,128)(2,1)S(1)} async-done(((bf16[32,16,512]{2,1,0:T(8,128)(2,1)}), bf16[32,16,512]{2,1,0:T(8,128)(2,1)S(1)}, u32[]{:S(2)}, u32[]{:S(2)}) %all-to-all-start.1) | async-done | bytes 524320 | tf_op jit(solution)/shard_map/all_to_all | solution.py:108
  155.8 3.2 %select_reduce_fusion.1 = (f32[256,512]{1,0:T(8,128)S(1)}, f32[256,512]{1,0:T(8,128)S(1)}) fusion(f32[256,2,512]{2,1,0:T(2,128)S(1)} %reshape.387, pred[256,2]{1,0:T(8,128)(4,1)S(1)} %copy.35, f32[256,2]{1,0:T(8,128)S(1)} %copy.37, f32[256,2,512]{2,1,0:T(2,128)S(1)} %reshape.388, pred[256,2]{1,0:T(8,128)(4,1)S(1)} %copy.38), kind=kLoop, calls=%fused_computation.58 | loop fusion | flops 1310720 | bytes 3148800 | tf_op jit(solution)/shard_map/reduce_sum | solution.py:115
  (94 shorter events, 33.3 us)
Async XLA Ops:
  0.6 10.7 %collective-permute-start = (bf16[256,512]{1,0:T(8,128)(2,1)}, bf16[256,512]{1,0:T(8,128)(2,1)S(1)}, u32[]{:S(2)}, u32[]{:S(2)}) collective-permute-start(bf16[256,512]{1,0:T(8,128)(2,1)} %param.8), channel_id=1, source_target_pairs={{0,1},{1,2},{2,3},{3,0},{4,5},{5,6},{6,7},{7,4},{8,9},{9,10},{10,1... | collective-permute-start | bytes 786440 | tf_op jit(solution)/shard_map/ppermute | solution.py:21
  2.8 14.2 %collective-permute-start.1 = (bf16[256,512]{1,0:T(8,128)(2,1)}, bf16[256,512]{1,0:T(8,128)(2,1)S(1)}, u32[]{:S(2)}, u32[]{:S(2)}) collective-permute-start(bf16[256,512]{1,0:T(8,128)(2,1)} %param.8), channel_id=1, source_target_pairs={{0,2},{1,3},{2,0},{3,1},{4,6},{5,7},{6,4},{7,5},{8,10},{9,11},{10,... | collective-permute-start | bytes 786440 | tf_op jit(solution)/shard_map/ppermute | solution.py:21
  5.4 11.6 %collective-permute-start.2 = (bf16[256,512]{1,0:T(8,128)(2,1)}, bf16[256,512]{1,0:T(8,128)(2,1)S(1)}, u32[]{:S(2)}, u32[]{:S(2)}) collective-permute-start(bf16[256,512]{1,0:T(8,128)(2,1)} %param.8), channel_id=1, source_target_pairs={{0,3},{1,0},{2,1},{3,2},{4,7},{5,4},{6,5},{7,6},{8,11},{9,8},{10,9... | collective-permute-start | bytes 786440 | tf_op jit(solution)/shard_map/ppermute | solution.py:21
  10.1 7.2 %copy-start.3 = (f32[2048]{0:T(1024)S(1)}, f32[2048]{0:T(1024)}, u32[]{:S(2)}) copy-start(f32[2048]{0:T(1024)} %param.11) | copy-start | bytes 24580
  19.6 37.8 %all-to-all-start.2 = ((bf16[32,16,2048]{2,1,0:T(8,128)(2,1)}), bf16[32,16,2048]{2,1,0:T(8,128)(2,1)S(1)}, u32[]{:S(2)}, u32[]{:S(2)}) async-start(bf16[32,16,2048]{2,1,0:T(8,128)(2,1)} %bitcast.103), calls=%async_computation.2 | async-start | bytes 4194304 | tf_op jit(solution)/shard_map/all_to_all | solution.py:97
  57.4 33.6 %all-to-all-start = ((bf16[32,16,2048]{2,1,0:T(8,128)(2,1)}), bf16[32,16,2048]{2,1,0:T(8,128)(2,1)}, u32[]{:S(2)}, u32[]{:S(2)}) async-start(bf16[32,16,2048]{2,1,0:T(8,128)(2,1)} %bitcast.104), calls=%async_computation | async-start | bytes 4194304 | tf_op jit(solution)/shard_map/all_to_all | solution.py:97
  62.6 12.1 %slice-start.2 = ((s8[5767168]{0:T(1024)(128)(4,1)}), s8[4194304]{0:T(1024)(128)(4,1)S(1)}, s32[]{:S(2)}) async-start(s8[5767168]{0:T(1024)(128)(4,1)} %bitcast.118), calls=%async_computation.6 | async-start | bytes 8388608
  74.7 6.6 %copy-start.5 = (bf16[512,1408]{1,0:T(8,128)(2,1)}, bf16[512,1408]{1,0:T(8,128)(2,1)S(1)}, u32[]{:S(2)}) copy-start(bf16[512,1408]{1,0:T(8,128)(2,1)S(1)} %fusion.14) | copy-start | bytes 4325380
  76.5 34.6 %collective-permute-start.6 = (bf16[512,512]{1,0:T(8,128)(2,1)}, bf16[512,512]{1,0:T(8,128)(2,1)S(1)}, u32[]{:S(2)}, u32[]{:S(2)}) collective-permute-start(bf16[512,512]{1,0:T(8,128)(2,1)} %fusion.42), channel_id=1, source_target_pairs={{0,1},{1,2},{2,3},{3,0},{4,5},{5,6},{6,7},{7,4},{8,9},{9,10},{10,1... | collective-permute-start | bytes 1572872 | tf_op jit(solution)/shard_map/ppermute | solution.py:21
  79.2 33.3 %collective-permute-start.7 = (bf16[512,512]{1,0:T(8,128)(2,1)}, bf16[512,512]{1,0:T(8,128)(2,1)S(1)}, u32[]{:S(2)}, u32[]{:S(2)}) collective-permute-start(bf16[512,512]{1,0:T(8,128)(2,1)} %fusion.48), channel_id=1, source_target_pairs={{0,2},{1,3},{2,0},{3,1},{4,6},{5,7},{6,4},{7,5},{8,10},{9,11},{10,... | collective-permute-start | bytes 1572872 | tf_op jit(solution)/shard_map/ppermute | solution.py:21
  81.3 16.2 %slice-start = ((s8[5767168]{0:T(1024)(128)(4,1)}), s8[1572864]{0:T(1024)(128)(4,1)S(1)}, s32[]{:S(2)}) async-start(s8[5767168]{0:T(1024)(128)(4,1)} %bitcast.116), calls=%async_computation.4 | async-start | bytes 3145728
  83.1 29.4 %collective-permute-start.8 = (bf16[512,512]{1,0:T(8,128)(2,1)}, bf16[512,512]{1,0:T(8,128)(2,1)}, u32[]{:S(2)}, u32[]{:S(2)}) collective-permute-start(bf16[512,512]{1,0:T(8,128)(2,1)} %fusion.54), channel_id=1, source_target_pairs={{0,3},{1,0},{2,1},{3,2},{4,7},{5,4},{6,5},{7,6},{8,11},{9,8},{10,9... | collective-permute-start | bytes 1572872 | tf_op jit(solution)/shard_map/ppermute | solution.py:21
  91.0 11.7 %slice-start.4 = ((s8[5767168]{0:T(1024)(128)(4,1)}), s8[4194304]{0:T(1024)(128)(4,1)S(1)}, s32[]{:S(2)}) async-start(s8[5767168]{0:T(1024)(128)(4,1)} %bitcast.120), calls=%async_computation.8 | async-start | bytes 8388608
  102.8 6.6 %copy-start.4 = (bf16[512,1408]{1,0:T(8,128)(2,1)}, bf16[512,1408]{1,0:T(8,128)(2,1)S(1)}, u32[]{:S(2)}) copy-start(bf16[512,1408]{1,0:T(8,128)(2,1)S(1)} %fusion.17) | copy-start | bytes 4325380
  104.6 16.6 %collective-permute-start.3 = (bf16[512,512]{1,0:T(8,128)(2,1)}, bf16[512,512]{1,0:T(8,128)(2,1)S(1)}, u32[]{:S(2)}, u32[]{:S(2)}) collective-permute-start(bf16[512,512]{1,0:T(8,128)(2,1)} %fusion.39), channel_id=1, source_target_pairs={{0,1},{1,2},{2,3},{3,0},{4,5},{5,6},{6,7},{7,4},{8,9},{9,10},{10,1... | collective-permute-start | bytes 1572872 | tf_op jit(solution)/shard_map/ppermute | solution.py:21
  107.3 22.9 %collective-permute-start.4 = (bf16[512,512]{1,0:T(8,128)(2,1)}, bf16[512,512]{1,0:T(8,128)(2,1)S(1)}, u32[]{:S(2)}, u32[]{:S(2)}) collective-permute-start(bf16[512,512]{1,0:T(8,128)(2,1)} %fusion.45), channel_id=1, source_target_pairs={{0,2},{1,3},{2,0},{3,1},{4,6},{5,7},{6,4},{7,5},{8,10},{9,11},{10,... | collective-permute-start | bytes 1572872 | tf_op jit(solution)/shard_map/ppermute | solution.py:21
  111.2 9.9 %copy-start.1 = (f32[256,2]{0,1:T(2,128)S(1)}, f32[256,2]{0,1:T(2,128)}, u32[]{:S(2)}) copy-start(f32[256,2]{0,1:T(2,128)} %param.10) | copy-start | bytes 6148
  111.2 21.4 %collective-permute-start.5 = (bf16[512,512]{1,0:T(8,128)(2,1)}, bf16[512,512]{1,0:T(8,128)(2,1)}, u32[]{:S(2)}, u32[]{:S(2)}) collective-permute-start(bf16[512,512]{1,0:T(8,128)(2,1)} %fusion.51), channel_id=1, source_target_pairs={{0,3},{1,0},{2,1},{3,2},{4,7},{5,4},{6,5},{7,6},{8,11},{9,8},{10,9... | collective-permute-start | bytes 1572872 | tf_op jit(solution)/shard_map/ppermute | solution.py:21
  115.4 20.9 %all-to-all-start.3 = ((bf16[32,16,512]{2,1,0:T(8,128)(2,1)}), bf16[32,16,512]{2,1,0:T(8,128)(2,1)S(1)}, u32[]{:S(2)}, u32[]{:S(2)}) async-start(bf16[32,16,512]{2,1,0:T(8,128)(2,1)} %bitcast.18), calls=%async_computation.3 | async-start | bytes 1048576 | tf_op jit(solution)/shard_map/all_to_all | solution.py:108
  136.3 16.8 %all-to-all-start.1 = ((bf16[32,16,512]{2,1,0:T(8,128)(2,1)}), bf16[32,16,512]{2,1,0:T(8,128)(2,1)S(1)}, u32[]{:S(2)}, u32[]{:S(2)}) async-start(bf16[32,16,512]{2,1,0:T(8,128)(2,1)} %bitcast.12), calls=%async_computation.1 | async-start | bytes 1048576 | tf_op jit(solution)/shard_map/all_to_all | solution.py:108
  155.8 10.4 %copy-start.2 = (f32[512]{0:T(512)S(1)}, f32[512]{0:T(512)}, u32[]{:S(2)}) copy-start(f32[512]{0:T(512)} %param.12) | copy-start | bytes 6148
  159.2 4.4 %collective-permute-start.9 = (f32[256]{0:T(256)S(1)}, f32[256]{0:T(256)S(1)}, u32[]{:S(2)}, u32[]{:S(2)}) collective-permute-start(f32[256]{0:T(256)S(1)} %get-tuple-element.8), channel_id=1, source_target_pairs={{0,1},{1,2},{2,3},{3,0},{4,5},{5,6},{6,7},{7,4},{8,9},{9,10},{10,1... | collective-permute-start | bytes 3080 | tf_op jit(solution)/shard_map/ppermute | solution.py:21
  160.9 3.9 %collective-permute-start.10 = (f32[256]{0:T(256)S(1)}, f32[256]{0:T(256)S(1)}, u32[]{:S(2)}, u32[]{:S(2)}) collective-permute-start(f32[256]{0:T(256)S(1)} %get-tuple-element.8), channel_id=1, source_target_pairs={{0,2},{1,3},{2,0},{3,1},{4,6},{5,7},{6,4},{7,5},{8,10},{9,11},{10,... | collective-permute-start | bytes 3080 | tf_op jit(solution)/shard_map/ppermute | solution.py:21
  162.8 2.7 %collective-permute-start.11 = (f32[256]{0:T(256)S(1)}, f32[256]{0:T(256)S(1)}, u32[]{:S(2)}, u32[]{:S(2)}) collective-permute-start(f32[256]{0:T(256)S(1)} %get-tuple-element.8), channel_id=1, source_target_pairs={{0,3},{1,0},{2,1},{3,2},{4,7},{5,4},{6,5},{7,6},{8,11},{9,8},{10,9... | collective-permute-start | bytes 3080 | tf_op jit(solution)/shard_map/ppermute | solution.py:21
  (5 other events, 27.1 us)

commit v11 on v8

--- a/solution.py
+++ b/solution.py
@@ -37,6 +37,23 @@
     return whole
 
 
+def gather_pair_tp(pair, cols, tp_count):
+    if tp_count != 4:
+        return gather_tp(pair[:, :cols], tp_count)
+    me = lax.axis_index("tp")
+    own = pair[:, :cols]
+    parts = {
+        0: own,
+        2: pair[:, cols:],
+        1: shift_tp(own, 1, tp_count),
+        3: shift_tp(own, 3, tp_count),
+    }
+    whole = jnp.zeros((pair.shape[0], tp_count * cols), pair.dtype)
+    for s, part in parts.items():
+        whole = lax.dynamic_update_slice_in_dim(whole, part, ((me - s) % tp_count) * cols, axis=1)
+    return whole
+
+
 def sum_tp(value, tp_count):
     ordered = by_source(value, tp_count)
     total = ordered[0]
@@ -68,7 +85,13 @@
     slot_count = CAP // copies
     chunk_items = slot_count // CHUNKS
     stream = hidden.astype(jnp.float32)
-    whole_rows = gather_tp(hidden, tp_count).astype(jnp.float32)
+    whole_raw = gather_tp(hidden, tp_count)
+    whole_rows = whole_raw.astype(jnp.float32)
+    me = lax.axis_index("tp")
+    far_cols = ((me + tp_count // 2) % tp_count) * col_part
+    pair_raw = jnp.concatenate(
+        [hidden, lax.dynamic_slice_in_dim(whole_raw, far_cols, col_part, axis=1)], axis=1
+    )
     normed_in = rms_norm(whole_rows, pre_gain).astype(jnp.bfloat16)
     top = routes.shape[1]
     chosen = routes.reshape(-1)
@@ -88,7 +111,7 @@
             hit = (slot_ids[:, None] == chunk_pairs[None, :, k]) & (owner_pairs[None, :, k] == c)
             dispatch = dispatch | hit
         relay = c == 0
-        source = hidden if relay else normed_in
+        source = pair_raw if relay else normed_in
         outgoing = jnp.dot(
             dispatch.astype(jnp.bfloat16), source, preferred_element_type=jnp.float32
         ).astype(jnp.bfloat16)
@@ -97,7 +120,7 @@
         sources, items, widths = pieces.shape
         flat_rows = pieces.reshape(sources * items, widths)
         if relay:
-            raw_rows = gather_tp(flat_rows, tp_count).astype(jnp.float32)
+            raw_rows = gather_pair_tp(flat_rows, col_part, tp_count).astype(jnp.float32)
             flat_rows = rms_norm(raw_rows, pre_gain).astype(jnp.bfloat16)
         gate_val = jnp.dot(flat_rows, gate_weight[0], preferred_element_type=jnp.float32)
         up_val = jnp.dot(flat_rows, up_weight[0], preferred_element_type=jnp.float32)

time: 160 us -> 164 us (1.025)
  starting transfers between devices: 52.2 us -> 43.4 us
  waiting for transfers between devices: 45.4 us -> 51.7 us
  local copies, waits for them, and re-layouts: 10.9 us -> 15.8 us
    all_to_all x2, waiting for transfers between devices: 10.7 us -> 19 us  [shards(): lax.all_to_all(outgoing, 'req', split_axis=0, concat_axis=0, tiled=True)]
    all_to_all x2, starting transfers between devices: 17.6 us -> 10.3 us  [shards(): lax.all_to_all(summed, 'req', split_axis=0, concat_axis=0, tiled=True)]
    all_to_all x2, waiting for transfers between devices: 12.7 us -> 9.01 us  [shards(): lax.all_to_all(summed, 'req', split_axis=0, concat_axis=0, tiled=True)]
    ppermute x15 -> x14, starting transfers between devices: 20.9 us -> 18.4 us  [shift_tp(): lax.ppermute(value, 'tp', [(j, (j + step) % tp_count) for j in range(tp_c...]
    dynamic_update_slice x0 -> x3, local copies, waits for them, and re-layouts: none -> 2.25 us  [gather_pair_tp(): lax.dynamic_update_slice_in_dim(whole, part, (me - s) % tp_count * cols,...]
    unnamed x28 -> x50, local copies, waits for them, and re-layouts: 1.02 us -> 3.02 us
    ppermute x15 -> x14, waiting for transfers between devices: 22.1 us -> 23.7 us  [shift_tp(): lax.ppermute(value, 'tp', [(j, (j + step) % tp_count) for j in range(tp_c...]
  transfers between devices with their start and end apart: 19 -> 18, of which waited for: 8 -> 10; matrix products, arithmetic and copies ran while one was open for 33% -> 33% of each run, Pallas kernels for 0% -> 0%
where the time goes in v11:
time: 164 us; the launch traced here: 163 us
  waiting for transfers between devices  51.7 us (32%)
  starting transfers between devices  43.4 us (26%)
  matrix products  42.3 us (26%)
  local copies, waits for them, and re-layouts  15.8 us (10%)
  other arithmetic  8.57 us (5%)
    ppermute x14, waiting for transfers between devices, shift_tp(): lax.ppermute(value, 'tp', [(j, (j + step) % tp_count) for j in range(tp_c...  23.7 us
    all_to_all x2, waiting for transfers between devices, shards(): lax.all_to_all(outgoing, 'req', split_axis=0, concat_axis=0, tiled=True)  19 us
    ppermute x14, starting transfers between devices, shift_tp(): lax.ppermute(value, 'tp', [(j, (j + step) % tp_count) for j in range(tp_c...  18.4 us
    dot_general x8, matrix products, down_scatter_sum_tp(): jnp.dot(activ, w_block, preferred_element_type=jnp.float32)  17.4 us
    all_to_all x2, starting transfers between devices, shards(): lax.all_to_all(outgoing, 'req', split_axis=0, concat_axis=0, tiled=True)  14.7 us
    dot_general x2, matrix products, shards(): jnp.dot(flat_rows, gate_weight[0], preferred_element_type=jnp.float32)  12.6 us
    all_to_all x2, starting transfers between devices, shards(): lax.all_to_all(summed, 'req', split_axis=0, concat_axis=0, tiled=True)  10.3 us
    all_to_all x2, waiting for transfers between devices, shards(): lax.all_to_all(summed, 'req', split_axis=0, concat_axis=0, tiled=True)  9.01 us
  transfers between devices with their start and end apart: 18, of which 10 were waited for; matrix products, arithmetic and copies ran while one was open for 33% of the time, Pallas kernels for 0%

profile of v11, /device:TPU:1, one launch (start us, length us, event | category | flops | bytes accessed | tf_op | source)
XLA Modules:
  0.0 163.1 jit_solution(12904160909651718374)
XLA Ops:
  0.6 2.2 %collective-permute-start = (bf16[256,512]{1,0:T(8,128)(2,1)}, bf16[256,512]{1,0:T(8,128)(2,1)S(1)}, u32[]{:S(2)}, u32[]{:S(2)}) collective-permute-start(bf16[256,512]{1,0:T(8,128)(2,1)} %param.8), channel_id=1, source_target_pairs={{0,1},{1,2},{2,3},{3,0},{4,5},{5,6},{6,7},{7,4},{8,9},{9,10},{10,1... | collective-permute-start | bytes 786440 | tf_op jit(solution)/shard_map/ppermute | solution.py:20
  2.8 2.6 %collective-permute-start.1 = (bf16[256,512]{1,0:T(8,128)(2,1)}, bf16[256,512]{1,0:T(8,128)(2,1)S(1)}, u32[]{:S(2)}, u32[]{:S(2)}) collective-permute-start(bf16[256,512]{1,0:T(8,128)(2,1)} %param.8), channel_id=1, source_target_pairs={{0,2},{1,3},{2,0},{3,1},{4,6},{5,7},{6,4},{7,5},{8,10},{9,11},{10,... | collective-permute-start | bytes 786440 | tf_op jit(solution)/shard_map/ppermute | solution.py:20
  11.9 5.1 %collective-permute-done.1 = bf16[256,512]{1,0:T(8,128)(2,1)S(1)} collective-permute-done((bf16[256,512]{1,0:T(8,128)(2,1)}, bf16[256,512]{1,0:T(8,128)(2,1)S(1)}, u32[]{:S(2)}, u32[]{:S(2)}) %collective-permute-start.1) | collective-permute-done | bytes 262176 | tf_op jit(solution)/shard_map/ppermute | solution.py:20
  18.6 9.5 %all-to-all-start = ((bf16[32,16,1024]{2,1,0:T(8,128)(2,1)}), bf16[32,16,1024]{2,1,0:T(8,128)(2,1)S(1)}, u32[]{:S(2)}, u32[]{:S(2)}) async-start(bf16[32,16,1024]{2,1,0:T(8,128)(2,1)} %bitcast.4), calls=%async_computation | async-start | bytes 2097152 | tf_op jit(solution)/shard_map/all_to_all | solution.py:119
  28.6 16.4 %all-to-all-done = bf16[32,16,1024]{2,1,0:T(8,128)(2,1)S(1)} async-done(((bf16[32,16,1024]{2,1,0:T(8,128)(2,1)}), bf16[32,16,1024]{2,1,0:T(8,128)(2,1)S(1)}, u32[]{:S(2)}, u32[]{:S(2)}) %all-to-all-start) | async-done | bytes 1048608 | tf_op jit(solution)/shard_map/all_to_all | solution.py:119
  50.8 2.2 %convolution_convert_fusion = bf16[512,2048]{1,0:T(8,128)(2,1)} fusion(bf16[256,2048]{1,0:T(8,128)(2,1)S(1)} %constant_dynamic-update-slice_fusion.3, f32[2048]{0:T(1024)S(1)} %copy-done.12, f32[256]{0:T(256)S(1)} %add_rsqrt_fusion.2, s32[256]{0:T(256)S(1)} %bitcast.107, s32[256]{0:T(256)S(1)} %bitcast.105, pred[256]{0:T(512)(128)(4,1)S(1)} %copy-done.11, ...), kind=kOutput, calls=%fused_computation.17 | convolution fusion | flops 540672000 | bytes 3157504 | tf_op jit(solution)/shard_map/dot_general | solution.py:115
  53.0 5.2 %all-to-all-start.2 = ((bf16[32,16,2048]{2,1,0:T(8,128)(2,1)}), bf16[32,16,2048]{2,1,0:T(8,128)(2,1)}, u32[]{:S(2)}, u32[]{:S(2)}) async-start(bf16[32,16,2048]{2,1,0:T(8,128)(2,1)} %bitcast.99), calls=%async_computation.2 | async-start | bytes 4194304 | tf_op jit(solution)/shard_map/all_to_all | solution.py:119
  58.3 4.8 %collective-permute-done.3 = bf16[512,512]{1,0:T(8,128)(2,1)} collective-permute-done((bf16[512,512]{1,0:T(8,128)(2,1)}, bf16[512,512]{1,0:T(8,128)(2,1)}, u32[]{:S(2)}, u32[]{:S(2)}) %collective-permute-start.3) | collective-permute-done | bytes 524320 | tf_op jit(solution)/shard_map/ppermute | solution.py:20
  65.8 6.1 %fusion.6 = f32[512,1408]{1,0:T(8,128)S(1)} fusion(bf16[1,2048,1408]{2,1,0:T(8,128)(2,1)} %param.13, bf16[512,2048]{1,0:T(8,128)(2,1)S(1)} %constant_dynamic-update-slice_fusion, f32[2048]{0:T(1024)S(1)} %copy-done.12, f32[512]{0:T(512)S(1)} %add_rsqrt_fusion), kind=kOutput, calls=%fused_computation.9 | convolution fusion | flops 2956984320 | bytes 10758144 | tf_op jit(solution)/shard_map/dot_general | solution.py:125
  72.0 3.5 %multiply_convert_fusion = bf16[512,1408]{1,0:T(8,128)(2,1)S(1)} fusion(f32[512,1408]{1,0:T(8,128)S(1)} %fusion.6, bf16[1,2048,1408]{2,1,0:T(8,128)(2,1)S(1)} %bitcast.112, bf16[512,2048]{1,0:T(8,128)(2,1)S(1)} %constant_dynamic-update-slice_fusion, f32[2048]{0:T(1024)S(1)} %copy-done.12, f32[512]{0:T(512)S(1)} %add_rsqrt_fusion), kind=kOutput, calls=%fused_computation.19 | convolution fusion | flops 2961309696 | bytes 12199936 | tf_op jit(solution)/shard_map/dot_general | solution.py:126
  79.1 2.4 %collective-permute-start.6 = (bf16[512,512]{1,0:T(8,128)(2,1)}, bf16[512,512]{1,0:T(8,128)(2,1)S(1)}, u32[]{:S(2)}, u32[]{:S(2)}) collective-permute-start(bf16[512,512]{1,0:T(8,128)(2,1)} %fusion.42), channel_id=1, source_target_pairs={{0,2},{1,3},{2,0},{3,1},{4,6},{5,7},{6,4},{7,5},{8,10},{9,11},{10,... | collective-permute-start | bytes 1572872 | tf_op jit(solution)/shard_map/ppermute | solution.py:20
  84.0 2.6 %all-to-all-done.2 = bf16[32,16,2048]{2,1,0:T(8,128)(2,1)} async-done(((bf16[32,16,2048]{2,1,0:T(8,128)(2,1)}), bf16[32,16,2048]{2,1,0:T(8,128)(2,1)}, u32[]{:S(2)}, u32[]{:S(2)}) %all-to-all-start.2) | async-done | bytes 2097184 | tf_op jit(solution)/shard_map/all_to_all | solution.py:119
  86.6 6.5 %fusion.4 = f32[512,1408]{1,0:T(8,128)S(1)} fusion(bf16[512,2048]{1,0:T(8,128)(2,1)} %bitcast.17, bf16[1,2048,1408]{2,1,0:T(8,128)(2,1)} %param.13), kind=kOutput, calls=%fused_computation.7 | convolution fusion | flops 2952790016 | bytes 10747904 | tf_op jit(solution)/shard_map/dot_general | solution.py:125
  93.2 5.2 %fusion.14 = bf16[512,1408]{1,0:T(8,128)(2,1)S(1)} fusion(bf16[512,2048]{1,0:T(8,128)(2,1)} %bitcast.17, bf16[1,2048,1408]{2,1,0:T(8,128)(2,1)S(1)} %bitcast.114, f32[512,1408]{1,0:T(8,128)S(1)} %fusion.4), kind=kOutput, calls=%fused_computation.18 | convolution fusion | flops 2957115392 | bytes 12189696 | tf_op jit(solution)/shard_map/dot_general | solution.py:126
  106.9 2.9 %add_convert_fusion.1 = bf16[512,512]{1,0:T(8,128)(2,1)} fusion(bf16[512,512]{1,0:T(8,128)(2,1)} %collective-permute-done.7, bf16[512,512]{1,0:T(8,128)(2,1)S(1)} %collective-permute-done.6, bf16[512,512]{1,0:T(8,128)(2,1)S(1)} %collective-permute-done.5, bf16[512,1408]{1,0:T(8,128)(2,1)S(1)} %copy-done.15, bf16[1,1408,2048]{2,1,0:T(8,128)(2,1)S(1)} %bitcast.118, ...), kind=kOutput, calls=%fused_computation.65 | convolution fusion | flops 740556800 | bytes 4980740 | tf_op jit(solution)/shard_map/dot_general | solution.py:71
  109.8 5.2 %all-to-all-start.1 = ((bf16[32,16,512]{2,1,0:T(8,128)(2,1)}), bf16[32,16,512]{2,1,0:T(8,128)(2,1)S(1)}, u32[]{:S(2)}, u32[]{:S(2)}) async-start(bf16[32,16,512]{2,1,0:T(8,128)(2,1)} %bitcast.12), calls=%async_computation.1 | async-start | bytes 1048576 | tf_op jit(solution)/shard_map/all_to_all | solution.py:130
  116.8 8.2 %collective-permute-done.9 = bf16[512,512]{1,0:T(8,128)(2,1)S(1)} collective-permute-done((bf16[512,512]{1,0:T(8,128)(2,1)}, bf16[512,512]{1,0:T(8,128)(2,1)S(1)}, u32[]{:S(2)}, u32[]{:S(2)}) %collective-permute-start.9) | collective-permute-done | bytes 524320 | tf_op jit(solution)/shard_map/ppermute | solution.py:20
  125.0 3.2 %collective-permute-done.10 = bf16[512,512]{1,0:T(8,128)(2,1)} collective-permute-done((bf16[512,512]{1,0:T(8,128)(2,1)}, bf16[512,512]{1,0:T(8,128)(2,1)}, u32[]{:S(2)}, u32[]{:S(2)}) %collective-permute-start.10) | collective-permute-done | bytes 524320 | tf_op jit(solution)/shard_map/ppermute | solution.py:20
  128.2 3.7 %add_convert_fusion = bf16[512,512]{1,0:T(8,128)(2,1)} fusion(bf16[512,512]{1,0:T(8,128)(2,1)} %collective-permute-done.10, bf16[512,512]{1,0:T(8,128)(2,1)S(1)} %collective-permute-done.9, bf16[512,512]{1,0:T(8,128)(2,1)S(1)} %collective-permute-done.8, bf16[512,1408]{1,0:T(8,128)(2,1)} %copy-done.13, bf16[1,1408,2048]{2,1,0:T(8,128)(2,1)} %param.15, ...), kind=kOutput, calls=%fused_computation.61 | convolution fusion | flops 740556800 | bytes 4980740 | tf_op jit(solution)/shard_map/dot_general | solution.py:71
  131.9 5.1 %all-to-all-start.3 = ((bf16[32,16,512]{2,1,0:T(8,128)(2,1)}), bf16[32,16,512]{2,1,0:T(8,128)(2,1)S(1)}, u32[]{:S(2)}, u32[]{:S(2)}) async-start(bf16[32,16,512]{2,1,0:T(8,128)(2,1)} %bitcast.18), calls=%async_computation.3 | async-start | bytes 1048576 | tf_op jit(solution)/shard_map/all_to_all | solution.py:130
  137.1 2.0 %gather_fusion = bf16[512,512]{1,0:T(8,128)(2,1)S(1)} fusion(bf16[512,512]{1,0:T(8,128)(2,1)S(1)} %bitcast.95, s32[1024]{0:T(1024)S(1)} %pad_clamp_fusion.1), kind=kCustom, calls=%fused_computation | custom fusion | bytes 1050624 | tf_op jit(solution)/shard_map/gather | solution.py:134
  139.8 9.0 %all-to-all-done.3 = bf16[32,16,512]{2,1,0:T(8,128)(2,1)S(1)} async-done(((bf16[32,16,512]{2,1,0:T(8,128)(2,1)}), bf16[32,16,512]{2,1,0:T(8,128)(2,1)S(1)}, u32[]{:S(2)}, u32[]{:S(2)}) %all-to-all-start.3) | async-done | bytes 524320 | tf_op jit(solution)/shard_map/all_to_all | solution.py:130
  151.4 4.0 %select_reduce_fusion.1 = (f32[256,512]{1,0:T(8,128)S(1)}, f32[256,512]{1,0:T(8,128)S(1)}) fusion(f32[256,2,512]{2,1,0:T(2,128)S(1)} %reshape.395, pred[256,2]{1,0:T(8,128)(4,1)} %copy.35, f32[256,2]{1,0:T(8,128)S(1)} %copy.37, f32[256,2,512]{2,1,0:T(2,128)S(1)} %reshape.396, pred[256,2]{1,0:T(8,128)(4,1)} %copy.38), kind=kLoop, calls=%fused_computation.64 | loop fusion | flops 1310720 | bytes 3148800 | tf_op jit(solution)/shard_map/reduce_sum | solution.py:137
  156.0 3.2 %collective-permute-start.12 = (f32[256]{0:T(256)S(1)}, f32[256]{0:T(256)S(1)}, u32[]{:S(2)}, u32[]{:S(2)}) collective-permute-start(f32[256]{0:T(256)S(1)} %get-tuple-element.8), channel_id=1, source_target_pairs={{0,2},{1,3},{2,0},{3,1},{4,6},{5,7},{6,4},{7,5},{8,10},{9,11},{10,... | collective-permute-start | bytes 3080 | tf_op jit(solution)/shard_map/ppermute | solution.py:20
  (129 shorter events, 41.1 us)
Async XLA Ops:
  0.6 11.2 %collective-permute-start = (bf16[256,512]{1,0:T(8,128)(2,1)}, bf16[256,512]{1,0:T(8,128)(2,1)S(1)}, u32[]{:S(2)}, u32[]{:S(2)}) collective-permute-start(bf16[256,512]{1,0:T(8,128)(2,1)} %param.8), channel_id=1, source_target_pairs={{0,1},{1,2},{2,3},{3,0},{4,5},{5,6},{6,7},{7,4},{8,9},{9,10},{10,1... | collective-permute-start | bytes 786440 | tf_op jit(solution)/shard_map/ppermute | solution.py:20
  2.8 14.2 %collective-permute-start.1 = (bf16[256,512]{1,0:T(8,128)(2,1)}, bf16[256,512]{1,0:T(8,128)(2,1)S(1)}, u32[]{:S(2)}, u32[]{:S(2)}) collective-permute-start(bf16[256,512]{1,0:T(8,128)(2,1)} %param.8), channel_id=1, source_target_pairs={{0,2},{1,3},{2,0},{3,1},{4,6},{5,7},{6,4},{7,5},{8,10},{9,11},{10,... | collective-permute-start | bytes 786440 | tf_op jit(solution)/shard_map/ppermute | solution.py:20
  5.4 11.6 %collective-permute-start.2 = (bf16[256,512]{1,0:T(8,128)(2,1)}, bf16[256,512]{1,0:T(8,128)(2,1)S(1)}, u32[]{:S(2)}, u32[]{:S(2)}) collective-permute-start(bf16[256,512]{1,0:T(8,128)(2,1)} %param.8), channel_id=1, source_target_pairs={{0,3},{1,0},{2,1},{3,2},{4,7},{5,4},{6,5},{7,6},{8,11},{9,8},{10,9... | collective-permute-start | bytes 786440 | tf_op jit(solution)/shard_map/ppermute | solution.py:20
  18.6 26.4 %all-to-all-start = ((bf16[32,16,1024]{2,1,0:T(8,128)(2,1)}), bf16[32,16,1024]{2,1,0:T(8,128)(2,1)S(1)}, u32[]{:S(2)}, u32[]{:S(2)}) async-start(bf16[32,16,1024]{2,1,0:T(8,128)(2,1)} %bitcast.4), calls=%async_computation | async-start | bytes 2097152 | tf_op jit(solution)/shard_map/all_to_all | solution.py:119
  28.5 22.3 %copy-start.7 = (s32[256,1]{0,1:T(1,128)S(1)}, s32[256,1]{0,1:T(1,128)}, u32[]{:S(2)}) copy-start(s32[256,1]{0,1:T(1,128)} %copy-done.6) | copy-start | bytes 3076
  28.5 22.3 %copy-start.9 = (s32[256,1]{0,1:T(1,128)S(1)}, s32[256,1]{0,1:T(1,128)}, u32[]{:S(2)}) copy-start(s32[256,1]{0,1:T(1,128)} %copy-done.8) | copy-start | bytes 3076
  28.5 22.2 %copy-start.10 = (pred[256]{0:T(512)(128)(4,1)S(1)}, pred[256]{0:T(512)(128)(4,1)}, u32[]{:S(2)}) copy-start(pred[256]{0:T(512)(128)(4,1)} %get-tuple-element.5) | copy-start | bytes 772
  28.6 22.2 %copy-start.11 = (pred[256]{0:T(512)(128)(4,1)S(1)}, pred[256]{0:T(512)(128)(4,1)}, u32[]{:S(2)}) copy-start(pred[256]{0:T(512)(128)(4,1)} %get-tuple-element.6) | copy-start | bytes 772
  28.6 22.2 %copy-start.12 = (f32[2048]{0:T(1024)S(1)}, f32[2048]{0:T(1024)}, u32[]{:S(2)}) copy-start(f32[2048]{0:T(1024)} %param.11) | copy-start | bytes 24580
  48.1 14.9 %collective-permute-start.3 = (bf16[512,512]{1,0:T(8,128)(2,1)}, bf16[512,512]{1,0:T(8,128)(2,1)}, u32[]{:S(2)}, u32[]{:S(2)}) collective-permute-start(bf16[512,512]{1,0:T(8,128)(2,1)} %get-tuple-element.13), channel_id=1, source_target_pairs={{0,1},{1,2},{2,3},{3,0},{4,5},{5,6},{6,7},{7,4},{8,9},{9,10},{10,1... | collective-permute-start | bytes 1572872 | tf_op jit(solution)/shard_map/ppermute | solution.py:20
  49.0 15.1 %collective-permute-start.4 = (bf16[512,512]{1,0:T(8,128)(2,1)}, bf16[512,512]{1,0:T(8,128)(2,1)}, u32[]{:S(2)}, u32[]{:S(2)}) collective-permute-start(bf16[512,512]{1,0:T(8,128)(2,1)} %get-tuple-element.13), channel_id=1, source_target_pairs={{0,3},{1,0},{2,1},{3,2},{4,7},{5,4},{6,5},{7,6},{8,11},{9,8},{10,9... | collective-permute-start | bytes 1572872 | tf_op jit(solution)/shard_map/ppermute | solution.py:20
  53.0 33.6 %all-to-all-start.2 = ((bf16[32,16,2048]{2,1,0:T(8,128)(2,1)}), bf16[32,16,2048]{2,1,0:T(8,128)(2,1)}, u32[]{:S(2)}, u32[]{:S(2)}) async-start(bf16[32,16,2048]{2,1,0:T(8,128)(2,1)} %bitcast.99), calls=%async_computation.2 | async-start | bytes 4194304 | tf_op jit(solution)/shard_map/all_to_all | solution.py:119
  77.3 28.3 %collective-permute-start.5 = (bf16[512,512]{1,0:T(8,128)(2,1)}, bf16[512,512]{1,0:T(8,128)(2,1)S(1)}, u32[]{:S(2)}, u32[]{:S(2)}) collective-permute-start(bf16[512,512]{1,0:T(8,128)(2,1)} %fusion.36), channel_id=1, source_target_pairs={{0,1},{1,2},{2,3},{3,0},{4,5},{5,6},{6,7},{7,4},{8,9},{9,10},{10,1... | collective-permute-start | bytes 1572872 | tf_op jit(solution)/shard_map/ppermute | solution.py:20
  79.1 27.8 %collective-permute-start.6 = (bf16[512,512]{1,0:T(8,128)(2,1)}, bf16[512,512]{1,0:T(8,128)(2,1)S(1)}, u32[]{:S(2)}, u32[]{:S(2)}) collective-permute-start(bf16[512,512]{1,0:T(8,128)(2,1)} %fusion.42), channel_id=1, source_target_pairs={{0,2},{1,3},{2,0},{3,1},{4,6},{5,7},{6,4},{7,5},{8,10},{9,11},{10,... | collective-permute-start | bytes 1572872 | tf_op jit(solution)/shard_map/ppermute | solution.py:20
  83.3 23.7 %collective-permute-start.7 = (bf16[512,512]{1,0:T(8,128)(2,1)}, bf16[512,512]{1,0:T(8,128)(2,1)}, u32[]{:S(2)}, u32[]{:S(2)}) collective-permute-start(bf16[512,512]{1,0:T(8,128)(2,1)} %fusion.48), channel_id=1, source_target_pairs={{0,3},{1,0},{2,1},{3,2},{4,7},{5,4},{6,5},{7,6},{8,11},{9,8},{10,9... | collective-permute-start | bytes 1572872 | tf_op jit(solution)/shard_map/ppermute | solution.py:20
  86.6 11.7 %slice-start.6 = ((s8[5767168]{0:T(1024)(128)(4,1)}), s8[4194304]{0:T(1024)(128)(4,1)S(1)}, s32[]{:S(2)}) async-start(s8[5767168]{0:T(1024)(128)(4,1)} %bitcast.117), calls=%async_computation.10 | async-start | bytes 8388608
  100.2 16.5 %collective-permute-start.8 = (bf16[512,512]{1,0:T(8,128)(2,1)}, bf16[512,512]{1,0:T(8,128)(2,1)S(1)}, u32[]{:S(2)}, u32[]{:S(2)}) collective-permute-start(bf16[512,512]{1,0:T(8,128)(2,1)} %fusion.39), channel_id=1, source_target_pairs={{0,1},{1,2},{2,3},{3,0},{4,5},{5,6},{6,7},{7,4},{8,9},{9,10},{10,1... | collective-permute-start | bytes 1572872 | tf_op jit(solution)/shard_map/ppermute | solution.py:20
  102.0 23.0 %collective-permute-start.9 = (bf16[512,512]{1,0:T(8,128)(2,1)}, bf16[512,512]{1,0:T(8,128)(2,1)S(1)}, u32[]{:S(2)}, u32[]{:S(2)}) collective-permute-start(bf16[512,512]{1,0:T(8,128)(2,1)} %fusion.45), channel_id=1, source_target_pairs={{0,2},{1,3},{2,0},{3,1},{4,6},{5,7},{6,4},{7,5},{8,10},{9,11},{10,... | collective-permute-start | bytes 1572872 | tf_op jit(solution)/shard_map/ppermute | solution.py:20
  105.6 22.6 %collective-permute-start.10 = (bf16[512,512]{1,0:T(8,128)(2,1)}, bf16[512,512]{1,0:T(8,128)(2,1)}, u32[]{:S(2)}, u32[]{:S(2)}) collective-permute-start(bf16[512,512]{1,0:T(8,128)(2,1)} %fusion.51), channel_id=1, source_target_pairs={{0,3},{1,0},{2,1},{3,2},{4,7},{5,4},{6,5},{7,6},{8,11},{9,8},{10,9... | collective-permute-start | bytes 1572872 | tf_op jit(solution)/shard_map/ppermute | solution.py:20
  109.8 22.1 %all-to-all-start.1 = ((bf16[32,16,512]{2,1,0:T(8,128)(2,1)}), bf16[32,16,512]{2,1,0:T(8,128)(2,1)S(1)}, u32[]{:S(2)}, u32[]{:S(2)}) async-start(bf16[32,16,512]{2,1,0:T(8,128)(2,1)} %bitcast.12), calls=%async_computation.1 | async-start | bytes 1048576 | tf_op jit(solution)/shard_map/all_to_all | solution.py:130
  131.9 16.8 %all-to-all-start.3 = ((bf16[32,16,512]{2,1,0:T(8,128)(2,1)}), bf16[32,16,512]{2,1,0:T(8,128)(2,1)S(1)}, u32[]{:S(2)}, u32[]{:S(2)}) async-start(bf16[32,16,512]{2,1,0:T(8,128)(2,1)} %bitcast.18), calls=%async_computation.3 | async-start | bytes 1048576 | tf_op jit(solution)/shard_map/all_to_all | solution.py:130
  155.6 3.7 %collective-permute-start.11 = (f32[256]{0:T(256)S(1)}, f32[256]{0:T(256)S(1)}, u32[]{:S(2)}, u32[]{:S(2)}) collective-permute-start(f32[256]{0:T(256)S(1)} %get-tuple-element.8), channel_id=1, source_target_pairs={{0,1},{1,2},{2,3},{3,0},{4,5},{5,6},{6,7},{7,4},{8,9},{9,10},{10,1... | collective-permute-start | bytes 3080 | tf_op jit(solution)/shard_map/ppermute | solution.py:20
  156.0 4.1 %collective-permute-start.12 = (f32[256]{0:T(256)S(1)}, f32[256]{0:T(256)S(1)}, u32[]{:S(2)}, u32[]{:S(2)}) collective-permute-start(f32[256]{0:T(256)S(1)} %get-tuple-element.8), channel_id=1, source_target_pairs={{0,2},{1,3},{2,0},{3,1},{4,6},{5,7},{6,4},{7,5},{8,10},{9,11},{10,... | collective-permute-start | bytes 3080 | tf_op jit(solution)/shard_map/ppermute | solution.py:20
  159.2 2.4 %collective-permute-start.13 = (f32[256]{0:T(256)S(1)}, f32[256]{0:T(256)S(1)}, u32[]{:S(2)}, u32[]{:S(2)}) collective-permute-start(f32[256]{0:T(256)S(1)} %get-tuple-element.8), channel_id=1, source_target_pairs={{0,3},{1,0},{2,1},{3,2},{4,7},{5,4},{6,5},{7,6},{8,11},{9,8},{10,9... | collective-permute-start | bytes 3080 | tf_op jit(solution)/shard_map/ppermute | solution.py:20
  (18 other events, 120.3 us)

commit v12 on v8

--- a/solution.py
+++ b/solution.py
@@ -106,12 +106,19 @@
         summed = summed.reshape(sources, items, col_part)
         back = lax.all_to_all(summed, "req", split_axis=0, concat_axis=0, tiled=True)
         returned.append(back.reshape(req_count * chunk_items, col_part))
+    weight_hi = route_weights.astype(jnp.bfloat16)
+    weight_lo = (route_weights - weight_hi.astype(jnp.float32)).astype(jnp.bfloat16)
     total_stream = stream
     for c in range(CHUNKS):
-        picked = returned[c][in_chunk].reshape(row_count, top, col_part).astype(jnp.float32)
-        mine = (owner_pairs == c)[:, :, None]
-        terms = jnp.where(mine, picked * route_weights[:, :, None], 0.0)
-        total_stream = total_stream + jnp.sum(terms, axis=1)
+        combine_hi = jnp.zeros((row_count, req_count * chunk_items), jnp.bfloat16)
+        combine_lo = jnp.zeros((row_count, req_count * chunk_items), jnp.bfloat16)
+        for k in range(top):
+            hit = (chunk_pairs[:, k][:, None] == slot_ids[None, :]) & (owner_pairs[:, k][:, None] == c)
+            combine_hi = jnp.where(hit, weight_hi[:, k][:, None], combine_hi)
+            combine_lo = jnp.where(hit, weight_lo[:, k][:, None], combine_lo)
+        mixed = jnp.dot(combine_hi, returned[c], preferred_element_type=jnp.float32)
+        mixed = mixed + jnp.dot(combine_lo, returned[c], preferred_element_type=jnp.float32)
+        total_stream = total_stream + mixed
     out_sums = sum_tp(jnp.sum(total_stream * total_stream, axis=1), tp_count)
     normed_out = (
         total_stream * lax.rsqrt(out_sums / full_width + epsilon)[:, None] * out_gain[None, :]

time: 160 us -> 154 us (0.963)
  waiting for transfers between devices: 45.4 us -> 59.7 us
  starting transfers between devices: 52.2 us -> 38.3 us
  local copies, waits for them, and re-layouts: 10.9 us -> 5.01 us
  other arithmetic: 7.24 us -> 3.78 us
  matrix products: 42.7 us -> 44.8 us
    ppermute x15, waiting for transfers between devices: 22.1 us -> 38.1 us  [shift_tp(): lax.ppermute(value, 'tp', [(j, (j + step) % tp_count) for j in range(tp_c...]
    all_to_all x2, starting transfers between devices: 17.6 us -> 8.43 us  [shards(): lax.all_to_all(summed, 'req', split_axis=0, concat_axis=0, tiled=True)]
    ppermute x15, starting transfers between devices: 20.9 us -> 16.3 us  [shift_tp(): lax.ppermute(value, 'tp', [(j, (j + step) % tp_count) for j in range(tp_c...]
    gather x2 -> x0, local copies, waits for them, and re-layouts: 3.94 us -> none  [shards(): returned[c][in_chunk].reshape(row_count, top, col_part).astype(jnp.float32)]
    reduce_sum x2 -> x0, other arithmetic: 3.41 us -> none  [the longest x1 3.25 us: shards(): total_stream = total_stream + jnp.sum(terms, axis=1)]
    dot_general x0 -> x4, matrix products: none -> 2.07 us  [the longest x2 1.09 us: shards(): jnp.dot(combine_lo, returned[c], preferred_element_type=jnp.float32)]
    all_to_all x2, waiting for transfers between devices: 12.7 us -> 10.7 us  [shards(): lax.all_to_all(summed, 'req', split_axis=0, concat_axis=0, tiled=True)]
  transfers between devices with their start and end apart: 19 -> 19, of which waited for: 8 -> 9; matrix products, arithmetic and copies ran while one was open for 33% -> 33% of each run, Pallas kernels for 0% -> 0%
where the time goes in v12:
time: 154 us; the launch traced here: 153 us
  waiting for transfers between devices  59.7 us (39%)
  matrix products  44.8 us (29%)
  starting transfers between devices  38.3 us (25%)
  local copies, waits for them, and re-layouts  5.01 us (3%)
  other arithmetic  3.78 us (2%)
    ppermute x15, waiting for transfers between devices, shift_tp(): lax.ppermute(value, 'tp', [(j, (j + step) % tp_count) for j in range(tp_c...  38.1 us
    dot_general x8, matrix products, down_scatter_sum_tp(): jnp.dot(activ, w_block, preferred_element_type=jnp.float32)  16.8 us
    ppermute x15, starting transfers between devices, shift_tp(): lax.ppermute(value, 'tp', [(j, (j + step) % tp_count) for j in range(tp_c...  16.3 us
    all_to_all x2, starting transfers between devices, shards(): lax.all_to_all(outgoing, 'req', split_axis=0, concat_axis=0, tiled=True)  13.6 us
    dot_general x2, matrix products, shards(): jnp.dot(flat_rows, gate_weight[0], preferred_element_type=jnp.float32)  12 us
    all_to_all x2, waiting for transfers between devices, shards(): lax.all_to_all(outgoing, 'req', split_axis=0, concat_axis=0, tiled=True)  10.9 us
    all_to_all x2, waiting for transfers between devices, shards(): lax.all_to_all(summed, 'req', split_axis=0, concat_axis=0, tiled=True)  10.7 us
    dot_general x2, matrix products, shards(): jnp.dot(flat_rows, up_weight[0], preferred_element_type=jnp.float32)  9.71 us
  transfers between devices with their start and end apart: 19, of which 9 were waited for; matrix products, arithmetic and copies ran while one was open for 33% of the time, Pallas kernels for 0%

profile of v12, /device:TPU:1, one launch (start us, length us, event | category | flops | bytes accessed | tf_op | source)
XLA Modules:
  0.0 152.9 jit_solution(18175119244036833349)
XLA Ops:
  0.7 2.2 %collective-permute-start.6 = (bf16[256,512]{1,0:T(8,128)(2,1)}, bf16[256,512]{1,0:T(8,128)(2,1)S(1)}, u32[]{:S(2)}, u32[]{:S(2)}) collective-permute-start(bf16[256,512]{1,0:T(8,128)(2,1)} %param.8), channel_id=1, source_target_pairs={{0,1},{1,2},{2,3},{3,0},{4,5},{5,6},{6,7},{7,4},{8,9},{9,10},{10,1... | collective-permute-start | bytes 786440 | tf_op jit(solution)/shard_map/ppermute | solution.py:20
  2.8 2.6 %collective-permute-start.7 = (bf16[256,512]{1,0:T(8,128)(2,1)}, bf16[256,512]{1,0:T(8,128)(2,1)S(1)}, u32[]{:S(2)}, u32[]{:S(2)}) collective-permute-start(bf16[256,512]{1,0:T(8,128)(2,1)} %param.8), channel_id=1, source_target_pairs={{0,2},{1,3},{2,0},{3,1},{4,6},{5,7},{6,4},{7,5},{8,10},{9,11},{10,... | collective-permute-start | bytes 786440 | tf_op jit(solution)/shard_map/ppermute | solution.py:20
  10.2 2.1 %convolution_convert_fusion.1 = bf16[512,512]{1,0:T(8,128)(2,1)} fusion(bf16[256,512]{1,0:T(8,128)(2,1)} %param.8, s32[256]{0:T(256)S(1)} %bitcast.116, s32[256]{0:T(256)S(1)} %bitcast.110, pred[256]{0:T(512)(128)(4,1)S(1)} %get-tuple-element.5, pred[256]{0:T(512)(128)(4,1)S(1)} %get-tuple-element.4), kind=kOutput, calls=%fused_computation.47 | convolution fusion | flops 135135232 | bytes 788992 | tf_op jit(solution)/shard_map/dot_general | solution.py:92
  12.2 9.4 %all-to-all-start = ((bf16[32,16,512]{2,1,0:T(8,128)(2,1)}), bf16[32,16,512]{2,1,0:T(8,128)(2,1)S(1)}, u32[]{:S(2)}, u32[]{:S(2)}) async-start(bf16[32,16,512]{2,1,0:T(8,128)(2,1)} %bitcast.4), calls=%async_computation | async-start | bytes 1048576 | tf_op jit(solution)/shard_map/all_to_all | solution.py:96
  22.4 10.9 %all-to-all-done = bf16[32,16,512]{2,1,0:T(8,128)(2,1)S(1)} async-done(((bf16[32,16,512]{2,1,0:T(8,128)(2,1)}), bf16[32,16,512]{2,1,0:T(8,128)(2,1)S(1)}, u32[]{:S(2)}, u32[]{:S(2)}) %all-to-all-start) | async-done | bytes 524320 | tf_op jit(solution)/shard_map/all_to_all | solution.py:96
  34.2 2.0 %collective-permute-start.2 = (bf16[512,512]{1,0:T(8,128)(2,1)S(1)}, bf16[512,512]{1,0:T(8,128)(2,1)S(1)}, u32[]{:S(2)}, u32[]{:S(2)}) collective-permute-start(bf16[512,512]{1,0:T(8,128)(2,1)S(1)} %bitcast.103), channel_id=1, source_target_pairs={{0,3},{1,0},{2,1},{3,2},{4,7},{5,4},{6,5},{7,6},{8,11},{9,8},{10,9... | collective-permute-start | bytes 1572872 | tf_op jit(solution)/shard_map/ppermute | solution.py:20
  36.2 2.2 %convolution_convert_fusion = bf16[512,2048]{1,0:T(8,128)(2,1)} fusion(bf16[256,2048]{1,0:T(8,128)(2,1)S(1)} %constant_dynamic-update-slice_fusion, f32[2048]{0:T(1024)S(1)} %copy-done.3, f32[256]{0:T(256)S(1)} %add_rsqrt_fusion.2, s32[256]{0:T(256)S(1)} %bitcast.117, s32[256]{0:T(256)S(1)} %bitcast.111, pred[256]{0:T(512)(128)(4,1)S(1)} %get-tuple-element.3, ...), kind=kOutput, calls=%fused_computation.15 | convolution fusion | flops 540672000 | bytes 3157504 | tf_op jit(solution)/shard_map/dot_general | solution.py:92
  38.4 4.2 %all-to-all-start.2 = ((bf16[32,16,2048]{2,1,0:T(8,128)(2,1)}), bf16[32,16,2048]{2,1,0:T(8,128)(2,1)S(1)}, u32[]{:S(2)}, u32[]{:S(2)}) async-start(bf16[32,16,2048]{2,1,0:T(8,128)(2,1)} %bitcast.100), calls=%async_computation.2 | async-start | bytes 4194304 | tf_op jit(solution)/shard_map/all_to_all | solution.py:96
  42.9 16.6 %collective-permute-done = bf16[512,512]{1,0:T(8,128)(2,1)} collective-permute-done((bf16[512,512]{1,0:T(8,128)(2,1)S(1)}, bf16[512,512]{1,0:T(8,128)(2,1)}, u32[]{:S(2)}, u32[]{:S(2)}) %collective-permute-start) | collective-permute-done | bytes 524320 | tf_op jit(solution)/shard_map/ppermute | solution.py:20
  62.4 6.1 %fusion.6 = f32[512,1408]{1,0:T(8,128)S(1)} fusion(bf16[1,2048,1408]{2,1,0:T(8,128)(2,1)} %param.13, bf16[512,2048]{1,0:T(8,128)(2,1)S(1)} %constant_dynamic-update-slice_fusion.4, f32[2048]{0:T(1024)S(1)} %copy-done.3, f32[512]{0:T(512)S(1)} %add_rsqrt_fusion), kind=kOutput, calls=%fused_computation.7 | convolution fusion | flops 2956984320 | bytes 10758144 | tf_op jit(solution)/shard_map/dot_general | solution.py:102
  68.5 3.5 %multiply_convert_fusion = bf16[512,1408]{1,0:T(8,128)(2,1)S(1)} fusion(f32[512,1408]{1,0:T(8,128)S(1)} %fusion.6, bf16[1,2048,1408]{2,1,0:T(8,128)(2,1)S(1)} %bitcast.127, bf16[512,2048]{1,0:T(8,128)(2,1)S(1)} %constant_dynamic-update-slice_fusion.4, f32[2048]{0:T(1024)S(1)} %copy-done.3, f32[512]{0:T(512)S(1)} %add_rsqrt_fusion), kind=kOutput, calls=%fused_computation.17 | convolution fusion | flops 2961309696 | bytes 12199936 | tf_op jit(solution)/shard_map/dot_general | solution.py:103
  72.1 1.8 %fusion.48 = bf16[512,512]{1,0:T(8,128)(2,1)} fusion(bf16[512,1408]{1,0:T(8,128)(2,1)S(1)} %multiply_convert_fusion, bf16[1,1408,2048]{2,1,0:T(8,128)(2,1)S(1)} %bitcast.129, s32[]{:T(128)S(6)} %select_n.183), kind=kOutput, calls=%fused_computation.43 | convolution fusion | flops 738459648 | bytes 3407876 | tf_op jit(solution)/shard_map/dot_general | solution.py:54
  76.3 1.8 %fusion.36 = bf16[512,512]{1,0:T(8,128)(2,1)} fusion(bf16[512,1408]{1,0:T(8,128)(2,1)S(1)} %multiply_convert_fusion, bf16[1,1408,2048]{2,1,0:T(8,128)(2,1)S(1)} %bitcast.129, s32[]{:T(128)S(6)} %select_n.179), kind=kOutput, calls=%fused_computation.39 | convolution fusion | flops 738459648 | bytes 3407876 | tf_op jit(solution)/shard_map/dot_general | solution.py:54
  79.0 5.9 %fusion.4 = f32[512,1408]{1,0:T(8,128)S(1)} fusion(bf16[512,2048]{1,0:T(8,128)(2,1)S(1)} %bitcast.98, bf16[1,2048,1408]{2,1,0:T(8,128)(2,1)} %param.13), kind=kOutput, calls=%fused_computation.5 | convolution fusion | flops 2952790016 | bytes 10747904 | tf_op jit(solution)/shard_map/dot_general | solution.py:102
  84.9 6.2 %fusion.14 = bf16[512,1408]{1,0:T(8,128)(2,1)S(1)} fusion(bf16[512,2048]{1,0:T(8,128)(2,1)S(1)} %bitcast.99, bf16[1,2048,1408]{2,1,0:T(8,128)(2,1)} %param.14, f32[512,1408]{1,0:T(8,128)S(1)} %fusion.4), kind=kOutput, calls=%fused_computation.16 | convolution fusion | flops 2957115392 | bytes 12189696 | tf_op jit(solution)/shard_map/dot_general | solution.py:103
  92.1 2.5 %collective-permute-start.11 = (bf16[512,512]{1,0:T(8,128)(2,1)S(1)}, bf16[512,512]{1,0:T(8,128)(2,1)S(1)}, u32[]{:S(2)}, u32[]{:S(2)}) collective-permute-start(bf16[512,512]{1,0:T(8,128)(2,1)S(1)} %fusion.51), channel_id=1, source_target_pairs={{0,3},{1,0},{2,1},{3,2},{4,7},{5,4},{6,5},{7,6},{8,11},{9,8},{10,9... | collective-permute-start | bytes 1572872 | tf_op jit(solution)/shard_map/ppermute | solution.py:20
  100.3 4.2 %collective-permute-done.3 = bf16[512,512]{1,0:T(8,128)(2,1)} collective-permute-done((bf16[512,512]{1,0:T(8,128)(2,1)}, bf16[512,512]{1,0:T(8,128)(2,1)}, u32[]{:S(2)}, u32[]{:S(2)}) %collective-permute-start.3) | collective-permute-done | bytes 524320 | tf_op jit(solution)/shard_map/ppermute | solution.py:20
  104.4 3.0 %add_convert_fusion.1 = bf16[512,512]{1,0:T(8,128)(2,1)} fusion(bf16[512,512]{1,0:T(8,128)(2,1)S(1)} %collective-permute-done.5, bf16[512,512]{1,0:T(8,128)(2,1)} %collective-permute-done.4, bf16[512,512]{1,0:T(8,128)(2,1)} %collective-permute-done.3, bf16[512,1408]{1,0:T(8,128)(2,1)S(1)} %copy-done.6, bf16[1,1408,2048]{2,1,0:T(8,128)(2,1)S(1)} %bitcast.131, ...), kind=kOutput, calls=%fused_computation.65 | convolution fusion | flops 740556800 | bytes 4980740 | tf_op jit(solution)/shard_map/dot_general | solution.py:54
  107.5 4.3 %all-to-all-start.1 = ((bf16[32,16,512]{2,1,0:T(8,128)(2,1)}), bf16[32,16,512]{2,1,0:T(8,128)(2,1)S(1)}, u32[]{:S(2)}, u32[]{:S(2)}) async-start(bf16[32,16,512]{2,1,0:T(8,128)(2,1)} %bitcast.12), calls=%async_computation.1 | async-start | bytes 1048576 | tf_op jit(solution)/shard_map/all_to_all | solution.py:107
  113.1 12.4 %collective-permute-done.9 = bf16[512,512]{1,0:T(8,128)(2,1)} collective-permute-done((bf16[512,512]{1,0:T(8,128)(2,1)}, bf16[512,512]{1,0:T(8,128)(2,1)}, u32[]{:S(2)}, u32[]{:S(2)}) %collective-permute-start.9) | collective-permute-done | bytes 524320 | tf_op jit(solution)/shard_map/ppermute | solution.py:20
  125.5 3.7 %add_convert_fusion = bf16[512,512]{1,0:T(8,128)(2,1)} fusion(bf16[512,512]{1,0:T(8,128)(2,1)S(1)} %collective-permute-done.11, bf16[512,512]{1,0:T(8,128)(2,1)S(1)} %collective-permute-done.10, bf16[512,512]{1,0:T(8,128)(2,1)} %collective-permute-done.9, bf16[512,1408]{1,0:T(8,128)(2,1)} %copy-done.4, bf16[1,1408,2048]{2,1,0:T(8,128)(2,1)} %param.15, ...), kind=kOutput, calls=%fused_computation.62 | convolution fusion | flops 740556800 | bytes 4980740 | tf_op jit(solution)/shard_map/dot_general | solution.py:54
  129.2 4.2 %all-to-all-start.3 = ((bf16[32,16,512]{2,1,0:T(8,128)(2,1)}), bf16[32,16,512]{2,1,0:T(8,128)(2,1)S(1)}, u32[]{:S(2)}, u32[]{:S(2)}) async-start(bf16[32,16,512]{2,1,0:T(8,128)(2,1)} %bitcast.16), calls=%async_computation.3 | async-start | bytes 1048576 | tf_op jit(solution)/shard_map/all_to_all | solution.py:107
  134.4 10.7 %all-to-all-done.3 = bf16[32,16,512]{2,1,0:T(8,128)(2,1)S(1)} async-done(((bf16[32,16,512]{2,1,0:T(8,128)(2,1)}), bf16[32,16,512]{2,1,0:T(8,128)(2,1)S(1)}, u32[]{:S(2)}, u32[]{:S(2)}) %all-to-all-start.3) | async-done | bytes 524320 | tf_op jit(solution)/shard_map/all_to_all | solution.py:107
  148.7 1.9 %collective-permute-done.13 = f32[256]{0:T(256)S(1)} collective-permute-done((f32[256]{0:T(256)S(1)}, f32[256]{0:T(256)S(1)}, u32[]{:S(2)}, u32[]{:S(2)}) %collective-permute-start.13) | collective-permute-done | bytes 1056 | tf_op jit(solution)/shard_map/ppermute | solution.py:20
  (100 shorter events, 27.4 us)
Async XLA Ops:
  0.6 21.2 %copy-start = (bf16[256,512]{1,0:T(8,128)(2,1)S(1)}, bf16[256,512]{1,0:T(8,128)(2,1)}, u32[]{:S(2)}) copy-start(bf16[256,512]{1,0:T(8,128)(2,1)} %param.8) | copy-start | bytes 786436
  0.6 21.0 %copy-start.2 = (f32[256,2]{0,1:T(2,128)S(1)}, f32[256,2]{0,1:T(2,128)}, u32[]{:S(2)}) copy-start(f32[256,2]{0,1:T(2,128)} %param.10) | copy-start | bytes 6148
  0.7 21.4 %collective-permute-start.6 = (bf16[256,512]{1,0:T(8,128)(2,1)}, bf16[256,512]{1,0:T(8,128)(2,1)S(1)}, u32[]{:S(2)}, u32[]{:S(2)}) collective-permute-start(bf16[256,512]{1,0:T(8,128)(2,1)} %param.8), channel_id=1, source_target_pairs={{0,1},{1,2},{2,3},{3,0},{4,5},{5,6},{6,7},{7,4},{8,9},{9,10},{10,1... | collective-permute-start | bytes 786440 | tf_op jit(solution)/shard_map/ppermute | solution.py:20
  2.8 19.2 %collective-permute-start.7 = (bf16[256,512]{1,0:T(8,128)(2,1)}, bf16[256,512]{1,0:T(8,128)(2,1)S(1)}, u32[]{:S(2)}, u32[]{:S(2)}) collective-permute-start(bf16[256,512]{1,0:T(8,128)(2,1)} %param.8), channel_id=1, source_target_pairs={{0,2},{1,3},{2,0},{3,1},{4,6},{5,7},{6,4},{7,5},{8,10},{9,11},{10,... | collective-permute-start | bytes 786440 | tf_op jit(solution)/shard_map/ppermute | solution.py:20
  5.5 16.6 %collective-permute-start.8 = (bf16[256,512]{1,0:T(8,128)(2,1)}, bf16[256,512]{1,0:T(8,128)(2,1)S(1)}, u32[]{:S(2)}, u32[]{:S(2)}) collective-permute-start(bf16[256,512]{1,0:T(8,128)(2,1)} %param.8), channel_id=1, source_target_pairs={{0,3},{1,0},{2,1},{3,2},{4,7},{5,4},{6,5},{7,6},{8,11},{9,8},{10,9... | collective-permute-start | bytes 786440 | tf_op jit(solution)/shard_map/ppermute | solution.py:20
  12.2 21.1 %all-to-all-start = ((bf16[32,16,512]{2,1,0:T(8,128)(2,1)}), bf16[32,16,512]{2,1,0:T(8,128)(2,1)S(1)}, u32[]{:S(2)}, u32[]{:S(2)}) async-start(bf16[32,16,512]{2,1,0:T(8,128)(2,1)} %bitcast.4), calls=%async_computation | async-start | bytes 1048576 | tf_op jit(solution)/shard_map/all_to_all | solution.py:96
  21.7 14.5 %copy-start.3 = (f32[2048]{0:T(1024)S(1)}, f32[2048]{0:T(1024)}, u32[]{:S(2)}) copy-start(f32[2048]{0:T(1024)} %param.11) | copy-start | bytes 24580
  33.3 26.2 %collective-permute-start = (bf16[512,512]{1,0:T(8,128)(2,1)S(1)}, bf16[512,512]{1,0:T(8,128)(2,1)}, u32[]{:S(2)}, u32[]{:S(2)}) collective-permute-start(bf16[512,512]{1,0:T(8,128)(2,1)S(1)} %bitcast.101), channel_id=1, source_target_pairs={{0,1},{1,2},{2,3},{3,0},{4,5},{5,6},{6,7},{7,4},{8,9},{9,10},{10,1... | collective-permute-start | bytes 1572872 | tf_op jit(solution)/shard_map/ppermute | solution.py:20
  33.7 26.9 %collective-permute-start.1 = (bf16[512,512]{1,0:T(8,128)(2,1)S(1)}, bf16[512,512]{1,0:T(8,128)(2,1)}, u32[]{:S(2)}, u32[]{:S(2)}) collective-permute-start(bf16[512,512]{1,0:T(8,128)(2,1)S(1)} %bitcast.102), channel_id=1, source_target_pairs={{0,2},{1,3},{2,0},{3,1},{4,6},{5,7},{6,4},{7,5},{8,10},{9,11},{10,... | collective-permute-start | bytes 1572872 | tf_op jit(solution)/shard_map/ppermute | solution.py:20
  34.2 27.5 %collective-permute-start.2 = (bf16[512,512]{1,0:T(8,128)(2,1)S(1)}, bf16[512,512]{1,0:T(8,128)(2,1)S(1)}, u32[]{:S(2)}, u32[]{:S(2)}) collective-permute-start(bf16[512,512]{1,0:T(8,128)(2,1)S(1)} %bitcast.103), channel_id=1, source_target_pairs={{0,3},{1,0},{2,1},{3,2},{4,7},{5,4},{6,5},{7,6},{8,11},{9,8},{10,9... | collective-permute-start | bytes 1572872 | tf_op jit(solution)/shard_map/ppermute | solution.py:20
  38.4 40.6 %all-to-all-start.2 = ((bf16[32,16,2048]{2,1,0:T(8,128)(2,1)}), bf16[32,16,2048]{2,1,0:T(8,128)(2,1)S(1)}, u32[]{:S(2)}, u32[]{:S(2)}) async-start(bf16[32,16,2048]{2,1,0:T(8,128)(2,1)} %bitcast.100), calls=%async_computation.2 | async-start | bytes 4194304 | tf_op jit(solution)/shard_map/all_to_all | solution.py:96
  62.4 9.7 %slice-start.2 = ((s8[5767168]{0:T(1024)(128)(4,1)}), s8[4194304]{0:T(1024)(128)(4,1)S(1)}, s32[]{:S(2)}) async-start(s8[5767168]{0:T(1024)(128)(4,1)} %bitcast.128), calls=%async_computation.6 | async-start | bytes 8388608
  73.9 25.5 %collective-permute-start.5 = (bf16[512,512]{1,0:T(8,128)(2,1)}, bf16[512,512]{1,0:T(8,128)(2,1)S(1)}, u32[]{:S(2)}, u32[]{:S(2)}) collective-permute-start(bf16[512,512]{1,0:T(8,128)(2,1)} %fusion.48), channel_id=1, source_target_pairs={{0,3},{1,0},{2,1},{3,2},{4,7},{5,4},{6,5},{7,6},{8,11},{9,8},{10,9... | collective-permute-start | bytes 1572872 | tf_op jit(solution)/shard_map/ppermute | solution.py:20
  76.3 24.0 %collective-permute-start.4 = (bf16[512,512]{1,0:T(8,128)(2,1)}, bf16[512,512]{1,0:T(8,128)(2,1)}, u32[]{:S(2)}, u32[]{:S(2)}) collective-permute-start(bf16[512,512]{1,0:T(8,128)(2,1)} %fusion.42), channel_id=1, source_target_pairs={{0,2},{1,3},{2,0},{3,1},{4,6},{5,7},{6,4},{7,5},{8,10},{9,11},{10,... | collective-permute-start | bytes 1572872 | tf_op jit(solution)/shard_map/ppermute | solution.py:20
  78.1 26.3 %collective-permute-start.3 = (bf16[512,512]{1,0:T(8,128)(2,1)}, bf16[512,512]{1,0:T(8,128)(2,1)}, u32[]{:S(2)}, u32[]{:S(2)}) collective-permute-start(bf16[512,512]{1,0:T(8,128)(2,1)} %fusion.36), channel_id=1, source_target_pairs={{0,1},{1,2},{2,3},{3,0},{4,5},{5,6},{6,7},{7,4},{8,9},{9,10},{10,1... | collective-permute-start | bytes 1572872 | tf_op jit(solution)/shard_map/ppermute | solution.py:20
  79.0 12.1 %slice-start.4 = ((s8[5767168]{0:T(1024)(128)(4,1)}), s8[4194304]{0:T(1024)(128)(4,1)S(1)}, s32[]{:S(2)}) async-start(s8[5767168]{0:T(1024)(128)(4,1)} %bitcast.130), calls=%async_computation.8 | async-start | bytes 8388608
  92.1 19.6 %collective-permute-start.11 = (bf16[512,512]{1,0:T(8,128)(2,1)S(1)}, bf16[512,512]{1,0:T(8,128)(2,1)S(1)}, u32[]{:S(2)}, u32[]{:S(2)}) collective-permute-start(bf16[512,512]{1,0:T(8,128)(2,1)S(1)} %fusion.51), channel_id=1, source_target_pairs={{0,3},{1,0},{2,1},{3,2},{4,7},{5,4},{6,5},{7,6},{8,11},{9,8},{10,9... | collective-permute-start | bytes 1572872 | tf_op jit(solution)/shard_map/ppermute | solution.py:20
  96.4 16.7 %collective-permute-start.10 = (bf16[512,512]{1,0:T(8,128)(2,1)}, bf16[512,512]{1,0:T(8,128)(2,1)S(1)}, u32[]{:S(2)}, u32[]{:S(2)}) collective-permute-start(bf16[512,512]{1,0:T(8,128)(2,1)} %fusion.45), channel_id=1, source_target_pairs={{0,2},{1,3},{2,0},{3,1},{4,6},{5,7},{6,4},{7,5},{8,10},{9,11},{10,... | collective-permute-start | bytes 1572872 | tf_op jit(solution)/shard_map/ppermute | solution.py:20
  99.4 26.1 %collective-permute-start.9 = (bf16[512,512]{1,0:T(8,128)(2,1)}, bf16[512,512]{1,0:T(8,128)(2,1)}, u32[]{:S(2)}, u32[]{:S(2)}) collective-permute-start(bf16[512,512]{1,0:T(8,128)(2,1)} %fusion.39), channel_id=1, source_target_pairs={{0,1},{1,2},{2,3},{3,0},{4,5},{5,6},{6,7},{7,4},{8,9},{9,10},{10,1... | collective-permute-start | bytes 1572872 | tf_op jit(solution)/shard_map/ppermute | solution.py:20
  107.5 21.8 %all-to-all-start.1 = ((bf16[32,16,512]{2,1,0:T(8,128)(2,1)}), bf16[32,16,512]{2,1,0:T(8,128)(2,1)S(1)}, u32[]{:S(2)}, u32[]{:S(2)}) async-start(bf16[32,16,512]{2,1,0:T(8,128)(2,1)} %bitcast.12), calls=%async_computation.1 | async-start | bytes 1048576 | tf_op jit(solution)/shard_map/all_to_all | solution.py:107
  129.2 15.9 %all-to-all-start.3 = ((bf16[32,16,512]{2,1,0:T(8,128)(2,1)}), bf16[32,16,512]{2,1,0:T(8,128)(2,1)S(1)}, u32[]{:S(2)}, u32[]{:S(2)}) async-start(bf16[32,16,512]{2,1,0:T(8,128)(2,1)} %bitcast.16), calls=%async_computation.3 | async-start | bytes 1048576 | tf_op jit(solution)/shard_map/all_to_all | solution.py:107
  146.2 2.5 %collective-permute-start.14 = (f32[256]{0:T(256)S(1)}, f32[256]{0:T(256)S(1)}, u32[]{:S(2)}, u32[]{:S(2)}) collective-permute-start(f32[256]{0:T(256)S(1)} %get-tuple-element.18), channel_id=1, source_target_pairs={{0,3},{1,0},{2,1},{3,2},{4,7},{5,4},{6,5},{7,6},{8,11},{9,8},{10,9... | collective-permute-start | bytes 3080 | tf_op jit(solution)/shard_map/ppermute | solution.py:20
  146.7 3.9 %collective-permute-start.13 = (f32[256]{0:T(256)S(1)}, f32[256]{0:T(256)S(1)}, u32[]{:S(2)}, u32[]{:S(2)}) collective-permute-start(f32[256]{0:T(256)S(1)} %get-tuple-element.18), channel_id=1, source_target_pairs={{0,2},{1,3},{2,0},{3,1},{4,6},{5,7},{6,4},{7,5},{8,10},{9,11},{10,... | collective-permute-start | bytes 3080 | tf_op jit(solution)/shard_map/ppermute | solution.py:20
  146.7 4.7 %collective-permute-start.12 = (f32[256]{0:T(256)S(1)}, f32[256]{0:T(256)S(1)}, u32[]{:S(2)}, u32[]{:S(2)}) collective-permute-start(f32[256]{0:T(256)S(1)} %get-tuple-element.18), channel_id=1, source_target_pairs={{0,1},{1,2},{2,3},{3,0},{4,5},{5,6},{6,7},{7,4},{8,9},{9,10},{10,1... | collective-permute-start | bytes 3080 | tf_op jit(solution)/shard_map/ppermute | solution.py:20
  (8 other events, 48.2 us)

commit v13 on v12

--- a/solution.py
+++ b/solution.py
@@ -27,12 +27,24 @@
     return jnp.take(stacked, (me - jnp.arange(tp_count)) % tp_count, axis=0)
 
 
-def gather_tp(value, tp_count):
+def gather_tp(value, tp_count, known=None):
     me = lax.axis_index("tp")
     rows, cols = value.shape
     whole = jnp.zeros((rows, tp_count * cols), value.dtype)
     for s in range(tp_count):
-        part = value if s == 0 else shift_tp(value, s, tp_count)
+        part = (known or {}).get(s)
+        if part is None:
+            part = value if s == 0 else shift_tp(value, s, tp_count)
+        whole = lax.dynamic_update_slice_in_dim(whole, part, ((me - s) % tp_count) * cols, axis=1)
+    return whole
+
+
+def gather_pair_tp(pair, cols, tp_count):
+    me = lax.axis_index("tp")
+    own = pair[:, :cols]
+    parts = {0: own, 2: pair[:, cols:], 1: shift_tp(own, 1, tp_count), 3: shift_tp(own, 3, tp_count)}
+    whole = jnp.zeros((pair.shape[0], tp_count * cols), pair.dtype)
+    for s, part in parts.items():
         whole = lax.dynamic_update_slice_in_dim(whole, part, ((me - s) % tp_count) * cols, axis=1)
     return whole
 
@@ -68,7 +80,10 @@
     slot_count = CAP // copies
     chunk_items = slot_count // CHUNKS
     stream = hidden.astype(jnp.float32)
-    whole_rows = gather_tp(hidden, tp_count).astype(jnp.float32)
+    me = lax.axis_index("tp")
+    half_turn = tp_count // 2
+    far = shift_tp(hidden, half_turn, tp_count) if tp_count == 4 else None
+    whole_rows = gather_tp(hidden, tp_count, {half_turn: far}).astype(jnp.float32)
     normed_in = rms_norm(whole_rows, pre_gain).astype(jnp.bfloat16)
     top = routes.shape[1]
     chosen = routes.reshape(-1)
@@ -88,7 +103,8 @@
             hit = (slot_ids[:, None] == chunk_pairs[None, :, k]) & (owner_pairs[None, :, k] == c)
             dispatch = dispatch | hit
         relay = c == 0
-        source = hidden if relay else normed_in
+        source = hidden if far is None else jnp.concatenate([hidden, far], axis=1)
+        source = source if relay else normed_in
         outgoing = jnp.dot(
             dispatch.astype(jnp.bfloat16), source, preferred_element_type=jnp.float32
         ).astype(jnp.bfloat16)
@@ -97,8 +113,11 @@
         sources, items, widths = pieces.shape
         flat_rows = pieces.reshape(sources * items, widths)
         if relay:
-            raw_rows = gather_tp(flat_rows, tp_count).astype(jnp.float32)
-            flat_rows = rms_norm(raw_rows, pre_gain).astype(jnp.bfloat16)
+            if far is not None:
+                raw_rows = gather_pair_tp(flat_rows, col_part, tp_count)
+            else:
+                raw_rows = gather_tp(flat_rows, tp_count)
+            flat_rows = rms_norm(raw_rows.astype(jnp.float32), pre_gain).astype(jnp.bfloat16)
         gate_val = jnp.dot(flat_rows, gate_weight[0], preferred_element_type=jnp.float32)
         up_val = jnp.dot(flat_rows, up_weight[0], preferred_element_type=jnp.float32)
         activ = (jax.nn.silu(gate_val) * up_val).astype(jnp.bfloat16)

time: 154 us -> 152 us (0.987)
  waiting for transfers between devices: 59.7 us -> 55.4 us
  starting transfers between devices: 38.3 us -> 40.1 us
    ppermute x15 -> x14, waiting for transfers between devices: 38.1 us -> 25.4 us  [shift_tp(): lax.ppermute(value, 'tp', [(j, (j + step) % tp_count) for j in range(tp_c...]
    all_to_all x2, waiting for transfers between devices: 10.9 us -> 19.3 us  [shards(): lax.all_to_all(outgoing, 'req', split_axis=0, concat_axis=0, tiled=True)]
    dynamic_update_slice x8 -> x4, local copies, waits for them, and re-layouts: 2.45 us -> 0.11 us  [gather_tp(): lax.dynamic_update_slice_in_dim(whole, part, (me - s) % tp_count * cols,...]
    dynamic_update_slice x0 -> x3, local copies, waits for them, and re-layouts: none -> 2.25 us  [gather_pair_tp(): lax.dynamic_update_slice_in_dim(whole, part, (me - s) % tp_count * cols,...]
    all_to_all x2, starting transfers between devices: 13.6 us -> 15.5 us  [shards(): lax.all_to_all(outgoing, 'req', split_axis=0, concat_axis=0, tiled=True)]
    ppermute x15 -> x14, starting transfers between devices: 16.3 us -> 15.8 us  [shift_tp(): lax.ppermute(value, 'tp', [(j, (j + step) % tp_count) for j in range(tp_c...]
  transfers between devices with their start and end apart: 19 -> 18, of which waited for: 9 -> 10; matrix products, arithmetic and copies ran while one was open for 33% -> 33% of each run, Pallas kernels for 0% -> 0%
where the time goes in v13:
time: 152 us; the launch traced here: 151 us
  waiting for transfers between devices  55.4 us (36%)
  matrix products  44.5 us (29%)
  starting transfers between devices  40.1 us (26%)
  local copies, waits for them, and re-layouts  5.86 us (4%)
  other arithmetic  3.78 us (2%)
    ppermute x14, waiting for transfers between devices, shift_tp(): lax.ppermute(value, 'tp', [(j, (j + step) % tp_count) for j in range(tp_c...  25.4 us
    all_to_all x2, waiting for transfers between devices, shards(): lax.all_to_all(outgoing, 'req', split_axis=0, concat_axis=0, tiled=True)  19.3 us
    dot_general x8, matrix products, down_scatter_sum_tp(): jnp.dot(activ, w_block, preferred_element_type=jnp.float32)  16.5 us
    ppermute x14, starting transfers between devices, shift_tp(): lax.ppermute(value, 'tp', [(j, (j + step) % tp_count) for j in range(tp_c...  15.8 us
    all_to_all x2, starting transfers between devices, shards(): lax.all_to_all(outgoing, 'req', split_axis=0, concat_axis=0, tiled=True)  15.5 us
    dot_general x2, matrix products, shards(): jnp.dot(flat_rows, gate_weight[0], preferred_element_type=jnp.float32)  12.6 us
    all_to_all x2, waiting for transfers between devices, shards(): lax.all_to_all(summed, 'req', split_axis=0, concat_axis=0, tiled=True)  10.7 us
    all_to_all x2, starting transfers between devices, shards(): lax.all_to_all(summed, 'req', split_axis=0, concat_axis=0, tiled=True)  8.83 us
  transfers between devices with their start and end apart: 18, of which 10 were waited for; matrix products, arithmetic and copies ran while one was open for 33% of the time, Pallas kernels for 0%

profile of v13, /device:TPU:1, one launch (start us, length us, event | category | flops | bytes accessed | tf_op | source)
XLA Modules:
  0.0 150.9 jit_solution(5467083299984024544)
XLA Ops:
  0.6 3.8 %collective-permute-start = (bf16[256,512]{1,0:T(8,128)(2,1)}, bf16[256,512]{1,0:T(8,128)(2,1)S(1)}, u32[]{:S(2)}, u32[]{:S(2)}) collective-permute-start(bf16[256,512]{1,0:T(8,128)(2,1)} %param.8), channel_id=1, source_target_pairs={{0,2},{1,3},{2,0},{3,1},{4,6},{5,7},{6,4},{7,5},{8,10},{9,11},{10,... | collective-permute-start | bytes 786440 | tf_op jit(solution)/shard_map/ppermute | solution.py:20
  4.8 2.3 %collective-permute-start.7 = (bf16[256,512]{1,0:T(8,128)(2,1)}, bf16[256,512]{1,0:T(8,128)(2,1)S(1)}, u32[]{:S(2)}, u32[]{:S(2)}) collective-permute-start(bf16[256,512]{1,0:T(8,128)(2,1)} %param.8), channel_id=1, source_target_pairs={{0,3},{1,0},{2,1},{3,2},{4,7},{5,4},{6,5},{7,6},{8,11},{9,8},{10,9... | collective-permute-start | bytes 786440 | tf_op jit(solution)/shard_map/ppermute | solution.py:20
  10.8 2.4 %convolution_convert_fusion.1 = bf16[512,1024]{1,0:T(8,128)(2,1)} fusion(bf16[256,512]{1,0:T(8,128)(2,1)S(1)} %collective-permute-done, bf16[256,512]{1,0:T(8,128)(2,1)} %param.8, s32[256]{0:T(256)S(1)} %bitcast.111, s32[256]{0:T(256)S(1)} %bitcast.105, pred[256]{0:T(512)(128)(4,1)S(1)} %get-tuple-element.5, pred[256]{0:T(512)(128)(4,1)S(1)} %get-tuple-element.4), kind=kOutput, calls=%fused_computation.23 | convolution fusion | flops 270663680 | bytes 1575424 | tf_op jit(solution)/shard_map/dot_general | solution.py:108
  13.2 10.5 %all-to-all-start = ((bf16[32,16,1024]{2,1,0:T(8,128)(2,1)}), bf16[32,16,1024]{2,1,0:T(8,128)(2,1)S(1)}, u32[]{:S(2)}, u32[]{:S(2)}) async-start(bf16[32,16,1024]{2,1,0:T(8,128)(2,1)} %bitcast.4), calls=%async_computation | async-start | bytes 2097152 | tf_op jit(solution)/shard_map/all_to_all | solution.py:112
  24.4 16.1 %all-to-all-done = bf16[32,16,1024]{2,1,0:T(8,128)(2,1)S(1)} async-done(((bf16[32,16,1024]{2,1,0:T(8,128)(2,1)}), bf16[32,16,1024]{2,1,0:T(8,128)(2,1)S(1)}, u32[]{:S(2)}, u32[]{:S(2)}) %all-to-all-start) | async-done | bytes 1048608 | tf_op jit(solution)/shard_map/all_to_all | solution.py:112
  44.5 2.2 %convolution_convert_fusion = bf16[512,2048]{1,0:T(8,128)(2,1)} fusion(bf16[256,2048]{1,0:T(8,128)(2,1)S(1)} %copy-done.1, f32[2048]{0:T(1024)S(1)} %copy-done.5, f32[256]{0:T(256)S(1)} %add_rsqrt_fusion.2, s32[256]{0:T(256)S(1)} %bitcast.112, s32[256]{0:T(256)S(1)} %bitcast.106, pred[256]{0:T(512)(128)(4,1)S(1)} %get-tuple-element.3, ...), kind=kOutput, calls=%fused_computation.15 | convolution fusion | flops 540672000 | bytes 3157504 | tf_op jit(solution)/shard_map/dot_general | solution.py:108
  46.7 5.0 %all-to-all-start.2 = ((bf16[32,16,2048]{2,1,0:T(8,128)(2,1)}), bf16[32,16,2048]{2,1,0:T(8,128)(2,1)}, u32[]{:S(2)}, u32[]{:S(2)}) async-start(bf16[32,16,2048]{2,1,0:T(8,128)(2,1)} %bitcast.99), calls=%async_computation.2 | async-start | bytes 4194304 | tf_op jit(solution)/shard_map/all_to_all | solution.py:112
  51.8 5.0 %collective-permute-done.1 = bf16[512,512]{1,0:T(8,128)(2,1)} collective-permute-done((bf16[512,512]{1,0:T(8,128)(2,1)}, bf16[512,512]{1,0:T(8,128)(2,1)}, u32[]{:S(2)}, u32[]{:S(2)}) %collective-permute-start.1) | collective-permute-done | bytes 524320 | tf_op jit(solution)/shard_map/ppermute | solution.py:20
  59.6 6.1 %fusion.6 = f32[512,1408]{1,0:T(8,128)S(1)} fusion(bf16[1,2048,1408]{2,1,0:T(8,128)(2,1)} %param.13, bf16[512,2048]{1,0:T(8,128)(2,1)S(1)} %constant_dynamic-update-slice_fusion.4, f32[2048]{0:T(1024)S(1)} %copy-done.5, f32[512]{0:T(512)S(1)} %add_rsqrt_fusion), kind=kOutput, calls=%fused_computation.7 | convolution fusion | flops 2956984320 | bytes 10758144 | tf_op jit(solution)/shard_map/dot_general | solution.py:121
  65.7 3.5 %multiply_convert_fusion = bf16[512,1408]{1,0:T(8,128)(2,1)S(1)} fusion(f32[512,1408]{1,0:T(8,128)S(1)} %fusion.6, bf16[1,2048,1408]{2,1,0:T(8,128)(2,1)S(1)} %bitcast.122, bf16[512,2048]{1,0:T(8,128)(2,1)S(1)} %constant_dynamic-update-slice_fusion.4, f32[2048]{0:T(1024)S(1)} %copy-done.5, f32[512]{0:T(512)S(1)} %add_rsqrt_fusion), kind=kOutput, calls=%fused_computation.17 | convolution fusion | flops 2961309696 | bytes 12199936 | tf_op jit(solution)/shard_map/dot_general | solution.py:122
  74.6 1.8 %fusion.36 = bf16[512,512]{1,0:T(8,128)(2,1)} fusion(bf16[512,1408]{1,0:T(8,128)(2,1)S(1)} %multiply_convert_fusion, bf16[1,1408,2048]{2,1,0:T(8,128)(2,1)S(1)} %bitcast.126, s32[]{:T(128)S(6)} %select_n.179), kind=kOutput, calls=%fused_computation.40 | convolution fusion | flops 738459648 | bytes 3407876 | tf_op jit(solution)/shard_map/dot_general | solution.py:66
  77.1 3.1 %all-to-all-done.2 = bf16[32,16,2048]{2,1,0:T(8,128)(2,1)} async-done(((bf16[32,16,2048]{2,1,0:T(8,128)(2,1)}), bf16[32,16,2048]{2,1,0:T(8,128)(2,1)}, u32[]{:S(2)}, u32[]{:S(2)}) %all-to-all-start.2) | async-done | bytes 2097184 | tf_op jit(solution)/shard_map/all_to_all | solution.py:112
  80.2 6.5 %fusion.4 = f32[512,1408]{1,0:T(8,128)S(1)} fusion(bf16[512,2048]{1,0:T(8,128)(2,1)} %bitcast.15, bf16[1,2048,1408]{2,1,0:T(8,128)(2,1)} %param.13), kind=kOutput, calls=%fused_computation.5 | convolution fusion | flops 2952790016 | bytes 10747904 | tf_op jit(solution)/shard_map/dot_general | solution.py:121
  86.8 5.2 %fusion.14 = bf16[512,1408]{1,0:T(8,128)(2,1)S(1)} fusion(bf16[512,2048]{1,0:T(8,128)(2,1)} %bitcast.15, bf16[1,2048,1408]{2,1,0:T(8,128)(2,1)S(1)} %bitcast.124, f32[512,1408]{1,0:T(8,128)S(1)} %fusion.4), kind=kOutput, calls=%fused_computation.16 | convolution fusion | flops 2957115392 | bytes 12189696 | tf_op jit(solution)/shard_map/dot_general | solution.py:122
  96.7 1.8 %fusion.39 = bf16[512,512]{1,0:T(8,128)(2,1)} fusion(bf16[512,1408]{1,0:T(8,128)(2,1)S(1)} %fusion.14, bf16[1,1408,2048]{2,1,0:T(8,128)(2,1)S(1)} %bitcast.128, s32[]{:T(128)S(6)} %select_n.179), kind=kOutput, calls=%fused_computation.41 | convolution fusion | flops 738459648 | bytes 3407876 | tf_op jit(solution)/shard_map/dot_general | solution.py:66
  99.1 2.2 %collective-permute-done.3 = bf16[512,512]{1,0:T(8,128)(2,1)} collective-permute-done((bf16[512,512]{1,0:T(8,128)(2,1)}, bf16[512,512]{1,0:T(8,128)(2,1)}, u32[]{:S(2)}, u32[]{:S(2)}) %collective-permute-start.3) | collective-permute-done | bytes 524320 | tf_op jit(solution)/shard_map/ppermute | solution.py:20
  101.3 2.9 %add_convert_fusion.1 = bf16[512,512]{1,0:T(8,128)(2,1)} fusion(bf16[512,512]{1,0:T(8,128)(2,1)S(1)} %collective-permute-done.5, bf16[512,512]{1,0:T(8,128)(2,1)S(1)} %collective-permute-done.4, bf16[512,512]{1,0:T(8,128)(2,1)} %collective-permute-done.3, bf16[512,1408]{1,0:T(8,128)(2,1)S(1)} %copy-done.8, bf16[1,1408,2048]{2,1,0:T(8,128)(2,1)S(1)} %bitcast.128, ...), kind=kOutput, calls=%fused_computation.65 | convolution fusion | flops 740556800 | bytes 4980740 | tf_op jit(solution)/shard_map/dot_general | solution.py:66
  104.2 4.8 %all-to-all-start.1 = ((bf16[32,16,512]{2,1,0:T(8,128)(2,1)}), bf16[32,16,512]{2,1,0:T(8,128)(2,1)S(1)}, u32[]{:S(2)}, u32[]{:S(2)}) async-start(bf16[32,16,512]{2,1,0:T(8,128)(2,1)} %bitcast.12), calls=%async_computation.1 | async-start | bytes 1048576 | tf_op jit(solution)/shard_map/all_to_all | solution.py:126
  109.1 2.1 %collective-permute-done.9 = bf16[512,512]{1,0:T(8,128)(2,1)S(1)} collective-permute-done((bf16[512,512]{1,0:T(8,128)(2,1)}, bf16[512,512]{1,0:T(8,128)(2,1)S(1)}, u32[]{:S(2)}, u32[]{:S(2)}) %collective-permute-start.9) | collective-permute-done | bytes 524320 | tf_op jit(solution)/shard_map/ppermute | solution.py:20
  111.2 12.4 %collective-permute-done.8 = bf16[512,512]{1,0:T(8,128)(2,1)} collective-permute-done((bf16[512,512]{1,0:T(8,128)(2,1)}, bf16[512,512]{1,0:T(8,128)(2,1)}, u32[]{:S(2)}, u32[]{:S(2)}) %collective-permute-start.8) | collective-permute-done | bytes 524320 | tf_op jit(solution)/shard_map/ppermute | solution.py:20
  123.6 3.7 %add_convert_fusion = bf16[512,512]{1,0:T(8,128)(2,1)} fusion(bf16[512,512]{1,0:T(8,128)(2,1)S(1)} %collective-permute-done.10, bf16[512,512]{1,0:T(8,128)(2,1)S(1)} %collective-permute-done.9, bf16[512,512]{1,0:T(8,128)(2,1)} %collective-permute-done.8, bf16[512,1408]{1,0:T(8,128)(2,1)} %copy-done.6, bf16[1,1408,2048]{2,1,0:T(8,128)(2,1)} %param.15, ...), kind=kOutput, calls=%fused_computation.62 | convolution fusion | flops 740556800 | bytes 4980740 | tf_op jit(solution)/shard_map/dot_general | solution.py:66
  127.4 4.0 %all-to-all-start.3 = ((bf16[32,16,512]{2,1,0:T(8,128)(2,1)}), bf16[32,16,512]{2,1,0:T(8,128)(2,1)S(1)}, u32[]{:S(2)}, u32[]{:S(2)}) async-start(bf16[32,16,512]{2,1,0:T(8,128)(2,1)} %bitcast.16), calls=%async_computation.3 | async-start | bytes 1048576 | tf_op jit(solution)/shard_map/all_to_all | solution.py:126
  132.4 10.7 %all-to-all-done.3 = bf16[32,16,512]{2,1,0:T(8,128)(2,1)S(1)} async-done(((bf16[32,16,512]{2,1,0:T(8,128)(2,1)}), bf16[32,16,512]{2,1,0:T(8,128)(2,1)S(1)}, u32[]{:S(2)}, u32[]{:S(2)}) %all-to-all-start.3) | async-done | bytes 524320 | tf_op jit(solution)/shard_map/all_to_all | solution.py:126
  146.7 1.8 %collective-permute-done.12 = f32[256]{0:T(256)S(1)} collective-permute-done((f32[256]{0:T(256)S(1)}, f32[256]{0:T(256)S(1)}, u32[]{:S(2)}, u32[]{:S(2)}) %collective-permute-start.12) | collective-permute-done | bytes 1056 | tf_op jit(solution)/shard_map/ppermute | solution.py:20
  (107 shorter events, 29.5 us)
Async XLA Ops:
  0.6 10.1 %collective-permute-start = (bf16[256,512]{1,0:T(8,128)(2,1)}, bf16[256,512]{1,0:T(8,128)(2,1)S(1)}, u32[]{:S(2)}, u32[]{:S(2)}) collective-permute-start(bf16[256,512]{1,0:T(8,128)(2,1)} %param.8), channel_id=1, source_target_pairs={{0,2},{1,3},{2,0},{3,1},{4,6},{5,7},{6,4},{7,5},{8,10},{9,11},{10,... | collective-permute-start | bytes 786440 | tf_op jit(solution)/shard_map/ppermute | solution.py:20
  4.5 19.6 %collective-permute-start.6 = (bf16[256,512]{1,0:T(8,128)(2,1)}, bf16[256,512]{1,0:T(8,128)(2,1)S(1)}, u32[]{:S(2)}, u32[]{:S(2)}) collective-permute-start(bf16[256,512]{1,0:T(8,128)(2,1)} %param.8), channel_id=1, source_target_pairs={{0,1},{1,2},{2,3},{3,0},{4,5},{5,6},{6,7},{7,4},{8,9},{9,10},{10,1... | collective-permute-start | bytes 786440 | tf_op jit(solution)/shard_map/ppermute | solution.py:20
  4.8 19.2 %collective-permute-start.7 = (bf16[256,512]{1,0:T(8,128)(2,1)}, bf16[256,512]{1,0:T(8,128)(2,1)S(1)}, u32[]{:S(2)}, u32[]{:S(2)}) collective-permute-start(bf16[256,512]{1,0:T(8,128)(2,1)} %param.8), channel_id=1, source_target_pairs={{0,3},{1,0},{2,1},{3,2},{4,7},{5,4},{6,5},{7,6},{8,11},{9,8},{10,9... | collective-permute-start | bytes 786440 | tf_op jit(solution)/shard_map/ppermute | solution.py:20
  10.8 12.9 %copy-start.4 = (f32[256,2]{0,1:T(2,128)S(1)}, f32[256,2]{0,1:T(2,128)}, u32[]{:S(2)}) copy-start(f32[256,2]{0,1:T(2,128)} %param.10) | copy-start | bytes 6148
  13.2 10.6 %copy-start.2 = (bf16[256,512]{1,0:T(8,128)(2,1)S(1)}, bf16[256,512]{1,0:T(8,128)(2,1)}, u32[]{:S(2)}) copy-start(bf16[256,512]{1,0:T(8,128)(2,1)} %param.8) | copy-start | bytes 786436
  13.2 27.4 %all-to-all-start = ((bf16[32,16,1024]{2,1,0:T(8,128)(2,1)}), bf16[32,16,1024]{2,1,0:T(8,128)(2,1)S(1)}, u32[]{:S(2)}, u32[]{:S(2)}) async-start(bf16[32,16,1024]{2,1,0:T(8,128)(2,1)} %bitcast.4), calls=%async_computation | async-start | bytes 2097152 | tf_op jit(solution)/shard_map/all_to_all | solution.py:112
  24.1 16.5 %copy-start = (bf16[256,2048]{1,0:T(8,128)(2,1)}, bf16[256,2048]{1,0:T(8,128)(2,1)S(1)}, u32[]{:S(2)}) copy-start(bf16[256,2048]{1,0:T(8,128)(2,1)S(1)} %constant_dynamic-update-slice_fusion) | copy-start | bytes 3145732
  24.4 20.1 %copy-start.5 = (f32[2048]{0:T(1024)S(1)}, f32[2048]{0:T(1024)}, u32[]{:S(2)}) copy-start(f32[2048]{0:T(1024)} %param.11) | copy-start | bytes 24580
  41.8 15.0 %collective-permute-start.1 = (bf16[512,512]{1,0:T(8,128)(2,1)}, bf16[512,512]{1,0:T(8,128)(2,1)}, u32[]{:S(2)}, u32[]{:S(2)}) collective-permute-start(bf16[512,512]{1,0:T(8,128)(2,1)} %get-tuple-element.14), channel_id=1, source_target_pairs={{0,1},{1,2},{2,3},{3,0},{4,5},{5,6},{6,7},{7,4},{8,9},{9,10},{10,1... | collective-permute-start | bytes 1572872 | tf_op jit(solution)/shard_map/ppermute | solution.py:20
  43.1 14.8 %collective-permute-start.2 = (bf16[512,512]{1,0:T(8,128)(2,1)}, bf16[512,512]{1,0:T(8,128)(2,1)}, u32[]{:S(2)}, u32[]{:S(2)}) collective-permute-start(bf16[512,512]{1,0:T(8,128)(2,1)} %get-tuple-element.14), channel_id=1, source_target_pairs={{0,3},{1,0},{2,1},{3,2},{4,7},{5,4},{6,5},{7,6},{8,11},{9,8},{10,9... | collective-permute-start | bytes 1572872 | tf_op jit(solution)/shard_map/ppermute | solution.py:20
  46.7 33.4 %all-to-all-start.2 = ((bf16[32,16,2048]{2,1,0:T(8,128)(2,1)}), bf16[32,16,2048]{2,1,0:T(8,128)(2,1)}, u32[]{:S(2)}, u32[]{:S(2)}) async-start(bf16[32,16,2048]{2,1,0:T(8,128)(2,1)} %bitcast.99), calls=%async_computation.2 | async-start | bytes 4194304 | tf_op jit(solution)/shard_map/all_to_all | solution.py:112
  71.1 27.4 %collective-permute-start.5 = (bf16[512,512]{1,0:T(8,128)(2,1)}, bf16[512,512]{1,0:T(8,128)(2,1)S(1)}, u32[]{:S(2)}, u32[]{:S(2)}) collective-permute-start(bf16[512,512]{1,0:T(8,128)(2,1)} %fusion.48), channel_id=1, source_target_pairs={{0,3},{1,0},{2,1},{3,2},{4,7},{5,4},{6,5},{7,6},{8,11},{9,8},{10,9... | collective-permute-start | bytes 1572872 | tf_op jit(solution)/shard_map/ppermute | solution.py:20
  74.2 24.9 %collective-permute-start.4 = (bf16[512,512]{1,0:T(8,128)(2,1)}, bf16[512,512]{1,0:T(8,128)(2,1)S(1)}, u32[]{:S(2)}, u32[]{:S(2)}) collective-permute-start(bf16[512,512]{1,0:T(8,128)(2,1)} %fusion.42), channel_id=1, source_target_pairs={{0,2},{1,3},{2,0},{3,1},{4,6},{5,7},{6,4},{7,5},{8,10},{9,11},{10,... | collective-permute-start | bytes 1572872 | tf_op jit(solution)/shard_map/ppermute | solution.py:20
  74.6 12.1 %slice-start.2 = ((s8[5767168]{0:T(1024)(128)(4,1)}), s8[1572864]{0:T(1024)(128)(4,1)S(1)}, s32[]{:S(2)}) async-start(s8[5767168]{0:T(1024)(128)(4,1)} %bitcast.123), calls=%async_computation.6 | async-start | bytes 3145728
  76.4 24.9 %collective-permute-start.3 = (bf16[512,512]{1,0:T(8,128)(2,1)}, bf16[512,512]{1,0:T(8,128)(2,1)}, u32[]{:S(2)}, u32[]{:S(2)}) collective-permute-start(bf16[512,512]{1,0:T(8,128)(2,1)} %fusion.36), channel_id=1, source_target_pairs={{0,1},{1,2},{2,3},{3,0},{4,5},{5,6},{6,7},{7,4},{8,9},{9,10},{10,1... | collective-permute-start | bytes 1572872 | tf_op jit(solution)/shard_map/ppermute | solution.py:20
  80.2 11.7 %slice-start.6 = ((s8[5767168]{0:T(1024)(128)(4,1)}), s8[4194304]{0:T(1024)(128)(4,1)S(1)}, s32[]{:S(2)}) async-start(s8[5767168]{0:T(1024)(128)(4,1)} %bitcast.127), calls=%async_computation.10 | async-start | bytes 8388608
  93.0 16.1 %collective-permute-start.10 = (bf16[512,512]{1,0:T(8,128)(2,1)S(1)}, bf16[512,512]{1,0:T(8,128)(2,1)S(1)}, u32[]{:S(2)}, u32[]{:S(2)}) collective-permute-start(bf16[512,512]{1,0:T(8,128)(2,1)S(1)} %fusion.51), channel_id=1, source_target_pairs={{0,3},{1,0},{2,1},{3,2},{4,7},{5,4},{6,5},{7,6},{8,11},{9,8},{10,9... | collective-permute-start | bytes 1572872 | tf_op jit(solution)/shard_map/ppermute | solution.py:20
  96.3 14.9 %collective-permute-start.9 = (bf16[512,512]{1,0:T(8,128)(2,1)}, bf16[512,512]{1,0:T(8,128)(2,1)S(1)}, u32[]{:S(2)}, u32[]{:S(2)}) collective-permute-start(bf16[512,512]{1,0:T(8,128)(2,1)} %fusion.45), channel_id=1, source_target_pairs={{0,2},{1,3},{2,0},{3,1},{4,6},{5,7},{6,4},{7,5},{8,10},{9,11},{10,... | collective-permute-start | bytes 1572872 | tf_op jit(solution)/shard_map/ppermute | solution.py:20
  98.5 25.2 %collective-permute-start.8 = (bf16[512,512]{1,0:T(8,128)(2,1)}, bf16[512,512]{1,0:T(8,128)(2,1)}, u32[]{:S(2)}, u32[]{:S(2)}) collective-permute-start(bf16[512,512]{1,0:T(8,128)(2,1)} %fusion.39), channel_id=1, source_target_pairs={{0,1},{1,2},{2,3},{3,0},{4,5},{5,6},{6,7},{7,4},{8,9},{9,10},{10,1... | collective-permute-start | bytes 1572872 | tf_op jit(solution)/shard_map/ppermute | solution.py:20
  104.2 23.2 %all-to-all-start.1 = ((bf16[32,16,512]{2,1,0:T(8,128)(2,1)}), bf16[32,16,512]{2,1,0:T(8,128)(2,1)S(1)}, u32[]{:S(2)}, u32[]{:S(2)}) async-start(bf16[32,16,512]{2,1,0:T(8,128)(2,1)} %bitcast.12), calls=%async_computation.1 | async-start | bytes 1048576 | tf_op jit(solution)/shard_map/all_to_all | solution.py:126
  127.4 15.8 %all-to-all-start.3 = ((bf16[32,16,512]{2,1,0:T(8,128)(2,1)}), bf16[32,16,512]{2,1,0:T(8,128)(2,1)S(1)}, u32[]{:S(2)}, u32[]{:S(2)}) async-start(bf16[32,16,512]{2,1,0:T(8,128)(2,1)} %bitcast.16), calls=%async_computation.3 | async-start | bytes 1048576 | tf_op jit(solution)/shard_map/all_to_all | solution.py:126
  144.2 2.5 %collective-permute-start.13 = (f32[256]{0:T(256)S(1)}, f32[256]{0:T(256)S(1)}, u32[]{:S(2)}, u32[]{:S(2)}) collective-permute-start(f32[256]{0:T(256)S(1)} %get-tuple-element.20), channel_id=1, source_target_pairs={{0,3},{1,0},{2,1},{3,2},{4,7},{5,4},{6,5},{7,6},{8,11},{9,8},{10,9... | collective-permute-start | bytes 3080 | tf_op jit(solution)/shard_map/ppermute | solution.py:20
  144.6 3.9 %collective-permute-start.12 = (f32[256]{0:T(256)S(1)}, f32[256]{0:T(256)S(1)}, u32[]{:S(2)}, u32[]{:S(2)}) collective-permute-start(f32[256]{0:T(256)S(1)} %get-tuple-element.20), channel_id=1, source_target_pairs={{0,2},{1,3},{2,0},{3,1},{4,6},{5,7},{6,4},{7,5},{8,10},{9,11},{10,... | collective-permute-start | bytes 3080 | tf_op jit(solution)/shard_map/ppermute | solution.py:20
  145.0 4.4 %collective-permute-start.11 = (f32[256]{0:T(256)S(1)}, f32[256]{0:T(256)S(1)}, u32[]{:S(2)}, u32[]{:S(2)}) collective-permute-start(f32[256]{0:T(256)S(1)} %get-tuple-element.20), channel_id=1, source_target_pairs={{0,1},{1,2},{2,3},{3,0},{4,5},{5,6},{6,7},{7,4},{8,9},{9,10},{10,1... | collective-permute-start | bytes 3080 | tf_op jit(solution)/shard_map/ppermute | solution.py:20
  (11 other events, 65.4 us)

commit v14 on v13

--- a/solution.py
+++ b/solution.py
@@ -78,7 +78,9 @@
     full_width = col_part * tp_count
     copies = req_count // E
     slot_count = CAP // copies
-    chunk_items = slot_count // CHUNKS
+    first_items = slot_count * 3 // 8
+    chunk_sizes = [first_items, slot_count - first_items]
+    chunk_starts = [0, first_items]
     stream = hidden.astype(jnp.float32)
     me = lax.axis_index("tp")
     half_turn = tp_count // 2
@@ -91,13 +93,16 @@
     slot_rank = jnp.sum((jnp.cumsum(onehot, axis=0) - 1) * onehot, axis=1)
     dest = (slot_rank % copies) * E + chosen
     item = slot_rank // copies
-    chunk_of = item // chunk_items
-    in_chunk = dest * chunk_items + item % chunk_items
+    chunk_of = (item >= chunk_starts[1]).astype(jnp.int32)
+    in_chunk = jnp.where(
+        chunk_of == 0, dest * chunk_sizes[0] + item, dest * chunk_sizes[1] + item - chunk_starts[1]
+    )
     chunk_pairs = in_chunk.reshape(row_count, top)
     owner_pairs = chunk_of.reshape(row_count, top)
-    slot_ids = jnp.arange(req_count * chunk_items, dtype=jnp.int32)
     returned = []
     for c in range(CHUNKS):
+        chunk_items = chunk_sizes[c]
+        slot_ids = jnp.arange(req_count * chunk_items, dtype=jnp.int32)
         dispatch = jnp.zeros((req_count * chunk_items, row_count), jnp.bool_)
         for k in range(top):
             hit = (slot_ids[:, None] == chunk_pairs[None, :, k]) & (owner_pairs[None, :, k] == c)
@@ -129,8 +134,9 @@
     weight_lo = (route_weights - weight_hi.astype(jnp.float32)).astype(jnp.bfloat16)
     total_stream = stream
     for c in range(CHUNKS):
-        combine_hi = jnp.zeros((row_count, req_count * chunk_items), jnp.bfloat16)
-        combine_lo = jnp.zeros((row_count, req_count * chunk_items), jnp.bfloat16)
+        slot_ids = jnp.arange(req_count * chunk_sizes[c], dtype=jnp.int32)
+        combine_hi = jnp.zeros((row_count, req_count * chunk_sizes[c]), jnp.bfloat16)
+        combine_lo = jnp.zeros((row_count, req_count * chunk_sizes[c]), jnp.bfloat16)
         for k in range(top):
             hit = (chunk_pairs[:, k][:, None] == slot_ids[None, :]) & (owner_pairs[:, k][:, None] == c)
             combine_hi = jnp.where(hit, weight_hi[:, k][:, None], combine_hi)

time: 152 us -> 192 us (1.26)
  waiting for transfers between devices: 55.4 us -> 73.8 us
  local copies, waits for them, and re-layouts: 5.86 us -> 21 us
  starting transfers between devices: 40.1 us -> 42.5 us
  matrix products: 44.5 us -> 46.7 us
    all_to_all x2, waiting for transfers between devices: 19.3 us -> 30.9 us  [shards(): lax.all_to_all(outgoing, 'req', split_axis=0, concat_axis=0, tiled=True)]
    reshape x0 -> x8, local copies, waits for them, and re-layouts: none -> 10.8 us  [the longest x2 6.31 us: shards(): outgoing = outgoing.reshape(req_count, chunk_items, source.shape[1])]
    ppermute x14, waiting for transfers between devices: 25.4 us -> 29.8 us  [shift_tp(): lax.ppermute(value, 'tp', [(j, (j + step) % tp_count) for j in range(tp_c...]
    dynamic_update_slice x3, local copies, waits for them, and re-layouts: 2.25 us -> 5.46 us  [gather_pair_tp(): lax.dynamic_update_slice_in_dim(whole, part, (me - s) % tp_count * cols,...]
    dot_general x2, matrix products: 8.66 us -> 11.5 us  [shards(): jnp.dot(flat_rows, up_weight[0], preferred_element_type=jnp.float32)]
    all_to_all x2, starting transfers between devices: 8.83 us -> 11.4 us  [shards(): lax.all_to_all(summed, 'req', split_axis=0, concat_axis=0, tiled=True)]
    all_to_all x2, waiting for transfers between devices: 10.7 us -> 13.1 us  [shards(): lax.all_to_all(summed, 'req', split_axis=0, concat_axis=0, tiled=True)]
  transfers between devices with their start and end apart: 18 -> 18, of which waited for: 10 -> 9; matrix products, arithmetic and copies ran while one was open for 33% -> 35% of each run, Pallas kernels for 0% -> 0%
where the time goes in v14:
time: 192 us; the launch traced here: 191 us
  waiting for transfers between devices  73.8 us (38%)
  matrix products  46.7 us (24%)
  starting transfers between devices  42.5 us (22%)
  local copies, waits for them, and re-layouts  21 us (11%)
  other arithmetic  5.24 us (3%)
    all_to_all x2, waiting for transfers between devices, shards(): lax.all_to_all(outgoing, 'req', split_axis=0, concat_axis=0, tiled=True)  30.9 us
    ppermute x14, waiting for transfers between devices, shift_tp(): lax.ppermute(value, 'tp', [(j, (j + step) % tp_count) for j in range(tp_c...  29.8 us
    ppermute x14, starting transfers between devices, shift_tp(): lax.ppermute(value, 'tp', [(j, (j + step) % tp_count) for j in range(tp_c...  17.1 us
    dot_general x8, matrix products, down_scatter_sum_tp(): jnp.dot(activ, w_block, preferred_element_type=jnp.float32)  15.3 us
    all_to_all x2, starting transfers between devices, shards(): lax.all_to_all(outgoing, 'req', split_axis=0, concat_axis=0, tiled=True)  14 us
    dot_general x2, matrix products, shards(): jnp.dot(flat_rows, gate_weight[0], preferred_element_type=jnp.float32)  13.9 us
    all_to_all x2, waiting for transfers between devices, shards(): lax.all_to_all(summed, 'req', split_axis=0, concat_axis=0, tiled=True)  13.1 us
    dot_general x2, matrix products, shards(): jnp.dot(flat_rows, up_weight[0], preferred_element_type=jnp.float32)  11.5 us
  transfers between devices with their start and end apart: 18, of which 9 were waited for; matrix products, arithmetic and copies ran while one was open for 35% of the time, Pallas kernels for 0%

profile of v14, /device:TPU:1, one launch (start us, length us, event | category | flops | bytes accessed | tf_op | source)
XLA Modules:
  0.0 190.6 jit_solution(1697394635200516138)
XLA Ops:
  0.6 2.2 %collective-permute-start.6 = (bf16[256,512]{1,0:T(8,128)(2,1)}, bf16[256,512]{1,0:T(8,128)(2,1)S(1)}, u32[]{:S(2)}, u32[]{:S(2)}) collective-permute-start(bf16[256,512]{1,0:T(8,128)(2,1)} %param.8), channel_id=1, source_target_pairs={{0,1},{1,2},{2,3},{3,0},{4,5},{5,6},{6,7},{7,4},{8,9},{9,10},{10,1... | collective-permute-start | bytes 786440 | tf_op jit(solution)/shard_map/ppermute | solution.py:20
  2.8 2.6 %collective-permute-start = (bf16[256,512]{1,0:T(8,128)(2,1)}, bf16[256,512]{1,0:T(8,128)(2,1)S(1)}, u32[]{:S(2)}, u32[]{:S(2)}) collective-permute-start(bf16[256,512]{1,0:T(8,128)(2,1)} %param.8), channel_id=1, source_target_pairs={{0,2},{1,3},{2,0},{3,1},{4,6},{5,7},{6,4},{7,5},{8,10},{9,11},{10,... | collective-permute-start | bytes 786440 | tf_op jit(solution)/shard_map/ppermute | solution.py:20
  10.2 6.8 %collective-permute-done = bf16[256,512]{1,0:T(8,128)(2,1)S(1)} collective-permute-done((bf16[256,512]{1,0:T(8,128)(2,1)}, bf16[256,512]{1,0:T(8,128)(2,1)S(1)}, u32[]{:S(2)}, u32[]{:S(2)}) %collective-permute-start) | collective-permute-done | bytes 262176 | tf_op jit(solution)/shard_map/ppermute | solution.py:20
  19.5 9.5 %all-to-all-start = ((bf16[32,12,1024]{2,1,0:T(8,128)(2,1)}), bf16[32,12,1024]{2,1,0:T(8,128)(2,1)S(1)}, u32[]{:S(2)}, u32[]{:S(2)}) async-start(bf16[32,12,1024]{2,1,0:T(8,128)(2,1)} %reshape.194), calls=%async_computation | async-start | bytes 2097152 | tf_op jit(solution)/shard_map/all_to_all | solution.py:117
  29.7 16.2 %all-to-all-done = bf16[32,12,1024]{2,1,0:T(8,128)(2,1)S(1)} async-done(((bf16[32,12,1024]{2,1,0:T(8,128)(2,1)}), bf16[32,12,1024]{2,1,0:T(8,128)(2,1)S(1)}, u32[]{:S(2)}, u32[]{:S(2)}) %all-to-all-start) | async-done | bytes 786464 | tf_op jit(solution)/shard_map/all_to_all | solution.py:117
  48.3 2.7 %collective-permute-start.2 = (bf16[384,512]{1,0:T(8,128)(2,1)S(1)}, bf16[384,512]{1,0:T(8,128)(2,1)}, u32[]{:S(2)}, u32[]{:S(2)}) collective-permute-start(bf16[384,512]{1,0:T(8,128)(2,1)S(1)} %get-tuple-element.14), channel_id=1, source_target_pairs={{0,3},{1,0},{2,1},{3,2},{4,7},{5,4},{6,5},{7,6},{8,11},{9,8},{10,9... | collective-permute-start | bytes 1179656 | tf_op jit(solution)/shard_map/ppermute | solution.py:20
  51.0 2.6 %convolution_convert_fusion = bf16[640,2048]{1,0:T(8,128)(2,1)} fusion(bf16[256,2048]{1,0:T(8,128)(2,1)S(1)} %constant_dynamic-update-slice_fusion, f32[2048]{0:T(1024)S(1)} %copy-done.10, f32[256]{0:T(256)S(1)} %add_rsqrt_fusion.2, s32[256]{0:T(256)S(1)} %bitcast.97, s32[256]{0:T(256)S(1)} %bitcast.91, pred[256]{0:T(512)(128)(4,1)S(1)} %get-tuple-element.3, ...), kind=kOutput, calls=%fused_computation.13 | convolution fusion | flops 675315712 | bytes 3681792 | tf_op jit(solution)/shard_map/dot_general | solution.py:113
  53.5 5.2 %reshape.198 = bf16[32,20,2048]{2,1,0:T(8,128)(2,1)} reshape(bf16[640,2048]{1,0:T(8,128)(2,1)} %convolution_convert_fusion) | data formatting | bytes 5242880 | tf_op jit(solution)/shard_map/reshape | solution.py:116
  58.7 4.5 %all-to-all-start.2 = ((bf16[32,20,2048]{2,1,0:T(8,128)(2,1)}), bf16[32,20,2048]{2,1,0:T(8,128)(2,1)S(1)}, u32[]{:S(2)}, u32[]{:S(2)}) async-start(bf16[32,20,2048]{2,1,0:T(8,128)(2,1)} %reshape.198), calls=%async_computation.2 | async-start | bytes 6291456 | tf_op jit(solution)/shard_map/all_to_all | solution.py:117
  70.7 5.9 %fusion.6 = f32[384,1408]{1,0:T(8,128)S(1)} fusion(bf16[1,2048,1408]{2,1,0:T(8,128)(2,1)} %param.13, bf16[384,2048]{1,0:T(8,128)(2,1)} %constant_dynamic-update-slice_fusion.4, f32[2048]{0:T(1024)S(1)} %copy-done.11, f32[384]{0:T(512)S(1)} %add_rsqrt_fusion), kind=kOutput, calls=%fused_computation.7 | convolution fusion | flops 2217738240 | bytes 9512448 | tf_op jit(solution)/shard_map/dot_general | solution.py:126
  76.6 4.3 %multiply_convert_fusion = bf16[384,1408]{1,0:T(8,128)(2,1)S(1)} fusion(f32[384,1408]{1,0:T(8,128)S(1)} %fusion.6, bf16[1,2048,1408]{2,1,0:T(8,128)(2,1)S(1)} %bitcast.107, bf16[384,2048]{1,0:T(8,128)(2,1)} %constant_dynamic-update-slice_fusion.4, f32[2048]{0:T(1024)S(1)} %copy-done.11, f32[384]{0:T(512)S(1)} %add_rsqrt_fusion), kind=kOutput, calls=%fused_computation.19 | convolution fusion | flops 2220982272 | bytes 10593792 | tf_op jit(solution)/shard_map/dot_general | solution.py:127
  88.3 14.7 %all-to-all-done.2 = bf16[32,20,2048]{2,1,0:T(8,128)(2,1)S(1)} async-done(((bf16[32,20,2048]{2,1,0:T(8,128)(2,1)}), bf16[32,20,2048]{2,1,0:T(8,128)(2,1)S(1)}, u32[]{:S(2)}, u32[]{:S(2)}) %all-to-all-start.2) | async-done | bytes 2621472 | tf_op jit(solution)/shard_map/all_to_all | solution.py:117
  103.0 2.2 %reshape.199 = bf16[640,2048]{1,0:T(8,128)(2,1)} reshape(bf16[32,20,2048]{2,1,0:T(8,128)(2,1)S(1)} %all-to-all-done.2) | data formatting | bytes 5242880 | tf_op jit(solution)/shard_map/reshape | solution.py:119
  105.2 8.0 %fusion.4 = f32[640,1408]{1,0:T(8,128)S(1)} fusion(bf16[640,2048]{1,0:T(8,128)(2,1)} %reshape.199, bf16[1,2048,1408]{2,1,0:T(8,128)(2,1)} %param.13), kind=kOutput, calls=%fused_computation.5 | convolution fusion | flops 3690987520 | bytes 11993088 | tf_op jit(solution)/shard_map/dot_general | solution.py:126
  113.3 7.2 %fusion.11 = bf16[640,1408]{1,0:T(8,128)(2,1)S(1)} fusion(bf16[640,2048]{1,0:T(8,128)(2,1)S(1)} %copy-done.1, bf16[1,2048,1408]{2,1,0:T(8,128)(2,1)} %param.14, f32[640,1408]{1,0:T(8,128)S(1)} %fusion.4), kind=kOutput, calls=%fused_computation.12 | convolution fusion | flops 3696394240 | bytes 13795328 | tf_op jit(solution)/shard_map/dot_general | solution.py:127
  120.5 2.1 %fusion.36 = bf16[640,512]{1,0:T(8,128)(2,1)} fusion(bf16[640,1408]{1,0:T(8,128)(2,1)S(1)} %fusion.11, bf16[1,1408,2048]{2,1,0:T(8,128)(2,1)S(1)} %bitcast.111, s32[]{:T(128)S(6)} %select_n.174), kind=kOutput, calls=%fused_computation.40 | convolution fusion | flops 923074560 | bytes 3899396 | tf_op jit(solution)/shard_map/dot_general | solution.py:66
  122.6 2.0 %fusion.39 = bf16[640,512]{1,0:T(8,128)(2,1)} fusion(bf16[640,1408]{1,0:T(8,128)(2,1)S(1)} %fusion.11, bf16[1,1408,2048]{2,1,0:T(8,128)(2,1)S(1)} %bitcast.111, s32[]{:T(128)S(6)} %select_n.176), kind=kOutput, calls=%fused_computation.41 | convolution fusion | flops 923074560 | bytes 3899396 | tf_op jit(solution)/shard_map/dot_general | solution.py:66
  128.6 2.0 %add_convert_fusion.1 = bf16[384,512]{1,0:T(8,128)(2,1)S(1)} fusion(bf16[384,512]{1,0:T(8,128)(2,1)} %collective-permute-done.5, bf16[384,512]{1,0:T(8,128)(2,1)} %collective-permute-done.4, bf16[384,512]{1,0:T(8,128)(2,1)} %collective-permute-done.3, bf16[384,1408]{1,0:T(8,128)(2,1)S(1)} %copy-done.13, bf16[1,1408,2048]{2,1,0:T(8,128)(2,1)S(1)} %bitcast.111, ...), kind=kOutput, calls=%fused_computation.65 | convolution fusion | flops 555417600 | bytes 4096004 | tf_op jit(solution)/shard_map/dot_general | solution.py:66
  131.6 5.5 %all-to-all-start.1 = ((bf16[32,12,512]{2,1,0:T(8,128)(2,1)}), bf16[32,12,512]{2,1,0:T(8,128)(2,1)S(1)}, u32[]{:S(2)}, u32[]{:S(2)}) async-start(bf16[32,12,512]{2,1,0:T(8,128)(2,1)} %reshape.196), calls=%async_computation.1 | async-start | bytes 1048576 | tf_op jit(solution)/shard_map/all_to_all | solution.py:131
  137.1 20.1 %collective-permute-done.8 = bf16[640,512]{1,0:T(8,128)(2,1)S(1)} collective-permute-done((bf16[640,512]{1,0:T(8,128)(2,1)}, bf16[640,512]{1,0:T(8,128)(2,1)S(1)}, u32[]{:S(2)}, u32[]{:S(2)}) %collective-permute-start.8) | collective-permute-done | bytes 655392 | tf_op jit(solution)/shard_map/ppermute | solution.py:20
  157.7 3.3 %add_convert_fusion = bf16[640,512]{1,0:T(8,128)(2,1)S(1)} fusion(bf16[640,512]{1,0:T(8,128)(2,1)} %collective-permute-done.10, bf16[640,512]{1,0:T(8,128)(2,1)S(1)} %collective-permute-done.9, bf16[640,512]{1,0:T(8,128)(2,1)S(1)} %collective-permute-done.8, bf16[640,1408]{1,0:T(8,128)(2,1)} %copy-done.14, bf16[1,1408,2048]{2,1,0:T(8,128)(2,1)} %param.15, ...), kind=kOutput, calls=%fused_computation.45 | convolution fusion | flops 925696000 | bytes 5865476 | tf_op jit(solution)/shard_map/dot_general | solution.py:66
  162.1 5.9 %all-to-all-start.3 = ((bf16[32,20,512]{2,1,0:T(8,128)(2,1)}), bf16[32,20,512]{2,1,0:T(8,128)(2,1)S(1)}, u32[]{:S(2)}, u32[]{:S(2)}) async-start(bf16[32,20,512]{2,1,0:T(8,128)(2,1)} %reshape.200), calls=%async_computation.3 | async-start | bytes 1572864 | tf_op jit(solution)/shard_map/all_to_all | solution.py:131
  169.1 13.1 %all-to-all-done.3 = bf16[32,20,512]{2,1,0:T(8,128)(2,1)S(1)} async-done(((bf16[32,20,512]{2,1,0:T(8,128)(2,1)}), bf16[32,20,512]{2,1,0:T(8,128)(2,1)S(1)}, u32[]{:S(2)}, u32[]{:S(2)}) %all-to-all-start.3) | async-done | bytes 655392 | tf_op jit(solution)/shard_map/all_to_all | solution.py:131
  183.7 3.0 %collective-permute-start.12 = (f32[256]{0:T(256)S(1)}, f32[256]{0:T(256)S(1)}, u32[]{:S(2)}, u32[]{:S(2)}) collective-permute-start(f32[256]{0:T(256)S(1)} %get-tuple-element.20), channel_id=1, source_target_pairs={{0,2},{1,3},{2,0},{3,1},{4,6},{5,7},{6,4},{7,5},{8,10},{9,11},{10,... | collective-permute-start | bytes 3080 | tf_op jit(solution)/shard_map/ppermute | solution.py:20
  (122 shorter events, 37.6 us)
Async XLA Ops:
  0.6 28.6 %collective-permute-start.6 = (bf16[256,512]{1,0:T(8,128)(2,1)}, bf16[256,512]{1,0:T(8,128)(2,1)S(1)}, u32[]{:S(2)}, u32[]{:S(2)}) collective-permute-start(bf16[256,512]{1,0:T(8,128)(2,1)} %param.8), channel_id=1, source_target_pairs={{0,1},{1,2},{2,3},{3,0},{4,5},{5,6},{6,7},{7,4},{8,9},{9,10},{10,1... | collective-permute-start | bytes 786440 | tf_op jit(solution)/shard_map/ppermute | solution.py:20
  2.8 14.2 %collective-permute-start = (bf16[256,512]{1,0:T(8,128)(2,1)}, bf16[256,512]{1,0:T(8,128)(2,1)S(1)}, u32[]{:S(2)}, u32[]{:S(2)}) collective-permute-start(bf16[256,512]{1,0:T(8,128)(2,1)} %param.8), channel_id=1, source_target_pairs={{0,2},{1,3},{2,0},{3,1},{4,6},{5,7},{6,4},{7,5},{8,10},{9,11},{10,... | collective-permute-start | bytes 786440 | tf_op jit(solution)/shard_map/ppermute | solution.py:20
  5.4 23.9 %collective-permute-start.7 = (bf16[256,512]{1,0:T(8,128)(2,1)}, bf16[256,512]{1,0:T(8,128)(2,1)S(1)}, u32[]{:S(2)}, u32[]{:S(2)}) collective-permute-start(bf16[256,512]{1,0:T(8,128)(2,1)} %param.8), channel_id=1, source_target_pairs={{0,3},{1,0},{2,1},{3,2},{4,7},{5,4},{6,5},{7,6},{8,11},{9,8},{10,9... | collective-permute-start | bytes 786440 | tf_op jit(solution)/shard_map/ppermute | solution.py:20
  10.1 9.4 %copy-start.6 = (pred[256]{0:T(512)(128)(4,1)}, pred[256]{0:T(512)(128)(4,1)S(1)}, u32[]{:S(2)}) copy-start(pred[256]{0:T(512)(128)(4,1)S(1)} %get-tuple-element.4) | copy-start | bytes 772
  10.1 9.4 %copy-start.8 = (pred[256]{0:T(512)(128)(4,1)}, pred[256]{0:T(512)(128)(4,1)S(1)}, u32[]{:S(2)}) copy-start(pred[256]{0:T(512)(128)(4,1)S(1)} %get-tuple-element.5) | copy-start | bytes 772
  18.3 10.8 %copy-start.2 = (bf16[256,512]{1,0:T(8,128)(2,1)S(1)}, bf16[256,512]{1,0:T(8,128)(2,1)}, u32[]{:S(2)}) copy-start(bf16[256,512]{1,0:T(8,128)(2,1)} %param.8) | copy-start | bytes 786436
  19.5 26.4 %all-to-all-start = ((bf16[32,12,1024]{2,1,0:T(8,128)(2,1)}), bf16[32,12,1024]{2,1,0:T(8,128)(2,1)S(1)}, u32[]{:S(2)}, u32[]{:S(2)}) async-start(bf16[32,12,1024]{2,1,0:T(8,128)(2,1)} %reshape.194), calls=%async_computation | async-start | bytes 2097152 | tf_op jit(solution)/shard_map/all_to_all | solution.py:117
  29.7 21.3 %copy-start.10 = (f32[2048]{0:T(1024)S(1)}, f32[2048]{0:T(1024)}, u32[]{:S(2)}) copy-start(f32[2048]{0:T(1024)} %param.11) | copy-start | bytes 24580
  48.3 16.8 %collective-permute-start.1 = (bf16[384,512]{1,0:T(8,128)(2,1)S(1)}, bf16[384,512]{1,0:T(8,128)(2,1)}, u32[]{:S(2)}, u32[]{:S(2)}) collective-permute-start(bf16[384,512]{1,0:T(8,128)(2,1)S(1)} %get-tuple-element.14), channel_id=1, source_target_pairs={{0,1},{1,2},{2,3},{3,0},{4,5},{5,6},{6,7},{7,4},{8,9},{9,10},{10,1... | collective-permute-start | bytes 1179656 | tf_op jit(solution)/shard_map/ppermute | solution.py:20
  48.3 18.6 %collective-permute-start.2 = (bf16[384,512]{1,0:T(8,128)(2,1)S(1)}, bf16[384,512]{1,0:T(8,128)(2,1)}, u32[]{:S(2)}, u32[]{:S(2)}) collective-permute-start(bf16[384,512]{1,0:T(8,128)(2,1)S(1)} %get-tuple-element.14), channel_id=1, source_target_pairs={{0,3},{1,0},{2,1},{3,2},{4,7},{5,4},{6,5},{7,6},{8,11},{9,8},{10,9... | collective-permute-start | bytes 1179656 | tf_op jit(solution)/shard_map/ppermute | solution.py:20
  58.7 44.3 %all-to-all-start.2 = ((bf16[32,20,2048]{2,1,0:T(8,128)(2,1)}), bf16[32,20,2048]{2,1,0:T(8,128)(2,1)S(1)}, u32[]{:S(2)}, u32[]{:S(2)}) async-start(bf16[32,20,2048]{2,1,0:T(8,128)(2,1)} %reshape.198), calls=%async_computation.2 | async-start | bytes 6291456 | tf_op jit(solution)/shard_map/all_to_all | solution.py:117
  70.7 10.3 %slice-start.2 = ((s8[5767168]{0:T(1024)(128)(4,1)}), s8[4194304]{0:T(1024)(128)(4,1)S(1)}, s32[]{:S(2)}) async-start(s8[5767168]{0:T(1024)(128)(4,1)} %bitcast.108), calls=%async_computation.6 | async-start | bytes 8388608
  82.5 44.3 %collective-permute-start.3 = (bf16[384,512]{1,0:T(8,128)(2,1)}, bf16[384,512]{1,0:T(8,128)(2,1)}, u32[]{:S(2)}, u32[]{:S(2)}) collective-permute-start(bf16[384,512]{1,0:T(8,128)(2,1)} %fusion.59), channel_id=1, source_target_pairs={{0,1},{1,2},{2,3},{3,0},{4,5},{5,6},{6,7},{7,4},{8,9},{9,10},{10,1... | collective-permute-start | bytes 1179656 | tf_op jit(solution)/shard_map/ppermute | solution.py:20
  84.1 44.5 %collective-permute-start.4 = (bf16[384,512]{1,0:T(8,128)(2,1)}, bf16[384,512]{1,0:T(8,128)(2,1)}, u32[]{:S(2)}, u32[]{:S(2)}) collective-permute-start(bf16[384,512]{1,0:T(8,128)(2,1)} %fusion.62), channel_id=1, source_target_pairs={{0,2},{1,3},{2,0},{3,1},{4,6},{5,7},{6,4},{7,5},{8,10},{9,11},{10,... | collective-permute-start | bytes 1179656 | tf_op jit(solution)/shard_map/ppermute | solution.py:20
  86.5 42.1 %collective-permute-start.5 = (bf16[384,512]{1,0:T(8,128)(2,1)}, bf16[384,512]{1,0:T(8,128)(2,1)}, u32[]{:S(2)}, u32[]{:S(2)}) collective-permute-start(bf16[384,512]{1,0:T(8,128)(2,1)} %fusion.65), channel_id=1, source_target_pairs={{0,3},{1,0},{2,1},{3,2},{4,7},{5,4},{6,5},{7,6},{8,11},{9,8},{10,9... | collective-permute-start | bytes 1179656 | tf_op jit(solution)/shard_map/ppermute | solution.py:20
  105.2 15.3 %slice-start.4 = ((s8[5767168]{0:T(1024)(128)(4,1)}), s8[4194304]{0:T(1024)(128)(4,1)S(1)}, s32[]{:S(2)}) async-start(s8[5767168]{0:T(1024)(128)(4,1)} %bitcast.110), calls=%async_computation.8 | async-start | bytes 8388608
  125.8 31.4 %collective-permute-start.8 = (bf16[640,512]{1,0:T(8,128)(2,1)}, bf16[640,512]{1,0:T(8,128)(2,1)S(1)}, u32[]{:S(2)}, u32[]{:S(2)}) collective-permute-start(bf16[640,512]{1,0:T(8,128)(2,1)} %fusion.36), channel_id=1, source_target_pairs={{0,1},{1,2},{2,3},{3,0},{4,5},{5,6},{6,7},{7,4},{8,9},{9,10},{10,1... | collective-permute-start | bytes 1966088 | tf_op jit(solution)/shard_map/ppermute | solution.py:20
  125.9 31.3 %collective-permute-start.9 = (bf16[640,512]{1,0:T(8,128)(2,1)}, bf16[640,512]{1,0:T(8,128)(2,1)S(1)}, u32[]{:S(2)}, u32[]{:S(2)}) collective-permute-start(bf16[640,512]{1,0:T(8,128)(2,1)} %fusion.39), channel_id=1, source_target_pairs={{0,2},{1,3},{2,0},{3,1},{4,6},{5,7},{6,4},{7,5},{8,10},{9,11},{10,... | collective-permute-start | bytes 1966088 | tf_op jit(solution)/shard_map/ppermute | solution.py:20
  126.8 30.9 %collective-permute-start.10 = (bf16[640,512]{1,0:T(8,128)(2,1)S(1)}, bf16[640,512]{1,0:T(8,128)(2,1)}, u32[]{:S(2)}, u32[]{:S(2)}) collective-permute-start(bf16[640,512]{1,0:T(8,128)(2,1)S(1)} %fusion.42), channel_id=1, source_target_pairs={{0,3},{1,0},{2,1},{3,2},{4,7},{5,4},{6,5},{7,6},{8,11},{9,8},{10,9... | collective-permute-start | bytes 1966088 | tf_op jit(solution)/shard_map/ppermute | solution.py:20
  131.6 30.5 %all-to-all-start.1 = ((bf16[32,12,512]{2,1,0:T(8,128)(2,1)}), bf16[32,12,512]{2,1,0:T(8,128)(2,1)S(1)}, u32[]{:S(2)}, u32[]{:S(2)}) async-start(bf16[32,12,512]{2,1,0:T(8,128)(2,1)} %reshape.196), calls=%async_computation.1 | async-start | bytes 1048576 | tf_op jit(solution)/shard_map/all_to_all | solution.py:131
  162.1 20.1 %all-to-all-start.3 = ((bf16[32,20,512]{2,1,0:T(8,128)(2,1)}), bf16[32,20,512]{2,1,0:T(8,128)(2,1)S(1)}, u32[]{:S(2)}, u32[]{:S(2)}) async-start(bf16[32,20,512]{2,1,0:T(8,128)(2,1)} %reshape.200), calls=%async_computation.3 | async-start | bytes 1572864 | tf_op jit(solution)/shard_map/all_to_all | solution.py:131
  183.6 3.7 %collective-permute-start.11 = (f32[256]{0:T(256)S(1)}, f32[256]{0:T(256)S(1)}, u32[]{:S(2)}, u32[]{:S(2)}) collective-permute-start(f32[256]{0:T(256)S(1)} %get-tuple-element.20), channel_id=1, source_target_pairs={{0,1},{1,2},{2,3},{3,0},{4,5},{5,6},{6,7},{7,4},{8,9},{9,10},{10,1... | collective-permute-start | bytes 3080 | tf_op jit(solution)/shard_map/ppermute | solution.py:20
  183.7 4.0 %collective-permute-start.12 = (f32[256]{0:T(256)S(1)}, f32[256]{0:T(256)S(1)}, u32[]{:S(2)}, u32[]{:S(2)}) collective-permute-start(f32[256]{0:T(256)S(1)} %get-tuple-element.20), channel_id=1, source_target_pairs={{0,2},{1,3},{2,0},{3,1},{4,6},{5,7},{6,4},{7,5},{8,10},{9,11},{10,... | collective-permute-start | bytes 3080 | tf_op jit(solution)/shard_map/ppermute | solution.py:20
  186.7 2.4 %collective-permute-start.13 = (f32[256]{0:T(256)S(1)}, f32[256]{0:T(256)S(1)}, u32[]{:S(2)}, u32[]{:S(2)}) collective-permute-start(f32[256]{0:T(256)S(1)} %get-tuple-element.20), channel_id=1, source_target_pairs={{0,3},{1,0},{2,1},{3,2},{4,7},{5,4},{6,5},{7,6},{8,11},{9,8},{10,9... | collective-permute-start | bytes 3080 | tf_op jit(solution)/shard_map/ppermute | solution.py:20
  (15 other events, 92.6 us)

commit v15 on v13

--- a/solution.py
+++ b/solution.py
@@ -60,15 +60,18 @@
 def down_scatter_sum_tp(activ, w_down, tp_count):
     me = lax.axis_index("tp")
     width = w_down.shape[1] // tp_count
-    terms = []
-    for s in list(range(1, tp_count)) + [0]:
+    far = tp_count // 2
+    order = [far] + [s for s in range(1, tp_count) if s != far] + [0]
+    terms = {}
+    for s in order:
         w_block = lax.dynamic_slice_in_dim(w_down, ((me + s) % tp_count) * width, width, axis=1)
         block = jnp.dot(activ, w_block, preferred_element_type=jnp.float32).astype(jnp.bfloat16)
-        terms.append(block if s == 0 else shift_tp(block, s, tp_count))
-    total = terms[0].astype(jnp.float32)
-    for term in terms[1:]:
-        total = total + term.astype(jnp.float32)
-    return total.astype(jnp.bfloat16)
+        terms[s] = block if s == 0 else shift_tp(block, s, tp_count)
+    near = terms[0].astype(jnp.float32)
+    for s in order[1:-1]:
+        near = near + terms[s].astype(jnp.float32)
+    near = lax.optimization_barrier(near)
+    return (near + terms[far].astype(jnp.float32)).astype(jnp.bfloat16)
 
 
 def shards(hidden, routes, route_weights, pre_gain, out_gain, gate_weight, up_weight, down_weight):

time: 152 us -> 153 us (level)
  waiting for transfers between devices: 55.4 us -> 48.3 us
  starting transfers between devices: 40.1 us -> 46.8 us
  other arithmetic: 3.78 us -> 6.45 us
    ppermute x14, waiting for transfers between devices: 25.4 us -> 17.7 us  [shift_tp(): lax.ppermute(value, 'tp', [(j, (j + step) % tp_count) for j in range(tp_c...]
    all_to_all x2, starting transfers between devices: 8.83 us -> 14.9 us  [shards(): lax.all_to_all(summed, 'req', split_axis=0, concat_axis=0, tiled=True)]
    dot_general x8, matrix products: 16.5 us -> 14.1 us  [down_scatter_sum_tp(): jnp.dot(activ, w_block, preferred_element_type=jnp.float32)]
    convert_element_type x0 -> x2, other arithmetic: none -> 1.91 us  [down_scatter_sum_tp(): return (near + terms[far].astype(jnp.float32)).astype(jnp.bfloat16)]
    dot_general x2, matrix products: 8.66 us -> 10.3 us  [shards(): jnp.dot(flat_rows, up_weight[0], preferred_element_type=jnp.float32)]
  transfers between devices with their start and end apart: 18 -> 18, of which waited for: 10 -> 9; matrix products, arithmetic and copies ran while one was open for 33% -> 34% of each run, Pallas kernels for 0% -> 0%
where the time goes in v15:
time: 153 us; the launch traced here: 152 us
  waiting for transfers between devices  48.3 us (32%)
  starting transfers between devices  46.8 us (31%)
  matrix products  43.8 us (29%)
  other arithmetic  6.45 us (4%)
  local copies, waits for them, and re-layouts  5.85 us (4%)
    all_to_all x2, waiting for transfers between devices, shards(): lax.all_to_all(outgoing, 'req', split_axis=0, concat_axis=0, tiled=True)  19.9 us
    ppermute x14, waiting for transfers between devices, shift_tp(): lax.ppermute(value, 'tp', [(j, (j + step) % tp_count) for j in range(tp_c...  17.7 us
    ppermute x14, starting transfers between devices, shift_tp(): lax.ppermute(value, 'tp', [(j, (j + step) % tp_count) for j in range(tp_c...  17.2 us
    all_to_all x2, starting transfers between devices, shards(): lax.all_to_all(summed, 'req', split_axis=0, concat_axis=0, tiled=True)  14.9 us
    all_to_all x2, starting transfers between devices, shards(): lax.all_to_all(outgoing, 'req', split_axis=0, concat_axis=0, tiled=True)  14.7 us
    dot_general x8, matrix products, down_scatter_sum_tp(): jnp.dot(activ, w_block, preferred_element_type=jnp.float32)  14.1 us
    dot_general x2, matrix products, shards(): jnp.dot(flat_rows, gate_weight[0], preferred_element_type=jnp.float32)  12.6 us
    all_to_all x2, waiting for transfers between devices, shards(): lax.all_to_all(summed, 'req', split_axis=0, concat_axis=0, tiled=True)  10.7 us
  transfers between devices with their start and end apart: 18, of which 9 were waited for; matrix products, arithmetic and copies ran while one was open for 34% of the time, Pallas kernels for 0%

profile of v15, /device:TPU:1, one launch (start us, length us, event | category | flops | bytes accessed | tf_op | source)
XLA Modules:
  0.0 152.4 jit_solution(10832841345869624612)
XLA Ops:
  0.6 3.8 %collective-permute-start = (bf16[256,512]{1,0:T(8,128)(2,1)}, bf16[256,512]{1,0:T(8,128)(2,1)S(1)}, u32[]{:S(2)}, u32[]{:S(2)}) collective-permute-start(bf16[256,512]{1,0:T(8,128)(2,1)} %param.8), channel_id=1, source_target_pairs={{0,2},{1,3},{2,0},{3,1},{4,6},{5,7},{6,4},{7,5},{8,10},{9,11},{10,... | collective-permute-start | bytes 786440 | tf_op jit(solution)/shard_map/ppermute | solution.py:20
  4.8 2.3 %collective-permute-start.7 = (bf16[256,512]{1,0:T(8,128)(2,1)}, bf16[256,512]{1,0:T(8,128)(2,1)S(1)}, u32[]{:S(2)}, u32[]{:S(2)}) collective-permute-start(bf16[256,512]{1,0:T(8,128)(2,1)} %param.8), channel_id=1, source_target_pairs={{0,3},{1,0},{2,1},{3,2},{4,7},{5,4},{6,5},{7,6},{8,11},{9,8},{10,9... | collective-permute-start | bytes 786440 | tf_op jit(solution)/shard_map/ppermute | solution.py:20
  11.5 2.4 %convolution_convert_fusion.1 = bf16[512,1024]{1,0:T(8,128)(2,1)} fusion(bf16[256,512]{1,0:T(8,128)(2,1)S(1)} %collective-permute-done, bf16[256,512]{1,0:T(8,128)(2,1)} %param.8, s32[256]{0:T(256)S(1)} %bitcast.111, s32[256]{0:T(256)S(1)} %bitcast.105, pred[256]{0:T(512)(128)(4,1)S(1)} %get-tuple-element.5, pred[256]{0:T(512)(128)(4,1)S(1)} %get-tuple-element.4), kind=kOutput, calls=%fused_computation.23 | convolution fusion | flops 270663680 | bytes 1575424 | tf_op jit(solution)/shard_map/dot_general | solution.py:111
  14.0 9.7 %all-to-all-start = ((bf16[32,16,1024]{2,1,0:T(8,128)(2,1)}), bf16[32,16,1024]{2,1,0:T(8,128)(2,1)S(1)}, u32[]{:S(2)}, u32[]{:S(2)}) async-start(bf16[32,16,1024]{2,1,0:T(8,128)(2,1)} %bitcast.4), calls=%async_computation | async-start | bytes 2097152 | tf_op jit(solution)/shard_map/all_to_all | solution.py:115
  24.4 16.1 %all-to-all-done = bf16[32,16,1024]{2,1,0:T(8,128)(2,1)S(1)} async-done(((bf16[32,16,1024]{2,1,0:T(8,128)(2,1)}), bf16[32,16,1024]{2,1,0:T(8,128)(2,1)S(1)}, u32[]{:S(2)}, u32[]{:S(2)}) %all-to-all-start) | async-done | bytes 1048608 | tf_op jit(solution)/shard_map/all_to_all | solution.py:115
  44.5 2.2 %convolution_convert_fusion = bf16[512,2048]{1,0:T(8,128)(2,1)} fusion(bf16[256,2048]{1,0:T(8,128)(2,1)S(1)} %copy-done.1, f32[2048]{0:T(1024)S(1)} %copy-done.4, f32[256]{0:T(256)S(1)} %add_rsqrt_fusion.2, s32[256]{0:T(256)S(1)} %bitcast.112, s32[256]{0:T(256)S(1)} %bitcast.106, pred[256]{0:T(512)(128)(4,1)S(1)} %get-tuple-element.3, ...), kind=kOutput, calls=%fused_computation.15 | convolution fusion | flops 540672000 | bytes 3157504 | tf_op jit(solution)/shard_map/dot_general | solution.py:111
  46.7 5.0 %all-to-all-start.2 = ((bf16[32,16,2048]{2,1,0:T(8,128)(2,1)}), bf16[32,16,2048]{2,1,0:T(8,128)(2,1)}, u32[]{:S(2)}, u32[]{:S(2)}) async-start(bf16[32,16,2048]{2,1,0:T(8,128)(2,1)} %bitcast.99), calls=%async_computation.2 | async-start | bytes 4194304 | tf_op jit(solution)/shard_map/all_to_all | solution.py:115
  51.8 5.0 %collective-permute-done.1 = bf16[512,512]{1,0:T(8,128)(2,1)} collective-permute-done((bf16[512,512]{1,0:T(8,128)(2,1)}, bf16[512,512]{1,0:T(8,128)(2,1)}, u32[]{:S(2)}, u32[]{:S(2)}) %collective-permute-start.1) | collective-permute-done | bytes 524320 | tf_op jit(solution)/shard_map/ppermute | solution.py:20
  59.6 6.1 %fusion.6 = f32[512,1408]{1,0:T(8,128)S(1)} fusion(bf16[1,2048,1408]{2,1,0:T(8,128)(2,1)} %param.13, bf16[512,2048]{1,0:T(8,128)(2,1)S(1)} %constant_dynamic-update-slice_fusion.4, f32[2048]{0:T(1024)S(1)} %copy-done.4, f32[512]{0:T(512)S(1)} %add_rsqrt_fusion), kind=kOutput, calls=%fused_computation.7 | convolution fusion | flops 2956984320 | bytes 10758144 | tf_op jit(solution)/shard_map/dot_general | solution.py:124
  65.7 3.5 %multiply_convert_fusion = bf16[512,1408]{1,0:T(8,128)(2,1)S(1)} fusion(f32[512,1408]{1,0:T(8,128)S(1)} %fusion.6, bf16[1,2048,1408]{2,1,0:T(8,128)(2,1)S(1)} %bitcast.122, bf16[512,2048]{1,0:T(8,128)(2,1)S(1)} %constant_dynamic-update-slice_fusion.4, f32[2048]{0:T(1024)S(1)} %copy-done.4, f32[512]{0:T(512)S(1)} %add_rsqrt_fusion), kind=kOutput, calls=%fused_computation.17 | convolution fusion | flops 2961309696 | bytes 12199936 | tf_op jit(solution)/shard_map/dot_general | solution.py:125
  73.0 1.8 %fusion.54 = bf16[512,512]{1,0:T(8,128)(2,1)} fusion(bf16[512,1408]{1,0:T(8,128)(2,1)S(1)} %multiply_convert_fusion, bf16[1,1408,2048]{2,1,0:T(8,128)(2,1)S(1)} %bitcast.124, s32[]{:T(128)S(6)} %select_n.183), kind=kOutput, calls=%fused_computation.46 | convolution fusion | flops 738459648 | bytes 3407876 | tf_op jit(solution)/shard_map/dot_general | solution.py:68
  76.4 3.8 %all-to-all-done.2 = bf16[32,16,2048]{2,1,0:T(8,128)(2,1)} async-done(((bf16[32,16,2048]{2,1,0:T(8,128)(2,1)}), bf16[32,16,2048]{2,1,0:T(8,128)(2,1)}, u32[]{:S(2)}, u32[]{:S(2)}) %all-to-all-start.2) | async-done | bytes 2097184 | tf_op jit(solution)/shard_map/all_to_all | solution.py:115
  80.1 6.5 %fusion.4 = f32[512,1408]{1,0:T(8,128)S(1)} fusion(bf16[512,2048]{1,0:T(8,128)(2,1)} %bitcast.15, bf16[1,2048,1408]{2,1,0:T(8,128)(2,1)} %param.13), kind=kOutput, calls=%fused_computation.5 | convolution fusion | flops 2952790016 | bytes 10747904 | tf_op jit(solution)/shard_map/dot_general | solution.py:124
  86.7 6.8 %fusion.14 = bf16[512,1408]{1,0:T(8,128)(2,1)S(1)} fusion(bf16[512,2048]{1,0:T(8,128)(2,1)} %bitcast.15, bf16[1,2048,1408]{2,1,0:T(8,128)(2,1)} %param.14, f32[512,1408]{1,0:T(8,128)S(1)} %fusion.4), kind=kOutput, calls=%fused_computation.16 | convolution fusion | flops 2957115392 | bytes 12189696 | tf_op jit(solution)/shard_map/dot_general | solution.py:125
  93.6 1.8 %fusion.51 = bf16[512,512]{1,0:T(8,128)(2,1)} fusion(bf16[512,1408]{1,0:T(8,128)(2,1)S(1)} %fusion.14, bf16[1,1408,2048]{2,1,0:T(8,128)(2,1)S(1)} %bitcast.126, s32[]{:T(128)S(6)} %select_n.181), kind=kOutput, calls=%fused_computation.45 | convolution fusion | flops 738459648 | bytes 3407876 | tf_op jit(solution)/shard_map/dot_general | solution.py:68
  96.9 1.8 %fusion.45 = bf16[512,512]{1,0:T(8,128)(2,1)} fusion(bf16[512,1408]{1,0:T(8,128)(2,1)S(1)} %fusion.14, bf16[1,1408,2048]{2,1,0:T(8,128)(2,1)S(1)} %bitcast.126, s32[]{:T(128)S(6)} %select_n.179), kind=kOutput, calls=%fused_computation.43 | convolution fusion | flops 738459648 | bytes 3407876 | tf_op jit(solution)/shard_map/dot_general | solution.py:68
  98.7 1.8 %fusion.57 = bf16[512,512]{1,0:T(8,128)(2,1)} fusion(bf16[512,1408]{1,0:T(8,128)(2,1)S(1)} %fusion.14, bf16[1,1408,2048]{2,1,0:T(8,128)(2,1)S(1)} %bitcast.126, s32[]{:T(128)S(6)} %select_n.183), kind=kOutput, calls=%fused_computation.47 | convolution fusion | flops 738459648 | bytes 3407876 | tf_op jit(solution)/shard_map/dot_general | solution.py:68
  102.1 2.0 %convert_add_fusion.1 = f32[512,512]{1,0:T(8,128)S(1)} fusion(bf16[512,512]{1,0:T(8,128)(2,1)S(1)} %collective-permute-done.4, bf16[512,512]{1,0:T(8,128)(2,1)} %collective-permute-done.3, bf16[512,1408]{1,0:T(8,128)(2,1)S(1)} %copy-done.6, bf16[1,1408,2048]{2,1,0:T(8,128)(2,1)S(1)} %bitcast.126, s32[]{:T(128)S(6)} %select_n.171), kind=kOutput, calls=%fused_computation.67 | convolution fusion | flops 739770368 | bytes 4980740 | tf_op jit(solution)/shard_map/dot_general | solution.py:68
  105.1 5.3 %all-to-all-start.1 = ((bf16[32,16,512]{2,1,0:T(8,128)(2,1)}), bf16[32,16,512]{2,1,0:T(8,128)(2,1)S(1)}, u32[]{:S(2)}, u32[]{:S(2)}) async-start(bf16[32,16,512]{2,1,0:T(8,128)(2,1)} %bitcast.12), calls=%async_computation.1 | async-start | bytes 1048576 | tf_op jit(solution)/shard_map/all_to_all | solution.py:129
  110.4 3.1 %collective-permute-done.8 = bf16[512,512]{1,0:T(8,128)(2,1)} collective-permute-done((bf16[512,512]{1,0:T(8,128)(2,1)}, bf16[512,512]{1,0:T(8,128)(2,1)}, u32[]{:S(2)}, u32[]{:S(2)}) %collective-permute-start.8) | collective-permute-done | bytes 524320 | tf_op jit(solution)/shard_map/ppermute | solution.py:20
  113.5 2.9 %convert_add_fusion = f32[512,512]{1,0:T(8,128)S(1)} fusion(bf16[512,512]{1,0:T(8,128)(2,1)S(1)} %collective-permute-done.9, bf16[512,512]{1,0:T(8,128)(2,1)} %collective-permute-done.8, bf16[512,1408]{1,0:T(8,128)(2,1)} %copy-done.7, bf16[1,1408,2048]{2,1,0:T(8,128)(2,1)} %param.15, s32[]{:T(128)S(6)} %select_n.171), kind=kOutput, calls=%fused_computation.63 | convolution fusion | flops 739770368 | bytes 4980740 | tf_op jit(solution)/shard_map/dot_general | solution.py:68
  116.4 6.2 %collective-permute-done.10 = bf16[512,512]{1,0:T(8,128)(2,1)S(1)} collective-permute-done((bf16[512,512]{1,0:T(8,128)(2,1)}, bf16[512,512]{1,0:T(8,128)(2,1)S(1)}, u32[]{:S(2)}, u32[]{:S(2)}) %collective-permute-start.10) | collective-permute-done | bytes 524320 | tf_op jit(solution)/shard_map/ppermute | solution.py:20
  123.5 9.7 %all-to-all-start.3 = ((bf16[32,16,512]{2,1,0:T(8,128)(2,1)}), bf16[32,16,512]{2,1,0:T(8,128)(2,1)S(1)}, u32[]{:S(2)}, u32[]{:S(2)}) async-start(bf16[32,16,512]{2,1,0:T(8,128)(2,1)} %bitcast.16), calls=%async_computation.3 | async-start | bytes 1048576 | tf_op jit(solution)/shard_map/all_to_all | solution.py:129
  134.2 10.7 %all-to-all-done.3 = bf16[32,16,512]{2,1,0:T(8,128)(2,1)S(1)} async-done(((bf16[32,16,512]{2,1,0:T(8,128)(2,1)}), bf16[32,16,512]{2,1,0:T(8,128)(2,1)S(1)}, u32[]{:S(2)}, u32[]{:S(2)}) %all-to-all-start.3) | async-done | bytes 524320 | tf_op jit(solution)/shard_map/all_to_all | solution.py:129
  (102 shorter events, 30.8 us)
Async XLA Ops:
  0.6 10.9 %collective-permute-start = (bf16[256,512]{1,0:T(8,128)(2,1)}, bf16[256,512]{1,0:T(8,128)(2,1)S(1)}, u32[]{:S(2)}, u32[]{:S(2)}) collective-permute-start(bf16[256,512]{1,0:T(8,128)(2,1)} %param.8), channel_id=1, source_target_pairs={{0,2},{1,3},{2,0},{3,1},{4,6},{5,7},{6,4},{7,5},{8,10},{9,11},{10,... | collective-permute-start | bytes 786440 | tf_op jit(solution)/shard_map/ppermute | solution.py:20
  4.5 19.5 %collective-permute-start.6 = (bf16[256,512]{1,0:T(8,128)(2,1)}, bf16[256,512]{1,0:T(8,128)(2,1)S(1)}, u32[]{:S(2)}, u32[]{:S(2)}) collective-permute-start(bf16[256,512]{1,0:T(8,128)(2,1)} %param.8), channel_id=1, source_target_pairs={{0,1},{1,2},{2,3},{3,0},{4,5},{5,6},{6,7},{7,4},{8,9},{9,10},{10,1... | collective-permute-start | bytes 786440 | tf_op jit(solution)/shard_map/ppermute | solution.py:20
  4.8 19.2 %collective-permute-start.7 = (bf16[256,512]{1,0:T(8,128)(2,1)}, bf16[256,512]{1,0:T(8,128)(2,1)S(1)}, u32[]{:S(2)}, u32[]{:S(2)}) collective-permute-start(bf16[256,512]{1,0:T(8,128)(2,1)} %param.8), channel_id=1, source_target_pairs={{0,3},{1,0},{2,1},{3,2},{4,7},{5,4},{6,5},{7,6},{8,11},{9,8},{10,9... | collective-permute-start | bytes 786440 | tf_op jit(solution)/shard_map/ppermute | solution.py:20
  14.0 9.8 %copy-start.2 = (bf16[256,512]{1,0:T(8,128)(2,1)S(1)}, bf16[256,512]{1,0:T(8,128)(2,1)}, u32[]{:S(2)}) copy-start(bf16[256,512]{1,0:T(8,128)(2,1)} %param.8) | copy-start | bytes 786436
  14.0 26.6 %all-to-all-start = ((bf16[32,16,1024]{2,1,0:T(8,128)(2,1)}), bf16[32,16,1024]{2,1,0:T(8,128)(2,1)S(1)}, u32[]{:S(2)}, u32[]{:S(2)}) async-start(bf16[32,16,1024]{2,1,0:T(8,128)(2,1)} %bitcast.4), calls=%async_computation | async-start | bytes 2097152 | tf_op jit(solution)/shard_map/all_to_all | solution.py:115
  24.1 16.5 %copy-start = (bf16[256,2048]{1,0:T(8,128)(2,1)}, bf16[256,2048]{1,0:T(8,128)(2,1)S(1)}, u32[]{:S(2)}) copy-start(bf16[256,2048]{1,0:T(8,128)(2,1)S(1)} %constant_dynamic-update-slice_fusion) | copy-start | bytes 3145732
  24.4 20.1 %copy-start.4 = (f32[2048]{0:T(1024)S(1)}, f32[2048]{0:T(1024)}, u32[]{:S(2)}) copy-start(f32[2048]{0:T(1024)} %param.11) | copy-start | bytes 24580
  41.8 15.0 %collective-permute-start.1 = (bf16[512,512]{1,0:T(8,128)(2,1)}, bf16[512,512]{1,0:T(8,128)(2,1)}, u32[]{:S(2)}, u32[]{:S(2)}) collective-permute-start(bf16[512,512]{1,0:T(8,128)(2,1)} %get-tuple-element.14), channel_id=1, source_target_pairs={{0,1},{1,2},{2,3},{3,0},{4,5},{5,6},{6,7},{7,4},{8,9},{9,10},{10,1... | collective-permute-start | bytes 1572872 | tf_op jit(solution)/shard_map/ppermute | solution.py:20
  43.1 14.9 %collective-permute-start.2 = (bf16[512,512]{1,0:T(8,128)(2,1)}, bf16[512,512]{1,0:T(8,128)(2,1)}, u32[]{:S(2)}, u32[]{:S(2)}) collective-permute-start(bf16[512,512]{1,0:T(8,128)(2,1)} %get-tuple-element.14), channel_id=1, source_target_pairs={{0,3},{1,0},{2,1},{3,2},{4,7},{5,4},{6,5},{7,6},{8,11},{9,8},{10,9... | collective-permute-start | bytes 1572872 | tf_op jit(solution)/shard_map/ppermute | solution.py:20
  46.7 33.4 %all-to-all-start.2 = ((bf16[32,16,2048]{2,1,0:T(8,128)(2,1)}), bf16[32,16,2048]{2,1,0:T(8,128)(2,1)}, u32[]{:S(2)}, u32[]{:S(2)}) async-start(bf16[32,16,2048]{2,1,0:T(8,128)(2,1)} %bitcast.99), calls=%async_computation.2 | async-start | bytes 4194304 | tf_op jit(solution)/shard_map/all_to_all | solution.py:115
  59.6 9.7 %slice-start.2 = ((s8[5767168]{0:T(1024)(128)(4,1)}), s8[4194304]{0:T(1024)(128)(4,1)S(1)}, s32[]{:S(2)}) async-start(s8[5767168]{0:T(1024)(128)(4,1)} %bitcast.123), calls=%async_computation.6 | async-start | bytes 8388608
  70.3 30.2 %collective-permute-start.4 = (bf16[512,512]{1,0:T(8,128)(2,1)S(1)}, bf16[512,512]{1,0:T(8,128)(2,1)S(1)}, u32[]{:S(2)}, u32[]{:S(2)}) collective-permute-start(bf16[512,512]{1,0:T(8,128)(2,1)S(1)} %fusion.48), channel_id=1, source_target_pairs={{0,3},{1,0},{2,1},{3,2},{4,7},{5,4},{6,5},{7,6},{8,11},{9,8},{10,9... | collective-permute-start | bytes 1572872 | tf_op jit(solution)/shard_map/ppermute | solution.py:20
  72.9 29.2 %collective-permute-start.3 = (bf16[512,512]{1,0:T(8,128)(2,1)S(1)}, bf16[512,512]{1,0:T(8,128)(2,1)}, u32[]{:S(2)}, u32[]{:S(2)}) collective-permute-start(bf16[512,512]{1,0:T(8,128)(2,1)S(1)} %fusion.42), channel_id=1, source_target_pairs={{0,1},{1,2},{2,3},{3,0},{4,5},{5,6},{6,7},{7,4},{8,9},{9,10},{10,1... | collective-permute-start | bytes 1572872 | tf_op jit(solution)/shard_map/ppermute | solution.py:20
  74.8 29.3 %collective-permute-start.5 = (bf16[512,512]{1,0:T(8,128)(2,1)}, bf16[512,512]{1,0:T(8,128)(2,1)S(1)}, u32[]{:S(2)}, u32[]{:S(2)}) collective-permute-start(bf16[512,512]{1,0:T(8,128)(2,1)} %fusion.54), channel_id=1, source_target_pairs={{0,2},{1,3},{2,0},{3,1},{4,6},{5,7},{6,4},{7,5},{8,10},{9,11},{10,... | collective-permute-start | bytes 1572872 | tf_op jit(solution)/shard_map/ppermute | solution.py:20
  80.1 13.4 %slice-start.4 = ((s8[5767168]{0:T(1024)(128)(4,1)}), s8[4194304]{0:T(1024)(128)(4,1)S(1)}, s32[]{:S(2)}) async-start(s8[5767168]{0:T(1024)(128)(4,1)} %bitcast.125), calls=%async_computation.8 | async-start | bytes 8388608
  86.7 6.9 %slice-start.5 = ((s8[5767168]{0:T(1024)(128)(4,1)}), s8[1572864]{0:T(1024)(128)(4,1)S(1)}, s32[]{:S(2)}) async-start(s8[5767168]{0:T(1024)(128)(4,1)} %bitcast.125), calls=%async_computation.9 | async-start | bytes 3145728
  95.4 15.0 %collective-permute-start.9 = (bf16[512,512]{1,0:T(8,128)(2,1)}, bf16[512,512]{1,0:T(8,128)(2,1)S(1)}, u32[]{:S(2)}, u32[]{:S(2)}) collective-permute-start(bf16[512,512]{1,0:T(8,128)(2,1)} %fusion.51), channel_id=1, source_target_pairs={{0,3},{1,0},{2,1},{3,2},{4,7},{5,4},{6,5},{7,6},{8,11},{9,8},{10,9... | collective-permute-start | bytes 1572872 | tf_op jit(solution)/shard_map/ppermute | solution.py:20
  98.7 14.9 %collective-permute-start.8 = (bf16[512,512]{1,0:T(8,128)(2,1)}, bf16[512,512]{1,0:T(8,128)(2,1)}, u32[]{:S(2)}, u32[]{:S(2)}) collective-permute-start(bf16[512,512]{1,0:T(8,128)(2,1)} %fusion.45), channel_id=1, source_target_pairs={{0,1},{1,2},{2,3},{3,0},{4,5},{5,6},{6,7},{7,4},{8,9},{9,10},{10,1... | collective-permute-start | bytes 1572872 | tf_op jit(solution)/shard_map/ppermute | solution.py:20
  100.5 22.1 %collective-permute-start.10 = (bf16[512,512]{1,0:T(8,128)(2,1)}, bf16[512,512]{1,0:T(8,128)(2,1)S(1)}, u32[]{:S(2)}, u32[]{:S(2)}) collective-permute-start(bf16[512,512]{1,0:T(8,128)(2,1)} %fusion.57), channel_id=1, source_target_pairs={{0,2},{1,3},{2,0},{3,1},{4,6},{5,7},{6,4},{7,5},{8,10},{9,11},{10,... | collective-permute-start | bytes 1572872 | tf_op jit(solution)/shard_map/ppermute | solution.py:20
  105.1 18.4 %all-to-all-start.1 = ((bf16[32,16,512]{2,1,0:T(8,128)(2,1)}), bf16[32,16,512]{2,1,0:T(8,128)(2,1)S(1)}, u32[]{:S(2)}, u32[]{:S(2)}) async-start(bf16[32,16,512]{2,1,0:T(8,128)(2,1)} %bitcast.12), calls=%async_computation.1 | async-start | bytes 1048576 | tf_op jit(solution)/shard_map/all_to_all | solution.py:129
  123.5 21.4 %all-to-all-start.3 = ((bf16[32,16,512]{2,1,0:T(8,128)(2,1)}), bf16[32,16,512]{2,1,0:T(8,128)(2,1)S(1)}, u32[]{:S(2)}, u32[]{:S(2)}) async-start(bf16[32,16,512]{2,1,0:T(8,128)(2,1)} %bitcast.16), calls=%async_computation.3 | async-start | bytes 1048576 | tf_op jit(solution)/shard_map/all_to_all | solution.py:129
  146.0 2.5 %collective-permute-start.13 = (f32[256]{0:T(256)S(1)}, f32[256]{0:T(256)S(1)}, u32[]{:S(2)}, u32[]{:S(2)}) collective-permute-start(f32[256]{0:T(256)S(1)} %get-tuple-element.20), channel_id=1, source_target_pairs={{0,3},{1,0},{2,1},{3,2},{4,7},{5,4},{6,5},{7,6},{8,11},{9,8},{10,9... | collective-permute-start | bytes 3080 | tf_op jit(solution)/shard_map/ppermute | solution.py:20
  146.1 4.0 %collective-permute-start.12 = (f32[256]{0:T(256)S(1)}, f32[256]{0:T(256)S(1)}, u32[]{:S(2)}, u32[]{:S(2)}) collective-permute-start(f32[256]{0:T(256)S(1)} %get-tuple-element.20), channel_id=1, source_target_pairs={{0,2},{1,3},{2,0},{3,1},{4,6},{5,7},{6,4},{7,5},{8,10},{9,11},{10,... | collective-permute-start | bytes 3080 | tf_op jit(solution)/shard_map/ppermute | solution.py:20
  146.2 4.7 %collective-permute-start.11 = (f32[256]{0:T(256)S(1)}, f32[256]{0:T(256)S(1)}, u32[]{:S(2)}, u32[]{:S(2)}) collective-permute-start(f32[256]{0:T(256)S(1)} %get-tuple-element.20), channel_id=1, source_target_pairs={{0,1},{1,2},{2,3},{3,0},{4,5},{5,6},{6,7},{7,4},{8,9},{9,10},{10,1... | collective-permute-start | bytes 3080 | tf_op jit(solution)/shard_map/ppermute | solution.py:20
  (8 other events, 39.2 us)

commit v16 on v13

--- a/solution.py
+++ b/solution.py
@@ -83,8 +83,7 @@
     me = lax.axis_index("tp")
     half_turn = tp_count // 2
     far = shift_tp(hidden, half_turn, tp_count) if tp_count == 4 else None
-    whole_rows = gather_tp(hidden, tp_count, {half_turn: far}).astype(jnp.float32)
-    normed_in = rms_norm(whole_rows, pre_gain).astype(jnp.bfloat16)
+    normed_in = None
     top = routes.shape[1]
     chosen = routes.reshape(-1)
     onehot = (chosen[:, None] == jnp.arange(E, dtype=jnp.int32)[None, :]).astype(jnp.int32)
@@ -97,6 +96,7 @@
     owner_pairs = chunk_of.reshape(row_count, top)
     slot_ids = jnp.arange(req_count * chunk_items, dtype=jnp.int32)
     returned = []
+    anchor = None
     for c in range(CHUNKS):
         dispatch = jnp.zeros((req_count * chunk_items, row_count), jnp.bool_)
         for k in range(top):
@@ -104,6 +104,10 @@
             dispatch = dispatch | hit
         relay = c == 0
         source = hidden if far is None else jnp.concatenate([hidden, far], axis=1)
+        if not relay and normed_in is None:
+            late = hidden if anchor is None else lax.optimization_barrier((hidden, anchor))[0]
+            whole_rows = gather_tp(late, tp_count, {half_turn: far}).astype(jnp.float32)
+            normed_in = rms_norm(whole_rows, pre_gain).astype(jnp.bfloat16)
         source = source if relay else normed_in
         outgoing = jnp.dot(
             dispatch.astype(jnp.bfloat16), source, preferred_element_type=jnp.float32
@@ -113,6 +117,7 @@
         sources, items, widths = pieces.shape
         flat_rows = pieces.reshape(sources * items, widths)
         if relay:
+            anchor = flat_rows
             if far is not None:
                 raw_rows = gather_pair_tp(flat_rows, col_part, tp_count)
             else:

time: 152 us -> 157 us (1.033)
  starting transfers between devices: 40.1 us -> 48.3 us
  waiting for transfers between devices: 55.4 us -> 51.7 us
    ppermute x14, starting transfers between devices: 15.8 us -> 22.5 us  [shift_tp(): lax.ppermute(value, 'tp', [(j, (j + step) % tp_count) for j in range(tp_c...]
    ppermute x14, waiting for transfers between devices: 25.4 us -> 20.1 us  [shift_tp(): lax.ppermute(value, 'tp', [(j, (j + step) % tp_count) for j in range(tp_c...]
    dot_general x2, matrix products: 8.66 us -> 10.5 us  [shards(): jnp.dot(flat_rows, up_weight[0], preferred_element_type=jnp.float32)]
    all_to_all x2, waiting for transfers between devices: 19.3 us -> 20.9 us  [shards(): lax.all_to_all(outgoing, 'req', split_axis=0, concat_axis=0, tiled=True)]
  transfers between devices with their start and end apart: 18 -> 18, of which waited for: 10 -> 10; matrix products, arithmetic and copies ran while one was open for 33% -> 32% of each run, Pallas kernels for 0% -> 0%
where the time goes in v16:
time: 157 us
  waiting for transfers between devices  51.7 us (33%)
  starting transfers between devices  48.3 us (31%)
  matrix products  45.9 us (29%)
  local copies, waits for them, and re-layouts  5.84 us (4%)
  other arithmetic  3.79 us (2%)
    ppermute x14, starting transfers between devices, shift_tp(): lax.ppermute(value, 'tp', [(j, (j + step) % tp_count) for j in range(tp_c...  22.5 us
    all_to_all x2, waiting for transfers between devices, shards(): lax.all_to_all(outgoing, 'req', split_axis=0, concat_axis=0, tiled=True)  20.9 us
    ppermute x14, waiting for transfers between devices, shift_tp(): lax.ppermute(value, 'tp', [(j, (j + step) % tp_count) for j in range(tp_c...  20.1 us
    dot_general x8, matrix products, down_scatter_sum_tp(): jnp.dot(activ, w_block, preferred_element_type=jnp.float32)  15.8 us
    all_to_all x2, starting transfers between devices, shards(): lax.all_to_all(outgoing, 'req', split_axis=0, concat_axis=0, tiled=True)  15.5 us
    dot_general x2, matrix products, shards(): jnp.dot(flat_rows, gate_weight[0], preferred_element_type=jnp.float32)  12.7 us
    all_to_all x2, waiting for transfers between devices, shards(): lax.all_to_all(summed, 'req', split_axis=0, concat_axis=0, tiled=True)  10.7 us
    dot_general x2, matrix products, shards(): jnp.dot(flat_rows, up_weight[0], preferred_element_type=jnp.float32)  10.5 us
  transfers between devices with their start and end apart: 18, of which 10 were waited for; matrix products, arithmetic and copies ran while one was open for 32% of the time, Pallas kernels for 0%

profile of v16, /device:TPU:1, one launch (start us, length us, event | category | flops | bytes accessed | tf_op | source)
XLA Modules:
  0.0 156.7 jit_solution(15043366536163070139)
XLA Ops:
  0.6 3.8 %collective-permute-start = (bf16[256,512]{1,0:T(8,128)(2,1)}, bf16[256,512]{1,0:T(8,128)(2,1)S(1)}, u32[]{:S(2)}, u32[]{:S(2)}) collective-permute-start(bf16[256,512]{1,0:T(8,128)(2,1)} %param.8), channel_id=1, source_target_pairs={{0,2},{1,3},{2,0},{3,1},{4,6},{5,7},{6,4},{7,5},{8,10},{9,11},{10,... | collective-permute-start | bytes 786440 | tf_op jit(solution)/shard_map/ppermute | solution.py:20
  8.1 2.3 %collective-permute-done = bf16[256,512]{1,0:T(8,128)(2,1)S(1)} collective-permute-done((bf16[256,512]{1,0:T(8,128)(2,1)}, bf16[256,512]{1,0:T(8,128)(2,1)S(1)}, u32[]{:S(2)}, u32[]{:S(2)}) %collective-permute-start) | collective-permute-done | bytes 262176 | tf_op jit(solution)/shard_map/ppermute | solution.py:20
  10.4 2.5 %convolution_convert_fusion.1 = bf16[512,1024]{1,0:T(8,128)(2,1)} fusion(bf16[256,512]{1,0:T(8,128)(2,1)S(1)} %collective-permute-done, bf16[256,512]{1,0:T(8,128)(2,1)} %param.8, s32[256]{0:T(256)S(1)} %bitcast.111, s32[256]{0:T(256)S(1)} %bitcast.105, pred[256]{0:T(512)(128)(4,1)S(1)} %get-tuple-element.7, pred[256]{0:T(512)(128)(4,1)S(1)} %get-tuple-element.6), kind=kOutput, calls=%fused_computation.23 | convolution fusion | flops 270663680 | bytes 1575424 | tf_op jit(solution)/shard_map/dot_general | solution.py:112
  12.9 9.5 %all-to-all-start = ((bf16[32,16,1024]{2,1,0:T(8,128)(2,1)}), bf16[32,16,1024]{2,1,0:T(8,128)(2,1)S(1)}, u32[]{:S(2)}, u32[]{:S(2)}) async-start(bf16[32,16,1024]{2,1,0:T(8,128)(2,1)} %bitcast.4), calls=%async_computation | async-start | bytes 2097152 | tf_op jit(solution)/shard_map/all_to_all | solution.py:116
  22.6 16.8 %all-to-all-done = bf16[32,16,1024]{2,1,0:T(8,128)(2,1)S(1)} async-done(((bf16[32,16,1024]{2,1,0:T(8,128)(2,1)}), bf16[32,16,1024]{2,1,0:T(8,128)(2,1)S(1)}, u32[]{:S(2)}, u32[]{:S(2)}) %all-to-all-start) | async-done | bytes 1048608 | tf_op jit(solution)/shard_map/all_to_all | solution.py:116
  43.3 2.7 %collective-permute-start.2 = (bf16[512,512]{1,0:T(8,128)(2,1)}, bf16[512,512]{1,0:T(8,128)(2,1)}, u32[]{:S(2)}, u32[]{:S(2)}) collective-permute-start(bf16[512,512]{1,0:T(8,128)(2,1)} %get-tuple-element.16), channel_id=1, source_target_pairs={{0,3},{1,0},{2,1},{3,2},{4,7},{5,4},{6,5},{7,6},{8,11},{9,8},{10,9... | collective-permute-start | bytes 1572872 | tf_op jit(solution)/shard_map/ppermute | solution.py:20
  46.2 2.3 %collective-permute-done.6 = bf16[256,512]{1,0:T(8,128)(2,1)S(1)} collective-permute-done((bf16[256,512]{1,0:T(8,128)(2,1)S(1)}, bf16[256,512]{1,0:T(8,128)(2,1)S(1)}, u32[]{:S(2)}, u32[]{:S(2)}) %collective-permute-start.6) | collective-permute-done | bytes 262176 | tf_op jit(solution)/shard_map/ppermute | solution.py:20
  48.9 2.2 %convolution_convert_fusion = bf16[512,2048]{1,0:T(8,128)(2,1)} fusion(bf16[256,2048]{1,0:T(8,128)(2,1)S(1)} %constant_dynamic-update-slice_fusion, f32[2048]{0:T(1024)S(1)} %copy-done.5, f32[256]{0:T(256)S(1)} %add_rsqrt_fusion.2, s32[256]{0:T(256)S(1)} %bitcast.112, s32[256]{0:T(256)S(1)} %bitcast.106, pred[256]{0:T(512)(128)(4,1)S(1)} %get-tuple-element.5, ...), kind=kOutput, calls=%fused_computation.15 | convolution fusion | flops 540672000 | bytes 3157504 | tf_op jit(solution)/shard_map/dot_general | solution.py:112
  51.1 6.0 %all-to-all-start.2 = ((bf16[32,16,2048]{2,1,0:T(8,128)(2,1)}), bf16[32,16,2048]{2,1,0:T(8,128)(2,1)}, u32[]{:S(2)}, u32[]{:S(2)}) async-start(bf16[32,16,2048]{2,1,0:T(8,128)(2,1)} %bitcast.99), calls=%async_computation.2 | async-start | bytes 4194304 | tf_op jit(solution)/shard_map/all_to_all | solution.py:116
  57.1 2.6 %collective-permute-done.1 = bf16[512,512]{1,0:T(8,128)(2,1)} collective-permute-done((bf16[512,512]{1,0:T(8,128)(2,1)}, bf16[512,512]{1,0:T(8,128)(2,1)}, u32[]{:S(2)}, u32[]{:S(2)}) %collective-permute-start.1) | collective-permute-done | bytes 524320 | tf_op jit(solution)/shard_map/ppermute | solution.py:20
  62.6 6.2 %fusion.6 = f32[512,1408]{1,0:T(8,128)S(1)} fusion(bf16[1,2048,1408]{2,1,0:T(8,128)(2,1)} %param.13, bf16[512,2048]{1,0:T(8,128)(2,1)S(1)} %constant_dynamic-update-slice_fusion.4, f32[2048]{0:T(1024)S(1)} %copy-done.5, f32[512]{0:T(512)S(1)} %add_rsqrt_fusion), kind=kOutput, calls=%fused_computation.7 | convolution fusion | flops 2956984320 | bytes 10758144 | tf_op jit(solution)/shard_map/dot_general | solution.py:126
  68.8 3.6 %multiply_convert_fusion = bf16[512,1408]{1,0:T(8,128)(2,1)S(1)} fusion(f32[512,1408]{1,0:T(8,128)S(1)} %fusion.6, bf16[1,2048,1408]{2,1,0:T(8,128)(2,1)S(1)} %bitcast.122, bf16[512,2048]{1,0:T(8,128)(2,1)S(1)} %constant_dynamic-update-slice_fusion.4, f32[2048]{0:T(1024)S(1)} %copy-done.5, f32[512]{0:T(512)S(1)} %add_rsqrt_fusion), kind=kOutput, calls=%fused_computation.17 | convolution fusion | flops 2961309696 | bytes 12199936 | tf_op jit(solution)/shard_map/dot_general | solution.py:127
  76.0 2.5 %collective-permute-start.4 = (bf16[512,512]{1,0:T(8,128)(2,1)}, bf16[512,512]{1,0:T(8,128)(2,1)S(1)}, u32[]{:S(2)}, u32[]{:S(2)}) collective-permute-start(bf16[512,512]{1,0:T(8,128)(2,1)} %fusion.42), channel_id=1, source_target_pairs={{0,2},{1,3},{2,0},{3,1},{4,6},{5,7},{6,4},{7,5},{8,10},{9,11},{10,... | collective-permute-start | bytes 1572872 | tf_op jit(solution)/shard_map/ppermute | solution.py:20
  81.5 4.1 %all-to-all-done.2 = bf16[32,16,2048]{2,1,0:T(8,128)(2,1)} async-done(((bf16[32,16,2048]{2,1,0:T(8,128)(2,1)}), bf16[32,16,2048]{2,1,0:T(8,128)(2,1)}, u32[]{:S(2)}, u32[]{:S(2)}) %all-to-all-start.2) | async-done | bytes 2097184 | tf_op jit(solution)/shard_map/all_to_all | solution.py:116
  85.6 6.5 %fusion.4 = f32[512,1408]{1,0:T(8,128)S(1)} fusion(bf16[512,2048]{1,0:T(8,128)(2,1)} %bitcast.15, bf16[1,2048,1408]{2,1,0:T(8,128)(2,1)} %param.13), kind=kOutput, calls=%fused_computation.5 | convolution fusion | flops 2952790016 | bytes 10747904 | tf_op jit(solution)/shard_map/dot_general | solution.py:126
  92.2 6.9 %fusion.14 = bf16[512,1408]{1,0:T(8,128)(2,1)S(1)} fusion(bf16[512,2048]{1,0:T(8,128)(2,1)} %bitcast.15, bf16[1,2048,1408]{2,1,0:T(8,128)(2,1)} %param.14, f32[512,1408]{1,0:T(8,128)S(1)} %fusion.4), kind=kOutput, calls=%fused_computation.16 | convolution fusion | flops 2957115392 | bytes 12189696 | tf_op jit(solution)/shard_map/dot_general | solution.py:127
  102.5 2.5 %collective-permute-start.9 = (bf16[512,512]{1,0:T(8,128)(2,1)S(1)}, bf16[512,512]{1,0:T(8,128)(2,1)S(1)}, u32[]{:S(2)}, u32[]{:S(2)}) collective-permute-start(bf16[512,512]{1,0:T(8,128)(2,1)S(1)} %fusion.45), channel_id=1, source_target_pairs={{0,2},{1,3},{2,0},{3,1},{4,6},{5,7},{6,4},{7,5},{8,10},{9,11},{10,... | collective-permute-start | bytes 1572872 | tf_op jit(solution)/shard_map/ppermute | solution.py:20
  107.8 2.9 %add_convert_fusion.1 = bf16[512,512]{1,0:T(8,128)(2,1)} fusion(bf16[512,512]{1,0:T(8,128)(2,1)} %collective-permute-done.5, bf16[512,512]{1,0:T(8,128)(2,1)S(1)} %collective-permute-done.4, bf16[512,512]{1,0:T(8,128)(2,1)S(1)} %collective-permute-done.3, bf16[512,1408]{1,0:T(8,128)(2,1)S(1)} %copy-done.8, bf16[1,1408,2048]{2,1,0:T(8,128)(2,1)S(1)} %bitcast.126, ...), kind=kOutput, calls=%fused_computation.65 | convolution fusion | flops 740556800 | bytes 4980740 | tf_op jit(solution)/shard_map/dot_general | solution.py:66
  110.7 5.2 %all-to-all-start.1 = ((bf16[32,16,512]{2,1,0:T(8,128)(2,1)}), bf16[32,16,512]{2,1,0:T(8,128)(2,1)S(1)}, u32[]{:S(2)}, u32[]{:S(2)}) async-start(bf16[32,16,512]{2,1,0:T(8,128)(2,1)} %bitcast.12), calls=%async_computation.1 | async-start | bytes 1048576 | tf_op jit(solution)/shard_map/all_to_all | solution.py:131
  116.0 10.3 %collective-permute-done.9 = bf16[512,512]{1,0:T(8,128)(2,1)S(1)} collective-permute-done((bf16[512,512]{1,0:T(8,128)(2,1)S(1)}, bf16[512,512]{1,0:T(8,128)(2,1)S(1)}, u32[]{:S(2)}, u32[]{:S(2)}) %collective-permute-start.9) | collective-permute-done | bytes 524320 | tf_op jit(solution)/shard_map/ppermute | solution.py:20
  127.2 3.7 %add_convert_fusion = bf16[512,512]{1,0:T(8,128)(2,1)} fusion(bf16[512,512]{1,0:T(8,128)(2,1)} %collective-permute-done.10, bf16[512,512]{1,0:T(8,128)(2,1)S(1)} %collective-permute-done.9, bf16[512,512]{1,0:T(8,128)(2,1)S(1)} %collective-permute-done.8, bf16[512,1408]{1,0:T(8,128)(2,1)} %copy-done.6, bf16[1,1408,2048]{2,1,0:T(8,128)(2,1)} %param.15, ...), kind=kOutput, calls=%fused_computation.62 | convolution fusion | flops 740556800 | bytes 4980740 | tf_op jit(solution)/shard_map/dot_general | solution.py:66
  131.0 5.1 %all-to-all-start.3 = ((bf16[32,16,512]{2,1,0:T(8,128)(2,1)}), bf16[32,16,512]{2,1,0:T(8,128)(2,1)S(1)}, u32[]{:S(2)}, u32[]{:S(2)}) async-start(bf16[32,16,512]{2,1,0:T(8,128)(2,1)} %bitcast.16), calls=%async_computation.3 | async-start | bytes 1048576 | tf_op jit(solution)/shard_map/all_to_all | solution.py:131
  137.1 10.7 %all-to-all-done.3 = bf16[32,16,512]{2,1,0:T(8,128)(2,1)S(1)} async-done(((bf16[32,16,512]{2,1,0:T(8,128)(2,1)}), bf16[32,16,512]{2,1,0:T(8,128)(2,1)S(1)}, u32[]{:S(2)}, u32[]{:S(2)}) %all-to-all-start.3) | async-done | bytes 524320 | tf_op jit(solution)/shard_map/all_to_all | solution.py:131
  148.9 2.0 %collective-permute-start.11 = (f32[256]{0:T(256)S(1)}, f32[256]{0:T(256)S(1)}, u32[]{:S(2)}, u32[]{:S(2)}) collective-permute-start(f32[256]{0:T(256)S(1)} %get-tuple-element.22), channel_id=1, source_target_pairs={{0,1},{1,2},{2,3},{3,0},{4,5},{5,6},{6,7},{7,4},{8,9},{9,10},{10,1... | collective-permute-start | bytes 3080 | tf_op jit(solution)/shard_map/ppermute | solution.py:20
  (102 shorter events, 32.3 us)
Async XLA Ops:
  0.6 9.8 %collective-permute-start = (bf16[256,512]{1,0:T(8,128)(2,1)}, bf16[256,512]{1,0:T(8,128)(2,1)S(1)}, u32[]{:S(2)}, u32[]{:S(2)}) collective-permute-start(bf16[256,512]{1,0:T(8,128)(2,1)} %param.8), channel_id=1, source_target_pairs={{0,2},{1,3},{2,0},{3,1},{4,6},{5,7},{6,4},{7,5},{8,10},{9,11},{10,... | collective-permute-start | bytes 786440 | tf_op jit(solution)/shard_map/ppermute | solution.py:20
  10.4 12.1 %copy-start.4 = (f32[256,2]{0,1:T(2,128)S(1)}, f32[256,2]{0,1:T(2,128)}, u32[]{:S(2)}) copy-start(f32[256,2]{0,1:T(2,128)} %param.10) | copy-start | bytes 6148
  10.4 28.9 %copy-start = (bf16[256,512]{1,0:T(8,128)(2,1)S(1)}, bf16[256,512]{1,0:T(8,128)(2,1)}, u32[]{:S(2)}) copy-start(bf16[256,512]{1,0:T(8,128)(2,1)} %param.8) | copy-start | bytes 786436
  12.9 26.4 %all-to-all-start = ((bf16[32,16,1024]{2,1,0:T(8,128)(2,1)}), bf16[32,16,1024]{2,1,0:T(8,128)(2,1)S(1)}, u32[]{:S(2)}, u32[]{:S(2)}) async-start(bf16[32,16,1024]{2,1,0:T(8,128)(2,1)} %bitcast.4), calls=%async_computation | async-start | bytes 2097152 | tf_op jit(solution)/shard_map/all_to_all | solution.py:116
  39.3 9.1 %collective-permute-start.6 = (bf16[256,512]{1,0:T(8,128)(2,1)S(1)}, bf16[256,512]{1,0:T(8,128)(2,1)S(1)}, u32[]{:S(2)}, u32[]{:S(2)}) collective-permute-start(bf16[256,512]{1,0:T(8,128)(2,1)S(1)} %copy-done), channel_id=1, source_target_pairs={{0,1},{1,2},{2,3},{3,0},{4,5},{5,6},{6,7},{7,4},{8,9},{9,10},{10,1... | collective-permute-start | bytes 786440 | tf_op jit(solution)/shard_map/ppermute | solution.py:20
  40.6 7.9 %collective-permute-start.7 = (bf16[256,512]{1,0:T(8,128)(2,1)S(1)}, bf16[256,512]{1,0:T(8,128)(2,1)S(1)}, u32[]{:S(2)}, u32[]{:S(2)}) collective-permute-start(bf16[256,512]{1,0:T(8,128)(2,1)S(1)} %copy-done), channel_id=1, source_target_pairs={{0,3},{1,0},{2,1},{3,2},{4,7},{5,4},{6,5},{7,6},{8,11},{9,8},{10,9... | collective-permute-start | bytes 786440 | tf_op jit(solution)/shard_map/ppermute | solution.py:20
  43.3 16.5 %collective-permute-start.1 = (bf16[512,512]{1,0:T(8,128)(2,1)}, bf16[512,512]{1,0:T(8,128)(2,1)}, u32[]{:S(2)}, u32[]{:S(2)}) collective-permute-start(bf16[512,512]{1,0:T(8,128)(2,1)} %get-tuple-element.16), channel_id=1, source_target_pairs={{0,1},{1,2},{2,3},{3,0},{4,5},{5,6},{6,7},{7,4},{8,9},{9,10},{10,1... | collective-permute-start | bytes 1572872 | tf_op jit(solution)/shard_map/ppermute | solution.py:20
  43.3 17.6 %collective-permute-start.2 = (bf16[512,512]{1,0:T(8,128)(2,1)}, bf16[512,512]{1,0:T(8,128)(2,1)}, u32[]{:S(2)}, u32[]{:S(2)}) collective-permute-start(bf16[512,512]{1,0:T(8,128)(2,1)} %get-tuple-element.16), channel_id=1, source_target_pairs={{0,3},{1,0},{2,1},{3,2},{4,7},{5,4},{6,5},{7,6},{8,11},{9,8},{10,9... | collective-permute-start | bytes 1572872 | tf_op jit(solution)/shard_map/ppermute | solution.py:20
  51.1 34.5 %all-to-all-start.2 = ((bf16[32,16,2048]{2,1,0:T(8,128)(2,1)}), bf16[32,16,2048]{2,1,0:T(8,128)(2,1)}, u32[]{:S(2)}, u32[]{:S(2)}) async-start(bf16[32,16,2048]{2,1,0:T(8,128)(2,1)} %bitcast.99), calls=%async_computation.2 | async-start | bytes 4194304 | tf_op jit(solution)/shard_map/all_to_all | solution.py:116
  62.5 9.8 %slice-start.2 = ((s8[5767168]{0:T(1024)(128)(4,1)}), s8[4194304]{0:T(1024)(128)(4,1)S(1)}, s32[]{:S(2)}) async-start(s8[5767168]{0:T(1024)(128)(4,1)} %bitcast.123), calls=%async_computation.6 | async-start | bytes 8388608
  74.2 32.6 %collective-permute-start.3 = (bf16[512,512]{1,0:T(8,128)(2,1)}, bf16[512,512]{1,0:T(8,128)(2,1)S(1)}, u32[]{:S(2)}, u32[]{:S(2)}) collective-permute-start(bf16[512,512]{1,0:T(8,128)(2,1)} %fusion.36), channel_id=1, source_target_pairs={{0,1},{1,2},{2,3},{3,0},{4,5},{5,6},{6,7},{7,4},{8,9},{9,10},{10,1... | collective-permute-start | bytes 1572872 | tf_op jit(solution)/shard_map/ppermute | solution.py:20
  76.0 31.7 %collective-permute-start.4 = (bf16[512,512]{1,0:T(8,128)(2,1)}, bf16[512,512]{1,0:T(8,128)(2,1)S(1)}, u32[]{:S(2)}, u32[]{:S(2)}) collective-permute-start(bf16[512,512]{1,0:T(8,128)(2,1)} %fusion.42), channel_id=1, source_target_pairs={{0,2},{1,3},{2,0},{3,1},{4,6},{5,7},{6,4},{7,5},{8,10},{9,11},{10,... | collective-permute-start | bytes 1572872 | tf_op jit(solution)/shard_map/ppermute | solution.py:20
  80.4 27.4 %collective-permute-start.5 = (bf16[512,512]{1,0:T(8,128)(2,1)}, bf16[512,512]{1,0:T(8,128)(2,1)}, u32[]{:S(2)}, u32[]{:S(2)}) collective-permute-start(bf16[512,512]{1,0:T(8,128)(2,1)} %fusion.48), channel_id=1, source_target_pairs={{0,3},{1,0},{2,1},{3,2},{4,7},{5,4},{6,5},{7,6},{8,11},{9,8},{10,9... | collective-permute-start | bytes 1572872 | tf_op jit(solution)/shard_map/ppermute | solution.py:20
  85.6 13.5 %slice-start.4 = ((s8[5767168]{0:T(1024)(128)(4,1)}), s8[4194304]{0:T(1024)(128)(4,1)S(1)}, s32[]{:S(2)}) async-start(s8[5767168]{0:T(1024)(128)(4,1)} %bitcast.125), calls=%async_computation.8 | async-start | bytes 8388608
  92.1 6.9 %slice-start.5 = ((s8[5767168]{0:T(1024)(128)(4,1)}), s8[1572864]{0:T(1024)(128)(4,1)S(1)}, s32[]{:S(2)}) async-start(s8[5767168]{0:T(1024)(128)(4,1)} %bitcast.125), calls=%async_computation.9 | async-start | bytes 3145728
  100.1 15.9 %collective-permute-start.8 = (bf16[512,512]{1,0:T(8,128)(2,1)S(1)}, bf16[512,512]{1,0:T(8,128)(2,1)S(1)}, u32[]{:S(2)}, u32[]{:S(2)}) collective-permute-start(bf16[512,512]{1,0:T(8,128)(2,1)S(1)} %fusion.39), channel_id=1, source_target_pairs={{0,1},{1,2},{2,3},{3,0},{4,5},{5,6},{6,7},{7,4},{8,9},{9,10},{10,1... | collective-permute-start | bytes 1572872 | tf_op jit(solution)/shard_map/ppermute | solution.py:20
  102.5 23.8 %collective-permute-start.9 = (bf16[512,512]{1,0:T(8,128)(2,1)S(1)}, bf16[512,512]{1,0:T(8,128)(2,1)S(1)}, u32[]{:S(2)}, u32[]{:S(2)}) collective-permute-start(bf16[512,512]{1,0:T(8,128)(2,1)S(1)} %fusion.45), channel_id=1, source_target_pairs={{0,2},{1,3},{2,0},{3,1},{4,6},{5,7},{6,4},{7,5},{8,10},{9,11},{10,... | collective-permute-start | bytes 1572872 | tf_op jit(solution)/shard_map/ppermute | solution.py:20
  106.8 20.4 %collective-permute-start.10 = (bf16[512,512]{1,0:T(8,128)(2,1)}, bf16[512,512]{1,0:T(8,128)(2,1)}, u32[]{:S(2)}, u32[]{:S(2)}) collective-permute-start(bf16[512,512]{1,0:T(8,128)(2,1)} %fusion.51), channel_id=1, source_target_pairs={{0,3},{1,0},{2,1},{3,2},{4,7},{5,4},{6,5},{7,6},{8,11},{9,8},{10,9... | collective-permute-start | bytes 1572872 | tf_op jit(solution)/shard_map/ppermute | solution.py:20
  110.7 20.3 %all-to-all-start.1 = ((bf16[32,16,512]{2,1,0:T(8,128)(2,1)}), bf16[32,16,512]{2,1,0:T(8,128)(2,1)S(1)}, u32[]{:S(2)}, u32[]{:S(2)}) async-start(bf16[32,16,512]{2,1,0:T(8,128)(2,1)} %bitcast.12), calls=%async_computation.1 | async-start | bytes 1048576 | tf_op jit(solution)/shard_map/all_to_all | solution.py:131
  131.0 16.8 %all-to-all-start.3 = ((bf16[32,16,512]{2,1,0:T(8,128)(2,1)}), bf16[32,16,512]{2,1,0:T(8,128)(2,1)S(1)}, u32[]{:S(2)}, u32[]{:S(2)}) async-start(bf16[32,16,512]{2,1,0:T(8,128)(2,1)} %bitcast.16), calls=%async_computation.3 | async-start | bytes 1048576 | tf_op jit(solution)/shard_map/all_to_all | solution.py:131
  147.8 8.1 %copy-start.3 = (f32[512]{0:T(512)S(1)}, f32[512]{0:T(512)}, u32[]{:S(2)}) copy-start(f32[512]{0:T(512)} %param.12) | copy-start | bytes 6148
  148.9 4.8 %collective-permute-start.11 = (f32[256]{0:T(256)S(1)}, f32[256]{0:T(256)S(1)}, u32[]{:S(2)}, u32[]{:S(2)}) collective-permute-start(f32[256]{0:T(256)S(1)} %get-tuple-element.22), channel_id=1, source_target_pairs={{0,1},{1,2},{2,3},{3,0},{4,5},{5,6},{6,7},{7,4},{8,9},{9,10},{10,1... | collective-permute-start | bytes 3080 | tf_op jit(solution)/shard_map/ppermute | solution.py:20
  150.9 3.9 %collective-permute-start.12 = (f32[256]{0:T(256)S(1)}, f32[256]{0:T(256)S(1)}, u32[]{:S(2)}, u32[]{:S(2)}) collective-permute-start(f32[256]{0:T(256)S(1)} %get-tuple-element.22), channel_id=1, source_target_pairs={{0,2},{1,3},{2,0},{3,1},{4,6},{5,7},{6,4},{7,5},{8,10},{9,11},{10,... | collective-permute-start | bytes 3080 | tf_op jit(solution)/shard_map/ppermute | solution.py:20
  152.5 2.7 %collective-permute-start.13 = (f32[256]{0:T(256)S(1)}, f32[256]{0:T(256)S(1)}, u32[]{:S(2)}, u32[]{:S(2)}) collective-permute-start(f32[256]{0:T(256)S(1)} %get-tuple-element.22), channel_id=1, source_target_pairs={{0,3},{1,0},{2,1},{3,2},{4,7},{5,4},{6,5},{7,6},{8,11},{9,8},{10,9... | collective-permute-start | bytes 3080 | tf_op jit(solution)/shard_map/ppermute | solution.py:20
  (9 other events, 45.5 us)

commit v17 on v13

--- a/solution.py
+++ b/solution.py
@@ -102,7 +102,7 @@
         for k in range(top):
             hit = (slot_ids[:, None] == chunk_pairs[None, :, k]) & (owner_pairs[None, :, k] == c)
             dispatch = dispatch | hit
-        relay = c == 0
+        relay = True
         source = hidden if far is None else jnp.concatenate([hidden, far], axis=1)
         source = source if relay else normed_in
         outgoing = jnp.dot(

time: 152 us -> 169 us (1.11)
  waiting for transfers between devices: 55.4 us -> 73.4 us
  matrix products: 44.5 us -> 34.1 us
  starting transfers between devices: 40.1 us -> 46.5 us
  local copies, waits for them, and re-layouts: 5.86 us -> 9.28 us
    all_to_all x2, waiting for transfers between devices: 19.3 us -> 28.4 us  [shards(): lax.all_to_all(outgoing, 'req', split_axis=0, concat_axis=0, tiled=True)]
    ppermute x14, waiting for transfers between devices: 25.4 us -> 33.8 us  [shift_tp(): lax.ppermute(value, 'tp', [(j, (j + step) % tp_count) for j in range(tp_c...]
    ppermute x14, starting transfers between devices: 15.8 us -> 21.7 us  [shift_tp(): lax.ppermute(value, 'tp', [(j, (j + step) % tp_count) for j in range(tp_c...]
    dot_general x8, matrix products: 16.5 us -> 12.3 us  [down_scatter_sum_tp(): jnp.dot(activ, w_block, preferred_element_type=jnp.float32)]
    dot_general x2, matrix products: 12.6 us -> 9.64 us  [shards(): jnp.dot(flat_rows, gate_weight[0], preferred_element_type=jnp.float32)]
    all_to_all x2, starting transfers between devices: 8.83 us -> 10.9 us  [shards(): lax.all_to_all(summed, 'req', split_axis=0, concat_axis=0, tiled=True)]
    dot_general x2, matrix products: 4.67 us -> 2.94 us  [shards(): jnp.dot(dispatch.astype(jnp.bfloat16), source, preferred_element_type=jnp...]
    dynamic_update_slice x3 -> x5, local copies, waits for them, and re-layouts: 2.25 us -> 3.53 us  [gather_pair_tp(): lax.dynamic_update_slice_in_dim(whole, part, (me - s) % tp_count * cols,...]
  transfers between devices with their start and end apart: 18 -> 18, of which waited for: 10 -> 12; matrix products, arithmetic and copies ran while one was open for 33% -> 18% of each run, Pallas kernels for 0% -> 0%
where the time goes in v17:
time: 169 us; the launch traced here: 168 us
  waiting for transfers between devices  73.4 us (43%)
  starting transfers between devices  46.5 us (28%)
  matrix products  34.1 us (20%)
  local copies, waits for them, and re-layouts  9.28 us (5%)
  other arithmetic  3.98 us (2%)
    ppermute x14, waiting for transfers between devices, shift_tp(): lax.ppermute(value, 'tp', [(j, (j + step) % tp_count) for j in range(tp_c...  33.8 us
    all_to_all x2, waiting for transfers between devices, shards(): lax.all_to_all(outgoing, 'req', split_axis=0, concat_axis=0, tiled=True)  28.4 us
    ppermute x14, starting transfers between devices, shift_tp(): lax.ppermute(value, 'tp', [(j, (j + step) % tp_count) for j in range(tp_c...  21.7 us
    all_to_all x2, starting transfers between devices, shards(): lax.all_to_all(outgoing, 'req', split_axis=0, concat_axis=0, tiled=True)  13.9 us
    dot_general x8, matrix products, down_scatter_sum_tp(): jnp.dot(activ, w_block, preferred_element_type=jnp.float32)  12.3 us
    all_to_all x2, waiting for transfers between devices, shards(): lax.all_to_all(summed, 'req', split_axis=0, concat_axis=0, tiled=True)  11.2 us
    all_to_all x2, starting transfers between devices, shards(): lax.all_to_all(summed, 'req', split_axis=0, concat_axis=0, tiled=True)  10.9 us
    dot_general x2, matrix products, shards(): jnp.dot(flat_rows, gate_weight[0], preferred_element_type=jnp.float32)  9.64 us
  transfers between devices with their start and end apart: 18, of which 12 were waited for; matrix products, arithmetic and copies ran while one was open for 18% of the time, Pallas kernels for 0%

profile of v17, /device:TPU:1, one launch (start us, length us, event | category | flops | bytes accessed | tf_op | source)
XLA Modules:
  0.0 168.5 jit_solution(3416447985781718493)
XLA Ops:
  0.6 3.8 %collective-permute-start = (bf16[256,512]{1,0:T(8,128)(2,1)}, bf16[256,512]{1,0:T(8,128)(2,1)S(1)}, u32[]{:S(2)}, u32[]{:S(2)}) collective-permute-start(bf16[256,512]{1,0:T(8,128)(2,1)} %param.8), channel_id=1, source_target_pairs={{0,2},{1,3},{2,0},{3,1},{4,6},{5,7},{6,4},{7,5},{8,10},{9,11},{10,... | collective-permute-start | bytes 786440 | tf_op jit(solution)/shard_map/ppermute | solution.py:20
  11.9 9.5 %all-to-all-start = ((bf16[32,16,1024]{2,1,0:T(8,128)(2,1)}), bf16[32,16,1024]{2,1,0:T(8,128)(2,1)S(1)}, u32[]{:S(2)}, u32[]{:S(2)}) async-start(bf16[32,16,1024]{2,1,0:T(8,128)(2,1)} %bitcast.4), calls=%async_computation | async-start | bytes 2097152 | tf_op jit(solution)/shard_map/all_to_all | solution.py:112
  22.9 15.5 %all-to-all-done = bf16[32,16,1024]{2,1,0:T(8,128)(2,1)S(1)} async-done(((bf16[32,16,1024]{2,1,0:T(8,128)(2,1)}), bf16[32,16,1024]{2,1,0:T(8,128)(2,1)S(1)}, u32[]{:S(2)}, u32[]{:S(2)}) %all-to-all-start) | async-done | bytes 1048608 | tf_op jit(solution)/shard_map/all_to_all | solution.py:112
  38.3 4.5 %all-to-all-start.2 = ((bf16[32,16,1024]{2,1,0:T(8,128)(2,1)}), bf16[32,16,1024]{2,1,0:T(8,128)(2,1)}, u32[]{:S(2)}, u32[]{:S(2)}) async-start(bf16[32,16,1024]{2,1,0:T(8,128)(2,1)} %bitcast.14), calls=%async_computation.2 | async-start | bytes 2097152 | tf_op jit(solution)/shard_map/all_to_all | solution.py:112
  46.8 12.9 %all-to-all-done.2 = bf16[32,16,1024]{2,1,0:T(8,128)(2,1)} async-done(((bf16[32,16,1024]{2,1,0:T(8,128)(2,1)}), bf16[32,16,1024]{2,1,0:T(8,128)(2,1)}, u32[]{:S(2)}, u32[]{:S(2)}) %all-to-all-start.2) | async-done | bytes 1048608 | tf_op jit(solution)/shard_map/all_to_all | solution.py:112
  66.4 9.6 %collective-permute-done.6 = bf16[512,512]{1,0:T(8,128)(2,1)S(1)} collective-permute-done((bf16[512,512]{1,0:T(8,128)(2,1)S(1)}, bf16[512,512]{1,0:T(8,128)(2,1)S(1)}, u32[]{:S(2)}, u32[]{:S(2)}) %collective-permute-start.6) | collective-permute-done | bytes 524320 | tf_op jit(solution)/shard_map/ppermute | solution.py:20
  77.9 6.2 %fusion.4 = f32[512,1408]{1,0:T(8,128)S(1)} fusion(bf16[1,2048,1408]{2,1,0:T(8,128)(2,1)} %param.13, bf16[512,2048]{1,0:T(8,128)(2,1)S(1)} %get-tuple-element.24, f32[512]{0:T(512)S(1)} %add_rsqrt_fusion, f32[2048]{0:T(1024)S(1)} %copy-done.3), kind=kOutput, calls=%fused_computation.5 | convolution fusion | flops 2956984320 | bytes 10758144 | tf_op jit(solution)/shard_map/dot_general | solution.py:121
  84.1 3.6 %multiply_convert_fusion = bf16[512,1408]{1,0:T(8,128)(2,1)S(1)} fusion(f32[512,1408]{1,0:T(8,128)S(1)} %fusion.4, bf16[1,2048,1408]{2,1,0:T(8,128)(2,1)S(1)} %bitcast.121, bf16[512,2048]{1,0:T(8,128)(2,1)S(1)} %get-tuple-element.24, f32[512]{0:T(512)S(1)} %add_rsqrt_fusion, f32[2048]{0:T(1024)S(1)} %copy-done.3), kind=kOutput, calls=%fused_computation.19 | convolution fusion | flops 2961309696 | bytes 12199936 | tf_op jit(solution)/shard_map/dot_general | solution.py:122
  90.6 3.0 %collective-permute-start.9 = (bf16[512,512]{1,0:T(8,128)(2,1)S(1)}, bf16[512,512]{1,0:T(8,128)(2,1)S(1)}, u32[]{:S(2)}, u32[]{:S(2)}) collective-permute-start(bf16[512,512]{1,0:T(8,128)(2,1)S(1)} %fusion.39), channel_id=1, source_target_pairs={{0,2},{1,3},{2,0},{3,1},{4,6},{5,7},{6,4},{7,5},{8,10},{9,11},{10,... | collective-permute-start | bytes 1572872 | tf_op jit(solution)/shard_map/ppermute | solution.py:20
  95.8 3.5 %fusion.6 = f32[512,1408]{1,0:T(8,128)S(1)} fusion(bf16[1,2048,1408]{2,1,0:T(8,128)(2,1)S(1)} %bitcast.119, bf16[512,2048]{1,0:T(8,128)(2,1)S(1)} %get-tuple-element.25, f32[2048]{0:T(1024)S(1)} %copy-done.3, f32[512]{0:T(512)S(1)} %add_rsqrt_fusion.1), kind=kOutput, calls=%fused_computation.7 | convolution fusion | flops 2956984320 | bytes 10758144 | tf_op jit(solution)/shard_map/dot_general | solution.py:121
  99.3 3.6 %multiply_convert_fusion.1 = bf16[512,1408]{1,0:T(8,128)(2,1)S(1)} fusion(f32[512,1408]{1,0:T(8,128)S(1)} %fusion.6, bf16[1,2048,1408]{2,1,0:T(8,128)(2,1)S(1)} %bitcast.121, bf16[512,2048]{1,0:T(8,128)(2,1)S(1)} %get-tuple-element.25, f32[2048]{0:T(1024)S(1)} %copy-done.3, f32[512]{0:T(512)S(1)} %add_rsqrt_fusion.1), kind=kOutput, calls=%fused_computation.20 | convolution fusion | flops 2961309696 | bytes 12199936 | tf_op jit(solution)/shard_map/dot_general | solution.py:122
  106.2 1.8 %fusion.42 = bf16[512,512]{1,0:T(8,128)(2,1)} fusion(bf16[512,1408]{1,0:T(8,128)(2,1)S(1)} %multiply_convert_fusion.1, bf16[1,1408,2048]{2,1,0:T(8,128)(2,1)S(1)} %bitcast.123, s32[]{:T(128)S(6)} %select_n.183), kind=kOutput, calls=%fused_computation.43 | convolution fusion | flops 738459648 | bytes 3407876 | tf_op jit(solution)/shard_map/dot_general | solution.py:66
  108.0 2.0 %collective-permute-start.5 = (bf16[512,512]{1,0:T(8,128)(2,1)}, bf16[512,512]{1,0:T(8,128)(2,1)}, u32[]{:S(2)}, u32[]{:S(2)}) collective-permute-start(bf16[512,512]{1,0:T(8,128)(2,1)} %fusion.42), channel_id=1, source_target_pairs={{0,3},{1,0},{2,1},{3,2},{4,7},{5,4},{6,5},{7,6},{8,11},{9,8},{10,9... | collective-permute-start | bytes 1572872 | tf_op jit(solution)/shard_map/ppermute | solution.py:20
  110.1 4.4 %collective-permute-done.9 = bf16[512,512]{1,0:T(8,128)(2,1)S(1)} collective-permute-done((bf16[512,512]{1,0:T(8,128)(2,1)S(1)}, bf16[512,512]{1,0:T(8,128)(2,1)S(1)}, u32[]{:S(2)}, u32[]{:S(2)}) %collective-permute-start.9) | collective-permute-done | bytes 524320 | tf_op jit(solution)/shard_map/ppermute | solution.py:20
  114.5 2.5 %collective-permute-done.10 = bf16[512,512]{1,0:T(8,128)(2,1)S(1)} collective-permute-done((bf16[512,512]{1,0:T(8,128)(2,1)S(1)}, bf16[512,512]{1,0:T(8,128)(2,1)S(1)}, u32[]{:S(2)}, u32[]{:S(2)}) %collective-permute-start.10) | collective-permute-done | bytes 524320 | tf_op jit(solution)/shard_map/ppermute | solution.py:20
  117.0 1.8 %add_convert_fusion = bf16[512,512]{1,0:T(8,128)(2,1)} fusion(bf16[512,512]{1,0:T(8,128)(2,1)S(1)} %collective-permute-done.10, bf16[512,512]{1,0:T(8,128)(2,1)S(1)} %collective-permute-done.9, bf16[512,512]{1,0:T(8,128)(2,1)S(1)} %collective-permute-done.8, bf16[512,1408]{1,0:T(8,128)(2,1)S(1)} %multiply_convert_fusion, ...), kind=kOutput, calls=%fused_computation.61 | convolution fusion | flops 740556800 | bytes 4980740 | tf_op jit(solution)/shard_map/dot_general | solution.py:66
  118.8 5.7 %all-to-all-start.3 = ((bf16[32,16,512]{2,1,0:T(8,128)(2,1)}), bf16[32,16,512]{2,1,0:T(8,128)(2,1)S(1)}, u32[]{:S(2)}, u32[]{:S(2)}) async-start(bf16[32,16,512]{2,1,0:T(8,128)(2,1)} %bitcast.16), calls=%async_computation.3 | async-start | bytes 1048576 | tf_op jit(solution)/shard_map/all_to_all | solution.py:126
  124.5 4.2 %collective-permute-done.3 = bf16[512,512]{1,0:T(8,128)(2,1)S(1)} collective-permute-done((bf16[512,512]{1,0:T(8,128)(2,1)S(1)}, bf16[512,512]{1,0:T(8,128)(2,1)S(1)}, u32[]{:S(2)}, u32[]{:S(2)}) %collective-permute-start.3) | collective-permute-done | bytes 524320 | tf_op jit(solution)/shard_map/ppermute | solution.py:20
  128.7 8.2 %collective-permute-done.4 = bf16[512,512]{1,0:T(8,128)(2,1)S(1)} collective-permute-done((bf16[512,512]{1,0:T(8,128)(2,1)S(1)}, bf16[512,512]{1,0:T(8,128)(2,1)S(1)}, u32[]{:S(2)}, u32[]{:S(2)}) %collective-permute-start.4) | collective-permute-done | bytes 524320 | tf_op jit(solution)/shard_map/ppermute | solution.py:20
  136.9 1.5 collective-permute-done.5
  138.5 3.8 %add_convert_fusion.1 = bf16[512,512]{1,0:T(8,128)(2,1)} fusion(bf16[512,512]{1,0:T(8,128)(2,1)} %collective-permute-done.5, bf16[512,512]{1,0:T(8,128)(2,1)S(1)} %collective-permute-done.4, bf16[512,512]{1,0:T(8,128)(2,1)S(1)} %collective-permute-done.3, bf16[512,1408]{1,0:T(8,128)(2,1)} %copy-done.4, bf16[1,1408,2048]{2,1,0:T(8,128)(2,1)} %param.15, ...), kind=kOutput, calls=%fused_computation.62 | convolution fusion | flops 740556800 | bytes 4980740 | tf_op jit(solution)/shard_map/dot_general | solution.py:66
  142.2 5.1 %all-to-all-start.1 = ((bf16[32,16,512]{2,1,0:T(8,128)(2,1)}), bf16[32,16,512]{2,1,0:T(8,128)(2,1)S(1)}, u32[]{:S(2)}, u32[]{:S(2)}) async-start(bf16[32,16,512]{2,1,0:T(8,128)(2,1)} %bitcast.12), calls=%async_computation.1 | async-start | bytes 1048576 | tf_op jit(solution)/shard_map/all_to_all | solution.py:126
  148.0 11.2 %all-to-all-done.1 = bf16[32,16,512]{2,1,0:T(8,128)(2,1)S(1)} async-done(((bf16[32,16,512]{2,1,0:T(8,128)(2,1)}), bf16[32,16,512]{2,1,0:T(8,128)(2,1)S(1)}, u32[]{:S(2)}, u32[]{:S(2)}) %all-to-all-start.1) | async-done | bytes 524320 | tf_op jit(solution)/shard_map/all_to_all | solution.py:126
  162.2 2.1 %collective-permute-start.12 = (f32[256]{0:T(256)S(1)}, f32[256]{0:T(256)S(1)}, u32[]{:S(2)}, u32[]{:S(2)}) collective-permute-start(f32[256]{0:T(256)S(1)} %get-tuple-element.22), channel_id=1, source_target_pairs={{0,2},{1,3},{2,0},{3,1},{4,6},{5,7},{6,4},{7,5},{8,10},{9,11},{10,... | collective-permute-start | bytes 3080 | tf_op jit(solution)/shard_map/ppermute | solution.py:20
  (95 shorter events, 37.3 us)
Async XLA Ops:
  0.6 9.8 %collective-permute-start = (bf16[256,512]{1,0:T(8,128)(2,1)}, bf16[256,512]{1,0:T(8,128)(2,1)S(1)}, u32[]{:S(2)}, u32[]{:S(2)}) collective-permute-start(bf16[256,512]{1,0:T(8,128)(2,1)} %param.8), channel_id=1, source_target_pairs={{0,2},{1,3},{2,0},{3,1},{4,6},{5,7},{6,4},{7,5},{8,10},{9,11},{10,... | collective-permute-start | bytes 786440 | tf_op jit(solution)/shard_map/ppermute | solution.py:20
  11.9 26.4 %all-to-all-start = ((bf16[32,16,1024]{2,1,0:T(8,128)(2,1)}), bf16[32,16,1024]{2,1,0:T(8,128)(2,1)S(1)}, u32[]{:S(2)}, u32[]{:S(2)}) async-start(bf16[32,16,1024]{2,1,0:T(8,128)(2,1)} %bitcast.4), calls=%async_computation | async-start | bytes 2097152 | tf_op jit(solution)/shard_map/all_to_all | solution.py:112
  38.3 21.4 %all-to-all-start.2 = ((bf16[32,16,1024]{2,1,0:T(8,128)(2,1)}), bf16[32,16,1024]{2,1,0:T(8,128)(2,1)}, u32[]{:S(2)}, u32[]{:S(2)}) async-start(bf16[32,16,1024]{2,1,0:T(8,128)(2,1)} %bitcast.14), calls=%async_computation.2 | async-start | bytes 2097152 | tf_op jit(solution)/shard_map/all_to_all | solution.py:112
  44.1 21.1 %collective-permute-start.1 = (bf16[512,512]{1,0:T(8,128)(2,1)}, bf16[512,512]{1,0:T(8,128)(2,1)}, u32[]{:S(2)}, u32[]{:S(2)}) collective-permute-start(bf16[512,512]{1,0:T(8,128)(2,1)} %get-tuple-element.16), channel_id=1, source_target_pairs={{0,1},{1,2},{2,3},{3,0},{4,5},{5,6},{6,7},{7,4},{8,9},{9,10},{10,1... | collective-permute-start | bytes 1572872 | tf_op jit(solution)/shard_map/ppermute | solution.py:20
  45.4 30.7 %collective-permute-start.2 = (bf16[512,512]{1,0:T(8,128)(2,1)}, bf16[512,512]{1,0:T(8,128)(2,1)}, u32[]{:S(2)}, u32[]{:S(2)}) collective-permute-start(bf16[512,512]{1,0:T(8,128)(2,1)} %get-tuple-element.16), channel_id=1, source_target_pairs={{0,3},{1,0},{2,1},{3,2},{4,7},{5,4},{6,5},{7,6},{8,11},{9,8},{10,9... | collective-permute-start | bytes 1572872 | tf_op jit(solution)/shard_map/ppermute | solution.py:20
  61.2 14.8 %collective-permute-start.6 = (bf16[512,512]{1,0:T(8,128)(2,1)S(1)}, bf16[512,512]{1,0:T(8,128)(2,1)S(1)}, u32[]{:S(2)}, u32[]{:S(2)}) collective-permute-start(bf16[512,512]{1,0:T(8,128)(2,1)S(1)} %get-tuple-element.14), channel_id=1, source_target_pairs={{0,1},{1,2},{2,3},{3,0},{4,5},{5,6},{6,7},{7,4},{8,9},{9,10},{10,1... | collective-permute-start | bytes 1572872 | tf_op jit(solution)/shard_map/ppermute | solution.py:20
  62.6 13.5 %collective-permute-start.7 = (bf16[512,512]{1,0:T(8,128)(2,1)S(1)}, bf16[512,512]{1,0:T(8,128)(2,1)S(1)}, u32[]{:S(2)}, u32[]{:S(2)}) collective-permute-start(bf16[512,512]{1,0:T(8,128)(2,1)S(1)} %get-tuple-element.14), channel_id=1, source_target_pairs={{0,3},{1,0},{2,1},{3,2},{4,7},{5,4},{6,5},{7,6},{8,11},{9,8},{10,9... | collective-permute-start | bytes 1572872 | tf_op jit(solution)/shard_map/ppermute | solution.py:20
  77.8 9.8 %slice-start.4 = ((s8[5767168]{0:T(1024)(128)(4,1)}), s8[4194304]{0:T(1024)(128)(4,1)S(1)}, s32[]{:S(2)}) async-start(s8[5767168]{0:T(1024)(128)(4,1)} %bitcast.122), calls=%async_computation.8 | async-start | bytes 8388608
  87.7 8.1 %slice-start = ((s8[5767168]{0:T(1024)(128)(4,1)}), s8[4194304]{0:T(1024)(128)(4,1)S(1)}, s32[]{:S(2)}) async-start(s8[5767168]{0:T(1024)(128)(4,1)} %bitcast.118), calls=%async_computation.4 | async-start | bytes 8388608
  88.7 7.1 %slice-start.1 = ((s8[5767168]{0:T(1024)(128)(4,1)}), s8[1572864]{0:T(1024)(128)(4,1)S(1)}, s32[]{:S(2)}) async-start(s8[5767168]{0:T(1024)(128)(4,1)} %bitcast.118), calls=%async_computation.5 | async-start | bytes 3145728
  88.7 19.3 %collective-permute-start.8 = (bf16[512,512]{1,0:T(8,128)(2,1)S(1)}, bf16[512,512]{1,0:T(8,128)(2,1)S(1)}, u32[]{:S(2)}, u32[]{:S(2)}) collective-permute-start(bf16[512,512]{1,0:T(8,128)(2,1)S(1)} %fusion.33), channel_id=1, source_target_pairs={{0,1},{1,2},{2,3},{3,0},{4,5},{5,6},{6,7},{7,4},{8,9},{9,10},{10,1... | collective-permute-start | bytes 1572872 | tf_op jit(solution)/shard_map/ppermute | solution.py:20
  90.6 23.9 %collective-permute-start.9 = (bf16[512,512]{1,0:T(8,128)(2,1)S(1)}, bf16[512,512]{1,0:T(8,128)(2,1)S(1)}, u32[]{:S(2)}, u32[]{:S(2)}) collective-permute-start(bf16[512,512]{1,0:T(8,128)(2,1)S(1)} %fusion.39), channel_id=1, source_target_pairs={{0,2},{1,3},{2,0},{3,1},{4,6},{5,7},{6,4},{7,5},{8,10},{9,11},{10,... | collective-permute-start | bytes 1572872 | tf_op jit(solution)/shard_map/ppermute | solution.py:20
  94.6 22.3 %collective-permute-start.10 = (bf16[512,512]{1,0:T(8,128)(2,1)S(1)}, bf16[512,512]{1,0:T(8,128)(2,1)S(1)}, u32[]{:S(2)}, u32[]{:S(2)}) collective-permute-start(bf16[512,512]{1,0:T(8,128)(2,1)S(1)} %fusion.45), channel_id=1, source_target_pairs={{0,3},{1,0},{2,1},{3,2},{4,7},{5,4},{6,5},{7,6},{8,11},{9,8},{10,9... | collective-permute-start | bytes 1572872 | tf_op jit(solution)/shard_map/ppermute | solution.py:20
  103.9 24.8 %collective-permute-start.3 = (bf16[512,512]{1,0:T(8,128)(2,1)S(1)}, bf16[512,512]{1,0:T(8,128)(2,1)S(1)}, u32[]{:S(2)}, u32[]{:S(2)}) collective-permute-start(bf16[512,512]{1,0:T(8,128)(2,1)S(1)} %fusion.30), channel_id=1, source_target_pairs={{0,1},{1,2},{2,3},{3,0},{4,5},{5,6},{6,7},{7,4},{8,9},{9,10},{10,1... | collective-permute-start | bytes 1572872 | tf_op jit(solution)/shard_map/ppermute | solution.py:20
  105.8 31.2 %collective-permute-start.4 = (bf16[512,512]{1,0:T(8,128)(2,1)S(1)}, bf16[512,512]{1,0:T(8,128)(2,1)S(1)}, u32[]{:S(2)}, u32[]{:S(2)}) collective-permute-start(bf16[512,512]{1,0:T(8,128)(2,1)S(1)} %fusion.36), channel_id=1, source_target_pairs={{0,2},{1,3},{2,0},{3,1},{4,6},{5,7},{6,4},{7,5},{8,10},{9,11},{10,... | collective-permute-start | bytes 1572872 | tf_op jit(solution)/shard_map/ppermute | solution.py:20
  108.0 16.5 %copy-start.2 = (f32[256,2]{0,1:T(2,128)S(1)}, f32[256,2]{0,1:T(2,128)}, u32[]{:S(2)}) copy-start(f32[256,2]{0,1:T(2,128)} %param.10) | copy-start | bytes 6148
  108.0 30.4 %collective-permute-start.5 = (bf16[512,512]{1,0:T(8,128)(2,1)}, bf16[512,512]{1,0:T(8,128)(2,1)}, u32[]{:S(2)}, u32[]{:S(2)}) collective-permute-start(bf16[512,512]{1,0:T(8,128)(2,1)} %fusion.42), channel_id=1, source_target_pairs={{0,3},{1,0},{2,1},{3,2},{4,7},{5,4},{6,5},{7,6},{8,11},{9,8},{10,9... | collective-permute-start | bytes 1572872 | tf_op jit(solution)/shard_map/ppermute | solution.py:20
  118.8 23.5 %all-to-all-start.3 = ((bf16[32,16,512]{2,1,0:T(8,128)(2,1)}), bf16[32,16,512]{2,1,0:T(8,128)(2,1)S(1)}, u32[]{:S(2)}, u32[]{:S(2)}) async-start(bf16[32,16,512]{2,1,0:T(8,128)(2,1)} %bitcast.16), calls=%async_computation.3 | async-start | bytes 1048576 | tf_op jit(solution)/shard_map/all_to_all | solution.py:126
  142.2 16.9 %all-to-all-start.1 = ((bf16[32,16,512]{2,1,0:T(8,128)(2,1)}), bf16[32,16,512]{2,1,0:T(8,128)(2,1)S(1)}, u32[]{:S(2)}, u32[]{:S(2)}) async-start(bf16[32,16,512]{2,1,0:T(8,128)(2,1)} %bitcast.12), calls=%async_computation.1 | async-start | bytes 1048576 | tf_op jit(solution)/shard_map/all_to_all | solution.py:126
  147.4 12.2 %copy-start = (bf16[256,512]{1,0:T(8,128)(2,1)S(1)}, bf16[256,512]{1,0:T(8,128)(2,1)}, u32[]{:S(2)}) copy-start(bf16[256,512]{1,0:T(8,128)(2,1)} %param.8) | copy-start | bytes 786436
  159.6 8.0 %copy-start.1 = (f32[512]{0:T(512)S(1)}, f32[512]{0:T(512)}, u32[]{:S(2)}) copy-start(f32[512]{0:T(512)} %param.12) | copy-start | bytes 6148
  160.7 4.3 %collective-permute-start.11 = (f32[256]{0:T(256)S(1)}, f32[256]{0:T(256)S(1)}, u32[]{:S(2)}, u32[]{:S(2)}) collective-permute-start(f32[256]{0:T(256)S(1)} %get-tuple-element.22), channel_id=1, source_target_pairs={{0,1},{1,2},{2,3},{3,0},{4,5},{5,6},{6,7},{7,4},{8,9},{9,10},{10,1... | collective-permute-start | bytes 3080 | tf_op jit(solution)/shard_map/ppermute | solution.py:20
  162.2 3.9 %collective-permute-start.12 = (f32[256]{0:T(256)S(1)}, f32[256]{0:T(256)S(1)}, u32[]{:S(2)}, u32[]{:S(2)}) collective-permute-start(f32[256]{0:T(256)S(1)} %get-tuple-element.22), channel_id=1, source_target_pairs={{0,2},{1,3},{2,0},{3,1},{4,6},{5,7},{6,4},{7,5},{8,10},{9,11},{10,... | collective-permute-start | bytes 3080 | tf_op jit(solution)/shard_map/ppermute | solution.py:20
  164.3 2.7 %collective-permute-start.13 = (f32[256]{0:T(256)S(1)}, f32[256]{0:T(256)S(1)}, u32[]{:S(2)}, u32[]{:S(2)}) collective-permute-start(f32[256]{0:T(256)S(1)} %get-tuple-element.22), channel_id=1, source_target_pairs={{0,3},{1,0},{2,1},{3,2},{4,7},{5,4},{6,5},{7,6},{8,11},{9,8},{10,9... | collective-permute-start | bytes 3080 | tf_op jit(solution)/shard_map/ppermute | solution.py:20
  (5 other events, 21.7 us)

commit v18 on v13

--- a/solution.py
+++ b/solution.py
@@ -50,7 +50,8 @@
 
 
 def sum_tp(value, tp_count):
-    ordered = by_source(value, tp_count)
+    spread = jnp.broadcast_to(value[None], (tp_count,) + value.shape)
+    ordered = lax.all_to_all(spread, "tp", 0, 0, tiled=True)
     total = ordered[0]
     for s in range(1, tp_count):
         total = total + ordered[s]

time: 152 us -> 152 us (level)
  blocking collectives: 0 us -> 6.48 us
  waiting for transfers between devices: 55.4 us -> 51 us
  starting transfers between devices: 40.1 us -> 38.2 us
    all_to_all x2, waiting for transfers between devices: 19.3 us -> 11.9 us  [shards(): lax.all_to_all(outgoing, 'req', split_axis=0, concat_axis=0, tiled=True)]
    all_to_all x0 -> x1, blocking collectives: none -> 6.48 us  [sum_tp(): ordered = lax.all_to_all(spread, 'tp', 0, 0, tiled=True)]
    ppermute x14 -> x11, waiting for transfers between devices: 25.4 us -> 28.4 us  [shift_tp(): lax.ppermute(value, 'tp', [(j, (j + step) % tp_count) for j in range(tp_c...]
    ppermute x14 -> x11, starting transfers between devices: 15.8 us -> 13.7 us  [shift_tp(): lax.ppermute(value, 'tp', [(j, (j + step) % tp_count) for j in range(tp_c...]
  transfers between devices with their start and end apart: 18 -> 15, of which waited for: 10 -> 9; matrix products, arithmetic and copies ran while one was open for 33% -> 34% of each run, Pallas kernels for 0% -> 0%
where the time goes in v18:
time: 152 us; the launch traced here: 151 us
  waiting for transfers between devices  51 us (34%)
  matrix products  45.5 us (30%)
  starting transfers between devices  38.2 us (25%)
  blocking collectives  6.48 us (4%)
  local copies, waits for them, and re-layouts  5.29 us (3%)
  other arithmetic  3.66 us (2%)
    ppermute x11, waiting for transfers between devices, shift_tp(): lax.ppermute(value, 'tp', [(j, (j + step) % tp_count) for j in range(tp_c...  28.4 us
    dot_general x8, matrix products, down_scatter_sum_tp(): jnp.dot(activ, w_block, preferred_element_type=jnp.float32)  17.4 us
    all_to_all x2, starting transfers between devices, shards(): lax.all_to_all(outgoing, 'req', split_axis=0, concat_axis=0, tiled=True)  15.7 us
    ppermute x11, starting transfers between devices, shift_tp(): lax.ppermute(value, 'tp', [(j, (j + step) % tp_count) for j in range(tp_c...  13.7 us
    dot_general x2, matrix products, shards(): jnp.dot(flat_rows, gate_weight[0], preferred_element_type=jnp.float32)  12.6 us
    all_to_all x2, waiting for transfers between devices, shards(): lax.all_to_all(outgoing, 'req', split_axis=0, concat_axis=0, tiled=True)  11.9 us
    all_to_all x2, waiting for transfers between devices, shards(): lax.all_to_all(summed, 'req', split_axis=0, concat_axis=0, tiled=True)  10.7 us
    all_to_all x2, starting transfers between devices, shards(): lax.all_to_all(summed, 'req', split_axis=0, concat_axis=0, tiled=True)  8.82 us
  transfers between devices with their start and end apart: 15, of which 9 were waited for; matrix products, arithmetic and copies ran while one was open for 34% of the time, Pallas kernels for 0%

profile of v18, /device:TPU:1, one launch (start us, length us, event | category | flops | bytes accessed | tf_op | source)
XLA Modules:
  0.0 151.3 jit_solution(4202829708083327113)
XLA Ops:
  0.6 3.8 %collective-permute-start = (bf16[256,512]{1,0:T(8,128)(2,1)}, bf16[256,512]{1,0:T(8,128)(2,1)S(1)}, u32[]{:S(2)}, u32[]{:S(2)}) collective-permute-start(bf16[256,512]{1,0:T(8,128)(2,1)} %param.8), channel_id=1, source_target_pairs={{0,2},{1,3},{2,0},{3,1},{4,6},{5,7},{6,4},{7,5},{8,10},{9,11},{10,... | collective-permute-start | bytes 786440 | tf_op jit(solution)/shard_map/ppermute | solution.py:20
  8.5 2.0 %collective-permute-done = bf16[256,512]{1,0:T(8,128)(2,1)S(1)} collective-permute-done((bf16[256,512]{1,0:T(8,128)(2,1)}, bf16[256,512]{1,0:T(8,128)(2,1)S(1)}, u32[]{:S(2)}, u32[]{:S(2)}) %collective-permute-start) | collective-permute-done | bytes 262176 | tf_op jit(solution)/shard_map/ppermute | solution.py:20
  10.5 2.5 %convolution_convert_fusion.1 = bf16[512,1024]{1,0:T(8,128)(2,1)} fusion(bf16[256,512]{1,0:T(8,128)(2,1)S(1)} %collective-permute-done, bf16[256,512]{1,0:T(8,128)(2,1)} %param.8, s32[256]{0:T(256)S(1)} %bitcast.105, s32[256]{0:T(256)S(1)} %bitcast.99, pred[256]{0:T(512)(128)(4,1)S(1)} %get-tuple-element.5, pred[256]{0:T(512)(128)(4,1)S(1)} %get-tuple-element.4), kind=kOutput, calls=%fused_computation.22 | convolution fusion | flops 270663680 | bytes 1575424 | tf_op jit(solution)/shard_map/dot_general | solution.py:109
  13.0 10.6 %all-to-all-start = ((bf16[32,16,1024]{2,1,0:T(8,128)(2,1)}), bf16[32,16,1024]{2,1,0:T(8,128)(2,1)S(1)}, u32[]{:S(2)}, u32[]{:S(2)}) async-start(bf16[32,16,1024]{2,1,0:T(8,128)(2,1)} %bitcast.4), calls=%async_computation | async-start | bytes 2097152 | tf_op jit(solution)/shard_map/all_to_all | solution.py:113
  25.6 5.8 %collective-permute-done.7 = bf16[256,512]{1,0:T(8,128)(2,1)S(1)} collective-permute-done((bf16[256,512]{1,0:T(8,128)(2,1)S(1)}, bf16[256,512]{1,0:T(8,128)(2,1)S(1)}, u32[]{:S(2)}, u32[]{:S(2)}) %collective-permute-start.7) | collective-permute-done | bytes 262176 | tf_op jit(solution)/shard_map/ppermute | solution.py:20
  31.7 8.8 %all-to-all-done = bf16[32,16,1024]{2,1,0:T(8,128)(2,1)S(1)} async-done(((bf16[32,16,1024]{2,1,0:T(8,128)(2,1)}), bf16[32,16,1024]{2,1,0:T(8,128)(2,1)S(1)}, u32[]{:S(2)}, u32[]{:S(2)}) %all-to-all-start) | async-done | bytes 1048608 | tf_op jit(solution)/shard_map/all_to_all | solution.py:113
  41.8 2.6 %collective-permute-start.2 = (bf16[512,512]{1,0:T(8,128)(2,1)}, bf16[512,512]{1,0:T(8,128)(2,1)}, u32[]{:S(2)}, u32[]{:S(2)}) collective-permute-start(bf16[512,512]{1,0:T(8,128)(2,1)} %get-tuple-element.14), channel_id=1, source_target_pairs={{0,3},{1,0},{2,1},{3,2},{4,7},{5,4},{6,5},{7,6},{8,11},{9,8},{10,9... | collective-permute-start | bytes 1572872 | tf_op jit(solution)/shard_map/ppermute | solution.py:20
  44.4 2.2 %convolution_convert_fusion = bf16[512,2048]{1,0:T(8,128)(2,1)} fusion(bf16[256,2048]{1,0:T(8,128)(2,1)S(1)} %copy-done.1, f32[2048]{0:T(1024)S(1)} %copy-done.5, f32[256]{0:T(256)S(1)} %add_rsqrt_fusion.2, s32[256]{0:T(256)S(1)} %bitcast.106, s32[256]{0:T(256)S(1)} %bitcast.100, pred[256]{0:T(512)(128)(4,1)S(1)} %get-tuple-element.3, ...), kind=kOutput, calls=%fused_computation.14 | convolution fusion | flops 540672000 | bytes 3157504 | tf_op jit(solution)/shard_map/dot_general | solution.py:109
  46.6 5.0 %all-to-all-start.2 = ((bf16[32,16,2048]{2,1,0:T(8,128)(2,1)}), bf16[32,16,2048]{2,1,0:T(8,128)(2,1)}, u32[]{:S(2)}, u32[]{:S(2)}) async-start(bf16[32,16,2048]{2,1,0:T(8,128)(2,1)} %bitcast.93), calls=%async_computation.2 | async-start | bytes 4194304 | tf_op jit(solution)/shard_map/all_to_all | solution.py:113
  51.7 4.9 %collective-permute-done.1 = bf16[512,512]{1,0:T(8,128)(2,1)} collective-permute-done((bf16[512,512]{1,0:T(8,128)(2,1)}, bf16[512,512]{1,0:T(8,128)(2,1)}, u32[]{:S(2)}, u32[]{:S(2)}) %collective-permute-start.1) | collective-permute-done | bytes 524320 | tf_op jit(solution)/shard_map/ppermute | solution.py:20
  59.4 6.1 %fusion.6 = f32[512,1408]{1,0:T(8,128)S(1)} fusion(bf16[1,2048,1408]{2,1,0:T(8,128)(2,1)} %param.13, bf16[512,2048]{1,0:T(8,128)(2,1)S(1)} %constant_dynamic-update-slice_fusion.4, f32[2048]{0:T(1024)S(1)} %copy-done.5, f32[512]{0:T(512)S(1)} %add_rsqrt_fusion), kind=kOutput, calls=%fused_computation.6 | convolution fusion | flops 2956984320 | bytes 10758144 | tf_op jit(solution)/shard_map/dot_general | solution.py:122
  65.5 3.5 %multiply_convert_fusion = bf16[512,1408]{1,0:T(8,128)(2,1)S(1)} fusion(f32[512,1408]{1,0:T(8,128)S(1)} %fusion.6, bf16[1,2048,1408]{2,1,0:T(8,128)(2,1)S(1)} %bitcast.112, bf16[512,2048]{1,0:T(8,128)(2,1)S(1)} %constant_dynamic-update-slice_fusion.4, f32[2048]{0:T(1024)S(1)} %copy-done.5, f32[512]{0:T(512)S(1)} %add_rsqrt_fusion), kind=kOutput, calls=%fused_computation.16 | convolution fusion | flops 2961309696 | bytes 12199936 | tf_op jit(solution)/shard_map/dot_general | solution.py:123
  74.4 1.8 %fusion.36 = bf16[512,512]{1,0:T(8,128)(2,1)} fusion(bf16[512,1408]{1,0:T(8,128)(2,1)S(1)} %multiply_convert_fusion, bf16[1,1408,2048]{2,1,0:T(8,128)(2,1)S(1)} %bitcast.116, s32[]{:T(128)S(6)} %select_n.142), kind=kOutput, calls=%fused_computation.39 | convolution fusion | flops 738459648 | bytes 3407876 | tf_op jit(solution)/shard_map/dot_general | solution.py:67
  77.0 3.1 %all-to-all-done.2 = bf16[32,16,2048]{2,1,0:T(8,128)(2,1)} async-done(((bf16[32,16,2048]{2,1,0:T(8,128)(2,1)}), bf16[32,16,2048]{2,1,0:T(8,128)(2,1)}, u32[]{:S(2)}, u32[]{:S(2)}) %all-to-all-start.2) | async-done | bytes 2097184 | tf_op jit(solution)/shard_map/all_to_all | solution.py:113
  80.1 6.5 %fusion.4 = f32[512,1408]{1,0:T(8,128)S(1)} fusion(bf16[512,2048]{1,0:T(8,128)(2,1)} %bitcast.15, bf16[1,2048,1408]{2,1,0:T(8,128)(2,1)} %param.13), kind=kOutput, calls=%fused_computation.4 | convolution fusion | flops 2952790016 | bytes 10747904 | tf_op jit(solution)/shard_map/dot_general | solution.py:122
  86.7 5.2 %fusion.14 = bf16[512,1408]{1,0:T(8,128)(2,1)S(1)} fusion(bf16[512,2048]{1,0:T(8,128)(2,1)} %bitcast.15, bf16[1,2048,1408]{2,1,0:T(8,128)(2,1)S(1)} %bitcast.114, f32[512,1408]{1,0:T(8,128)S(1)} %fusion.4), kind=kOutput, calls=%fused_computation.15 | convolution fusion | flops 2957115392 | bytes 12189696 | tf_op jit(solution)/shard_map/dot_general | solution.py:123
  101.2 2.9 %add_convert_fusion.1 = bf16[512,512]{1,0:T(8,128)(2,1)} fusion(bf16[512,512]{1,0:T(8,128)(2,1)S(1)} %collective-permute-done.5, bf16[512,512]{1,0:T(8,128)(2,1)S(1)} %collective-permute-done.4, bf16[512,512]{1,0:T(8,128)(2,1)} %collective-permute-done.3, bf16[512,1408]{1,0:T(8,128)(2,1)S(1)} %copy-done.8, bf16[1,1408,2048]{2,1,0:T(8,128)(2,1)S(1)} %bitcast.118, ...), kind=kOutput, calls=%fused_computation.64 | convolution fusion | flops 740556800 | bytes 4980740 | tf_op jit(solution)/shard_map/dot_general | solution.py:67
  104.1 4.8 %all-to-all-start.1 = ((bf16[32,16,512]{2,1,0:T(8,128)(2,1)}), bf16[32,16,512]{2,1,0:T(8,128)(2,1)S(1)}, u32[]{:S(2)}, u32[]{:S(2)}) async-start(bf16[32,16,512]{2,1,0:T(8,128)(2,1)} %bitcast.12), calls=%async_computation.1 | async-start | bytes 1048576 | tf_op jit(solution)/shard_map/all_to_all | solution.py:127
  109.0 2.1 %collective-permute-done.9 = bf16[512,512]{1,0:T(8,128)(2,1)S(1)} collective-permute-done((bf16[512,512]{1,0:T(8,128)(2,1)}, bf16[512,512]{1,0:T(8,128)(2,1)S(1)}, u32[]{:S(2)}, u32[]{:S(2)}) %collective-permute-start.9) | collective-permute-done | bytes 524320 | tf_op jit(solution)/shard_map/ppermute | solution.py:20
  111.1 12.2 %collective-permute-done.8 = bf16[512,512]{1,0:T(8,128)(2,1)} collective-permute-done((bf16[512,512]{1,0:T(8,128)(2,1)}, bf16[512,512]{1,0:T(8,128)(2,1)}, u32[]{:S(2)}, u32[]{:S(2)}) %collective-permute-start.8) | collective-permute-done | bytes 524320 | tf_op jit(solution)/shard_map/ppermute | solution.py:20
  123.3 3.7 %add_convert_fusion = bf16[512,512]{1,0:T(8,128)(2,1)} fusion(bf16[512,512]{1,0:T(8,128)(2,1)S(1)} %collective-permute-done.10, bf16[512,512]{1,0:T(8,128)(2,1)S(1)} %collective-permute-done.9, bf16[512,512]{1,0:T(8,128)(2,1)} %collective-permute-done.8, bf16[512,1408]{1,0:T(8,128)(2,1)} %copy-done.6, bf16[1,1408,2048]{2,1,0:T(8,128)(2,1)} %param.15, ...), kind=kOutput, calls=%fused_computation.61 | convolution fusion | flops 740556800 | bytes 4980740 | tf_op jit(solution)/shard_map/dot_general | solution.py:67
  127.1 4.0 %all-to-all-start.3 = ((bf16[32,16,512]{2,1,0:T(8,128)(2,1)}), bf16[32,16,512]{2,1,0:T(8,128)(2,1)S(1)}, u32[]{:S(2)}, u32[]{:S(2)}) async-start(bf16[32,16,512]{2,1,0:T(8,128)(2,1)} %bitcast.16), calls=%async_computation.3 | async-start | bytes 1048576 | tf_op jit(solution)/shard_map/all_to_all | solution.py:127
  132.1 10.7 %all-to-all-done.3 = bf16[32,16,512]{2,1,0:T(8,128)(2,1)S(1)} async-done(((bf16[32,16,512]{2,1,0:T(8,128)(2,1)}), bf16[32,16,512]{2,1,0:T(8,128)(2,1)S(1)}, u32[]{:S(2)}, u32[]{:S(2)}) %all-to-all-start.3) | async-done | bytes 524320 | tf_op jit(solution)/shard_map/all_to_all | solution.py:127
  143.9 6.5 %all_to_all.26 = f32[4,1,256]{2,1,0:T(1,128)S(1)} all-to-all(f32[4,1,256]{2,1,0:T(1,128)S(1)} %broadcast_in_dim.80), channel_id=1, replica_groups=mesh['req'=32,'tp'=4] {'tp'}, dimensions={0} | all-to-all | bytes 8192 | tf_op jit(solution)/shard_map/all_to_all | solution.py:54
  (97 shorter events, 28.6 us)
Async XLA Ops:
  0.6 9.8 %collective-permute-start = (bf16[256,512]{1,0:T(8,128)(2,1)}, bf16[256,512]{1,0:T(8,128)(2,1)S(1)}, u32[]{:S(2)}, u32[]{:S(2)}) collective-permute-start(bf16[256,512]{1,0:T(8,128)(2,1)} %param.8), channel_id=1, source_target_pairs={{0,2},{1,3},{2,0},{3,1},{4,6},{5,7},{6,4},{7,5},{8,10},{9,11},{10,... | collective-permute-start | bytes 786440 | tf_op jit(solution)/shard_map/ppermute | solution.py:20
  4.5 21.1 %collective-permute-start.6 = (bf16[256,512]{1,0:T(8,128)(2,1)}, bf16[256,512]{1,0:T(8,128)(2,1)S(1)}, u32[]{:S(2)}, u32[]{:S(2)}) collective-permute-start(bf16[256,512]{1,0:T(8,128)(2,1)} %param.8), channel_id=1, source_target_pairs={{0,1},{1,2},{2,3},{3,0},{4,5},{5,6},{6,7},{7,4},{8,9},{9,10},{10,1... | collective-permute-start | bytes 786440 | tf_op jit(solution)/shard_map/ppermute | solution.py:20
  10.5 13.2 %copy-start.2 = (bf16[256,512]{1,0:T(8,128)(2,1)S(1)}, bf16[256,512]{1,0:T(8,128)(2,1)}, u32[]{:S(2)}) copy-start(bf16[256,512]{1,0:T(8,128)(2,1)} %param.8) | copy-start | bytes 786436
  13.0 27.6 %all-to-all-start = ((bf16[32,16,1024]{2,1,0:T(8,128)(2,1)}), bf16[32,16,1024]{2,1,0:T(8,128)(2,1)S(1)}, u32[]{:S(2)}, u32[]{:S(2)}) async-start(bf16[32,16,1024]{2,1,0:T(8,128)(2,1)} %bitcast.4), calls=%async_computation | async-start | bytes 2097152 | tf_op jit(solution)/shard_map/all_to_all | solution.py:113
  23.6 7.7 %collective-permute-start.7 = (bf16[256,512]{1,0:T(8,128)(2,1)S(1)}, bf16[256,512]{1,0:T(8,128)(2,1)S(1)}, u32[]{:S(2)}, u32[]{:S(2)}) collective-permute-start(bf16[256,512]{1,0:T(8,128)(2,1)S(1)} %copy-done.2), channel_id=1, source_target_pairs={{0,3},{1,0},{2,1},{3,2},{4,7},{5,4},{6,5},{7,6},{8,11},{9,8},{10,9... | collective-permute-start | bytes 786440 | tf_op jit(solution)/shard_map/ppermute | solution.py:20
  31.4 9.1 %copy-start = (bf16[256,2048]{1,0:T(8,128)(2,1)}, bf16[256,2048]{1,0:T(8,128)(2,1)S(1)}, u32[]{:S(2)}) copy-start(bf16[256,2048]{1,0:T(8,128)(2,1)S(1)} %constant_dynamic-update-slice_fusion) | copy-start | bytes 3145732
  31.7 12.7 %copy-start.5 = (f32[2048]{0:T(1024)S(1)}, f32[2048]{0:T(1024)}, u32[]{:S(2)}) copy-start(f32[2048]{0:T(1024)} %param.11) | copy-start | bytes 24580
  41.7 14.9 %collective-permute-start.1 = (bf16[512,512]{1,0:T(8,128)(2,1)}, bf16[512,512]{1,0:T(8,128)(2,1)}, u32[]{:S(2)}, u32[]{:S(2)}) collective-permute-start(bf16[512,512]{1,0:T(8,128)(2,1)} %get-tuple-element.14), channel_id=1, source_target_pairs={{0,1},{1,2},{2,3},{3,0},{4,5},{5,6},{6,7},{7,4},{8,9},{9,10},{10,1... | collective-permute-start | bytes 1572872 | tf_op jit(solution)/shard_map/ppermute | solution.py:20
  41.8 15.9 %collective-permute-start.2 = (bf16[512,512]{1,0:T(8,128)(2,1)}, bf16[512,512]{1,0:T(8,128)(2,1)}, u32[]{:S(2)}, u32[]{:S(2)}) collective-permute-start(bf16[512,512]{1,0:T(8,128)(2,1)} %get-tuple-element.14), channel_id=1, source_target_pairs={{0,3},{1,0},{2,1},{3,2},{4,7},{5,4},{6,5},{7,6},{8,11},{9,8},{10,9... | collective-permute-start | bytes 1572872 | tf_op jit(solution)/shard_map/ppermute | solution.py:20
  46.6 33.5 %all-to-all-start.2 = ((bf16[32,16,2048]{2,1,0:T(8,128)(2,1)}), bf16[32,16,2048]{2,1,0:T(8,128)(2,1)}, u32[]{:S(2)}, u32[]{:S(2)}) async-start(bf16[32,16,2048]{2,1,0:T(8,128)(2,1)} %bitcast.93), calls=%async_computation.2 | async-start | bytes 4194304 | tf_op jit(solution)/shard_map/all_to_all | solution.py:113
  59.4 9.7 %slice-start.4 = ((s8[5767168]{0:T(1024)(128)(4,1)}), s8[4194304]{0:T(1024)(128)(4,1)S(1)}, s32[]{:S(2)}) async-start(s8[5767168]{0:T(1024)(128)(4,1)} %bitcast.115), calls=%async_computation.9 | async-start | bytes 8388608
  70.9 28.1 %collective-permute-start.5 = (bf16[512,512]{1,0:T(8,128)(2,1)}, bf16[512,512]{1,0:T(8,128)(2,1)S(1)}, u32[]{:S(2)}, u32[]{:S(2)}) collective-permute-start(bf16[512,512]{1,0:T(8,128)(2,1)} %fusion.48), channel_id=1, source_target_pairs={{0,3},{1,0},{2,1},{3,2},{4,7},{5,4},{6,5},{7,6},{8,11},{9,8},{10,9... | collective-permute-start | bytes 1572872 | tf_op jit(solution)/shard_map/ppermute | solution.py:20
  73.9 25.9 %collective-permute-start.4 = (bf16[512,512]{1,0:T(8,128)(2,1)}, bf16[512,512]{1,0:T(8,128)(2,1)S(1)}, u32[]{:S(2)}, u32[]{:S(2)}) collective-permute-start(bf16[512,512]{1,0:T(8,128)(2,1)} %fusion.42), channel_id=1, source_target_pairs={{0,2},{1,3},{2,0},{3,1},{4,6},{5,7},{6,4},{7,5},{8,10},{9,11},{10,... | collective-permute-start | bytes 1572872 | tf_op jit(solution)/shard_map/ppermute | solution.py:20
  74.3 12.3 %slice-start.2 = ((s8[5767168]{0:T(1024)(128)(4,1)}), s8[1572864]{0:T(1024)(128)(4,1)S(1)}, s32[]{:S(2)}) async-start(s8[5767168]{0:T(1024)(128)(4,1)} %bitcast.113), calls=%async_computation.7 | async-start | bytes 3145728
  76.2 25.1 %collective-permute-start.3 = (bf16[512,512]{1,0:T(8,128)(2,1)}, bf16[512,512]{1,0:T(8,128)(2,1)}, u32[]{:S(2)}, u32[]{:S(2)}) collective-permute-start(bf16[512,512]{1,0:T(8,128)(2,1)} %fusion.36), channel_id=1, source_target_pairs={{0,1},{1,2},{2,3},{3,0},{4,5},{5,6},{6,7},{7,4},{8,9},{9,10},{10,1... | collective-permute-start | bytes 1572872 | tf_op jit(solution)/shard_map/ppermute | solution.py:20
  80.1 11.7 %slice-start.6 = ((s8[5767168]{0:T(1024)(128)(4,1)}), s8[4194304]{0:T(1024)(128)(4,1)S(1)}, s32[]{:S(2)}) async-start(s8[5767168]{0:T(1024)(128)(4,1)} %bitcast.117), calls=%async_computation.11 | async-start | bytes 8388608
  91.9 7.1 %copy-start.6 = (bf16[512,1408]{1,0:T(8,128)(2,1)}, bf16[512,1408]{1,0:T(8,128)(2,1)S(1)}, u32[]{:S(2)}) copy-start(bf16[512,1408]{1,0:T(8,128)(2,1)S(1)} %fusion.14) | copy-start | bytes 4325380
  93.7 15.3 %collective-permute-start.10 = (bf16[512,512]{1,0:T(8,128)(2,1)}, bf16[512,512]{1,0:T(8,128)(2,1)S(1)}, u32[]{:S(2)}, u32[]{:S(2)}) collective-permute-start(bf16[512,512]{1,0:T(8,128)(2,1)} %fusion.51), channel_id=1, source_target_pairs={{0,3},{1,0},{2,1},{3,2},{4,7},{5,4},{6,5},{7,6},{8,11},{9,8},{10,9... | collective-permute-start | bytes 1572872 | tf_op jit(solution)/shard_map/ppermute | solution.py:20
  95.8 15.3 %collective-permute-start.9 = (bf16[512,512]{1,0:T(8,128)(2,1)}, bf16[512,512]{1,0:T(8,128)(2,1)S(1)}, u32[]{:S(2)}, u32[]{:S(2)}) collective-permute-start(bf16[512,512]{1,0:T(8,128)(2,1)} %fusion.45), channel_id=1, source_target_pairs={{0,2},{1,3},{2,0},{3,1},{4,6},{5,7},{6,4},{7,5},{8,10},{9,11},{10,... | collective-permute-start | bytes 1572872 | tf_op jit(solution)/shard_map/ppermute | solution.py:20
  98.9 10.0 %copy-start.4 = (f32[256,2]{0,1:T(2,128)S(1)}, f32[256,2]{0,1:T(2,128)}, u32[]{:S(2)}) copy-start(f32[256,2]{0,1:T(2,128)} %param.10) | copy-start | bytes 6148
  98.9 24.4 %collective-permute-start.8 = (bf16[512,512]{1,0:T(8,128)(2,1)}, bf16[512,512]{1,0:T(8,128)(2,1)}, u32[]{:S(2)}, u32[]{:S(2)}) collective-permute-start(bf16[512,512]{1,0:T(8,128)(2,1)} %fusion.39), channel_id=1, source_target_pairs={{0,1},{1,2},{2,3},{3,0},{4,5},{5,6},{6,7},{7,4},{8,9},{9,10},{10,1... | collective-permute-start | bytes 1572872 | tf_op jit(solution)/shard_map/ppermute | solution.py:20
  104.1 22.9 %all-to-all-start.1 = ((bf16[32,16,512]{2,1,0:T(8,128)(2,1)}), bf16[32,16,512]{2,1,0:T(8,128)(2,1)S(1)}, u32[]{:S(2)}, u32[]{:S(2)}) async-start(bf16[32,16,512]{2,1,0:T(8,128)(2,1)} %bitcast.12), calls=%async_computation.1 | async-start | bytes 1048576 | tf_op jit(solution)/shard_map/all_to_all | solution.py:127
  127.1 15.8 %all-to-all-start.3 = ((bf16[32,16,512]{2,1,0:T(8,128)(2,1)}), bf16[32,16,512]{2,1,0:T(8,128)(2,1)S(1)}, u32[]{:S(2)}, u32[]{:S(2)}) async-start(bf16[32,16,512]{2,1,0:T(8,128)(2,1)} %bitcast.16), calls=%async_computation.3 | async-start | bytes 1048576 | tf_op jit(solution)/shard_map/all_to_all | solution.py:127
  142.8 7.6 %copy-start.3 = (f32[512]{0:T(512)S(1)}, f32[512]{0:T(512)}, u32[]{:S(2)}) copy-start(f32[512]{0:T(512)} %param.12) | copy-start | bytes 6148
  (8 other events, 42.6 us)

commit v19 on v13

--- a/solution.py
+++ b/solution.py
@@ -50,10 +50,9 @@
 
 
 def sum_tp(value, tp_count):
-    ordered = by_source(value, tp_count)
-    total = ordered[0]
+    total = value
     for s in range(1, tp_count):
-        total = total + ordered[s]
+        total = total + shift_tp(value, s, tp_count)
     return total
 
 

time: 152 us -> 151 us (level)
    all_to_all x2, waiting for transfers between devices: 19.3 us -> 11.9 us  [shards(): lax.all_to_all(outgoing, 'req', split_axis=0, concat_axis=0, tiled=True)]
    ppermute x14, waiting for transfers between devices: 25.4 us -> 31.9 us  [shift_tp(): lax.ppermute(value, 'tp', [(j, (j + step) % tp_count) for j in range(tp_c...]
  transfers between devices with their start and end apart: 18 -> 18, of which waited for: 10 -> 12; matrix products, arithmetic and copies ran while one was open for 33% -> 34% of each run, Pallas kernels for 0% -> 0%
where the time goes in v19:
time: 151 us; the launch traced here: 150 us
  waiting for transfers between devices  54.5 us (36%)
  matrix products  45.4 us (30%)
  starting transfers between devices  39.8 us (26%)
  local copies, waits for them, and re-layouts  5.29 us (4%)
  other arithmetic  3.66 us (2%)
    ppermute x14, waiting for transfers between devices, shift_tp(): lax.ppermute(value, 'tp', [(j, (j + step) % tp_count) for j in range(tp_c...  31.9 us
    dot_general x8, matrix products, down_scatter_sum_tp(): jnp.dot(activ, w_block, preferred_element_type=jnp.float32)  17.3 us
    all_to_all x2, starting transfers between devices, shards(): lax.all_to_all(outgoing, 'req', split_axis=0, concat_axis=0, tiled=True)  15.7 us
    ppermute x14, starting transfers between devices, shift_tp(): lax.ppermute(value, 'tp', [(j, (j + step) % tp_count) for j in range(tp_c...  15.3 us
    dot_general x2, matrix products, shards(): jnp.dot(flat_rows, gate_weight[0], preferred_element_type=jnp.float32)  12.6 us
    all_to_all x2, waiting for transfers between devices, shards(): lax.all_to_all(outgoing, 'req', split_axis=0, concat_axis=0, tiled=True)  11.9 us
    all_to_all x2, waiting for transfers between devices, shards(): lax.all_to_all(summed, 'req', split_axis=0, concat_axis=0, tiled=True)  10.7 us
    all_to_all x2, starting transfers between devices, shards(): lax.all_to_all(summed, 'req', split_axis=0, concat_axis=0, tiled=True)  8.83 us
  transfers between devices with their start and end apart: 18, of which 12 were waited for; matrix products, arithmetic and copies ran while one was open for 34% of the time, Pallas kernels for 0%

profile of v19, /device:TPU:1, one launch (start us, length us, event | category | flops | bytes accessed | tf_op | source)
XLA Modules:
  0.0 149.9 jit_solution(951506447345655926)
XLA Ops:
  0.6 3.8 %collective-permute-start = (bf16[256,512]{1,0:T(8,128)(2,1)}, bf16[256,512]{1,0:T(8,128)(2,1)S(1)}, u32[]{:S(2)}, u32[]{:S(2)}) collective-permute-start(bf16[256,512]{1,0:T(8,128)(2,1)} %param.8), channel_id=1, source_target_pairs={{0,2},{1,3},{2,0},{3,1},{4,6},{5,7},{6,4},{7,5},{8,10},{9,11},{10,... | collective-permute-start | bytes 786440 | tf_op jit(solution)/shard_map/ppermute | solution.py:20
  8.5 2.0 %collective-permute-done = bf16[256,512]{1,0:T(8,128)(2,1)S(1)} collective-permute-done((bf16[256,512]{1,0:T(8,128)(2,1)}, bf16[256,512]{1,0:T(8,128)(2,1)S(1)}, u32[]{:S(2)}, u32[]{:S(2)}) %collective-permute-start) | collective-permute-done | bytes 262176 | tf_op jit(solution)/shard_map/ppermute | solution.py:20
  10.5 2.5 %convolution_convert_fusion.1 = bf16[512,1024]{1,0:T(8,128)(2,1)} fusion(bf16[256,512]{1,0:T(8,128)(2,1)S(1)} %collective-permute-done, bf16[256,512]{1,0:T(8,128)(2,1)} %param.8, s32[256]{0:T(256)S(1)} %bitcast.103, s32[256]{0:T(256)S(1)} %bitcast.97, pred[256]{0:T(512)(128)(4,1)S(1)} %get-tuple-element.5, pred[256]{0:T(512)(128)(4,1)S(1)} %get-tuple-element.4), kind=kOutput, calls=%fused_computation.22 | convolution fusion | flops 270663680 | bytes 1575424 | tf_op jit(solution)/shard_map/dot_general | solution.py:107
  13.0 10.6 %all-to-all-start = ((bf16[32,16,1024]{2,1,0:T(8,128)(2,1)}), bf16[32,16,1024]{2,1,0:T(8,128)(2,1)S(1)}, u32[]{:S(2)}, u32[]{:S(2)}) async-start(bf16[32,16,1024]{2,1,0:T(8,128)(2,1)} %bitcast.4), calls=%async_computation | async-start | bytes 2097152 | tf_op jit(solution)/shard_map/all_to_all | solution.py:111
  25.6 5.8 %collective-permute-done.7 = bf16[256,512]{1,0:T(8,128)(2,1)S(1)} collective-permute-done((bf16[256,512]{1,0:T(8,128)(2,1)S(1)}, bf16[256,512]{1,0:T(8,128)(2,1)S(1)}, u32[]{:S(2)}, u32[]{:S(2)}) %collective-permute-start.7) | collective-permute-done | bytes 262176 | tf_op jit(solution)/shard_map/ppermute | solution.py:20
  31.7 8.8 %all-to-all-done = bf16[32,16,1024]{2,1,0:T(8,128)(2,1)S(1)} async-done(((bf16[32,16,1024]{2,1,0:T(8,128)(2,1)}), bf16[32,16,1024]{2,1,0:T(8,128)(2,1)S(1)}, u32[]{:S(2)}, u32[]{:S(2)}) %all-to-all-start) | async-done | bytes 1048608 | tf_op jit(solution)/shard_map/all_to_all | solution.py:111
  41.8 2.6 %collective-permute-start.2 = (bf16[512,512]{1,0:T(8,128)(2,1)}, bf16[512,512]{1,0:T(8,128)(2,1)}, u32[]{:S(2)}, u32[]{:S(2)}) collective-permute-start(bf16[512,512]{1,0:T(8,128)(2,1)} %get-tuple-element.14), channel_id=1, source_target_pairs={{0,3},{1,0},{2,1},{3,2},{4,7},{5,4},{6,5},{7,6},{8,11},{9,8},{10,9... | collective-permute-start | bytes 1572872 | tf_op jit(solution)/shard_map/ppermute | solution.py:20
  44.4 2.2 %convolution_convert_fusion = bf16[512,2048]{1,0:T(8,128)(2,1)} fusion(bf16[256,2048]{1,0:T(8,128)(2,1)S(1)} %copy-done.1, f32[2048]{0:T(1024)S(1)} %copy-done.5, f32[256]{0:T(256)S(1)} %add_rsqrt_fusion.2, s32[256]{0:T(256)S(1)} %bitcast.104, s32[256]{0:T(256)S(1)} %bitcast.98, pred[256]{0:T(512)(128)(4,1)S(1)} %get-tuple-element.3, ...), kind=kOutput, calls=%fused_computation.14 | convolution fusion | flops 540672000 | bytes 3157504 | tf_op jit(solution)/shard_map/dot_general | solution.py:107
  46.6 5.1 %all-to-all-start.2 = ((bf16[32,16,2048]{2,1,0:T(8,128)(2,1)}), bf16[32,16,2048]{2,1,0:T(8,128)(2,1)}, u32[]{:S(2)}, u32[]{:S(2)}) async-start(bf16[32,16,2048]{2,1,0:T(8,128)(2,1)} %bitcast.92), calls=%async_computation.2 | async-start | bytes 4194304 | tf_op jit(solution)/shard_map/all_to_all | solution.py:111
  51.7 4.9 %collective-permute-done.1 = bf16[512,512]{1,0:T(8,128)(2,1)} collective-permute-done((bf16[512,512]{1,0:T(8,128)(2,1)}, bf16[512,512]{1,0:T(8,128)(2,1)}, u32[]{:S(2)}, u32[]{:S(2)}) %collective-permute-start.1) | collective-permute-done | bytes 524320 | tf_op jit(solution)/shard_map/ppermute | solution.py:20
  59.4 6.1 %fusion.6 = f32[512,1408]{1,0:T(8,128)S(1)} fusion(bf16[1,2048,1408]{2,1,0:T(8,128)(2,1)} %param.13, bf16[512,2048]{1,0:T(8,128)(2,1)S(1)} %constant_dynamic-update-slice_fusion.4, f32[2048]{0:T(1024)S(1)} %copy-done.5, f32[512]{0:T(512)S(1)} %add_rsqrt_fusion), kind=kOutput, calls=%fused_computation.6 | convolution fusion | flops 2956984320 | bytes 10758144 | tf_op jit(solution)/shard_map/dot_general | solution.py:120
  65.5 3.5 %multiply_convert_fusion = bf16[512,1408]{1,0:T(8,128)(2,1)S(1)} fusion(f32[512,1408]{1,0:T(8,128)S(1)} %fusion.6, bf16[1,2048,1408]{2,1,0:T(8,128)(2,1)S(1)} %bitcast.110, bf16[512,2048]{1,0:T(8,128)(2,1)S(1)} %constant_dynamic-update-slice_fusion.4, f32[2048]{0:T(1024)S(1)} %copy-done.5, f32[512]{0:T(512)S(1)} %add_rsqrt_fusion), kind=kOutput, calls=%fused_computation.16 | convolution fusion | flops 2961309696 | bytes 12199936 | tf_op jit(solution)/shard_map/dot_general | solution.py:121
  74.3 1.8 %fusion.36 = bf16[512,512]{1,0:T(8,128)(2,1)} fusion(bf16[512,1408]{1,0:T(8,128)(2,1)S(1)} %multiply_convert_fusion, bf16[1,1408,2048]{2,1,0:T(8,128)(2,1)S(1)} %bitcast.114, s32[]{:T(128)S(6)} %select_n.142), kind=kOutput, calls=%fused_computation.39 | convolution fusion | flops 738459648 | bytes 3407876 | tf_op jit(solution)/shard_map/dot_general | solution.py:65
  77.0 3.1 %all-to-all-done.2 = bf16[32,16,2048]{2,1,0:T(8,128)(2,1)} async-done(((bf16[32,16,2048]{2,1,0:T(8,128)(2,1)}), bf16[32,16,2048]{2,1,0:T(8,128)(2,1)}, u32[]{:S(2)}, u32[]{:S(2)}) %all-to-all-start.2) | async-done | bytes 2097184 | tf_op jit(solution)/shard_map/all_to_all | solution.py:111
  80.1 6.5 %fusion.4 = f32[512,1408]{1,0:T(8,128)S(1)} fusion(bf16[512,2048]{1,0:T(8,128)(2,1)} %bitcast.15, bf16[1,2048,1408]{2,1,0:T(8,128)(2,1)} %param.13), kind=kOutput, calls=%fused_computation.4 | convolution fusion | flops 2952790016 | bytes 10747904 | tf_op jit(solution)/shard_map/dot_general | solution.py:120
  86.7 5.2 %fusion.14 = bf16[512,1408]{1,0:T(8,128)(2,1)S(1)} fusion(bf16[512,2048]{1,0:T(8,128)(2,1)} %bitcast.15, bf16[1,2048,1408]{2,1,0:T(8,128)(2,1)S(1)} %bitcast.112, f32[512,1408]{1,0:T(8,128)S(1)} %fusion.4), kind=kOutput, calls=%fused_computation.15 | convolution fusion | flops 2957115392 | bytes 12189696 | tf_op jit(solution)/shard_map/dot_general | solution.py:121
  101.2 2.9 %add_convert_fusion.1 = bf16[512,512]{1,0:T(8,128)(2,1)} fusion(bf16[512,512]{1,0:T(8,128)(2,1)S(1)} %collective-permute-done.5, bf16[512,512]{1,0:T(8,128)(2,1)S(1)} %collective-permute-done.4, bf16[512,512]{1,0:T(8,128)(2,1)} %collective-permute-done.3, bf16[512,1408]{1,0:T(8,128)(2,1)S(1)} %copy-done.8, bf16[1,1408,2048]{2,1,0:T(8,128)(2,1)S(1)} %bitcast.116, ...), kind=kOutput, calls=%fused_computation.64 | convolution fusion | flops 740556800 | bytes 4980740 | tf_op jit(solution)/shard_map/dot_general | solution.py:65
  104.1 4.8 %all-to-all-start.1 = ((bf16[32,16,512]{2,1,0:T(8,128)(2,1)}), bf16[32,16,512]{2,1,0:T(8,128)(2,1)S(1)}, u32[]{:S(2)}, u32[]{:S(2)}) async-start(bf16[32,16,512]{2,1,0:T(8,128)(2,1)} %bitcast.12), calls=%async_computation.1 | async-start | bytes 1048576 | tf_op jit(solution)/shard_map/all_to_all | solution.py:125
  109.0 2.1 %collective-permute-done.9 = bf16[512,512]{1,0:T(8,128)(2,1)S(1)} collective-permute-done((bf16[512,512]{1,0:T(8,128)(2,1)}, bf16[512,512]{1,0:T(8,128)(2,1)S(1)}, u32[]{:S(2)}, u32[]{:S(2)}) %collective-permute-start.9) | collective-permute-done | bytes 524320 | tf_op jit(solution)/shard_map/ppermute | solution.py:20
  111.1 12.2 %collective-permute-done.8 = bf16[512,512]{1,0:T(8,128)(2,1)} collective-permute-done((bf16[512,512]{1,0:T(8,128)(2,1)}, bf16[512,512]{1,0:T(8,128)(2,1)}, u32[]{:S(2)}, u32[]{:S(2)}) %collective-permute-start.8) | collective-permute-done | bytes 524320 | tf_op jit(solution)/shard_map/ppermute | solution.py:20
  123.3 3.7 %add_convert_fusion = bf16[512,512]{1,0:T(8,128)(2,1)} fusion(bf16[512,512]{1,0:T(8,128)(2,1)S(1)} %collective-permute-done.10, bf16[512,512]{1,0:T(8,128)(2,1)S(1)} %collective-permute-done.9, bf16[512,512]{1,0:T(8,128)(2,1)} %collective-permute-done.8, bf16[512,1408]{1,0:T(8,128)(2,1)} %copy-done.6, bf16[1,1408,2048]{2,1,0:T(8,128)(2,1)} %param.15, ...), kind=kOutput, calls=%fused_computation.61 | convolution fusion | flops 740556800 | bytes 4980740 | tf_op jit(solution)/shard_map/dot_general | solution.py:65
  127.0 4.0 %all-to-all-start.3 = ((bf16[32,16,512]{2,1,0:T(8,128)(2,1)}), bf16[32,16,512]{2,1,0:T(8,128)(2,1)S(1)}, u32[]{:S(2)}, u32[]{:S(2)}) async-start(bf16[32,16,512]{2,1,0:T(8,128)(2,1)} %bitcast.16), calls=%async_computation.3 | async-start | bytes 1048576 | tf_op jit(solution)/shard_map/all_to_all | solution.py:125
  132.1 10.7 %all-to-all-done.3 = bf16[32,16,512]{2,1,0:T(8,128)(2,1)S(1)} async-done(((bf16[32,16,512]{2,1,0:T(8,128)(2,1)}), bf16[32,16,512]{2,1,0:T(8,128)(2,1)S(1)}, u32[]{:S(2)}, u32[]{:S(2)}) %all-to-all-start.3) | async-done | bytes 524320 | tf_op jit(solution)/shard_map/all_to_all | solution.py:125
  146.4 1.8 %collective-permute-done.12 = f32[256]{0:T(256)S(1)} collective-permute-done((f32[256]{0:T(256)S(1)}, f32[256]{0:T(256)S(1)}, u32[]{:S(2)}, u32[]{:S(2)}) %collective-permute-start.12) | collective-permute-done | bytes 1056 | tf_op jit(solution)/shard_map/ppermute | solution.py:20
  (101 shorter events, 31.9 us)
Async XLA Ops:
  0.6 9.8 %collective-permute-start = (bf16[256,512]{1,0:T(8,128)(2,1)}, bf16[256,512]{1,0:T(8,128)(2,1)S(1)}, u32[]{:S(2)}, u32[]{:S(2)}) collective-permute-start(bf16[256,512]{1,0:T(8,128)(2,1)} %param.8), channel_id=1, source_target_pairs={{0,2},{1,3},{2,0},{3,1},{4,6},{5,7},{6,4},{7,5},{8,10},{9,11},{10,... | collective-permute-start | bytes 786440 | tf_op jit(solution)/shard_map/ppermute | solution.py:20
  4.5 21.0 %collective-permute-start.6 = (bf16[256,512]{1,0:T(8,128)(2,1)}, bf16[256,512]{1,0:T(8,128)(2,1)S(1)}, u32[]{:S(2)}, u32[]{:S(2)}) collective-permute-start(bf16[256,512]{1,0:T(8,128)(2,1)} %param.8), channel_id=1, source_target_pairs={{0,1},{1,2},{2,3},{3,0},{4,5},{5,6},{6,7},{7,4},{8,9},{9,10},{10,1... | collective-permute-start | bytes 786440 | tf_op jit(solution)/shard_map/ppermute | solution.py:20
  10.5 13.2 %copy-start.2 = (bf16[256,512]{1,0:T(8,128)(2,1)S(1)}, bf16[256,512]{1,0:T(8,128)(2,1)}, u32[]{:S(2)}) copy-start(bf16[256,512]{1,0:T(8,128)(2,1)} %param.8) | copy-start | bytes 786436
  13.0 27.6 %all-to-all-start = ((bf16[32,16,1024]{2,1,0:T(8,128)(2,1)}), bf16[32,16,1024]{2,1,0:T(8,128)(2,1)S(1)}, u32[]{:S(2)}, u32[]{:S(2)}) async-start(bf16[32,16,1024]{2,1,0:T(8,128)(2,1)} %bitcast.4), calls=%async_computation | async-start | bytes 2097152 | tf_op jit(solution)/shard_map/all_to_all | solution.py:111
  23.6 7.7 %collective-permute-start.7 = (bf16[256,512]{1,0:T(8,128)(2,1)S(1)}, bf16[256,512]{1,0:T(8,128)(2,1)S(1)}, u32[]{:S(2)}, u32[]{:S(2)}) collective-permute-start(bf16[256,512]{1,0:T(8,128)(2,1)S(1)} %copy-done.2), channel_id=1, source_target_pairs={{0,3},{1,0},{2,1},{3,2},{4,7},{5,4},{6,5},{7,6},{8,11},{9,8},{10,9... | collective-permute-start | bytes 786440 | tf_op jit(solution)/shard_map/ppermute | solution.py:20
  31.7 12.7 %copy-start.5 = (f32[2048]{0:T(1024)S(1)}, f32[2048]{0:T(1024)}, u32[]{:S(2)}) copy-start(f32[2048]{0:T(1024)} %param.11) | copy-start | bytes 24580
  41.7 14.9 %collective-permute-start.1 = (bf16[512,512]{1,0:T(8,128)(2,1)}, bf16[512,512]{1,0:T(8,128)(2,1)}, u32[]{:S(2)}, u32[]{:S(2)}) collective-permute-start(bf16[512,512]{1,0:T(8,128)(2,1)} %get-tuple-element.14), channel_id=1, source_target_pairs={{0,1},{1,2},{2,3},{3,0},{4,5},{5,6},{6,7},{7,4},{8,9},{9,10},{10,1... | collective-permute-start | bytes 1572872 | tf_op jit(solution)/shard_map/ppermute | solution.py:20
  41.8 15.9 %collective-permute-start.2 = (bf16[512,512]{1,0:T(8,128)(2,1)}, bf16[512,512]{1,0:T(8,128)(2,1)}, u32[]{:S(2)}, u32[]{:S(2)}) collective-permute-start(bf16[512,512]{1,0:T(8,128)(2,1)} %get-tuple-element.14), channel_id=1, source_target_pairs={{0,3},{1,0},{2,1},{3,2},{4,7},{5,4},{6,5},{7,6},{8,11},{9,8},{10,9... | collective-permute-start | bytes 1572872 | tf_op jit(solution)/shard_map/ppermute | solution.py:20
  46.6 33.5 %all-to-all-start.2 = ((bf16[32,16,2048]{2,1,0:T(8,128)(2,1)}), bf16[32,16,2048]{2,1,0:T(8,128)(2,1)}, u32[]{:S(2)}, u32[]{:S(2)}) async-start(bf16[32,16,2048]{2,1,0:T(8,128)(2,1)} %bitcast.92), calls=%async_computation.2 | async-start | bytes 4194304 | tf_op jit(solution)/shard_map/all_to_all | solution.py:111
  59.4 9.7 %slice-start.4 = ((s8[5767168]{0:T(1024)(128)(4,1)}), s8[4194304]{0:T(1024)(128)(4,1)S(1)}, s32[]{:S(2)}) async-start(s8[5767168]{0:T(1024)(128)(4,1)} %bitcast.113), calls=%async_computation.8 | async-start | bytes 8388608
  70.9 28.1 %collective-permute-start.5 = (bf16[512,512]{1,0:T(8,128)(2,1)}, bf16[512,512]{1,0:T(8,128)(2,1)S(1)}, u32[]{:S(2)}, u32[]{:S(2)}) collective-permute-start(bf16[512,512]{1,0:T(8,128)(2,1)} %fusion.48), channel_id=1, source_target_pairs={{0,3},{1,0},{2,1},{3,2},{4,7},{5,4},{6,5},{7,6},{8,11},{9,8},{10,9... | collective-permute-start | bytes 1572872 | tf_op jit(solution)/shard_map/ppermute | solution.py:20
  73.9 26.0 %collective-permute-start.4 = (bf16[512,512]{1,0:T(8,128)(2,1)}, bf16[512,512]{1,0:T(8,128)(2,1)S(1)}, u32[]{:S(2)}, u32[]{:S(2)}) collective-permute-start(bf16[512,512]{1,0:T(8,128)(2,1)} %fusion.42), channel_id=1, source_target_pairs={{0,2},{1,3},{2,0},{3,1},{4,6},{5,7},{6,4},{7,5},{8,10},{9,11},{10,... | collective-permute-start | bytes 1572872 | tf_op jit(solution)/shard_map/ppermute | solution.py:20
  74.3 12.3 %slice-start.2 = ((s8[5767168]{0:T(1024)(128)(4,1)}), s8[1572864]{0:T(1024)(128)(4,1)S(1)}, s32[]{:S(2)}) async-start(s8[5767168]{0:T(1024)(128)(4,1)} %bitcast.111), calls=%async_computation.6 | async-start | bytes 3145728
  76.1 25.1 %collective-permute-start.3 = (bf16[512,512]{1,0:T(8,128)(2,1)}, bf16[512,512]{1,0:T(8,128)(2,1)}, u32[]{:S(2)}, u32[]{:S(2)}) collective-permute-start(bf16[512,512]{1,0:T(8,128)(2,1)} %fusion.36), channel_id=1, source_target_pairs={{0,1},{1,2},{2,3},{3,0},{4,5},{5,6},{6,7},{7,4},{8,9},{9,10},{10,1... | collective-permute-start | bytes 1572872 | tf_op jit(solution)/shard_map/ppermute | solution.py:20
  80.1 11.7 %slice-start.6 = ((s8[5767168]{0:T(1024)(128)(4,1)}), s8[4194304]{0:T(1024)(128)(4,1)S(1)}, s32[]{:S(2)}) async-start(s8[5767168]{0:T(1024)(128)(4,1)} %bitcast.115), calls=%async_computation.10 | async-start | bytes 8388608
  93.7 15.3 %collective-permute-start.10 = (bf16[512,512]{1,0:T(8,128)(2,1)}, bf16[512,512]{1,0:T(8,128)(2,1)S(1)}, u32[]{:S(2)}, u32[]{:S(2)}) collective-permute-start(bf16[512,512]{1,0:T(8,128)(2,1)} %fusion.51), channel_id=1, source_target_pairs={{0,3},{1,0},{2,1},{3,2},{4,7},{5,4},{6,5},{7,6},{8,11},{9,8},{10,9... | collective-permute-start | bytes 1572872 | tf_op jit(solution)/shard_map/ppermute | solution.py:20
  95.8 15.3 %collective-permute-start.9 = (bf16[512,512]{1,0:T(8,128)(2,1)}, bf16[512,512]{1,0:T(8,128)(2,1)S(1)}, u32[]{:S(2)}, u32[]{:S(2)}) collective-permute-start(bf16[512,512]{1,0:T(8,128)(2,1)} %fusion.45), channel_id=1, source_target_pairs={{0,2},{1,3},{2,0},{3,1},{4,6},{5,7},{6,4},{7,5},{8,10},{9,11},{10,... | collective-permute-start | bytes 1572872 | tf_op jit(solution)/shard_map/ppermute | solution.py:20
  98.9 10.0 %copy-start.4 = (f32[256,2]{0,1:T(2,128)S(1)}, f32[256,2]{0,1:T(2,128)}, u32[]{:S(2)}) copy-start(f32[256,2]{0,1:T(2,128)} %param.10) | copy-start | bytes 6148
  98.9 24.4 %collective-permute-start.8 = (bf16[512,512]{1,0:T(8,128)(2,1)}, bf16[512,512]{1,0:T(8,128)(2,1)}, u32[]{:S(2)}, u32[]{:S(2)}) collective-permute-start(bf16[512,512]{1,0:T(8,128)(2,1)} %fusion.39), channel_id=1, source_target_pairs={{0,1},{1,2},{2,3},{3,0},{4,5},{5,6},{6,7},{7,4},{8,9},{9,10},{10,1... | collective-permute-start | bytes 1572872 | tf_op jit(solution)/shard_map/ppermute | solution.py:20
  104.1 22.9 %all-to-all-start.1 = ((bf16[32,16,512]{2,1,0:T(8,128)(2,1)}), bf16[32,16,512]{2,1,0:T(8,128)(2,1)S(1)}, u32[]{:S(2)}, u32[]{:S(2)}) async-start(bf16[32,16,512]{2,1,0:T(8,128)(2,1)} %bitcast.12), calls=%async_computation.1 | async-start | bytes 1048576 | tf_op jit(solution)/shard_map/all_to_all | solution.py:125
  127.0 15.8 %all-to-all-start.3 = ((bf16[32,16,512]{2,1,0:T(8,128)(2,1)}), bf16[32,16,512]{2,1,0:T(8,128)(2,1)S(1)}, u32[]{:S(2)}, u32[]{:S(2)}) async-start(bf16[32,16,512]{2,1,0:T(8,128)(2,1)} %bitcast.16), calls=%async_computation.3 | async-start | bytes 1048576 | tf_op jit(solution)/shard_map/all_to_all | solution.py:125
  143.9 2.5 %collective-permute-start.13 = (f32[256]{0:T(256)S(1)}, f32[256]{0:T(256)S(1)}, u32[]{:S(2)}, u32[]{:S(2)}) collective-permute-start(f32[256]{0:T(256)S(1)} %get-tuple-element.20), channel_id=1, source_target_pairs={{0,3},{1,0},{2,1},{3,2},{4,7},{5,4},{6,5},{7,6},{8,11},{9,8},{10,9... | collective-permute-start | bytes 3080 | tf_op jit(solution)/shard_map/ppermute | solution.py:20
  144.3 3.9 %collective-permute-start.12 = (f32[256]{0:T(256)S(1)}, f32[256]{0:T(256)S(1)}, u32[]{:S(2)}, u32[]{:S(2)}) collective-permute-start(f32[256]{0:T(256)S(1)} %get-tuple-element.20), channel_id=1, source_target_pairs={{0,2},{1,3},{2,0},{3,1},{4,6},{5,7},{6,4},{7,5},{8,10},{9,11},{10,... | collective-permute-start | bytes 3080 | tf_op jit(solution)/shard_map/ppermute | solution.py:20
  145.0 4.0 %collective-permute-start.11 = (f32[256]{0:T(256)S(1)}, f32[256]{0:T(256)S(1)}, u32[]{:S(2)}, u32[]{:S(2)}) collective-permute-start(f32[256]{0:T(256)S(1)} %get-tuple-element.20), channel_id=1, source_target_pairs={{0,1},{1,2},{2,3},{3,0},{4,5},{5,6},{6,7},{7,4},{8,9},{9,10},{10,1... | collective-permute-start | bytes 3080 | tf_op jit(solution)/shard_map/ppermute | solution.py:20
  (11 other events, 65.1 us)

commit v20 on v19

--- a/solution.py
+++ b/solution.py
@@ -60,7 +60,8 @@
     me = lax.axis_index("tp")
     width = w_down.shape[1] // tp_count
     terms = []
-    for s in list(range(1, tp_count)) + [0]:
+    far_first = [tp_count // 2] + [s for s in range(1, tp_count) if s != tp_count // 2]
+    for s in far_first + [0]:
         w_block = lax.dynamic_slice_in_dim(w_down, ((me + s) % tp_count) * width, width, axis=1)
         block = jnp.dot(activ, w_block, preferred_element_type=jnp.float32).astype(jnp.bfloat16)
         terms.append(block if s == 0 else shift_tp(block, s, tp_count))

time: 151 us -> 150 us (level)
  waiting for transfers between devices: 54.5 us -> 50.1 us
  starting transfers between devices: 39.8 us -> 43.6 us
    ppermute x14, waiting for transfers between devices: 31.9 us -> 28 us  [shift_tp(): lax.ppermute(value, 'tp', [(j, (j + step) % tp_count) for j in range(tp_c...]
    all_to_all x2, starting transfers between devices: 8.83 us -> 11.2 us  [shards(): lax.all_to_all(summed, 'req', split_axis=0, concat_axis=0, tiled=True)]
  transfers between devices with their start and end apart: 18 -> 18, of which waited for: 12 -> 11; matrix products, arithmetic and copies ran while one was open for 34% -> 34% of each run, Pallas kernels for 0% -> 0%
where the time goes in v20:
time: 150 us; the launch traced here: 149 us
  waiting for transfers between devices  50.1 us (33%)
  matrix products  45.4 us (30%)
  starting transfers between devices  43.6 us (29%)
  local copies, waits for them, and re-layouts  5.29 us (4%)
  other arithmetic  3.66 us (2%)
    ppermute x14, waiting for transfers between devices, shift_tp(): lax.ppermute(value, 'tp', [(j, (j + step) % tp_count) for j in range(tp_c...  28 us
    dot_general x8, matrix products, down_scatter_sum_tp(): jnp.dot(activ, w_block, preferred_element_type=jnp.float32)  17.3 us
    ppermute x14, starting transfers between devices, shift_tp(): lax.ppermute(value, 'tp', [(j, (j + step) % tp_count) for j in range(tp_c...  16.7 us
    all_to_all x2, starting transfers between devices, shards(): lax.all_to_all(outgoing, 'req', split_axis=0, concat_axis=0, tiled=True)  15.7 us
    dot_general x2, matrix products, shards(): jnp.dot(flat_rows, gate_weight[0], preferred_element_type=jnp.float32)  12.6 us
    all_to_all x2, waiting for transfers between devices, shards(): lax.all_to_all(outgoing, 'req', split_axis=0, concat_axis=0, tiled=True)  11.3 us
    all_to_all x2, starting transfers between devices, shards(): lax.all_to_all(summed, 'req', split_axis=0, concat_axis=0, tiled=True)  11.2 us
    all_to_all x2, waiting for transfers between devices, shards(): lax.all_to_all(summed, 'req', split_axis=0, concat_axis=0, tiled=True)  10.7 us
  transfers between devices with their start and end apart: 18, of which 11 were waited for; matrix products, arithmetic and copies ran while one was open for 34% of the time, Pallas kernels for 0%

profile of v20, /device:TPU:1, one launch (start us, length us, event | category | flops | bytes accessed | tf_op | source)
XLA Modules:
  0.0 149.2 jit_solution(12175812397655601411)
XLA Ops:
  0.6 3.8 %collective-permute-start = (bf16[256,512]{1,0:T(8,128)(2,1)}, bf16[256,512]{1,0:T(8,128)(2,1)S(1)}, u32[]{:S(2)}, u32[]{:S(2)}) collective-permute-start(bf16[256,512]{1,0:T(8,128)(2,1)} %param.8), channel_id=1, source_target_pairs={{0,2},{1,3},{2,0},{3,1},{4,6},{5,7},{6,4},{7,5},{8,10},{9,11},{10,... | collective-permute-start | bytes 786440 | tf_op jit(solution)/shard_map/ppermute | solution.py:20
  8.5 2.0 %collective-permute-done = bf16[256,512]{1,0:T(8,128)(2,1)S(1)} collective-permute-done((bf16[256,512]{1,0:T(8,128)(2,1)}, bf16[256,512]{1,0:T(8,128)(2,1)S(1)}, u32[]{:S(2)}, u32[]{:S(2)}) %collective-permute-start) | collective-permute-done | bytes 262176 | tf_op jit(solution)/shard_map/ppermute | solution.py:20
  10.5 2.5 %convolution_convert_fusion.1 = bf16[512,1024]{1,0:T(8,128)(2,1)} fusion(bf16[256,512]{1,0:T(8,128)(2,1)S(1)} %collective-permute-done, bf16[256,512]{1,0:T(8,128)(2,1)} %param.8, s32[256]{0:T(256)S(1)} %bitcast.103, s32[256]{0:T(256)S(1)} %bitcast.97, pred[256]{0:T(512)(128)(4,1)S(1)} %get-tuple-element.5, pred[256]{0:T(512)(128)(4,1)S(1)} %get-tuple-element.4), kind=kOutput, calls=%fused_computation.22 | convolution fusion | flops 270663680 | bytes 1575424 | tf_op jit(solution)/shard_map/dot_general | solution.py:108
  13.0 10.6 %all-to-all-start = ((bf16[32,16,1024]{2,1,0:T(8,128)(2,1)}), bf16[32,16,1024]{2,1,0:T(8,128)(2,1)S(1)}, u32[]{:S(2)}, u32[]{:S(2)}) async-start(bf16[32,16,1024]{2,1,0:T(8,128)(2,1)} %bitcast.4), calls=%async_computation | async-start | bytes 2097152 | tf_op jit(solution)/shard_map/all_to_all | solution.py:112
  25.6 5.8 %collective-permute-done.7 = bf16[256,512]{1,0:T(8,128)(2,1)S(1)} collective-permute-done((bf16[256,512]{1,0:T(8,128)(2,1)S(1)}, bf16[256,512]{1,0:T(8,128)(2,1)S(1)}, u32[]{:S(2)}, u32[]{:S(2)}) %collective-permute-start.7) | collective-permute-done | bytes 262176 | tf_op jit(solution)/shard_map/ppermute | solution.py:20
  31.7 8.8 %all-to-all-done = bf16[32,16,1024]{2,1,0:T(8,128)(2,1)S(1)} async-done(((bf16[32,16,1024]{2,1,0:T(8,128)(2,1)}), bf16[32,16,1024]{2,1,0:T(8,128)(2,1)S(1)}, u32[]{:S(2)}, u32[]{:S(2)}) %all-to-all-start) | async-done | bytes 1048608 | tf_op jit(solution)/shard_map/all_to_all | solution.py:112
  41.8 2.6 %collective-permute-start.2 = (bf16[512,512]{1,0:T(8,128)(2,1)}, bf16[512,512]{1,0:T(8,128)(2,1)}, u32[]{:S(2)}, u32[]{:S(2)}) collective-permute-start(bf16[512,512]{1,0:T(8,128)(2,1)} %get-tuple-element.14), channel_id=1, source_target_pairs={{0,3},{1,0},{2,1},{3,2},{4,7},{5,4},{6,5},{7,6},{8,11},{9,8},{10,9... | collective-permute-start | bytes 1572872 | tf_op jit(solution)/shard_map/ppermute | solution.py:20
  44.4 2.2 %convolution_convert_fusion = bf16[512,2048]{1,0:T(8,128)(2,1)} fusion(bf16[256,2048]{1,0:T(8,128)(2,1)S(1)} %copy-done.1, f32[2048]{0:T(1024)S(1)} %copy-done.5, f32[256]{0:T(256)S(1)} %add_rsqrt_fusion.2, s32[256]{0:T(256)S(1)} %bitcast.104, s32[256]{0:T(256)S(1)} %bitcast.98, pred[256]{0:T(512)(128)(4,1)S(1)} %get-tuple-element.3, ...), kind=kOutput, calls=%fused_computation.14 | convolution fusion | flops 540672000 | bytes 3157504 | tf_op jit(solution)/shard_map/dot_general | solution.py:108
  46.6 5.1 %all-to-all-start.2 = ((bf16[32,16,2048]{2,1,0:T(8,128)(2,1)}), bf16[32,16,2048]{2,1,0:T(8,128)(2,1)}, u32[]{:S(2)}, u32[]{:S(2)}) async-start(bf16[32,16,2048]{2,1,0:T(8,128)(2,1)} %bitcast.92), calls=%async_computation.2 | async-start | bytes 4194304 | tf_op jit(solution)/shard_map/all_to_all | solution.py:112
  51.7 4.9 %collective-permute-done.1 = bf16[512,512]{1,0:T(8,128)(2,1)} collective-permute-done((bf16[512,512]{1,0:T(8,128)(2,1)}, bf16[512,512]{1,0:T(8,128)(2,1)}, u32[]{:S(2)}, u32[]{:S(2)}) %collective-permute-start.1) | collective-permute-done | bytes 524320 | tf_op jit(solution)/shard_map/ppermute | solution.py:20
  59.4 6.1 %fusion.6 = f32[512,1408]{1,0:T(8,128)S(1)} fusion(bf16[1,2048,1408]{2,1,0:T(8,128)(2,1)} %param.13, bf16[512,2048]{1,0:T(8,128)(2,1)S(1)} %constant_dynamic-update-slice_fusion.4, f32[2048]{0:T(1024)S(1)} %copy-done.5, f32[512]{0:T(512)S(1)} %add_rsqrt_fusion), kind=kOutput, calls=%fused_computation.6 | convolution fusion | flops 2956984320 | bytes 10758144 | tf_op jit(solution)/shard_map/dot_general | solution.py:121
  65.5 3.5 %multiply_convert_fusion = bf16[512,1408]{1,0:T(8,128)(2,1)S(1)} fusion(f32[512,1408]{1,0:T(8,128)S(1)} %fusion.6, bf16[1,2048,1408]{2,1,0:T(8,128)(2,1)S(1)} %bitcast.110, bf16[512,2048]{1,0:T(8,128)(2,1)S(1)} %constant_dynamic-update-slice_fusion.4, f32[2048]{0:T(1024)S(1)} %copy-done.5, f32[512]{0:T(512)S(1)} %add_rsqrt_fusion), kind=kOutput, calls=%fused_computation.16 | convolution fusion | flops 2961309696 | bytes 12199936 | tf_op jit(solution)/shard_map/dot_general | solution.py:122
  72.1 1.8 %fusion.42 = bf16[512,512]{1,0:T(8,128)(2,1)} fusion(bf16[512,1408]{1,0:T(8,128)(2,1)S(1)} %multiply_convert_fusion, bf16[1,1408,2048]{2,1,0:T(8,128)(2,1)S(1)} %bitcast.114, s32[]{:T(128)S(6)} %select_n.144), kind=kOutput, calls=%fused_computation.41 | convolution fusion | flops 738459648 | bytes 3407876 | tf_op jit(solution)/shard_map/dot_general | solution.py:66
  77.6 2.5 %all-to-all-done.2 = bf16[32,16,2048]{2,1,0:T(8,128)(2,1)} async-done(((bf16[32,16,2048]{2,1,0:T(8,128)(2,1)}), bf16[32,16,2048]{2,1,0:T(8,128)(2,1)}, u32[]{:S(2)}, u32[]{:S(2)}) %all-to-all-start.2) | async-done | bytes 2097184 | tf_op jit(solution)/shard_map/all_to_all | solution.py:112
  80.1 6.5 %fusion.4 = f32[512,1408]{1,0:T(8,128)S(1)} fusion(bf16[512,2048]{1,0:T(8,128)(2,1)} %bitcast.15, bf16[1,2048,1408]{2,1,0:T(8,128)(2,1)} %param.13), kind=kOutput, calls=%fused_computation.4 | convolution fusion | flops 2952790016 | bytes 10747904 | tf_op jit(solution)/shard_map/dot_general | solution.py:121
  86.7 5.2 %fusion.14 = bf16[512,1408]{1,0:T(8,128)(2,1)S(1)} fusion(bf16[512,2048]{1,0:T(8,128)(2,1)} %bitcast.15, bf16[1,2048,1408]{2,1,0:T(8,128)(2,1)S(1)} %bitcast.112, f32[512,1408]{1,0:T(8,128)S(1)} %fusion.4), kind=kOutput, calls=%fused_computation.15 | convolution fusion | flops 2957115392 | bytes 12189696 | tf_op jit(solution)/shard_map/dot_general | solution.py:122
  94.0 1.8 %fusion.45 = bf16[512,512]{1,0:T(8,128)(2,1)} fusion(bf16[512,1408]{1,0:T(8,128)(2,1)S(1)} %fusion.14, bf16[1,1408,2048]{2,1,0:T(8,128)(2,1)S(1)} %bitcast.116, s32[]{:T(128)S(6)} %select_n.144), kind=kOutput, calls=%fused_computation.42 | convolution fusion | flops 738459648 | bytes 3407876 | tf_op jit(solution)/shard_map/dot_general | solution.py:66
  100.5 2.9 %add_convert_fusion.1 = bf16[512,512]{1,0:T(8,128)(2,1)} fusion(bf16[512,512]{1,0:T(8,128)(2,1)S(1)} %collective-permute-done.5, bf16[512,512]{1,0:T(8,128)(2,1)S(1)} %collective-permute-done.4, bf16[512,512]{1,0:T(8,128)(2,1)} %collective-permute-done.3, bf16[512,1408]{1,0:T(8,128)(2,1)S(1)} %copy-done.8, bf16[1,1408,2048]{2,1,0:T(8,128)(2,1)S(1)} %bitcast.116, ...), kind=kOutput, calls=%fused_computation.64 | convolution fusion | flops 740556800 | bytes 4980740 | tf_op jit(solution)/shard_map/dot_general | solution.py:66
  103.3 5.2 %all-to-all-start.1 = ((bf16[32,16,512]{2,1,0:T(8,128)(2,1)}), bf16[32,16,512]{2,1,0:T(8,128)(2,1)S(1)}, u32[]{:S(2)}, u32[]{:S(2)}) async-start(bf16[32,16,512]{2,1,0:T(8,128)(2,1)} %bitcast.12), calls=%async_computation.1 | async-start | bytes 1048576 | tf_op jit(solution)/shard_map/all_to_all | solution.py:126
  108.7 3.1 %collective-permute-done.9 = bf16[512,512]{1,0:T(8,128)(2,1)S(1)} collective-permute-done((bf16[512,512]{1,0:T(8,128)(2,1)}, bf16[512,512]{1,0:T(8,128)(2,1)S(1)}, u32[]{:S(2)}, u32[]{:S(2)}) %collective-permute-start.9) | collective-permute-done | bytes 524320 | tf_op jit(solution)/shard_map/ppermute | solution.py:20
  111.7 9.3 %collective-permute-done.8 = bf16[512,512]{1,0:T(8,128)(2,1)} collective-permute-done((bf16[512,512]{1,0:T(8,128)(2,1)}, bf16[512,512]{1,0:T(8,128)(2,1)}, u32[]{:S(2)}, u32[]{:S(2)}) %collective-permute-start.8) | collective-permute-done | bytes 524320 | tf_op jit(solution)/shard_map/ppermute | solution.py:20
  121.0 3.7 %add_convert_fusion = bf16[512,512]{1,0:T(8,128)(2,1)} fusion(bf16[512,512]{1,0:T(8,128)(2,1)S(1)} %collective-permute-done.10, bf16[512,512]{1,0:T(8,128)(2,1)S(1)} %collective-permute-done.9, bf16[512,512]{1,0:T(8,128)(2,1)} %collective-permute-done.8, bf16[512,1408]{1,0:T(8,128)(2,1)} %copy-done.6, bf16[1,1408,2048]{2,1,0:T(8,128)(2,1)} %param.15, ...), kind=kOutput, calls=%fused_computation.61 | convolution fusion | flops 740556800 | bytes 4980740 | tf_op jit(solution)/shard_map/dot_general | solution.py:66
  124.7 5.9 %all-to-all-start.3 = ((bf16[32,16,512]{2,1,0:T(8,128)(2,1)}), bf16[32,16,512]{2,1,0:T(8,128)(2,1)S(1)}, u32[]{:S(2)}, u32[]{:S(2)}) async-start(bf16[32,16,512]{2,1,0:T(8,128)(2,1)} %bitcast.16), calls=%async_computation.3 | async-start | bytes 1048576 | tf_op jit(solution)/shard_map/all_to_all | solution.py:126
  131.7 10.7 %all-to-all-done.3 = bf16[32,16,512]{2,1,0:T(8,128)(2,1)S(1)} async-done(((bf16[32,16,512]{2,1,0:T(8,128)(2,1)}), bf16[32,16,512]{2,1,0:T(8,128)(2,1)S(1)}, u32[]{:S(2)}, u32[]{:S(2)}) %all-to-all-start.3) | async-done | bytes 524320 | tf_op jit(solution)/shard_map/all_to_all | solution.py:126
  (101 shorter events, 31.5 us)
Async XLA Ops:
  0.6 9.8 %collective-permute-start = (bf16[256,512]{1,0:T(8,128)(2,1)}, bf16[256,512]{1,0:T(8,128)(2,1)S(1)}, u32[]{:S(2)}, u32[]{:S(2)}) collective-permute-start(bf16[256,512]{1,0:T(8,128)(2,1)} %param.8), channel_id=1, source_target_pairs={{0,2},{1,3},{2,0},{3,1},{4,6},{5,7},{6,4},{7,5},{8,10},{9,11},{10,... | collective-permute-start | bytes 786440 | tf_op jit(solution)/shard_map/ppermute | solution.py:20
  4.5 21.0 %collective-permute-start.6 = (bf16[256,512]{1,0:T(8,128)(2,1)}, bf16[256,512]{1,0:T(8,128)(2,1)S(1)}, u32[]{:S(2)}, u32[]{:S(2)}) collective-permute-start(bf16[256,512]{1,0:T(8,128)(2,1)} %param.8), channel_id=1, source_target_pairs={{0,1},{1,2},{2,3},{3,0},{4,5},{5,6},{6,7},{7,4},{8,9},{9,10},{10,1... | collective-permute-start | bytes 786440 | tf_op jit(solution)/shard_map/ppermute | solution.py:20
  10.5 13.2 %copy-start.2 = (bf16[256,512]{1,0:T(8,128)(2,1)S(1)}, bf16[256,512]{1,0:T(8,128)(2,1)}, u32[]{:S(2)}) copy-start(bf16[256,512]{1,0:T(8,128)(2,1)} %param.8) | copy-start | bytes 786436
  13.0 27.6 %all-to-all-start = ((bf16[32,16,1024]{2,1,0:T(8,128)(2,1)}), bf16[32,16,1024]{2,1,0:T(8,128)(2,1)S(1)}, u32[]{:S(2)}, u32[]{:S(2)}) async-start(bf16[32,16,1024]{2,1,0:T(8,128)(2,1)} %bitcast.4), calls=%async_computation | async-start | bytes 2097152 | tf_op jit(solution)/shard_map/all_to_all | solution.py:112
  23.6 7.7 %collective-permute-start.7 = (bf16[256,512]{1,0:T(8,128)(2,1)S(1)}, bf16[256,512]{1,0:T(8,128)(2,1)S(1)}, u32[]{:S(2)}, u32[]{:S(2)}) collective-permute-start(bf16[256,512]{1,0:T(8,128)(2,1)S(1)} %copy-done.2), channel_id=1, source_target_pairs={{0,3},{1,0},{2,1},{3,2},{4,7},{5,4},{6,5},{7,6},{8,11},{9,8},{10,9... | collective-permute-start | bytes 786440 | tf_op jit(solution)/shard_map/ppermute | solution.py:20
  31.7 12.7 %copy-start.5 = (f32[2048]{0:T(1024)S(1)}, f32[2048]{0:T(1024)}, u32[]{:S(2)}) copy-start(f32[2048]{0:T(1024)} %param.11) | copy-start | bytes 24580
  41.7 14.9 %collective-permute-start.1 = (bf16[512,512]{1,0:T(8,128)(2,1)}, bf16[512,512]{1,0:T(8,128)(2,1)}, u32[]{:S(2)}, u32[]{:S(2)}) collective-permute-start(bf16[512,512]{1,0:T(8,128)(2,1)} %get-tuple-element.14), channel_id=1, source_target_pairs={{0,1},{1,2},{2,3},{3,0},{4,5},{5,6},{6,7},{7,4},{8,9},{9,10},{10,1... | collective-permute-start | bytes 1572872 | tf_op jit(solution)/shard_map/ppermute | solution.py:20
  41.8 15.9 %collective-permute-start.2 = (bf16[512,512]{1,0:T(8,128)(2,1)}, bf16[512,512]{1,0:T(8,128)(2,1)}, u32[]{:S(2)}, u32[]{:S(2)}) collective-permute-start(bf16[512,512]{1,0:T(8,128)(2,1)} %get-tuple-element.14), channel_id=1, source_target_pairs={{0,3},{1,0},{2,1},{3,2},{4,7},{5,4},{6,5},{7,6},{8,11},{9,8},{10,9... | collective-permute-start | bytes 1572872 | tf_op jit(solution)/shard_map/ppermute | solution.py:20
  46.6 33.5 %all-to-all-start.2 = ((bf16[32,16,2048]{2,1,0:T(8,128)(2,1)}), bf16[32,16,2048]{2,1,0:T(8,128)(2,1)}, u32[]{:S(2)}, u32[]{:S(2)}) async-start(bf16[32,16,2048]{2,1,0:T(8,128)(2,1)} %bitcast.92), calls=%async_computation.2 | async-start | bytes 4194304 | tf_op jit(solution)/shard_map/all_to_all | solution.py:112
  59.4 9.7 %slice-start.4 = ((s8[5767168]{0:T(1024)(128)(4,1)}), s8[4194304]{0:T(1024)(128)(4,1)S(1)}, s32[]{:S(2)}) async-start(s8[5767168]{0:T(1024)(128)(4,1)} %bitcast.113), calls=%async_computation.8 | async-start | bytes 8388608
  70.9 27.9 %collective-permute-start.5 = (bf16[512,512]{1,0:T(8,128)(2,1)}, bf16[512,512]{1,0:T(8,128)(2,1)S(1)}, u32[]{:S(2)}, u32[]{:S(2)}) collective-permute-start(bf16[512,512]{1,0:T(8,128)(2,1)} %fusion.48), channel_id=1, source_target_pairs={{0,3},{1,0},{2,1},{3,2},{4,7},{5,4},{6,5},{7,6},{8,11},{9,8},{10,9... | collective-permute-start | bytes 1572872 | tf_op jit(solution)/shard_map/ppermute | solution.py:20
  73.9 26.5 %collective-permute-start.4 = (bf16[512,512]{1,0:T(8,128)(2,1)}, bf16[512,512]{1,0:T(8,128)(2,1)S(1)}, u32[]{:S(2)}, u32[]{:S(2)}) collective-permute-start(bf16[512,512]{1,0:T(8,128)(2,1)} %fusion.42), channel_id=1, source_target_pairs={{0,1},{1,2},{2,3},{3,0},{4,5},{5,6},{6,7},{7,4},{8,9},{9,10},{10,1... | collective-permute-start | bytes 1572872 | tf_op jit(solution)/shard_map/ppermute | solution.py:20
  74.1 12.5 %slice-start.2 = ((s8[5767168]{0:T(1024)(128)(4,1)}), s8[1572864]{0:T(1024)(128)(4,1)S(1)}, s32[]{:S(2)}) async-start(s8[5767168]{0:T(1024)(128)(4,1)} %bitcast.111), calls=%async_computation.6 | async-start | bytes 3145728
  75.9 24.6 %collective-permute-start.3 = (bf16[512,512]{1,0:T(8,128)(2,1)}, bf16[512,512]{1,0:T(8,128)(2,1)}, u32[]{:S(2)}, u32[]{:S(2)}) collective-permute-start(bf16[512,512]{1,0:T(8,128)(2,1)} %fusion.36), channel_id=1, source_target_pairs={{0,2},{1,3},{2,0},{3,1},{4,6},{5,7},{6,4},{7,5},{8,10},{9,11},{10,... | collective-permute-start | bytes 1572872 | tf_op jit(solution)/shard_map/ppermute | solution.py:20
  80.1 11.7 %slice-start.6 = ((s8[5767168]{0:T(1024)(128)(4,1)}), s8[4194304]{0:T(1024)(128)(4,1)S(1)}, s32[]{:S(2)}) async-start(s8[5767168]{0:T(1024)(128)(4,1)} %bitcast.115), calls=%async_computation.10 | async-start | bytes 8388608
  93.7 15.0 %collective-permute-start.10 = (bf16[512,512]{1,0:T(8,128)(2,1)}, bf16[512,512]{1,0:T(8,128)(2,1)S(1)}, u32[]{:S(2)}, u32[]{:S(2)}) collective-permute-start(bf16[512,512]{1,0:T(8,128)(2,1)} %fusion.51), channel_id=1, source_target_pairs={{0,3},{1,0},{2,1},{3,2},{4,7},{5,4},{6,5},{7,6},{8,11},{9,8},{10,9... | collective-permute-start | bytes 1572872 | tf_op jit(solution)/shard_map/ppermute | solution.py:20
  95.8 15.9 %collective-permute-start.9 = (bf16[512,512]{1,0:T(8,128)(2,1)}, bf16[512,512]{1,0:T(8,128)(2,1)S(1)}, u32[]{:S(2)}, u32[]{:S(2)}) collective-permute-start(bf16[512,512]{1,0:T(8,128)(2,1)} %fusion.45), channel_id=1, source_target_pairs={{0,1},{1,2},{2,3},{3,0},{4,5},{5,6},{6,7},{7,4},{8,9},{9,10},{10,1... | collective-permute-start | bytes 1572872 | tf_op jit(solution)/shard_map/ppermute | solution.py:20
  98.7 9.9 %copy-start.4 = (f32[256,2]{0,1:T(2,128)S(1)}, f32[256,2]{0,1:T(2,128)}, u32[]{:S(2)}) copy-start(f32[256,2]{0,1:T(2,128)} %param.10) | copy-start | bytes 6148
  98.7 22.3 %collective-permute-start.8 = (bf16[512,512]{1,0:T(8,128)(2,1)}, bf16[512,512]{1,0:T(8,128)(2,1)}, u32[]{:S(2)}, u32[]{:S(2)}) collective-permute-start(bf16[512,512]{1,0:T(8,128)(2,1)} %fusion.39), channel_id=1, source_target_pairs={{0,2},{1,3},{2,0},{3,1},{4,6},{5,7},{6,4},{7,5},{8,10},{9,11},{10,... | collective-permute-start | bytes 1572872 | tf_op jit(solution)/shard_map/ppermute | solution.py:20
  103.3 21.4 %all-to-all-start.1 = ((bf16[32,16,512]{2,1,0:T(8,128)(2,1)}), bf16[32,16,512]{2,1,0:T(8,128)(2,1)S(1)}, u32[]{:S(2)}, u32[]{:S(2)}) async-start(bf16[32,16,512]{2,1,0:T(8,128)(2,1)} %bitcast.12), calls=%async_computation.1 | async-start | bytes 1048576 | tf_op jit(solution)/shard_map/all_to_all | solution.py:126
  124.7 17.7 %all-to-all-start.3 = ((bf16[32,16,512]{2,1,0:T(8,128)(2,1)}), bf16[32,16,512]{2,1,0:T(8,128)(2,1)S(1)}, u32[]{:S(2)}, u32[]{:S(2)}) async-start(bf16[32,16,512]{2,1,0:T(8,128)(2,1)} %bitcast.16), calls=%async_computation.3 | async-start | bytes 1048576 | tf_op jit(solution)/shard_map/all_to_all | solution.py:126
  143.5 2.5 %collective-permute-start.13 = (f32[256]{0:T(256)S(1)}, f32[256]{0:T(256)S(1)}, u32[]{:S(2)}, u32[]{:S(2)}) collective-permute-start(f32[256]{0:T(256)S(1)} %get-tuple-element.20), channel_id=1, source_target_pairs={{0,3},{1,0},{2,1},{3,2},{4,7},{5,4},{6,5},{7,6},{8,11},{9,8},{10,9... | collective-permute-start | bytes 3080 | tf_op jit(solution)/shard_map/ppermute | solution.py:20
  143.6 4.0 %collective-permute-start.12 = (f32[256]{0:T(256)S(1)}, f32[256]{0:T(256)S(1)}, u32[]{:S(2)}, u32[]{:S(2)}) collective-permute-start(f32[256]{0:T(256)S(1)} %get-tuple-element.20), channel_id=1, source_target_pairs={{0,2},{1,3},{2,0},{3,1},{4,6},{5,7},{6,4},{7,5},{8,10},{9,11},{10,... | collective-permute-start | bytes 3080 | tf_op jit(solution)/shard_map/ppermute | solution.py:20
  144.6 3.8 %collective-permute-start.11 = (f32[256]{0:T(256)S(1)}, f32[256]{0:T(256)S(1)}, u32[]{:S(2)}, u32[]{:S(2)}) collective-permute-start(f32[256]{0:T(256)S(1)} %get-tuple-element.20), channel_id=1, source_target_pairs={{0,1},{1,2},{2,3},{3,0},{4,5},{5,6},{6,7},{7,4},{8,9},{9,10},{10,1... | collective-permute-start | bytes 3080 | tf_op jit(solution)/shard_map/ppermute | solution.py:20
  (11 other events, 63.6 us)
